TPU v7x, 512 devices: a whole 4x4x16 slice. The times are simulated.
512 devices in a mesh: line: 32 (over z_lo, x, core), seg: 16 (over z_hi, y).
Axes of the slice: x: 4, y: 4, z: 16 (z_hi: 4, z_lo: 4; z = z_hi * 4 + z_lo), core: 2. Of those that a mesh axis runs over, the one named last changes fastest.
Arguments:
- right_side: float32 [32, 128, 96, 128], P('line', 'seg'), may hold values from -24 to 24
- band_blocks: bfloat16 [32, 128, 4, 96, 96], P('line', 'seg')
- knot_pairs: int32 [32, 16, 6, 2, 2], P('line', 'seg'), may hold values from 0 to 7
- pair_counts: int32 [32, 16, 6], P('line', 'seg'), may hold values from 1 to 2, as said below
- cross_blocks: bfloat16 [32, 16, 6, 2, 96, 96], P('line', 'seg'), may hold values from -0.359375 to 0.359375
Outputs:
- solution: float32 [32, 128, 96, 128], P('line', 'seg')
Inputs may be any that keep to these rules, and one draw needn't show every extreme that they name: `knot_pairs`: entry s of bucket b counts only if s < pair_counts of that bucket; other entries are unused. `pair_counts`: every bucket holds at least one pair, and in every draw some line and segment has all buckets full.
All inputs are finite; a program needn't handle non-finite values.
Results may differ from a plain program's by a relative error of at most 0.0028.
Values may be sent and summed in bfloat16 or wider, within the bound.
No kernel may reach another device: no remote copies, remote signals or barrier semaphores. Data moves between devices by JAX's collectives and lax.ppermute only.
A program may use at most 64 MiB of HBM per device.

v0:
```python
import jax
import jax.numpy as jnp
from jax import lax
from jax.sharding import PartitionSpec as P

ITERS = 3


LO_BOUND = 1.5
HI_BOUND = 12.0


def passed_along(value, axis, steps):
    count = lax.axis_size(axis)
    initial, last = (max(0, -steps), min(count, count - steps))
    return lax.ppermute(value, axis, [(source, source + steps) for source in range(initial, last)])


def passed_along_2(x, axis, by):
    count = lax.axis_size(axis)
    return lax.ppermute(x, axis, [(i, (i + by) % count) for i in range(count)])


def padded(block, sides, width):
    for axis, dim in sides:
        count = lax.axis_size(axis)
        forward = [(i, i + 1) for i in range(count - 1)]
        backward = [(target, source) for source, target in forward]
        low = lax.ppermute(
            lax.slice_in_dim(block, block.shape[dim] - width, None, axis=dim), axis, forward
        )
        high = lax.ppermute(lax.slice_in_dim(block, 0, width, axis=dim), axis, backward)
        block = jnp.concatenate([low, block, high], axis=dim)
    return block


def body(right_side, band_blocks, knot_pairs, pair_counts, cross_blocks):
    right_rows = right_side[0]
    blocks = band_blocks[0]
    my_pairs = knot_pairs[0, 0]
    used_count = pair_counts[0, 0]
    pair_coupling_term = cross_blocks[0, 0]
    count_of_knots = right_rows.shape[0]
    buckets = my_pairs.shape[0]
    slot_count = my_pairs.shape[1]
    group_span = buckets // 2 + 1
    offsets = [
        b - (group_span - 1) if b < group_span - 1 else b - group_span + 2 for b in range(buckets)
    ]
    boundary_blocks = passed_along(blocks[count_of_knots - 3 :], "seg", 1)
    lower_blocks = jnp.concatenate([boundary_blocks, blocks], axis=0)
    slot_ids = jnp.arange(slot_count, dtype=jnp.int32)
    asked_knots = []
    keep_masks = []
    for bucket, shift_by in enumerate(offsets):
        asked_knots.append(passed_along_2(my_pairs[bucket, :, 1], "line", shift_by))
        keep_masks.append((slot_ids < used_count[bucket]).astype(jnp.bfloat16)[:, None, None])
    center = (HI_BOUND + LO_BOUND) / 2.0
    radius = (HI_BOUND - LO_BOUND) / 2.0
    coeff = radius / center
    solution = jnp.zeros(right_rows.shape, jnp.float32)
    residual = right_rows
    direction = right_rows / center
    for turn in range(ITERS):
        probe_bf = direction.astype(jnp.bfloat16)
        solution = solution + direction
        extended = padded(probe_bf, (("seg", 0),), 3)
        summed = jnp.zeros(probe_bf.shape, jnp.float32)
        for step in range(4):
            summed = summed + jnp.einsum(
                "kab,kbr->kar",
                blocks[:, step],
                extended[3 + step : 3 + step + count_of_knots],
                preferred_element_type=jnp.float32,
            )
        for step in range(1, 4):
            summed = summed + jnp.einsum(
                "kba,kbr->kar",
                lower_blocks[3 - step : 3 - step + count_of_knots, step],
                extended[3 - step : 3 - step + count_of_knots],
                preferred_element_type=jnp.float32,
            )
        targets = []
        entry_values = []
        for apply_bucket, apply_shift_by in enumerate(offsets):
            answer_rows = jnp.take(probe_bf, asked_knots[apply_bucket], axis=0)
            fetched_rows = (
                passed_along_2(answer_rows, "line", -apply_shift_by) * keep_masks[apply_bucket]
            )
            entry_values.append(
                jnp.einsum(
                    "dqp,dpc->dqc",
                    pair_coupling_term[apply_bucket],
                    fetched_rows,
                    preferred_element_type=jnp.float32,
                )
            )
            targets.append(my_pairs[apply_bucket, :, 0])
            resident_rows = (
                jnp.take(probe_bf, my_pairs[apply_bucket, :, 0], axis=0) * keep_masks[apply_bucket]
            )
            product = jnp.einsum(
                "edu,edq->euq",
                pair_coupling_term[apply_bucket],
                resident_rows,
                preferred_element_type=jnp.float32,
            )
            entry_values.append(
                passed_along_2(product.astype(jnp.bfloat16), "line", apply_shift_by).astype(
                    product.dtype
                )
            )
            targets.append(asked_knots[apply_bucket])
        target_index = jnp.concatenate(targets, axis=0)
        target_values = jnp.concatenate(entry_values, axis=0)
        onehot = (
            jnp.arange(count_of_knots, dtype=jnp.int32)[:, None] == target_index[None, :]
        ).astype(jnp.float32)
        residual = residual - (
            summed
            + jnp.einsum("ks,spr->kpr", onehot, target_values, precision=lax.Precision.HIGHEST)
        )
        coeff_next = 1.0 / (2.0 * center / radius - coeff)
        direction = coeff_next * coeff * direction + 2.0 * coeff_next / radius * residual
        coeff = coeff_next
    return (solution + direction)[None]


def solution(mesh):
    return jax.shard_map(
        body,
        mesh=mesh,
        in_specs=(
            P("line", "seg", None, None),
            P("line", "seg", None, None, None),
            P("line", "seg", None, None, None),
            P("line", "seg", None),
            P("line", "seg", None, None, None, None),
        ),
        out_specs=P("line", "seg", None, None),
        check_vma=False,
    )
```

profile of v0, /device:TPU:24, one launch (start us, length us, event | category | flops | bytes accessed | tf_op | source)
XLA Modules:
  0.0 331.2 jit_solution(3124836291106836818)
XLA Ops:
  1.7 2.8 collective-permute-start.8
  4.6 3.4 %collective-permute-start.7 = (s32[2]{0:T(128)S(1)}, s32[2]{0:T(128)S(1)}, u32[]{:S(2)}, u32[]{:S(2)}) collective-permute-start(s32[2]{0:T(128)S(1)} %get-tuple-element.8), channel_id=1, source_target_pairs={{0,32},{16,48},{32,64},{48,80},{64,96},{80,112},{96,128},{112,144}... | collective-permute-start | bytes 32 | tf_op jit(solution)/shard_map/ppermute | solution.py:21
  8.0 2.9 collective-permute-start.6
  10.9 6.9 %collective-permute-start.5 = (s32[2]{0:T(128)S(1)}, s32[2]{0:T(128)S(1)}, u32[]{:S(2)}, u32[]{:S(2)}) collective-permute-start(s32[2]{0:T(128)S(1)} %get-tuple-element.12), channel_id=1, source_target_pairs={{0,496},{16,0},{32,16},{48,32},{64,48},{80,64},{96,80},{112,96},{1... | collective-permute-start | bytes 32 | tf_op jit(solution)/shard_map/ppermute | solution.py:21
  17.8 2.3 collective-permute-start.4
  34.4 2.9 collective-permute-start.3
  37.4 6.6 %collective-permute-start.10 = (bf16[2,96,128]{2,0,1:T(2,128)(2,1)S(1)}, bf16[2,96,128]{2,0,1:T(2,128)(2,1)S(1)}, u32[]{:S(2)}, u32[]{:S(2)}) collective-permute-start(bf16[2,96,128]{2,0,1:T(2,128)(2,1)S(1)} %bitcast.346), channel_id=1, source_target_pairs={{0,464},{16,480},{32,496},{48,0},{64,16},{80,32},{96,48},{112,64},... | collective-permute-start | bytes 147464 | tf_op jit(solution)/shard_map/ppermute | solution.py:21
  44.0 2.9 collective-permute-start.12
  47.0 1.9 collective-permute-start.14
  49.0 2.4 collective-permute-start.16
  55.0 2.5 collective-permute-start.9
  60.3 4.3 %collective-permute-done.9 = bf16[2,96,128]{2,1,0:T(8,128)(2,1)S(1)} collective-permute-done((bf16[2,96,128]{2,1,0:T(8,128)(2,1)S(1)}, bf16[2,96,128]{2,1,0:T(8,128)(2,1)S(1)}, u32[]{:S(2)}, u32[]{:S(2)}) %collective-permute-start.9) | collective-permute-done | bytes 49184 | tf_op jit(solution)/shard_map/ppermute | solution.py:21
  64.6 3.2 collective-permute-start.11
  68.0 6.5 %collective-permute-done.11 = bf16[2,96,128]{2,1,0:T(8,128)(2,1)S(1)} collective-permute-done((bf16[2,96,128]{2,1,0:T(8,128)(2,1)S(1)}, bf16[2,96,128]{2,1,0:T(8,128)(2,1)S(1)}, u32[]{:S(2)}, u32[]{:S(2)}) %collective-permute-start.11) | collective-permute-done | bytes 49184 | tf_op jit(solution)/shard_map/ppermute | solution.py:21
  76.7 7.2 %collective-permute-done.13 = bf16[2,96,128]{2,1,0:T(8,128)(2,1)S(1)} collective-permute-done((bf16[2,96,128]{2,1,0:T(8,128)(2,1)S(1)}, bf16[2,96,128]{2,1,0:T(8,128)(2,1)S(1)}, u32[]{:S(2)}, u32[]{:S(2)}) %collective-permute-start.13) | collective-permute-done | bytes 49184 | tf_op jit(solution)/shard_map/ppermute | solution.py:21
  89.6 3.8 %collective-permute-done.17 = bf16[2,96,128]{2,1,0:T(8,128)(2,1)S(1)} collective-permute-done((bf16[2,96,128]{2,1,0:T(8,128)(2,1)S(1)}, bf16[2,96,128]{2,1,0:T(8,128)(2,1)S(1)}, u32[]{:S(2)}, u32[]{:S(2)}) %collective-permute-start.17) | collective-permute-done | bytes 49184 | tf_op jit(solution)/shard_map/ppermute | solution.py:21
  93.4 6.1 %collective-permute-start.19 = (bf16[2,96,128]{2,1,0:T(8,128)(2,1)S(1)}, bf16[2,96,128]{2,1,0:T(8,128)(2,1)S(1)}, u32[]{:S(2)}, u32[]{:S(2)}) collective-permute-start(bf16[2,96,128]{2,1,0:T(8,128)(2,1)S(1)} %broadcast_select_fusion.2), channel_id=1, source_target_pairs={{0,464},{16,480},{32,496},{48,0},{64,16},{80,32},{96,48},{112,64},... | collective-permute-start | bytes 147464 | tf_op jit(solution)/shard_map/ppermute | solution.py:21
  99.8 6.9 %collective-permute-start.18 = (bf16[2,96,128]{2,0,1:T(2,128)(2,1)S(1)}, bf16[2,96,128]{2,0,1:T(2,128)(2,1)S(1)}, u32[]{:S(2)}, u32[]{:S(2)}) collective-permute-start(bf16[2,96,128]{2,0,1:T(2,128)(2,1)S(1)} %bitcast.342), channel_id=1, source_target_pairs={{0,32},{16,48},{32,64},{48,80},{64,96},{80,112},{96,128},{112,144}... | collective-permute-start | bytes 147464 | tf_op jit(solution)/shard_map/ppermute | solution.py:21
  106.9 1.9 collective-permute-start.20
  110.2 2.6 collective-permute-start
  112.9 9.2 %collective-permute-start.2 = (bf16[3,96,128]{2,1,0:T(8,128)(2,1)}, bf16[3,96,128]{2,1,0:T(8,128)(2,1)S(1)}, u32[]{:S(2)}, u32[]{:S(2)}) collective-permute-start(bf16[3,96,128]{2,1,0:T(8,128)(2,1)} %get-tuple-element.28), channel_id=1, source_target_pairs={{0,1},{1,2},{2,3},{3,4},{4,5},{5,6},{6,7},{7,8},{8,9},{9,10},{10,1... | collective-permute-start | bytes 221192 | tf_op jit(solution)/shard_map/ppermute | solution.py:29
  122.1 2.7 collective-permute-start.1
  125.5 3.3 concatenate.54
  147.3 19.0 %collective-permute-start.24 = (bf16[2,96,128]{2,0,1:T(2,128)(2,1)S(1)}, bf16[2,96,128]{2,0,1:T(2,128)(2,1)S(1)}, u32[]{:S(2)}, u32[]{:S(2)}) collective-permute-start(bf16[2,96,128]{2,0,1:T(2,128)(2,1)S(1)} %bitcast.358), channel_id=1, source_target_pairs={{0,464},{16,480},{32,496},{48,0},{64,16},{80,32},{96,48},{112,64},... | collective-permute-start | bytes 147464 | tf_op jit(solution)/shard_map/ppermute | solution.py:21
  166.4 1.9 collective-permute-start.25
  168.3 7.8 %collective-permute-start.26 = (bf16[2,96,128]{2,0,1:T(2,128)(2,1)S(1)}, bf16[2,96,128]{2,0,1:T(2,128)(2,1)S(1)}, u32[]{:S(2)}, u32[]{:S(2)}) collective-permute-start(bf16[2,96,128]{2,0,1:T(2,128)(2,1)S(1)} %bitcast.356), channel_id=1, source_target_pairs={{0,480},{16,496},{32,0},{48,16},{64,32},{80,48},{96,64},{112,80},{... | collective-permute-start | bytes 147464 | tf_op jit(solution)/shard_map/ppermute | solution.py:21
  176.1 1.9 collective-permute-start.27
  178.1 7.5 %collective-permute-start.28 = (bf16[2,96,128]{2,0,1:T(2,128)(2,1)S(1)}, bf16[2,96,128]{2,0,1:T(2,128)(2,1)S(1)}, u32[]{:S(2)}, u32[]{:S(2)}) collective-permute-start(bf16[2,96,128]{2,0,1:T(2,128)(2,1)S(1)} %bitcast.354), channel_id=1, source_target_pairs={{0,496},{16,0},{32,16},{48,32},{64,48},{80,64},{96,80},{112,96},{1... | collective-permute-start | bytes 147464 | tf_op jit(solution)/shard_map/ppermute | solution.py:21
  185.8 1.9 collective-permute-start.29
  188.0 2.4 collective-permute-start.30
  192.8 3.8 %collective-permute-done.31 = bf16[2,96,128]{2,1,0:T(8,128)(2,1)S(1)} collective-permute-done((bf16[2,96,128]{2,1,0:T(8,128)(2,1)S(1)}, bf16[2,96,128]{2,1,0:T(8,128)(2,1)S(1)}, u32[]{:S(2)}, u32[]{:S(2)}) %collective-permute-start.31) | collective-permute-done | bytes 49184 | tf_op jit(solution)/shard_map/ppermute | solution.py:21
  196.6 5.6 %collective-permute-start.33 = (bf16[2,96,128]{2,1,0:T(8,128)(2,1)S(1)}, bf16[2,96,128]{2,1,0:T(8,128)(2,1)S(1)}, u32[]{:S(2)}, u32[]{:S(2)}) collective-permute-start(bf16[2,96,128]{2,1,0:T(8,128)(2,1)S(1)} %broadcast_select_fusion.1), channel_id=1, source_target_pairs={{0,464},{16,480},{32,496},{48,0},{64,16},{80,32},{96,48},{112,64},... | collective-permute-start | bytes 147464 | tf_op jit(solution)/shard_map/ppermute | solution.py:21
  202.5 6.9 %collective-permute-start.32 = (bf16[2,96,128]{2,0,1:T(2,128)(2,1)S(1)}, bf16[2,96,128]{2,0,1:T(2,128)(2,1)S(1)}, u32[]{:S(2)}, u32[]{:S(2)}) collective-permute-start(bf16[2,96,128]{2,0,1:T(2,128)(2,1)S(1)} %bitcast.350), channel_id=1, source_target_pairs={{0,32},{16,48},{32,64},{48,80},{64,96},{80,112},{96,128},{112,144}... | collective-permute-start | bytes 147464 | tf_op jit(solution)/shard_map/ppermute | solution.py:21
  209.5 1.9 collective-permute-start.34
  217.8 10.6 %collective-permute-start.22 = (bf16[3,96,128]{2,1,0:T(8,128)(2,1)}, bf16[3,96,128]{2,1,0:T(8,128)(2,1)S(1)}, u32[]{:S(2)}, u32[]{:S(2)}) collective-permute-start(bf16[3,96,128]{2,1,0:T(8,128)(2,1)} %get-tuple-element.26), channel_id=1, source_target_pairs={{0,1},{1,2},{2,3},{3,4},{4,5},{5,6},{6,7},{7,8},{8,9},{9,10},{10,1... | collective-permute-start | bytes 221192 | tf_op jit(solution)/shard_map/ppermute | solution.py:29
  229.1 3.5 %concatenate.57 = f32[24,96,128]{2,0,1:T(8,128)S(1)} concatenate(f32[2,96,128]{2,0,1:T(2,128)} %bitcast.327, bf16[2,96,128]{2,0,1:T(2,128)(2,1)} %copy-done.18, f32[2,96,128]{2,0,1:T(2,128)} %bitcast.330, bf16[2,96,128]{2,0,1:T(2,128)(2,1)} %copy-done.20, f32[2,96,128]{2,0,1:T(2,128)} %bitcast.332, bf16[2,96,128]{2,0,1:T(2,128)(2,1)} %copy-done.22, f32[2,96,128]{2,0,1:T(2,128)} %bitcast.334, ...), dimensions={0} | concatenate | bytes 2064384 | tf_op jit(solution)/shard_map/concatenate | solution.py:115
  250.9 7.8 %collective-permute-start.38 = (bf16[2,96,128]{2,0,1:T(2,128)(2,1)S(1)}, bf16[2,96,128]{2,0,1:T(2,128)(2,1)S(1)}, u32[]{:S(2)}, u32[]{:S(2)}) collective-permute-start(bf16[2,96,128]{2,0,1:T(2,128)(2,1)S(1)} %bitcast.357), channel_id=1, source_target_pairs={{0,464},{16,480},{32,496},{48,0},{64,16},{80,32},{96,48},{112,64},... | collective-permute-start | bytes 147464 | tf_op jit(solution)/shard_map/ppermute | solution.py:21
  258.7 1.9 collective-permute-start.39
  260.7 7.8 %collective-permute-start.40 = (bf16[2,96,128]{2,0,1:T(2,128)(2,1)S(1)}, bf16[2,96,128]{2,0,1:T(2,128)(2,1)S(1)}, u32[]{:S(2)}, u32[]{:S(2)}) collective-permute-start(bf16[2,96,128]{2,0,1:T(2,128)(2,1)S(1)} %bitcast.355), channel_id=1, source_target_pairs={{0,480},{16,496},{32,0},{48,16},{64,32},{80,48},{96,64},{112,80},{... | collective-permute-start | bytes 147464 | tf_op jit(solution)/shard_map/ppermute | solution.py:21
  270.4 7.5 %collective-permute-start.42 = (bf16[2,96,128]{2,0,1:T(2,128)(2,1)S(1)}, bf16[2,96,128]{2,0,1:T(2,128)(2,1)S(1)}, u32[]{:S(2)}, u32[]{:S(2)}) collective-permute-start(bf16[2,96,128]{2,0,1:T(2,128)(2,1)S(1)} %bitcast.353), channel_id=1, source_target_pairs={{0,496},{16,0},{32,16},{48,32},{64,48},{80,64},{96,80},{112,96},{1... | collective-permute-start | bytes 147464 | tf_op jit(solution)/shard_map/ppermute | solution.py:21
  280.4 2.4 collective-permute-start.44
  285.2 3.8 %collective-permute-done.45 = bf16[2,96,128]{2,1,0:T(8,128)(2,1)S(1)} collective-permute-done((bf16[2,96,128]{2,1,0:T(8,128)(2,1)S(1)}, bf16[2,96,128]{2,1,0:T(8,128)(2,1)S(1)}, u32[]{:S(2)}, u32[]{:S(2)}) %collective-permute-start.45) | collective-permute-done | bytes 49184 | tf_op jit(solution)/shard_map/ppermute | solution.py:21
  289.0 5.6 %collective-permute-start.47 = (bf16[2,96,128]{2,1,0:T(8,128)(2,1)S(1)}, bf16[2,96,128]{2,1,0:T(8,128)(2,1)S(1)}, u32[]{:S(2)}, u32[]{:S(2)}) collective-permute-start(bf16[2,96,128]{2,1,0:T(8,128)(2,1)S(1)} %broadcast_select_fusion), channel_id=1, source_target_pairs={{0,464},{16,480},{32,496},{48,0},{64,16},{80,32},{96,48},{112,64},... | collective-permute-start | bytes 147464 | tf_op jit(solution)/shard_map/ppermute | solution.py:21
  294.9 6.9 %collective-permute-start.46 = (bf16[2,96,128]{2,0,1:T(2,128)(2,1)S(1)}, bf16[2,96,128]{2,0,1:T(2,128)(2,1)S(1)}, u32[]{:S(2)}, u32[]{:S(2)}) collective-permute-start(bf16[2,96,128]{2,0,1:T(2,128)(2,1)S(1)} %bitcast.349), channel_id=1, source_target_pairs={{0,32},{16,48},{32,64},{48,80},{64,96},{80,112},{96,128},{112,144}... | collective-permute-start | bytes 147464 | tf_op jit(solution)/shard_map/ppermute | solution.py:21
  301.8 1.9 collective-permute-start.48
  308.9 9.9 %collective-permute-start.36 = (bf16[3,96,128]{2,1,0:T(8,128)(2,1)}, bf16[3,96,128]{2,1,0:T(8,128)(2,1)}, u32[]{:S(2)}, u32[]{:S(2)}) collective-permute-start(bf16[3,96,128]{2,1,0:T(8,128)(2,1)} %get-tuple-element.24), channel_id=1, source_target_pairs={{0,1},{1,2},{2,3},{3,4},{4,5},{5,6},{6,7},{7,8},{8,9},{9,10},{10,1... | collective-permute-start | bytes 221192 | tf_op jit(solution)/shard_map/ppermute | solution.py:29
  319.6 3.4 %concatenate.60 = f32[24,96,128]{2,0,1:T(8,128)S(1)} concatenate(f32[2,96,128]{2,0,1:T(2,128)S(1)} %bitcast.328, bf16[2,96,128]{2,0,1:T(2,128)(2,1)} %copy-done.17, f32[2,96,128]{2,0,1:T(2,128)S(1)} %bitcast.331, bf16[2,96,128]{2,0,1:T(2,128)(2,1)} %copy-done.19, f32[2,96,128]{2,0,1:T(2,128)} %bitcast.333, bf16[2,96,128]{2,0,1:T(2,128)(2,1)} %copy-done.21, ...), dimensions={0} | concatenate | bytes 2064384 | tf_op jit(solution)/shard_map/concatenate | solution.py:115
  329.3 1.9 fusion.24
  (445 shorter events, 96.6 us)
Async XLA Ops:
  1.7 32.7 %collective-permute-start.8 = (s32[2]{0:T(128)S(1)}, s32[2]{0:T(128)S(1)}, u32[]{:S(2)}, u32[]{:S(2)}) collective-permute-start(s32[2]{0:T(128)S(1)} %get-tuple-element.7), channel_id=1, source_target_pairs={{0,48},{16,64},{32,80},{48,96},{64,112},{80,128},{96,144},{112,160... | collective-permute-start | bytes 32 | tf_op jit(solution)/shard_map/ppermute | solution.py:21
  4.6 32.8 %collective-permute-start.7 = (s32[2]{0:T(128)S(1)}, s32[2]{0:T(128)S(1)}, u32[]{:S(2)}, u32[]{:S(2)}) collective-permute-start(s32[2]{0:T(128)S(1)} %get-tuple-element.8), channel_id=1, source_target_pairs={{0,32},{16,48},{32,64},{48,80},{64,96},{80,112},{96,128},{112,144}... | collective-permute-start | bytes 32 | tf_op jit(solution)/shard_map/ppermute | solution.py:21
  8.0 36.1 %collective-permute-start.6 = (s32[2]{0:T(128)S(1)}, s32[2]{0:T(128)S(1)}, u32[]{:S(2)}, u32[]{:S(2)}) collective-permute-start(s32[2]{0:T(128)S(1)} %get-tuple-element.10), channel_id=1, source_target_pairs={{0,16},{16,32},{32,48},{48,64},{64,80},{80,96},{96,112},{112,128},... | collective-permute-start | bytes 32 | tf_op jit(solution)/shard_map/ppermute | solution.py:21
  10.9 36.1 %collective-permute-start.5 = (s32[2]{0:T(128)S(1)}, s32[2]{0:T(128)S(1)}, u32[]{:S(2)}, u32[]{:S(2)}) collective-permute-start(s32[2]{0:T(128)S(1)} %get-tuple-element.12), channel_id=1, source_target_pairs={{0,496},{16,0},{32,16},{48,32},{64,48},{80,64},{96,80},{112,96},{1... | collective-permute-start | bytes 32 | tf_op jit(solution)/shard_map/ppermute | solution.py:21
  17.8 31.2 %collective-permute-start.4 = (s32[2]{0:T(128)S(1)}, s32[2]{0:T(128)S(1)}, u32[]{:S(2)}, u32[]{:S(2)}) collective-permute-start(s32[2]{0:T(128)S(1)} %get-tuple-element.14), channel_id=1, source_target_pairs={{0,480},{16,496},{32,0},{48,16},{64,32},{80,48},{96,64},{112,80},{... | collective-permute-start | bytes 32 | tf_op jit(solution)/shard_map/ppermute | solution.py:21
  34.4 17.0 %collective-permute-start.3 = (s32[2]{0:T(128)S(1)}, s32[2]{0:T(128)S(1)}, u32[]{:S(2)}, u32[]{:S(2)}) collective-permute-start(s32[2]{0:T(128)S(1)} %get-tuple-element.16), channel_id=1, source_target_pairs={{0,464},{16,480},{32,496},{48,0},{64,16},{80,32},{96,48},{112,64},... | collective-permute-start | bytes 32 | tf_op jit(solution)/shard_map/ppermute | solution.py:21
  37.4 62.5 %collective-permute-start.10 = (bf16[2,96,128]{2,0,1:T(2,128)(2,1)S(1)}, bf16[2,96,128]{2,0,1:T(2,128)(2,1)S(1)}, u32[]{:S(2)}, u32[]{:S(2)}) collective-permute-start(bf16[2,96,128]{2,0,1:T(2,128)(2,1)S(1)} %bitcast.346), channel_id=1, source_target_pairs={{0,464},{16,480},{32,496},{48,0},{64,16},{80,32},{96,48},{112,64},... | collective-permute-start | bytes 147464 | tf_op jit(solution)/shard_map/ppermute | solution.py:21
  44.0 66.2 %collective-permute-start.12 = (bf16[2,96,128]{2,0,1:T(2,128)(2,1)S(1)}, bf16[2,96,128]{2,0,1:T(2,128)(2,1)S(1)}, u32[]{:S(2)}, u32[]{:S(2)}) collective-permute-start(bf16[2,96,128]{2,0,1:T(2,128)(2,1)S(1)} %bitcast.345), channel_id=1, source_target_pairs={{0,480},{16,496},{32,0},{48,16},{64,32},{80,48},{96,64},{112,80},{... | collective-permute-start | bytes 147464 | tf_op jit(solution)/shard_map/ppermute | solution.py:21
  47.0 65.8 %collective-permute-start.14 = (bf16[2,96,128]{2,0,1:T(2,128)(2,1)S(1)}, bf16[2,96,128]{2,0,1:T(2,128)(2,1)S(1)}, u32[]{:S(2)}, u32[]{:S(2)}) collective-permute-start(bf16[2,96,128]{2,0,1:T(2,128)(2,1)S(1)} %bitcast.344), channel_id=1, source_target_pairs={{0,496},{16,0},{32,16},{48,32},{64,48},{80,64},{96,80},{112,96},{1... | collective-permute-start | bytes 147464 | tf_op jit(solution)/shard_map/ppermute | solution.py:21
  49.0 73.1 %collective-permute-start.16 = (bf16[2,96,128]{2,0,1:T(2,128)(2,1)S(1)}, bf16[2,96,128]{2,0,1:T(2,128)(2,1)S(1)}, u32[]{:S(2)}, u32[]{:S(2)}) collective-permute-start(bf16[2,96,128]{2,0,1:T(2,128)(2,1)S(1)} %bitcast.343), channel_id=1, source_target_pairs={{0,16},{16,32},{32,48},{48,64},{64,80},{80,96},{96,112},{112,128},... | collective-permute-start | bytes 147464 | tf_op jit(solution)/shard_map/ppermute | solution.py:21
  55.0 9.6 %collective-permute-start.9 = (bf16[2,96,128]{2,1,0:T(8,128)(2,1)S(1)}, bf16[2,96,128]{2,1,0:T(8,128)(2,1)S(1)}, u32[]{:S(2)}, u32[]{:S(2)}) collective-permute-start(bf16[2,96,128]{2,1,0:T(8,128)(2,1)S(1)} %broadcast_select_fusion.17), channel_id=1, source_target_pairs={{0,48},{16,64},{32,80},{48,96},{64,112},{80,128},{96,144},{112,160... | collective-permute-start | bytes 147464 | tf_op jit(solution)/shard_map/ppermute | solution.py:21
  64.6 10.0 %collective-permute-start.11 = (bf16[2,96,128]{2,1,0:T(8,128)(2,1)S(1)}, bf16[2,96,128]{2,1,0:T(8,128)(2,1)S(1)}, u32[]{:S(2)}, u32[]{:S(2)}) collective-permute-start(bf16[2,96,128]{2,1,0:T(8,128)(2,1)S(1)} %broadcast_select_fusion.14), channel_id=1, source_target_pairs={{0,32},{16,48},{32,64},{48,80},{64,96},{80,112},{96,128},{112,144}... | collective-permute-start | bytes 147464 | tf_op jit(solution)/shard_map/ppermute | solution.py:21
  74.5 9.3 %collective-permute-start.13 = (bf16[2,96,128]{2,1,0:T(8,128)(2,1)S(1)}, bf16[2,96,128]{2,1,0:T(8,128)(2,1)S(1)}, u32[]{:S(2)}, u32[]{:S(2)}) collective-permute-start(bf16[2,96,128]{2,1,0:T(8,128)(2,1)S(1)} %broadcast_select_fusion.11), channel_id=1, source_target_pairs={{0,16},{16,32},{32,48},{48,64},{64,80},{80,96},{96,112},{112,128},... | collective-permute-start | bytes 147464 | tf_op jit(solution)/shard_map/ppermute | solution.py:21
  87.5 6.0 %collective-permute-start.17 = (bf16[2,96,128]{2,1,0:T(8,128)(2,1)S(1)}, bf16[2,96,128]{2,1,0:T(8,128)(2,1)S(1)}, u32[]{:S(2)}, u32[]{:S(2)}) collective-permute-start(bf16[2,96,128]{2,1,0:T(8,128)(2,1)S(1)} %broadcast_select_fusion.5), channel_id=1, source_target_pairs={{0,480},{16,496},{32,0},{48,16},{64,32},{80,48},{96,64},{112,80},{... | collective-permute-start | bytes 147464 | tf_op jit(solution)/shard_map/ppermute | solution.py:21
  93.4 13.4 %collective-permute-start.19 = (bf16[2,96,128]{2,1,0:T(8,128)(2,1)S(1)}, bf16[2,96,128]{2,1,0:T(8,128)(2,1)S(1)}, u32[]{:S(2)}, u32[]{:S(2)}) collective-permute-start(bf16[2,96,128]{2,1,0:T(8,128)(2,1)S(1)} %broadcast_select_fusion.2), channel_id=1, source_target_pairs={{0,464},{16,480},{32,496},{48,0},{64,16},{80,32},{96,48},{112,64},... | collective-permute-start | bytes 147464 | tf_op jit(solution)/shard_map/ppermute | solution.py:21
  99.8 25.0 %collective-permute-start.18 = (bf16[2,96,128]{2,0,1:T(2,128)(2,1)S(1)}, bf16[2,96,128]{2,0,1:T(2,128)(2,1)S(1)}, u32[]{:S(2)}, u32[]{:S(2)}) collective-permute-start(bf16[2,96,128]{2,0,1:T(2,128)(2,1)S(1)} %bitcast.342), channel_id=1, source_target_pairs={{0,32},{16,48},{32,64},{48,80},{64,96},{80,112},{96,128},{112,144}... | collective-permute-start | bytes 147464 | tf_op jit(solution)/shard_map/ppermute | solution.py:21
  106.9 18.0 %collective-permute-start.20 = (bf16[2,96,128]{2,0,1:T(2,128)(2,1)S(1)}, bf16[2,96,128]{2,0,1:T(2,128)(2,1)S(1)}, u32[]{:S(2)}, u32[]{:S(2)}) collective-permute-start(bf16[2,96,128]{2,0,1:T(2,128)(2,1)S(1)} %bitcast.341), channel_id=1, source_target_pairs={{0,48},{16,64},{32,80},{48,96},{64,112},{80,128},{96,144},{112,160... | collective-permute-start | bytes 147464 | tf_op jit(solution)/shard_map/ppermute | solution.py:21
  110.2 19.1 %collective-permute-start = (bf16[3,96,128]{2,1,0:T(8,128)(2,1)}, bf16[3,96,128]{2,1,0:T(8,128)(2,1)S(1)}, u32[]{:S(2)}, u32[]{:S(2)}) collective-permute-start(bf16[3,96,128]{2,1,0:T(8,128)(2,1)} %get-tuple-element.27), channel_id=1, source_target_pairs={{1,0},{2,1},{3,2},{4,3},{5,4},{6,5},{7,6},{8,7},{9,8},{10,9},{11,1... | collective-permute-start | bytes 221192 | tf_op jit(solution)/shard_map/ppermute | solution.py:32
  112.9 19.2 %collective-permute-start.2 = (bf16[3,96,128]{2,1,0:T(8,128)(2,1)}, bf16[3,96,128]{2,1,0:T(8,128)(2,1)S(1)}, u32[]{:S(2)}, u32[]{:S(2)}) collective-permute-start(bf16[3,96,128]{2,1,0:T(8,128)(2,1)} %get-tuple-element.28), channel_id=1, source_target_pairs={{0,1},{1,2},{2,3},{3,4},{4,5},{5,6},{6,7},{7,8},{8,9},{9,10},{10,1... | collective-permute-start | bytes 221192 | tf_op jit(solution)/shard_map/ppermute | solution.py:29
  122.1 8.9 %collective-permute-start.1 = (bf16[3,4,96,96]{3,2,0,1:T(8,128)(2,1)}, bf16[3,4,96,96]{3,2,0,1:T(8,128)(2,1)}, u32[]{:S(2)}, u32[]{:S(2)}) collective-permute-start(bf16[3,4,96,96]{3,2,0,1:T(8,128)(2,1)} %slice_bitcast_fusion), channel_id=1, source_target_pairs={{0,1},{1,2},{2,3},{3,4},{4,5},{5,6},{6,7},{7,8},{8,9},{9,10},{10,1... | collective-permute-start | bytes 663560 | tf_op jit(solution)/shard_map/ppermute | solution.py:16
  145.0 33.0 %collective-permute-start.23 = (bf16[2,96,128]{2,1,0:T(8,128)(2,1)S(1)}, bf16[2,96,128]{2,1,0:T(8,128)(2,1)S(1)}, u32[]{:S(2)}, u32[]{:S(2)}) collective-permute-start(bf16[2,96,128]{2,1,0:T(8,128)(2,1)S(1)} %broadcast_select_fusion.16), channel_id=1, source_target_pairs={{0,48},{16,64},{32,80},{48,96},{64,112},{80,128},{96,144},{112,160... | collective-permute-start | bytes 147464 | tf_op jit(solution)/shard_map/ppermute | solution.py:21
  147.3 55.2 %collective-permute-start.24 = (bf16[2,96,128]{2,0,1:T(2,128)(2,1)S(1)}, bf16[2,96,128]{2,0,1:T(2,128)(2,1)S(1)}, u32[]{:S(2)}, u32[]{:S(2)}) collective-permute-start(bf16[2,96,128]{2,0,1:T(2,128)(2,1)S(1)} %bitcast.358), channel_id=1, source_target_pairs={{0,464},{16,480},{32,496},{48,0},{64,16},{80,32},{96,48},{112,64},... | collective-permute-start | bytes 147464 | tf_op jit(solution)/shard_map/ppermute | solution.py:21
  166.4 19.5 %collective-permute-start.25 = (bf16[2,96,128]{2,1,0:T(8,128)(2,1)S(1)}, bf16[2,96,128]{2,1,0:T(8,128)(2,1)S(1)}, u32[]{:S(2)}, u32[]{:S(2)}) collective-permute-start(bf16[2,96,128]{2,1,0:T(8,128)(2,1)S(1)} %broadcast_select_fusion.13), channel_id=1, source_target_pairs={{0,32},{16,48},{32,64},{48,80},{64,96},{80,112},{96,128},{112,144}... | collective-permute-start | bytes 147464 | tf_op jit(solution)/shard_map/ppermute | solution.py:21
  168.3 47.6 %collective-permute-start.26 = (bf16[2,96,128]{2,0,1:T(2,128)(2,1)S(1)}, bf16[2,96,128]{2,0,1:T(2,128)(2,1)S(1)}, u32[]{:S(2)}, u32[]{:S(2)}) collective-permute-start(bf16[2,96,128]{2,0,1:T(2,128)(2,1)S(1)} %bitcast.356), channel_id=1, source_target_pairs={{0,480},{16,496},{32,0},{48,16},{64,32},{80,48},{96,64},{112,80},{... | collective-permute-start | bytes 147464 | tf_op jit(solution)/shard_map/ppermute | solution.py:21
  176.1 11.9 %collective-permute-start.27 = (bf16[2,96,128]{2,1,0:T(8,128)(2,1)S(1)}, bf16[2,96,128]{2,1,0:T(8,128)(2,1)S(1)}, u32[]{:S(2)}, u32[]{:S(2)}) collective-permute-start(bf16[2,96,128]{2,1,0:T(8,128)(2,1)S(1)} %broadcast_select_fusion.10), channel_id=1, source_target_pairs={{0,16},{16,32},{32,48},{48,64},{64,80},{80,96},{96,112},{112,128},... | collective-permute-start | bytes 147464 | tf_op jit(solution)/shard_map/ppermute | solution.py:21
  178.1 39.8 %collective-permute-start.28 = (bf16[2,96,128]{2,0,1:T(2,128)(2,1)S(1)}, bf16[2,96,128]{2,0,1:T(2,128)(2,1)S(1)}, u32[]{:S(2)}, u32[]{:S(2)}) collective-permute-start(bf16[2,96,128]{2,0,1:T(2,128)(2,1)S(1)} %bitcast.354), channel_id=1, source_target_pairs={{0,496},{16,0},{32,16},{48,32},{64,48},{80,64},{96,80},{112,96},{1... | collective-permute-start | bytes 147464 | tf_op jit(solution)/shard_map/ppermute | solution.py:21
  185.8 4.8 %collective-permute-start.29 = (bf16[2,96,128]{2,1,0:T(8,128)(2,1)S(1)}, bf16[2,96,128]{2,1,0:T(8,128)(2,1)S(1)}, u32[]{:S(2)}, u32[]{:S(2)}) collective-permute-start(bf16[2,96,128]{2,1,0:T(8,128)(2,1)S(1)} %broadcast_select_fusion.7), channel_id=1, source_target_pairs={{0,496},{16,0},{32,16},{48,32},{64,48},{80,64},{96,80},{112,96},{1... | collective-permute-start | bytes 147464 | tf_op jit(solution)/shard_map/ppermute | solution.py:21
  188.0 40.4 %collective-permute-start.30 = (bf16[2,96,128]{2,0,1:T(2,128)(2,1)S(1)}, bf16[2,96,128]{2,0,1:T(2,128)(2,1)S(1)}, u32[]{:S(2)}, u32[]{:S(2)}) collective-permute-start(bf16[2,96,128]{2,0,1:T(2,128)(2,1)S(1)} %bitcast.352), channel_id=1, source_target_pairs={{0,16},{16,32},{32,48},{48,64},{64,80},{80,96},{96,112},{112,128},... | collective-permute-start | bytes 147464 | tf_op jit(solution)/shard_map/ppermute | solution.py:21
  190.6 6.0 %collective-permute-start.31 = (bf16[2,96,128]{2,1,0:T(8,128)(2,1)S(1)}, bf16[2,96,128]{2,1,0:T(8,128)(2,1)S(1)}, u32[]{:S(2)}, u32[]{:S(2)}) collective-permute-start(bf16[2,96,128]{2,1,0:T(8,128)(2,1)S(1)} %broadcast_select_fusion.4), channel_id=1, source_target_pairs={{0,480},{16,496},{32,0},{48,16},{64,32},{80,48},{96,64},{112,80},{... | collective-permute-start | bytes 147464 | tf_op jit(solution)/shard_map/ppermute | solution.py:21
  196.6 12.8 %collective-permute-start.33 = (bf16[2,96,128]{2,1,0:T(8,128)(2,1)S(1)}, bf16[2,96,128]{2,1,0:T(8,128)(2,1)S(1)}, u32[]{:S(2)}, u32[]{:S(2)}) collective-permute-start(bf16[2,96,128]{2,1,0:T(8,128)(2,1)S(1)} %broadcast_select_fusion.1), channel_id=1, source_target_pairs={{0,464},{16,480},{32,496},{48,0},{64,16},{80,32},{96,48},{112,64},... | collective-permute-start | bytes 147464 | tf_op jit(solution)/shard_map/ppermute | solution.py:21
  202.5 25.9 %collective-permute-start.32 = (bf16[2,96,128]{2,0,1:T(2,128)(2,1)S(1)}, bf16[2,96,128]{2,0,1:T(2,128)(2,1)S(1)}, u32[]{:S(2)}, u32[]{:S(2)}) collective-permute-start(bf16[2,96,128]{2,0,1:T(2,128)(2,1)S(1)} %bitcast.350), channel_id=1, source_target_pairs={{0,32},{16,48},{32,64},{48,80},{64,96},{80,112},{96,128},{112,144}... | collective-permute-start | bytes 147464 | tf_op jit(solution)/shard_map/ppermute | solution.py:21
  209.5 19.0 %collective-permute-start.34 = (bf16[2,96,128]{2,0,1:T(2,128)(2,1)S(1)}, bf16[2,96,128]{2,0,1:T(2,128)(2,1)S(1)}, u32[]{:S(2)}, u32[]{:S(2)}) collective-permute-start(bf16[2,96,128]{2,0,1:T(2,128)(2,1)S(1)} %bitcast.348), channel_id=1, source_target_pairs={{0,48},{16,64},{32,80},{48,96},{64,112},{80,128},{96,144},{112,160... | collective-permute-start | bytes 147464 | tf_op jit(solution)/shard_map/ppermute | solution.py:21
  215.9 18.4 %collective-permute-start.21 = (bf16[3,96,128]{2,1,0:T(8,128)(2,1)}, bf16[3,96,128]{2,1,0:T(8,128)(2,1)S(1)}, u32[]{:S(2)}, u32[]{:S(2)}) collective-permute-start(bf16[3,96,128]{2,1,0:T(8,128)(2,1)} %get-tuple-element.25), channel_id=1, source_target_pairs={{1,0},{2,1},{3,2},{4,3},{5,4},{6,5},{7,6},{8,7},{9,8},{10,9},{11,1... | collective-permute-start | bytes 221192 | tf_op jit(solution)/shard_map/ppermute | solution.py:32
  217.8 15.3 %collective-permute-start.22 = (bf16[3,96,128]{2,1,0:T(8,128)(2,1)}, bf16[3,96,128]{2,1,0:T(8,128)(2,1)S(1)}, u32[]{:S(2)}, u32[]{:S(2)}) collective-permute-start(bf16[3,96,128]{2,1,0:T(8,128)(2,1)} %get-tuple-element.26), channel_id=1, source_target_pairs={{0,1},{1,2},{2,3},{3,4},{4,5},{5,6},{6,7},{7,8},{8,9},{9,10},{10,1... | collective-permute-start | bytes 221192 | tf_op jit(solution)/shard_map/ppermute | solution.py:29
  248.6 21.8 %collective-permute-start.37 = (bf16[2,96,128]{2,1,0:T(8,128)(2,1)S(1)}, bf16[2,96,128]{2,1,0:T(8,128)(2,1)S(1)}, u32[]{:S(2)}, u32[]{:S(2)}) collective-permute-start(bf16[2,96,128]{2,1,0:T(8,128)(2,1)S(1)} %broadcast_select_fusion.15), channel_id=1, source_target_pairs={{0,48},{16,64},{32,80},{48,96},{64,112},{80,128},{96,144},{112,160... | collective-permute-start | bytes 147464 | tf_op jit(solution)/shard_map/ppermute | solution.py:21
  250.9 44.0 %collective-permute-start.38 = (bf16[2,96,128]{2,0,1:T(2,128)(2,1)S(1)}, bf16[2,96,128]{2,0,1:T(2,128)(2,1)S(1)}, u32[]{:S(2)}, u32[]{:S(2)}) collective-permute-start(bf16[2,96,128]{2,0,1:T(2,128)(2,1)S(1)} %bitcast.357), channel_id=1, source_target_pairs={{0,464},{16,480},{32,496},{48,0},{64,16},{80,32},{96,48},{112,64},... | collective-permute-start | bytes 147464 | tf_op jit(solution)/shard_map/ppermute | solution.py:21
  258.7 19.5 %collective-permute-start.39 = (bf16[2,96,128]{2,1,0:T(8,128)(2,1)S(1)}, bf16[2,96,128]{2,1,0:T(8,128)(2,1)S(1)}, u32[]{:S(2)}, u32[]{:S(2)}) collective-permute-start(bf16[2,96,128]{2,1,0:T(8,128)(2,1)S(1)} %broadcast_select_fusion.12), channel_id=1, source_target_pairs={{0,32},{16,48},{32,64},{48,80},{64,96},{80,112},{96,128},{112,144}... | collective-permute-start | bytes 147464 | tf_op jit(solution)/shard_map/ppermute | solution.py:21
  260.7 46.3 %collective-permute-start.40 = (bf16[2,96,128]{2,0,1:T(2,128)(2,1)S(1)}, bf16[2,96,128]{2,0,1:T(2,128)(2,1)S(1)}, u32[]{:S(2)}, u32[]{:S(2)}) collective-permute-start(bf16[2,96,128]{2,0,1:T(2,128)(2,1)S(1)} %bitcast.355), channel_id=1, source_target_pairs={{0,480},{16,496},{32,0},{48,16},{64,32},{80,48},{96,64},{112,80},{... | collective-permute-start | bytes 147464 | tf_op jit(solution)/shard_map/ppermute | solution.py:21
  268.5 11.9 %collective-permute-start.41 = (bf16[2,96,128]{2,1,0:T(8,128)(2,1)S(1)}, bf16[2,96,128]{2,1,0:T(8,128)(2,1)S(1)}, u32[]{:S(2)}, u32[]{:S(2)}) collective-permute-start(bf16[2,96,128]{2,1,0:T(8,128)(2,1)S(1)} %broadcast_select_fusion.9), channel_id=1, source_target_pairs={{0,16},{16,32},{32,48},{48,64},{64,80},{80,96},{96,112},{112,128},... | collective-permute-start | bytes 147464 | tf_op jit(solution)/shard_map/ppermute | solution.py:21
  270.4 38.5 %collective-permute-start.42 = (bf16[2,96,128]{2,0,1:T(2,128)(2,1)S(1)}, bf16[2,96,128]{2,0,1:T(2,128)(2,1)S(1)}, u32[]{:S(2)}, u32[]{:S(2)}) collective-permute-start(bf16[2,96,128]{2,0,1:T(2,128)(2,1)S(1)} %bitcast.353), channel_id=1, source_target_pairs={{0,496},{16,0},{32,16},{48,32},{64,48},{80,64},{96,80},{112,96},{1... | collective-permute-start | bytes 147464 | tf_op jit(solution)/shard_map/ppermute | solution.py:21
  278.2 4.8 %collective-permute-start.43 = (bf16[2,96,128]{2,1,0:T(8,128)(2,1)S(1)}, bf16[2,96,128]{2,1,0:T(8,128)(2,1)S(1)}, u32[]{:S(2)}, u32[]{:S(2)}) collective-permute-start(bf16[2,96,128]{2,1,0:T(8,128)(2,1)S(1)} %broadcast_select_fusion.6), channel_id=1, source_target_pairs={{0,496},{16,0},{32,16},{48,32},{64,48},{80,64},{96,80},{112,96},{1... | collective-permute-start | bytes 147464 | tf_op jit(solution)/shard_map/ppermute | solution.py:21
  280.4 38.5 %collective-permute-start.44 = (bf16[2,96,128]{2,0,1:T(2,128)(2,1)S(1)}, bf16[2,96,128]{2,0,1:T(2,128)(2,1)S(1)}, u32[]{:S(2)}, u32[]{:S(2)}) collective-permute-start(bf16[2,96,128]{2,0,1:T(2,128)(2,1)S(1)} %bitcast.351), channel_id=1, source_target_pairs={{0,16},{16,32},{32,48},{48,64},{64,80},{80,96},{96,112},{112,128},... | collective-permute-start | bytes 147464 | tf_op jit(solution)/shard_map/ppermute | solution.py:21
  283.0 6.0 %collective-permute-start.45 = (bf16[2,96,128]{2,1,0:T(8,128)(2,1)S(1)}, bf16[2,96,128]{2,1,0:T(8,128)(2,1)S(1)}, u32[]{:S(2)}, u32[]{:S(2)}) collective-permute-start(bf16[2,96,128]{2,1,0:T(8,128)(2,1)S(1)} %broadcast_select_fusion.3), channel_id=1, source_target_pairs={{0,480},{16,496},{32,0},{48,16},{64,32},{80,48},{96,64},{112,80},{... | collective-permute-start | bytes 147464 | tf_op jit(solution)/shard_map/ppermute | solution.py:21
  289.0 12.8 %collective-permute-start.47 = (bf16[2,96,128]{2,1,0:T(8,128)(2,1)S(1)}, bf16[2,96,128]{2,1,0:T(8,128)(2,1)S(1)}, u32[]{:S(2)}, u32[]{:S(2)}) collective-permute-start(bf16[2,96,128]{2,1,0:T(8,128)(2,1)S(1)} %broadcast_select_fusion), channel_id=1, source_target_pairs={{0,464},{16,480},{32,496},{48,0},{64,16},{80,32},{96,48},{112,64},... | collective-permute-start | bytes 147464 | tf_op jit(solution)/shard_map/ppermute | solution.py:21
  294.9 24.0 %collective-permute-start.46 = (bf16[2,96,128]{2,0,1:T(2,128)(2,1)S(1)}, bf16[2,96,128]{2,0,1:T(2,128)(2,1)S(1)}, u32[]{:S(2)}, u32[]{:S(2)}) collective-permute-start(bf16[2,96,128]{2,0,1:T(2,128)(2,1)S(1)} %bitcast.349), channel_id=1, source_target_pairs={{0,32},{16,48},{32,64},{48,80},{64,96},{80,112},{96,128},{112,144}... | collective-permute-start | bytes 147464 | tf_op jit(solution)/shard_map/ppermute | solution.py:21
  301.8 17.1 %collective-permute-start.48 = (bf16[2,96,128]{2,0,1:T(2,128)(2,1)S(1)}, bf16[2,96,128]{2,0,1:T(2,128)(2,1)S(1)}, u32[]{:S(2)}, u32[]{:S(2)}) collective-permute-start(bf16[2,96,128]{2,0,1:T(2,128)(2,1)S(1)} %bitcast.347), channel_id=1, source_target_pairs={{0,48},{16,64},{32,80},{48,96},{64,112},{80,128},{96,144},{112,160... | collective-permute-start | bytes 147464 | tf_op jit(solution)/shard_map/ppermute | solution.py:21
  307.0 20.2 %collective-permute-start.35 = (bf16[3,96,128]{2,1,0:T(8,128)(2,1)}, bf16[3,96,128]{2,1,0:T(8,128)(2,1)}, u32[]{:S(2)}, u32[]{:S(2)}) collective-permute-start(bf16[3,96,128]{2,1,0:T(8,128)(2,1)} %get-tuple-element.23), channel_id=1, source_target_pairs={{1,0},{2,1},{3,2},{4,3},{5,4},{6,5},{7,6},{8,7},{9,8},{10,9},{11,1... | collective-permute-start | bytes 221192 | tf_op jit(solution)/shard_map/ppermute | solution.py:32
  308.9 14.5 %collective-permute-start.36 = (bf16[3,96,128]{2,1,0:T(8,128)(2,1)}, bf16[3,96,128]{2,1,0:T(8,128)(2,1)}, u32[]{:S(2)}, u32[]{:S(2)}) collective-permute-start(bf16[3,96,128]{2,1,0:T(8,128)(2,1)} %get-tuple-element.24), channel_id=1, source_target_pairs={{0,1},{1,2},{2,3},{3,4},{4,5},{5,6},{6,7},{7,8},{8,9},{9,10},{10,1... | collective-permute-start | bytes 221192 | tf_op jit(solution)/shard_map/ppermute | solution.py:29
  (99 other events, 1581.6 us)
where the time goes:
time: 336 us; the launch traced here: 331 us
  starting transfers between devices  211 us (63%)
  local copies, waits for them, and re-layouts  53.8 us (16%)
  waiting for transfers between devices  32.2 us (10%)
  matrix products  23.7 us (7%)
  other arithmetic  7.42 us (2%)
    ppermute x42, starting transfers between devices, passed_along_2(): return lax.ppermute(x, axis, [(i, (i + by) % count) for i in range(count)])  172 us
    ppermute x42, waiting for transfers between devices, passed_along_2(): return lax.ppermute(x, axis, [(i, (i + by) % count) for i in range(count)])  31.1 us
    ppermute x3, starting transfers between devices, padded(): lax.ppermute(lax.slice_in_dim(block, block.shape[dim] - width, None, axis...  29.7 us
    gather x18, local copies, waits for them, and re-layouts, body(): answer_rows = jnp.take(probe_bf, asked_knots[apply_bucket], axis=0)  11.6 us
    gather x18, local copies, waits for them, and re-layouts, body(): jnp.take(probe_bf, my_pairs[apply_bucket, :, 0], axis=0)  11 us
    concatenate x3, local copies, waits for them, and re-layouts, body(): target_values = jnp.concatenate(entry_values, axis=0)  10.2 us
    dot_general x12, matrix products, body(): jnp.einsum('kab,kbr->kar', blocks[:, step], extended[3 + step:3 + step +...  9.07 us
    dot_general x18, local copies, waits for them, and re-layouts, body(): jnp.einsum('dqp,dpc->dqc', pair_coupling_term[apply_bucket], fetched_rows...  8.35 us
  transfers between devices with their start and end apart: 49, of which 8 were waited for; matrix products, arithmetic and copies ran while one was open for 14% of the time, Pallas kernels for 0%

commit v1 on v0

v1 whole, which is shorter than its diff:
```python
import jax
import jax.numpy as jnp
from jax import lax
from jax.sharding import PartitionSpec as P

ITERS = 3


LO_BOUND = 1.5
HI_BOUND = 12.0


def shifted_open(value, axis, steps):
    count = lax.axis_size(axis)
    initial, last = (max(0, -steps), min(count, count - steps))
    return lax.ppermute(value, axis, [(source, source + steps) for source in range(initial, last)])


def shifted_ring(value, axis, steps):
    count = lax.axis_size(axis)
    return lax.ppermute(value, axis, [(i, (i + steps) % count) for i in range(count)])


def body(right_side, band_blocks, knot_pairs, pair_counts, cross_blocks):
    right_rows = right_side[0]
    blocks = band_blocks[0]
    my_pairs = knot_pairs[0, 0]
    used_count = pair_counts[0, 0]
    couplings = cross_blocks[0, 0]
    knots, params, probes = right_rows.shape
    buckets, slots = my_pairs.shape[0], my_pairs.shape[1]
    group_span = buckets // 2 + 1
    offsets = [
        b - (group_span - 1) if b < group_span - 1 else b - group_span + 2 for b in range(buckets)
    ]
    bucket_of = {o: b for b, o in enumerate(offsets)}
    shifts = [o for o in offsets if o > 0] + [o for o in offsets if o < 0]
    lines = lax.axis_size("line")
    me = lax.axis_index("line")

    boundary_blocks = shifted_open(blocks[knots - 3 :], "seg", 1)
    lower_blocks = jnp.concatenate([boundary_blocks, blocks], axis=0)

    used = jnp.arange(slots, dtype=jnp.int32)[None, :] < used_count[:, None]
    own_knot = jnp.where(used, my_pairs[:, :, 0], -1)
    far_knot = jnp.where(used, my_pairs[:, :, 1], -1)
    table = lax.all_gather(far_knot, "line")

    answer_knots = []
    landing_knots = []
    for s in shifts:
        answer_knots.append(lax.dynamic_index_in_dim(table, (me + s) % lines, 0, False)[bucket_of[-s]])
        landing_knots.append(lax.dynamic_index_in_dim(table, (me - s + lines) % lines, 0, False)[bucket_of[s]])
    knot_ids = jnp.arange(knots, dtype=jnp.int32)
    pick_index = jnp.concatenate([own_knot.reshape(-1)] + answer_knots)
    pick = (pick_index[:, None] == knot_ids[None, :]).astype(jnp.bfloat16)
    own_place = (own_knot.reshape(-1)[None, :] == knot_ids[:, None]).astype(jnp.float32)
    land_place = (jnp.concatenate(landing_knots)[None, :] == knot_ids[:, None]).astype(jnp.bfloat16)

    center = (HI_BOUND + LO_BOUND) / 2.0
    radius = (HI_BOUND - LO_BOUND) / 2.0
    coeff = radius / center
    solution = jnp.zeros(right_rows.shape, jnp.float32)
    residual = right_rows
    direction = right_rows / center
    own_rows = buckets * slots
    for turn in range(ITERS):
        probe_bf = direction.astype(jnp.bfloat16)
        solution = solution + direction
        picked = jnp.einsum(
            "sk,kpr->spr", pick, probe_bf, preferred_element_type=jnp.float32
        ).astype(jnp.bfloat16)
        resident = picked[:own_rows].reshape(buckets, slots, params, probes)
        answers = picked[own_rows:].reshape(len(shifts), slots, params, probes)
        product = jnp.einsum(
            "bsqp,bsqr->bspr", couplings, resident, preferred_element_type=jnp.float32
        ).astype(jnp.bfloat16)
        fetched = [None] * buckets
        landed = []
        for t, s in enumerate(shifts):
            message = jnp.concatenate([answers[t], product[bucket_of[s]]], axis=0)
            got = shifted_ring(message, "line", s)
            fetched[bucket_of[-s]] = got[:slots]
            landed.append(got[slots:])
        low = shifted_open(probe_bf[knots - 3 :], "seg", 1)
        high = shifted_open(probe_bf[:3], "seg", -1)
        extended = jnp.concatenate([low, probe_bf, high], axis=0)
        summed = jnp.zeros(probe_bf.shape, jnp.float32)
        for step in range(4):
            summed = summed + jnp.einsum(
                "kab,kbr->kar",
                blocks[:, step],
                extended[3 + step : 3 + step + knots],
                preferred_element_type=jnp.float32,
            )
        for step in range(1, 4):
            summed = summed + jnp.einsum(
                "kba,kbr->kar",
                lower_blocks[3 - step : 3 - step + knots, step],
                extended[3 - step : 3 - step + knots],
                preferred_element_type=jnp.float32,
            )
        fetched = jnp.stack(fetched)
        forward = jnp.einsum(
            "bsqp,bspr->bsqr", couplings, fetched, preferred_element_type=jnp.float32
        ).reshape(own_rows, params, probes)
        landed = jnp.concatenate(landed, axis=0)
        cross = jnp.einsum(
            "ks,spr->kpr", own_place, forward, precision=lax.Precision.HIGHEST
        ) + jnp.einsum("ks,spr->kpr", land_place, landed, preferred_element_type=jnp.float32)
        residual = residual - (summed + cross)
        coeff_next = 1.0 / (2.0 * center / radius - coeff)
        direction = coeff_next * coeff * direction + 2.0 * coeff_next / radius * residual
        coeff = coeff_next
    return (solution + direction)[None]


def solution(mesh):
    return jax.shard_map(
        body,
        mesh=mesh,
        in_specs=(
            P("line", "seg", None, None),
            P("line", "seg", None, None, None),
            P("line", "seg", None, None, None),
            P("line", "seg", None),
            P("line", "seg", None, None, None, None),
        ),
        out_specs=P("line", "seg", None, None),
        check_vma=False,
    )
```

time: 336 us -> 219 us (0.65)
  the two profiles are of different devices: /device:TPU:24 before, /device:TPU:359 now
where the time goes in v1:
time: 219 us; the launch traced here: 218 us
  starting transfers between devices  90.4 us (41%)
  waiting for transfers between devices  47.3 us (22%)
  blocking collectives  37.3 us (17%)
  matrix products  19.6 us (9%)
  local copies, waits for them, and re-layouts  15.9 us (7%)
  other arithmetic  5.72 us (3%)
    ppermute x18, starting transfers between devices, shifted_ring(): lax.ppermute(value, axis, [(i, (i + steps) % count) for i in range(count)])  64.8 us
    all_gather x1, blocking collectives, body(): table = lax.all_gather(far_knot, 'line')  37.3 us
    ppermute x7, waiting for transfers between devices, shifted_open(): lax.ppermute(value, axis, [(source, source + steps) for source in range(i...  34.1 us
    ppermute x7, starting transfers between devices, shifted_open(): lax.ppermute(value, axis, [(source, source + steps) for source in range(i...  25.5 us
    ppermute x18, waiting for transfers between devices, shifted_ring(): lax.ppermute(value, axis, [(i, (i + steps) % count) for i in range(count)])  13.2 us
    dot_general x9, matrix products, body(): jnp.einsum('kba,kbr->kar', lower_blocks[3 - step:3 - step + knots, step],...  6.79 us
    dot_general x12, matrix products, body(): jnp.einsum('kab,kbr->kar', blocks[:, step], extended[3 + step:3 + step +...  6.68 us
    unnamed x95, local copies, waits for them, and re-layouts  6.22 us
  transfers between devices with their start and end apart: 25, of which 7 were waited for; matrix products, arithmetic and copies ran while one was open for 10% of the time, Pallas kernels for 0%

profile of v1, /device:TPU:359, one launch (start us, length us, event | category | flops | bytes accessed | tf_op | source)
XLA Modules:
  0.0 217.7 jit_solution(16500613254363797501)
XLA Ops:
  0.2 1.0 fusion.32
  1.6 37.3 %all_gather.4 = s32[32,6,2]{1,2,0:T(2,128)S(1)} all-gather(s32[1,6,2]{1,2,0:T(2,128)S(1)} %compare_select_fusion), channel_id=1, replica_groups=mesh['line'=32,'seg'=16] {'line'}, dimensions={0}, use_global_device_ids=true | all-gather | bytes 1584 | tf_op jit(solution)/shard_map/all_gather | solution.py:47
  41.2 0.7 pad_maximum_fusion.15
  41.9 8.3 %collective-permute-start.5 = (bf16[4,96,128]{2,0,1:T(4,128)(2,1)}, bf16[4,96,128]{2,0,1:T(4,128)(2,1)S(1)}, u32[]{:S(2)}, u32[]{:S(2)}) collective-permute-start(bf16[4,96,128]{2,0,1:T(4,128)(2,1)} %pad_maximum_fusion.15), channel_id=1, source_target_pairs={{0,16},{16,32},{32,48},{48,64},{64,80},{80,96},{96,112},{112,128},... | collective-permute-start | bytes 294920 | tf_op jit(solution)/shard_map/ppermute | solution.py:21
  51.0 1.9 collective-permute-start.4
  53.7 1.9 collective-permute-start.3
  56.3 3.6 %collective-permute-start.8 = (bf16[4,96,128]{2,0,1:T(4,128)(2,1)}, bf16[4,96,128]{2,0,1:T(4,128)(2,1)S(1)}, u32[]{:S(2)}, u32[]{:S(2)}) collective-permute-start(bf16[4,96,128]{2,0,1:T(4,128)(2,1)} %pad_maximum_fusion.18), channel_id=1, source_target_pairs={{0,464},{16,480},{32,496},{48,0},{64,16},{80,32},{96,48},{112,64},... | collective-permute-start | bytes 294920 | tf_op jit(solution)/shard_map/ppermute | solution.py:21
  60.6 5.5 %collective-permute-start = (bf16[3,96,128]{2,1,0:T(8,128)(2,1)S(1)}, bf16[3,96,128]{2,1,0:T(8,128)(2,1)S(1)}, u32[]{:S(2)}, u32[]{:S(2)}) collective-permute-start(bf16[3,96,128]{2,1,0:T(8,128)(2,1)S(1)} %get-tuple-element.50), channel_id=1, source_target_pairs={{1,0},{2,1},{3,2},{4,3},{5,4},{6,5},{7,6},{8,7},{9,8},{10,9},{11,1... | collective-permute-start | bytes 221192 | tf_op jit(solution)/shard_map/ppermute | solution.py:16
  68.1 3.4 %collective-permute-start.7 = (bf16[4,96,128]{2,0,1:T(4,128)(2,1)S(1)}, bf16[4,96,128]{2,0,1:T(4,128)(2,1)S(1)}, u32[]{:S(2)}, u32[]{:S(2)}) collective-permute-start(bf16[4,96,128]{2,0,1:T(4,128)(2,1)S(1)} %pad_maximum_fusion.17), channel_id=1, source_target_pairs={{0,480},{16,496},{32,0},{48,16},{64,32},{80,48},{96,64},{112,80},{... | collective-permute-start | bytes 294920 | tf_op jit(solution)/shard_map/ppermute | solution.py:21
  71.6 0.9 fusion.87
  72.6 2.9 %collective-permute-start.6 = (bf16[4,96,128]{2,0,1:T(4,128)(2,1)S(1)}, bf16[4,96,128]{2,0,1:T(4,128)(2,1)S(1)}, u32[]{:S(2)}, u32[]{:S(2)}) collective-permute-start(bf16[4,96,128]{2,0,1:T(4,128)(2,1)S(1)} %pad_maximum_fusion.16), channel_id=1, source_target_pairs={{0,496},{16,0},{32,16},{48,32},{64,48},{80,64},{96,80},{112,96},{1... | collective-permute-start | bytes 294920 | tf_op jit(solution)/shard_map/ppermute | solution.py:21
  75.6 1.9 collective-permute-start.1
  77.6 3.0 %collective-permute-start.2 = (bf16[3,96,128]{2,1,0:T(8,128)(2,1)}, bf16[3,96,128]{2,1,0:T(8,128)(2,1)S(1)}, u32[]{:S(2)}, u32[]{:S(2)}) collective-permute-start(bf16[3,96,128]{2,1,0:T(8,128)(2,1)} %get-tuple-element.51), channel_id=1, source_target_pairs={{0,1},{1,2},{2,3},{3,4},{4,5},{5,6},{6,7},{7,8},{8,9},{9,10},{10,1... | collective-permute-start | bytes 221192 | tf_op jit(solution)/shard_map/ppermute | solution.py:16
  80.6 2.7 %collective-permute-done.6 = bf16[4,96,128]{2,0,1:T(4,128)(2,1)S(1)} collective-permute-done((bf16[4,96,128]{2,0,1:T(4,128)(2,1)S(1)}, bf16[4,96,128]{2,0,1:T(4,128)(2,1)S(1)}, u32[]{:S(2)}, u32[]{:S(2)}) %collective-permute-start.6) | collective-permute-done | bytes 98336 | tf_op jit(solution)/shard_map/ppermute | solution.py:21
  83.7 1.5 fusion.29
  86.4 22.4 %collective-permute-done.1 = bf16[3,4,96,96]{3,2,0,1:T(8,128)(2,1)S(1)} collective-permute-done((bf16[3,4,96,96]{3,2,0,1:T(8,128)(2,1)}, bf16[3,4,96,96]{3,2,0,1:T(8,128)(2,1)S(1)}, u32[]{:S(2)}, u32[]{:S(2)}) %collective-permute-start.1) | collective-permute-done | bytes 221216 | tf_op jit(solution)/shard_map/ppermute | solution.py:16
  109.0 1.5 collective-permute-done.2
  114.1 9.2 %collective-permute-start.13 = (bf16[4,96,128]{2,0,1:T(4,128)(2,1)S(1)}, bf16[4,96,128]{2,0,1:T(4,128)(2,1)S(1)}, u32[]{:S(2)}, u32[]{:S(2)}) collective-permute-start(bf16[4,96,128]{2,0,1:T(4,128)(2,1)S(1)} %pad_maximum_fusion.21), channel_id=1, source_target_pairs={{0,16},{16,32},{32,48},{48,64},{64,80},{80,96},{96,112},{112,128},... | collective-permute-start | bytes 294920 | tf_op jit(solution)/shard_map/ppermute | solution.py:21
  123.4 1.9 collective-permute-start.12
  125.4 1.9 collective-permute-start.11
  127.5 3.6 %collective-permute-start.16 = (bf16[4,96,128]{2,0,1:T(4,128)(2,1)S(1)}, bf16[4,96,128]{2,0,1:T(4,128)(2,1)S(1)}, u32[]{:S(2)}, u32[]{:S(2)}) collective-permute-start(bf16[4,96,128]{2,0,1:T(4,128)(2,1)S(1)} %pad_maximum_fusion.24), channel_id=1, source_target_pairs={{0,464},{16,480},{32,496},{48,0},{64,16},{80,32},{96,48},{112,64},... | collective-permute-start | bytes 294920 | tf_op jit(solution)/shard_map/ppermute | solution.py:21
  131.1 1.9 collective-permute-start.10
  133.3 9.1 %collective-permute-done.10 = bf16[3,96,128]{2,1,0:T(8,128)(2,1)S(1)} collective-permute-done((bf16[3,96,128]{2,1,0:T(8,128)(2,1)S(1)}, bf16[3,96,128]{2,1,0:T(8,128)(2,1)S(1)}, u32[]{:S(2)}, u32[]{:S(2)}) %collective-permute-start.10) | collective-permute-done | bytes 73760 | tf_op jit(solution)/shard_map/ppermute | solution.py:16
  142.3 1.9 collective-permute-start.9
  144.2 1.0 fusion.80
  145.3 1.0 fusion.57
  146.3 1.2 collective-permute-done.9
  147.4 4.8 %collective-permute-start.15 = (bf16[4,96,128]{2,0,1:T(4,128)(2,1)S(1)}, bf16[4,96,128]{2,0,1:T(4,128)(2,1)S(1)}, u32[]{:S(2)}, u32[]{:S(2)}) collective-permute-start(bf16[4,96,128]{2,0,1:T(4,128)(2,1)S(1)} %pad_maximum_fusion.23), channel_id=1, source_target_pairs={{0,480},{16,496},{32,0},{48,16},{64,32},{80,48},{96,64},{112,80},{... | collective-permute-start | bytes 294920 | tf_op jit(solution)/shard_map/ppermute | solution.py:21
  152.3 1.0 convolution_add_fusion.3
  153.2 1.0 fusion.60
  154.2 4.0 %collective-permute-start.14 = (bf16[4,96,128]{2,0,1:T(4,128)(2,1)S(1)}, bf16[4,96,128]{2,0,1:T(4,128)(2,1)S(1)}, u32[]{:S(2)}, u32[]{:S(2)}) collective-permute-start(bf16[4,96,128]{2,0,1:T(4,128)(2,1)S(1)} %pad_maximum_fusion.22), channel_id=1, source_target_pairs={{0,496},{16,0},{32,16},{48,32},{64,48},{80,64},{96,80},{112,96},{1... | collective-permute-start | bytes 294920 | tf_op jit(solution)/shard_map/ppermute | solution.py:21
  158.3 1.0 fusion.82
  160.0 5.9 %collective-permute-done.14 = bf16[4,96,128]{2,0,1:T(4,128)(2,1)S(1)} collective-permute-done((bf16[4,96,128]{2,0,1:T(4,128)(2,1)S(1)}, bf16[4,96,128]{2,0,1:T(4,128)(2,1)S(1)}, u32[]{:S(2)}, u32[]{:S(2)}) %collective-permute-start.14) | collective-permute-done | bytes 98336 | tf_op jit(solution)/shard_map/ppermute | solution.py:21
  171.3 1.9 collective-permute-start.18
  173.2 9.4 %collective-permute-start.17 = (bf16[3,96,128]{2,1,0:T(8,128)(2,1)S(1)}, bf16[3,96,128]{2,1,0:T(8,128)(2,1)S(1)}, u32[]{:S(2)}, u32[]{:S(2)}) collective-permute-start(bf16[3,96,128]{2,1,0:T(8,128)(2,1)S(1)} %get-tuple-element.46), channel_id=1, source_target_pairs={{1,0},{2,1},{3,2},{4,3},{5,4},{6,5},{7,6},{8,7},{9,8},{10,9},{11,1... | collective-permute-start | bytes 221192 | tf_op jit(solution)/shard_map/ppermute | solution.py:16
  183.5 2.7 %collective-permute-start.21 = (bf16[4,96,128]{2,0,1:T(4,128)(2,1)S(1)}, bf16[4,96,128]{2,0,1:T(4,128)(2,1)S(1)}, u32[]{:S(2)}, u32[]{:S(2)}) collective-permute-start(bf16[4,96,128]{2,0,1:T(4,128)(2,1)S(1)} %pad_maximum_fusion.27), channel_id=1, source_target_pairs={{0,16},{16,32},{32,48},{48,64},{64,80},{80,96},{96,112},{112,128},... | collective-permute-start | bytes 294920 | tf_op jit(solution)/shard_map/ppermute | solution.py:21
  186.3 1.9 collective-permute-start.20
  188.4 1.9 collective-permute-start.19
  190.7 3.6 %collective-permute-start.24 = (bf16[4,96,128]{2,0,1:T(4,128)(2,1)S(1)}, bf16[4,96,128]{2,0,1:T(4,128)(2,1)S(1)}, u32[]{:S(2)}, u32[]{:S(2)}) collective-permute-start(bf16[4,96,128]{2,0,1:T(4,128)(2,1)S(1)} %pad_maximum_fusion.30), channel_id=1, source_target_pairs={{0,464},{16,480},{32,496},{48,0},{64,16},{80,32},{96,48},{112,64},... | collective-permute-start | bytes 294920 | tf_op jit(solution)/shard_map/ppermute | solution.py:21
  194.3 1.0 fusion.76
  195.3 1.0 fusion.47
  196.3 3.4 %collective-permute-start.23 = (bf16[4,96,128]{2,0,1:T(4,128)(2,1)S(1)}, bf16[4,96,128]{2,0,1:T(4,128)(2,1)S(1)}, u32[]{:S(2)}, u32[]{:S(2)}) collective-permute-start(bf16[4,96,128]{2,0,1:T(4,128)(2,1)S(1)} %pad_maximum_fusion.29), channel_id=1, source_target_pairs={{0,480},{16,496},{32,0},{48,16},{64,32},{80,48},{96,64},{112,80},{... | collective-permute-start | bytes 294920 | tf_op jit(solution)/shard_map/ppermute | solution.py:21
  199.9 1.0 fusion.50
  200.9 3.7 %collective-permute-start.22 = (bf16[4,96,128]{2,0,1:T(4,128)(2,1)S(1)}, bf16[4,96,128]{2,0,1:T(4,128)(2,1)S(1)}, u32[]{:S(2)}, u32[]{:S(2)}) collective-permute-start(bf16[4,96,128]{2,0,1:T(4,128)(2,1)S(1)} %pad_maximum_fusion.28), channel_id=1, source_target_pairs={{0,496},{16,0},{32,16},{48,32},{64,48},{80,64},{96,80},{112,96},{1... | collective-permute-start | bytes 294920 | tf_op jit(solution)/shard_map/ppermute | solution.py:21
  204.6 0.9 fusion.78
  206.6 4.5 %collective-permute-done.22 = bf16[4,96,128]{2,0,1:T(4,128)(2,1)S(1)} collective-permute-done((bf16[4,96,128]{2,0,1:T(4,128)(2,1)S(1)}, bf16[4,96,128]{2,0,1:T(4,128)(2,1)S(1)}, u32[]{:S(2)}, u32[]{:S(2)}) %collective-permute-start.22) | collective-permute-done | bytes 98336 | tf_op jit(solution)/shard_map/ppermute | solution.py:21
  212.4 1.3 concatenate.134
  216.5 1.2 fusion.24
  (210 shorter events, 25.6 us)
Async XLA Ops:
  0.0 40.4 %copy-start = (bf16[1,1,6,2,96,96]{5,4,3,2,1,0:T(8,128)(2,1)S(1)}, bf16[1,1,6,2,96,96]{5,4,3,2,1,0:T(8,128)(2,1)}, u32[]{:S(2)}) copy-start(bf16[1,1,6,2,96,96]{5,4,3,2,1,0:T(8,128)(2,1)} %param.9) | copy-start | bytes 663556
  0.0 1.2 copy-start.37
  0.0 1.4 copy-start.36
  40.9 25.2 %copy-start.13 = (bf16[1,8,4,96,96]{4,3,2,1,0:T(8,128)(2,1)S(1)}, bf16[1,8,4,96,96]{4,3,2,1,0:T(8,128)(2,1)}, u32[]{:S(2)}) copy-start(bf16[1,8,4,96,96]{4,3,2,1,0:T(8,128)(2,1)} %param.6) | copy-start | bytes 1769476
  41.9 35.6 %collective-permute-start.5 = (bf16[4,96,128]{2,0,1:T(4,128)(2,1)}, bf16[4,96,128]{2,0,1:T(4,128)(2,1)S(1)}, u32[]{:S(2)}, u32[]{:S(2)}) collective-permute-start(bf16[4,96,128]{2,0,1:T(4,128)(2,1)} %pad_maximum_fusion.15), channel_id=1, source_target_pairs={{0,16},{16,32},{32,48},{48,64},{64,80},{80,96},{96,112},{112,128},... | collective-permute-start | bytes 294920 | tf_op jit(solution)/shard_map/ppermute | solution.py:21
  51.0 24.6 %collective-permute-start.4 = (bf16[4,96,128]{2,0,1:T(4,128)(2,1)}, bf16[4,96,128]{2,0,1:T(4,128)(2,1)S(1)}, u32[]{:S(2)}, u32[]{:S(2)}) collective-permute-start(bf16[4,96,128]{2,0,1:T(4,128)(2,1)} %pad_maximum_fusion.14), channel_id=1, source_target_pairs={{0,32},{16,48},{32,64},{48,80},{64,96},{80,112},{96,128},{112,144}... | collective-permute-start | bytes 294920 | tf_op jit(solution)/shard_map/ppermute | solution.py:21
  53.7 18.9 %collective-permute-start.3 = (bf16[4,96,128]{2,0,1:T(4,128)(2,1)}, bf16[4,96,128]{2,0,1:T(4,128)(2,1)S(1)}, u32[]{:S(2)}, u32[]{:S(2)}) collective-permute-start(bf16[4,96,128]{2,0,1:T(4,128)(2,1)} %pad_maximum_fusion.13), channel_id=1, source_target_pairs={{0,48},{16,64},{32,80},{48,96},{64,112},{80,128},{96,144},{112,160... | collective-permute-start | bytes 294920 | tf_op jit(solution)/shard_map/ppermute | solution.py:21
  56.3 27.1 %collective-permute-start.8 = (bf16[4,96,128]{2,0,1:T(4,128)(2,1)}, bf16[4,96,128]{2,0,1:T(4,128)(2,1)S(1)}, u32[]{:S(2)}, u32[]{:S(2)}) collective-permute-start(bf16[4,96,128]{2,0,1:T(4,128)(2,1)} %pad_maximum_fusion.18), channel_id=1, source_target_pairs={{0,464},{16,480},{32,496},{48,0},{64,16},{80,32},{96,48},{112,64},... | collective-permute-start | bytes 294920 | tf_op jit(solution)/shard_map/ppermute | solution.py:21
  60.6 7.5 %collective-permute-start = (bf16[3,96,128]{2,1,0:T(8,128)(2,1)S(1)}, bf16[3,96,128]{2,1,0:T(8,128)(2,1)S(1)}, u32[]{:S(2)}, u32[]{:S(2)}) collective-permute-start(bf16[3,96,128]{2,1,0:T(8,128)(2,1)S(1)} %get-tuple-element.50), channel_id=1, source_target_pairs={{1,0},{2,1},{3,2},{4,3},{5,4},{6,5},{7,6},{8,7},{9,8},{10,9},{11,1... | collective-permute-start | bytes 221192 | tf_op jit(solution)/shard_map/ppermute | solution.py:16
  68.1 15.3 %collective-permute-start.7 = (bf16[4,96,128]{2,0,1:T(4,128)(2,1)S(1)}, bf16[4,96,128]{2,0,1:T(4,128)(2,1)S(1)}, u32[]{:S(2)}, u32[]{:S(2)}) collective-permute-start(bf16[4,96,128]{2,0,1:T(4,128)(2,1)S(1)} %pad_maximum_fusion.17), channel_id=1, source_target_pairs={{0,480},{16,496},{32,0},{48,16},{64,32},{80,48},{96,64},{112,80},{... | collective-permute-start | bytes 294920 | tf_op jit(solution)/shard_map/ppermute | solution.py:21
  72.6 10.7 %collective-permute-start.6 = (bf16[4,96,128]{2,0,1:T(4,128)(2,1)S(1)}, bf16[4,96,128]{2,0,1:T(4,128)(2,1)S(1)}, u32[]{:S(2)}, u32[]{:S(2)}) collective-permute-start(bf16[4,96,128]{2,0,1:T(4,128)(2,1)S(1)} %pad_maximum_fusion.16), channel_id=1, source_target_pairs={{0,496},{16,0},{32,16},{48,32},{64,48},{80,64},{96,80},{112,96},{1... | collective-permute-start | bytes 294920 | tf_op jit(solution)/shard_map/ppermute | solution.py:21
  75.6 33.3 %collective-permute-start.1 = (bf16[3,4,96,96]{3,2,0,1:T(8,128)(2,1)}, bf16[3,4,96,96]{3,2,0,1:T(8,128)(2,1)S(1)}, u32[]{:S(2)}, u32[]{:S(2)}) collective-permute-start(bf16[3,4,96,96]{3,2,0,1:T(8,128)(2,1)} %slice_bitcast_fusion), channel_id=1, source_target_pairs={{0,1},{1,2},{2,3},{3,4},{4,5},{5,6},{6,7},{7,8},{8,9},{9,10},{10,1... | collective-permute-start | bytes 663560 | tf_op jit(solution)/shard_map/ppermute | solution.py:16
  77.6 32.9 %collective-permute-start.2 = (bf16[3,96,128]{2,1,0:T(8,128)(2,1)}, bf16[3,96,128]{2,1,0:T(8,128)(2,1)S(1)}, u32[]{:S(2)}, u32[]{:S(2)}) collective-permute-start(bf16[3,96,128]{2,1,0:T(8,128)(2,1)} %get-tuple-element.51), channel_id=1, source_target_pairs={{0,1},{1,2},{2,3},{3,4},{4,5},{5,6},{6,7},{7,8},{8,9},{9,10},{10,1... | collective-permute-start | bytes 221192 | tf_op jit(solution)/shard_map/ppermute | solution.py:16
  110.7 1.1 copy-start.3
  110.7 1.2 copy-start.12
  114.1 40.1 %collective-permute-start.13 = (bf16[4,96,128]{2,0,1:T(4,128)(2,1)S(1)}, bf16[4,96,128]{2,0,1:T(4,128)(2,1)S(1)}, u32[]{:S(2)}, u32[]{:S(2)}) collective-permute-start(bf16[4,96,128]{2,0,1:T(4,128)(2,1)S(1)} %pad_maximum_fusion.21), channel_id=1, source_target_pairs={{0,16},{16,32},{32,48},{48,64},{64,80},{80,96},{96,112},{112,128},... | collective-permute-start | bytes 294920 | tf_op jit(solution)/shard_map/ppermute | solution.py:21
  123.4 35.9 %collective-permute-start.12 = (bf16[4,96,128]{2,0,1:T(4,128)(2,1)S(1)}, bf16[4,96,128]{2,0,1:T(4,128)(2,1)S(1)}, u32[]{:S(2)}, u32[]{:S(2)}) collective-permute-start(bf16[4,96,128]{2,0,1:T(4,128)(2,1)S(1)} %pad_maximum_fusion.20), channel_id=1, source_target_pairs={{0,32},{16,48},{32,64},{48,80},{64,96},{80,112},{96,128},{112,144}... | collective-permute-start | bytes 294920 | tf_op jit(solution)/shard_map/ppermute | solution.py:21
  125.4 34.0 %collective-permute-start.11 = (bf16[4,96,128]{2,0,1:T(4,128)(2,1)S(1)}, bf16[4,96,128]{2,0,1:T(4,128)(2,1)S(1)}, u32[]{:S(2)}, u32[]{:S(2)}) collective-permute-start(bf16[4,96,128]{2,0,1:T(4,128)(2,1)S(1)} %pad_maximum_fusion.19), channel_id=1, source_target_pairs={{0,48},{16,64},{32,80},{48,96},{64,112},{80,128},{96,144},{112,160... | collective-permute-start | bytes 294920 | tf_op jit(solution)/shard_map/ppermute | solution.py:21
  127.5 32.0 %collective-permute-start.16 = (bf16[4,96,128]{2,0,1:T(4,128)(2,1)S(1)}, bf16[4,96,128]{2,0,1:T(4,128)(2,1)S(1)}, u32[]{:S(2)}, u32[]{:S(2)}) collective-permute-start(bf16[4,96,128]{2,0,1:T(4,128)(2,1)S(1)} %pad_maximum_fusion.24), channel_id=1, source_target_pairs={{0,464},{16,480},{32,496},{48,0},{64,16},{80,32},{96,48},{112,64},... | collective-permute-start | bytes 294920 | tf_op jit(solution)/shard_map/ppermute | solution.py:21
  131.1 11.2 %collective-permute-start.10 = (bf16[3,96,128]{2,1,0:T(8,128)(2,1)S(1)}, bf16[3,96,128]{2,1,0:T(8,128)(2,1)S(1)}, u32[]{:S(2)}, u32[]{:S(2)}) collective-permute-start(bf16[3,96,128]{2,1,0:T(8,128)(2,1)S(1)} %get-tuple-element.49), channel_id=1, source_target_pairs={{0,1},{1,2},{2,3},{3,4},{4,5},{5,6},{6,7},{7,8},{8,9},{9,10},{10,1... | collective-permute-start | bytes 221192 | tf_op jit(solution)/shard_map/ppermute | solution.py:16
  142.3 5.1 %collective-permute-start.9 = (bf16[3,96,128]{2,1,0:T(8,128)(2,1)S(1)}, bf16[3,96,128]{2,1,0:T(8,128)(2,1)S(1)}, u32[]{:S(2)}, u32[]{:S(2)}) collective-permute-start(bf16[3,96,128]{2,1,0:T(8,128)(2,1)S(1)} %get-tuple-element.48), channel_id=1, source_target_pairs={{1,0},{2,1},{3,2},{4,3},{5,4},{6,5},{7,6},{8,7},{9,8},{10,9},{11,1... | collective-permute-start | bytes 221192 | tf_op jit(solution)/shard_map/ppermute | solution.py:16
  147.4 12.5 %collective-permute-start.15 = (bf16[4,96,128]{2,0,1:T(4,128)(2,1)S(1)}, bf16[4,96,128]{2,0,1:T(4,128)(2,1)S(1)}, u32[]{:S(2)}, u32[]{:S(2)}) collective-permute-start(bf16[4,96,128]{2,0,1:T(4,128)(2,1)S(1)} %pad_maximum_fusion.23), channel_id=1, source_target_pairs={{0,480},{16,496},{32,0},{48,16},{64,32},{80,48},{96,64},{112,80},{... | collective-permute-start | bytes 294920 | tf_op jit(solution)/shard_map/ppermute | solution.py:21
  154.2 11.7 %collective-permute-start.14 = (bf16[4,96,128]{2,0,1:T(4,128)(2,1)S(1)}, bf16[4,96,128]{2,0,1:T(4,128)(2,1)S(1)}, u32[]{:S(2)}, u32[]{:S(2)}) collective-permute-start(bf16[4,96,128]{2,0,1:T(4,128)(2,1)S(1)} %pad_maximum_fusion.22), channel_id=1, source_target_pairs={{0,496},{16,0},{32,16},{48,32},{64,48},{80,64},{96,80},{112,96},{1... | collective-permute-start | bytes 294920 | tf_op jit(solution)/shard_map/ppermute | solution.py:21
  159.4 6.5 %copy-start.22 = (bf16[4,96,128]{2,0,1:T(4,128)(2,1)}, bf16[4,96,128]{2,0,1:T(4,128)(2,1)S(1)}, u32[]{:S(2)}) copy-start(bf16[4,96,128]{2,0,1:T(4,128)(2,1)S(1)} %collective-permute-done.11) | copy-start | bytes 294916
  159.5 6.4 %copy-start.18 = (bf16[4,96,128]{2,0,1:T(4,128)(2,1)}, bf16[4,96,128]{2,0,1:T(4,128)(2,1)S(1)}, u32[]{:S(2)}) copy-start(bf16[4,96,128]{2,0,1:T(4,128)(2,1)S(1)} %collective-permute-done.16) | copy-start | bytes 294916
  159.9 6.0 %copy-start.30 = (bf16[4,96,128]{2,0,1:T(4,128)(2,1)}, bf16[4,96,128]{2,0,1:T(4,128)(2,1)S(1)}, u32[]{:S(2)}) copy-start(bf16[4,96,128]{2,0,1:T(4,128)(2,1)S(1)} %collective-permute-done.15) | copy-start | bytes 294916
  167.3 1.1 copy-start.31
  167.3 1.1 copy-start.19
  168.5 1.1 copy-start.11
  168.7 1.2 copy-start.6
  168.7 1.3 copy-start.7
  171.3 19.4 %collective-permute-start.18 = (bf16[3,96,128]{2,1,0:T(8,128)(2,1)S(1)}, bf16[3,96,128]{2,1,0:T(8,128)(2,1)S(1)}, u32[]{:S(2)}, u32[]{:S(2)}) collective-permute-start(bf16[3,96,128]{2,1,0:T(8,128)(2,1)S(1)} %get-tuple-element.47), channel_id=1, source_target_pairs={{0,1},{1,2},{2,3},{3,4},{4,5},{5,6},{6,7},{7,8},{8,9},{9,10},{10,1... | collective-permute-start | bytes 221192 | tf_op jit(solution)/shard_map/ppermute | solution.py:16
  173.2 23.1 %collective-permute-start.17 = (bf16[3,96,128]{2,1,0:T(8,128)(2,1)S(1)}, bf16[3,96,128]{2,1,0:T(8,128)(2,1)S(1)}, u32[]{:S(2)}, u32[]{:S(2)}) collective-permute-start(bf16[3,96,128]{2,1,0:T(8,128)(2,1)S(1)} %get-tuple-element.46), channel_id=1, source_target_pairs={{1,0},{2,1},{3,2},{4,3},{5,4},{6,5},{7,6},{8,7},{9,8},{10,9},{11,1... | collective-permute-start | bytes 221192 | tf_op jit(solution)/shard_map/ppermute | solution.py:16
  183.5 17.4 %collective-permute-start.21 = (bf16[4,96,128]{2,0,1:T(4,128)(2,1)S(1)}, bf16[4,96,128]{2,0,1:T(4,128)(2,1)S(1)}, u32[]{:S(2)}, u32[]{:S(2)}) collective-permute-start(bf16[4,96,128]{2,0,1:T(4,128)(2,1)S(1)} %pad_maximum_fusion.27), channel_id=1, source_target_pairs={{0,16},{16,32},{32,48},{48,64},{64,80},{80,96},{96,112},{112,128},... | collective-permute-start | bytes 294920 | tf_op jit(solution)/shard_map/ppermute | solution.py:21
  186.3 19.3 %collective-permute-start.20 = (bf16[4,96,128]{2,0,1:T(4,128)(2,1)S(1)}, bf16[4,96,128]{2,0,1:T(4,128)(2,1)S(1)}, u32[]{:S(2)}, u32[]{:S(2)}) collective-permute-start(bf16[4,96,128]{2,0,1:T(4,128)(2,1)S(1)} %pad_maximum_fusion.26), channel_id=1, source_target_pairs={{0,32},{16,48},{32,64},{48,80},{64,96},{80,112},{96,128},{112,144}... | collective-permute-start | bytes 294920 | tf_op jit(solution)/shard_map/ppermute | solution.py:21
  188.4 17.3 %collective-permute-start.19 = (bf16[4,96,128]{2,0,1:T(4,128)(2,1)S(1)}, bf16[4,96,128]{2,0,1:T(4,128)(2,1)S(1)}, u32[]{:S(2)}, u32[]{:S(2)}) collective-permute-start(bf16[4,96,128]{2,0,1:T(4,128)(2,1)S(1)} %pad_maximum_fusion.25), channel_id=1, source_target_pairs={{0,48},{16,64},{32,80},{48,96},{64,112},{80,128},{96,144},{112,160... | collective-permute-start | bytes 294920 | tf_op jit(solution)/shard_map/ppermute | solution.py:21
  190.7 15.1 %collective-permute-start.24 = (bf16[4,96,128]{2,0,1:T(4,128)(2,1)S(1)}, bf16[4,96,128]{2,0,1:T(4,128)(2,1)S(1)}, u32[]{:S(2)}, u32[]{:S(2)}) collective-permute-start(bf16[4,96,128]{2,0,1:T(4,128)(2,1)S(1)} %pad_maximum_fusion.30), channel_id=1, source_target_pairs={{0,464},{16,480},{32,496},{48,0},{64,16},{80,32},{96,48},{112,64},... | collective-permute-start | bytes 294920 | tf_op jit(solution)/shard_map/ppermute | solution.py:21
  196.3 9.6 %collective-permute-start.23 = (bf16[4,96,128]{2,0,1:T(4,128)(2,1)S(1)}, bf16[4,96,128]{2,0,1:T(4,128)(2,1)S(1)}, u32[]{:S(2)}, u32[]{:S(2)}) collective-permute-start(bf16[4,96,128]{2,0,1:T(4,128)(2,1)S(1)} %pad_maximum_fusion.29), channel_id=1, source_target_pairs={{0,480},{16,496},{32,0},{48,16},{64,32},{80,48},{96,64},{112,80},{... | collective-permute-start | bytes 294920 | tf_op jit(solution)/shard_map/ppermute | solution.py:21
  200.9 10.2 %copy-start.14 = (bf16[4,96,128]{2,0,1:T(4,128)(2,1)}, bf16[4,96,128]{2,0,1:T(4,128)(2,1)S(1)}, u32[]{:S(2)}) copy-start(bf16[4,96,128]{2,0,1:T(4,128)(2,1)S(1)} %collective-permute-done.21) | copy-start | bytes 294916
  200.9 10.2 %collective-permute-start.22 = (bf16[4,96,128]{2,0,1:T(4,128)(2,1)S(1)}, bf16[4,96,128]{2,0,1:T(4,128)(2,1)S(1)}, u32[]{:S(2)}, u32[]{:S(2)}) collective-permute-start(bf16[4,96,128]{2,0,1:T(4,128)(2,1)S(1)} %pad_maximum_fusion.28), channel_id=1, source_target_pairs={{0,496},{16,0},{32,16},{48,32},{64,48},{80,64},{96,80},{112,96},{1... | collective-permute-start | bytes 294920 | tf_op jit(solution)/shard_map/ppermute | solution.py:21
  205.6 5.5 %copy-start.20 = (bf16[4,96,128]{2,0,1:T(4,128)(2,1)}, bf16[4,96,128]{2,0,1:T(4,128)(2,1)S(1)}, u32[]{:S(2)}) copy-start(bf16[4,96,128]{2,0,1:T(4,128)(2,1)S(1)} %collective-permute-done.20) | copy-start | bytes 294916
  205.7 5.4 %copy-start.24 = (bf16[4,96,128]{2,0,1:T(4,128)(2,1)}, bf16[4,96,128]{2,0,1:T(4,128)(2,1)S(1)}, u32[]{:S(2)}) copy-start(bf16[4,96,128]{2,0,1:T(4,128)(2,1)S(1)} %collective-permute-done.19) | copy-start | bytes 294916
  205.8 5.3 %copy-start.26 = (bf16[4,96,128]{2,0,1:T(4,128)(2,1)}, bf16[4,96,128]{2,0,1:T(4,128)(2,1)S(1)}, u32[]{:S(2)}) copy-start(bf16[4,96,128]{2,0,1:T(4,128)(2,1)S(1)} %collective-permute-done.24) | copy-start | bytes 294916
  205.9 5.2 %copy-start.28 = (bf16[4,96,128]{2,0,1:T(4,128)(2,1)}, bf16[4,96,128]{2,0,1:T(4,128)(2,1)S(1)}, u32[]{:S(2)}) copy-start(bf16[4,96,128]{2,0,1:T(4,128)(2,1)S(1)} %collective-permute-done.23) | copy-start | bytes 294916
  213.8 1.1 copy-start.29
  213.8 1.1 copy-start.27
  215.2 1.1 copy-start.5
  215.2 1.2 copy-start.8
  (15 other events, 13.7 us)

commit v2 on v1

--- a/solution.py
+++ b/solution.py
@@ -35,8 +35,6 @@
     ]
     bucket_of = {o: b for b, o in enumerate(offsets)}
     shifts = [o for o in offsets if o > 0] + [o for o in offsets if o < 0]
-    lines = lax.axis_size("line")
-    me = lax.axis_index("line")
 
     boundary_blocks = shifted_open(blocks[knots - 3 :], "seg", 1)
     lower_blocks = jnp.concatenate([boundary_blocks, blocks], axis=0)
@@ -44,18 +42,15 @@
     used = jnp.arange(slots, dtype=jnp.int32)[None, :] < used_count[:, None]
     own_knot = jnp.where(used, my_pairs[:, :, 0], -1)
     far_knot = jnp.where(used, my_pairs[:, :, 1], -1)
-    table = lax.all_gather(far_knot, "line")
-
-    answer_knots = []
-    landing_knots = []
-    for s in shifts:
-        answer_knots.append(lax.dynamic_index_in_dim(table, (me + s) % lines, 0, False)[bucket_of[-s]])
-        landing_knots.append(lax.dynamic_index_in_dim(table, (me - s + lines) % lines, 0, False)[bucket_of[s]])
     knot_ids = jnp.arange(knots, dtype=jnp.int32)
-    pick_index = jnp.concatenate([own_knot.reshape(-1)] + answer_knots)
-    pick = (pick_index[:, None] == knot_ids[None, :]).astype(jnp.bfloat16)
+    own_pick = (own_knot.reshape(-1)[:, None] == knot_ids[None, :]).astype(jnp.bfloat16)
     own_place = (own_knot.reshape(-1)[None, :] == knot_ids[:, None]).astype(jnp.float32)
-    land_place = (jnp.concatenate(landing_knots)[None, :] == knot_ids[:, None]).astype(jnp.bfloat16)
+    far_pick = (far_knot[:, :, None] == knot_ids[None, None, :]).astype(jnp.bfloat16)
+    index_rows = jnp.zeros((buckets, 1, params, probes), jnp.bfloat16)
+    index_rows = index_rows.at[:, 0, 0, :slots].set(far_knot.astype(jnp.bfloat16))
+    knot_vals = knot_ids.astype(jnp.float32)
+    answer_pick = None
+    land_place = None
 
     center = (HI_BOUND + LO_BOUND) / 2.0
     radius = (HI_BOUND - LO_BOUND) / 2.0
@@ -67,21 +62,53 @@
     for turn in range(ITERS):
         probe_bf = direction.astype(jnp.bfloat16)
         solution = solution + direction
-        picked = jnp.einsum(
-            "sk,kpr->spr", pick, probe_bf, preferred_element_type=jnp.float32
-        ).astype(jnp.bfloat16)
-        resident = picked[:own_rows].reshape(buckets, slots, params, probes)
-        answers = picked[own_rows:].reshape(len(shifts), slots, params, probes)
+        if answer_pick is None:
+            picked = jnp.einsum(
+                "sk,kpr->spr", own_pick, probe_bf, preferred_element_type=jnp.float32
+            ).astype(jnp.bfloat16)
+            resident = picked.reshape(buckets, slots, params, probes)
+        else:
+            picked = jnp.einsum(
+                "sk,kpr->spr",
+                jnp.concatenate([own_pick, answer_pick], axis=0),
+                probe_bf,
+                preferred_element_type=jnp.float32,
+            ).astype(jnp.bfloat16)
+            resident = picked[:own_rows].reshape(buckets, slots, params, probes)
+            answers = picked[own_rows:].reshape(len(shifts), slots, params, probes)
         product = jnp.einsum(
             "bsqp,bsqr->bspr", couplings, resident, preferred_element_type=jnp.float32
         ).astype(jnp.bfloat16)
         fetched = [None] * buckets
         landed = []
+        got_index = {}
         for t, s in enumerate(shifts):
-            message = jnp.concatenate([answers[t], product[bucket_of[s]]], axis=0)
+            if answer_pick is None:
+                message = jnp.concatenate(
+                    [probe_bf, product[bucket_of[s]], index_rows[bucket_of[s]]], axis=0
+                )
+            else:
+                message = jnp.concatenate([answers[t], product[bucket_of[s]]], axis=0)
             got = shifted_ring(message, "line", s)
-            fetched[bucket_of[-s]] = got[:slots]
-            landed.append(got[slots:])
+            if answer_pick is None:
+                fetched[bucket_of[-s]] = jnp.einsum(
+                    "sk,kpr->spr",
+                    far_pick[bucket_of[-s]],
+                    got[:knots],
+                    preferred_element_type=jnp.float32,
+                ).astype(jnp.bfloat16)
+                landed.append(got[knots : knots + slots])
+                got_index[s] = got[knots + slots, 0, :slots].astype(jnp.float32)
+            else:
+                fetched[bucket_of[-s]] = got[:slots]
+                landed.append(got[slots:])
+        if answer_pick is None:
+            answer_pick = jnp.concatenate(
+                [(got_index[-s][:, None] == knot_vals[None, :]) for s in shifts], axis=0
+            ).astype(jnp.bfloat16)
+            land_place = jnp.concatenate(
+                [(got_index[s][None, :] == knot_vals[:, None]) for s in shifts], axis=1
+            ).astype(jnp.bfloat16)
         low = shifted_open(probe_bf[knots - 3 :], "seg", 1)
         high = shifted_open(probe_bf[:3], "seg", -1)
         extended = jnp.concatenate([low, probe_bf, high], axis=0)

time: 219 us -> 219 us (level)
  the two profiles are of different devices: /device:TPU:359 before, /device:TPU:487 now
where the time goes in v2:
time: 219 us; the launch traced here: 217 us
  starting transfers between devices  81.7 us (37%)
  waiting for transfers between devices  80.4 us (37%)
  matrix products  26.5 us (12%)
  local copies, waits for them, and re-layouts  18.7 us (9%)
  other arithmetic  8.86 us (4%)
    ppermute x18, starting transfers between devices, shifted_ring(): lax.ppermute(value, axis, [(i, (i + steps) % count) for i in range(count)])  54.9 us
    ppermute x7, waiting for transfers between devices, shifted_open(): lax.ppermute(value, axis, [(source, source + steps) for source in range(i...  52.4 us
    ppermute x18, waiting for transfers between devices, shifted_ring(): lax.ppermute(value, axis, [(i, (i + steps) % count) for i in range(count)])  28 us
    ppermute x7, starting transfers between devices, shifted_open(): lax.ppermute(value, axis, [(source, source + steps) for source in range(i...  26.9 us
    dot_general x9, matrix products, body(): jnp.einsum('kba,kbr->kar', lower_blocks[3 - step:3 - step + knots, step],...  9.16 us
    unnamed x82, local copies, waits for them, and re-layouts  8.96 us
    dot_general x12, matrix products, body(): jnp.einsum('kab,kbr->kar', blocks[:, step], extended[3 + step:3 + step +...  8.27 us
  transfers between devices with their start and end apart: 25, of which 9 were waited for; matrix products, arithmetic and copies ran while one was open for 8% of the time, Pallas kernels for 0%

profile of v2, /device:TPU:487, one launch (start us, length us, event | category | flops | bytes accessed | tf_op | source)
XLA Modules:
  0.0 217.3 jit_solution(2371888662827749713)
XLA Ops:
  0.0 1.1 fusion.47
  4.5 1.2 fusion.64
  5.7 4.0 %collective-permute-start.5 = (bf16[11,96,128]{2,1,0:T(8,128)(2,1)}, bf16[11,96,128]{2,1,0:T(8,128)(2,1)}, u32[]{:S(2)}, u32[]{:S(2)}) collective-permute-start(bf16[11,96,128]{2,1,0:T(8,128)(2,1)} %get-tuple-element.59), channel_id=1, source_target_pairs={{0,16},{16,32},{32,48},{48,64},{64,80},{80,96},{96,112},{112,128},... | collective-permute-start | bytes 811016 | tf_op jit(solution)/shard_map/ppermute | solution.py:21
  9.7 3.1 %collective-permute-start.4 = (bf16[11,96,128]{2,1,0:T(8,128)(2,1)}, bf16[11,96,128]{2,1,0:T(8,128)(2,1)}, u32[]{:S(2)}, u32[]{:S(2)}) collective-permute-start(bf16[11,96,128]{2,1,0:T(8,128)(2,1)} %get-tuple-element.58), channel_id=1, source_target_pairs={{0,32},{16,48},{32,64},{48,80},{64,96},{80,112},{96,128},{112,144}... | collective-permute-start | bytes 811016 | tf_op jit(solution)/shard_map/ppermute | solution.py:21
  12.8 3.1 %collective-permute-start.3 = (bf16[11,96,128]{2,1,0:T(8,128)(2,1)}, bf16[11,96,128]{2,1,0:T(8,128)(2,1)}, u32[]{:S(2)}, u32[]{:S(2)}) collective-permute-start(bf16[11,96,128]{2,1,0:T(8,128)(2,1)} %get-tuple-element.57), channel_id=1, source_target_pairs={{0,48},{16,64},{32,80},{48,96},{64,112},{80,128},{96,144},{112,160... | collective-permute-start | bytes 811016 | tf_op jit(solution)/shard_map/ppermute | solution.py:21
  16.0 2.4 %collective-permute-start.8 = (bf16[11,96,128]{2,1,0:T(8,128)(2,1)}, bf16[11,96,128]{2,1,0:T(8,128)(2,1)}, u32[]{:S(2)}, u32[]{:S(2)}) collective-permute-start(bf16[11,96,128]{2,1,0:T(8,128)(2,1)} %get-tuple-element.61), channel_id=1, source_target_pairs={{0,464},{16,480},{32,496},{48,0},{64,16},{80,32},{96,48},{112,64},... | collective-permute-start | bytes 811016 | tf_op jit(solution)/shard_map/ppermute | solution.py:21
  18.4 7.6 %collective-permute-start = (bf16[3,96,128]{2,1,0:T(8,128)(2,1)S(1)}, bf16[3,96,128]{2,1,0:T(8,128)(2,1)S(1)}, u32[]{:S(2)}, u32[]{:S(2)}) collective-permute-start(bf16[3,96,128]{2,1,0:T(8,128)(2,1)S(1)} %get-tuple-element.62), channel_id=1, source_target_pairs={{1,0},{2,1},{3,2},{4,3},{5,4},{6,5},{7,6},{8,7},{9,8},{10,9},{11,1... | collective-permute-start | bytes 221192 | tf_op jit(solution)/shard_map/ppermute | solution.py:16
  26.6 1.9 collective-permute-done
  28.4 1.9 collective-permute-start.1
  31.5 31.4 %collective-permute-done.1 = bf16[3,4,96,96]{3,2,0,1:T(8,128)(2,1)S(1)} collective-permute-done((bf16[3,4,96,96]{3,2,0,1:T(8,128)(2,1)S(1)}, bf16[3,4,96,96]{3,2,0,1:T(8,128)(2,1)S(1)}, u32[]{:S(2)}, u32[]{:S(2)}) %collective-permute-start.1) | collective-permute-done | bytes 221216 | tf_op jit(solution)/shard_map/ppermute | solution.py:16
  62.9 2.0 collective-permute-start.2
  65.1 9.1 %collective-permute-done.2 = bf16[3,96,128]{2,1,0:T(8,128)(2,1)S(1)} collective-permute-done((bf16[3,96,128]{2,1,0:T(8,128)(2,1)S(1)}, bf16[3,96,128]{2,1,0:T(8,128)(2,1)S(1)}, u32[]{:S(2)}, u32[]{:S(2)}) %collective-permute-start.2) | collective-permute-done | bytes 73760 | tf_op jit(solution)/shard_map/ppermute | solution.py:16
  74.1 3.5 %collective-permute-start.6 = (bf16[11,96,128]{2,1,0:T(8,128)(2,1)S(1)}, bf16[11,96,128]{2,1,0:T(8,128)(2,1)S(1)}, u32[]{:S(2)}, u32[]{:S(2)}) collective-permute-start(bf16[11,96,128]{2,1,0:T(8,128)(2,1)S(1)} %copy-done.13), channel_id=1, source_target_pairs={{0,496},{16,0},{32,16},{48,32},{64,48},{80,64},{96,80},{112,96},{1... | collective-permute-start | bytes 811016 | tf_op jit(solution)/shard_map/ppermute | solution.py:21
  77.7 1.0 fusion.105
  79.7 1.0 fusion.91
  80.7 12.2 %collective-permute-done.6 = bf16[11,96,128]{2,1,0:T(8,128)(2,1)S(1)} collective-permute-done((bf16[11,96,128]{2,1,0:T(8,128)(2,1)S(1)}, bf16[11,96,128]{2,1,0:T(8,128)(2,1)S(1)}, u32[]{:S(2)}, u32[]{:S(2)}) %collective-permute-start.6) | collective-permute-done | bytes 270368 | tf_op jit(solution)/shard_map/ppermute | solution.py:21
  93.0 1.9 collective-permute-start.7
  96.9 7.2 %collective-permute-done.7 = bf16[11,96,128]{2,1,0:T(8,128)(2,1)S(1)} collective-permute-done((bf16[11,96,128]{2,1,0:T(8,128)(2,1)S(1)}, bf16[11,96,128]{2,1,0:T(8,128)(2,1)S(1)}, u32[]{:S(2)}, u32[]{:S(2)}) %collective-permute-start.7) | collective-permute-done | bytes 270368 | tf_op jit(solution)/shard_map/ppermute | solution.py:21
  110.2 1.5 fusion.42
  117.7 1.9 fusion.122
  121.5 1.9 collective-permute-start.13
  123.5 1.9 collective-permute-start.12
  125.6 1.9 collective-permute-start.11
  127.6 4.0 %collective-permute-start.16 = (bf16[4,96,128]{2,0,1:T(4,128)(2,1)S(1)}, bf16[4,96,128]{2,0,1:T(4,128)(2,1)S(1)}, u32[]{:S(2)}, u32[]{:S(2)}) collective-permute-start(bf16[4,96,128]{2,0,1:T(4,128)(2,1)S(1)} %pad_maximum_fusion.24), channel_id=1, source_target_pairs={{0,464},{16,480},{32,496},{48,0},{64,16},{80,32},{96,48},{112,64},... | collective-permute-start | bytes 294920 | tf_op jit(solution)/shard_map/ppermute | solution.py:21
  131.6 1.9 collective-permute-start.10
  133.8 9.0 %collective-permute-done.10 = bf16[3,96,128]{2,1,0:T(8,128)(2,1)S(1)} collective-permute-done((bf16[3,96,128]{2,1,0:T(8,128)(2,1)S(1)}, bf16[3,96,128]{2,1,0:T(8,128)(2,1)S(1)}, u32[]{:S(2)}, u32[]{:S(2)}) %collective-permute-start.10) | collective-permute-done | bytes 73760 | tf_op jit(solution)/shard_map/ppermute | solution.py:16
  142.7 1.9 collective-permute-start.9
  144.7 1.0 fusion.101
  145.7 1.0 fusion.78
  146.7 1.1 collective-permute-done.9
  147.8 3.2 %collective-permute-start.15 = (bf16[4,96,128]{2,0,1:T(4,128)(2,1)S(1)}, bf16[4,96,128]{2,0,1:T(4,128)(2,1)S(1)}, u32[]{:S(2)}, u32[]{:S(2)}) collective-permute-start(bf16[4,96,128]{2,0,1:T(4,128)(2,1)S(1)} %pad_maximum_fusion.23), channel_id=1, source_target_pairs={{0,480},{16,496},{32,0},{48,16},{64,32},{80,48},{96,64},{112,80},{... | collective-permute-start | bytes 294920 | tf_op jit(solution)/shard_map/ppermute | solution.py:21
  152.0 1.0 fusion.81
  153.1 6.5 %collective-permute-start.14 = (bf16[4,96,128]{2,0,1:T(4,128)(2,1)S(1)}, bf16[4,96,128]{2,0,1:T(4,128)(2,1)S(1)}, u32[]{:S(2)}, u32[]{:S(2)}) collective-permute-start(bf16[4,96,128]{2,0,1:T(4,128)(2,1)S(1)} %pad_maximum_fusion.22), channel_id=1, source_target_pairs={{0,496},{16,0},{32,16},{48,32},{64,48},{80,64},{96,80},{112,96},{1... | collective-permute-start | bytes 294920 | tf_op jit(solution)/shard_map/ppermute | solution.py:21
  161.3 4.1 %collective-permute-done.14 = bf16[4,96,128]{2,0,1:T(4,128)(2,1)S(1)} collective-permute-done((bf16[4,96,128]{2,0,1:T(4,128)(2,1)S(1)}, bf16[4,96,128]{2,0,1:T(4,128)(2,1)S(1)}, u32[]{:S(2)}, u32[]{:S(2)}) %collective-permute-start.14) | collective-permute-done | bytes 98336 | tf_op jit(solution)/shard_map/ppermute | solution.py:21
  170.7 1.9 collective-permute-start.18
  172.7 9.6 %collective-permute-start.17 = (bf16[3,96,128]{2,1,0:T(8,128)(2,1)S(1)}, bf16[3,96,128]{2,1,0:T(8,128)(2,1)S(1)}, u32[]{:S(2)}, u32[]{:S(2)}) collective-permute-start(bf16[3,96,128]{2,1,0:T(8,128)(2,1)S(1)} %get-tuple-element.52), channel_id=1, source_target_pairs={{1,0},{2,1},{3,2},{4,3},{5,4},{6,5},{7,6},{8,7},{9,8},{10,9},{11,1... | collective-permute-start | bytes 221192 | tf_op jit(solution)/shard_map/ppermute | solution.py:16
  183.2 2.5 %collective-permute-start.21 = (bf16[4,96,128]{2,0,1:T(4,128)(2,1)S(1)}, bf16[4,96,128]{2,0,1:T(4,128)(2,1)S(1)}, u32[]{:S(2)}, u32[]{:S(2)}) collective-permute-start(bf16[4,96,128]{2,0,1:T(4,128)(2,1)S(1)} %pad_maximum_fusion.27), channel_id=1, source_target_pairs={{0,16},{16,32},{32,48},{48,64},{64,80},{80,96},{96,112},{112,128},... | collective-permute-start | bytes 294920 | tf_op jit(solution)/shard_map/ppermute | solution.py:21
  185.8 1.9 collective-permute-start.20
  187.8 1.9 collective-permute-start.19
  190.1 3.6 %collective-permute-start.24 = (bf16[4,96,128]{2,0,1:T(4,128)(2,1)S(1)}, bf16[4,96,128]{2,0,1:T(4,128)(2,1)S(1)}, u32[]{:S(2)}, u32[]{:S(2)}) collective-permute-start(bf16[4,96,128]{2,0,1:T(4,128)(2,1)S(1)} %pad_maximum_fusion.30), channel_id=1, source_target_pairs={{0,464},{16,480},{32,496},{48,0},{64,16},{80,32},{96,48},{112,64},... | collective-permute-start | bytes 294920 | tf_op jit(solution)/shard_map/ppermute | solution.py:21
  193.7 1.0 fusion.97
  194.7 1.0 fusion.68
  195.8 3.4 %collective-permute-start.23 = (bf16[4,96,128]{2,0,1:T(4,128)(2,1)S(1)}, bf16[4,96,128]{2,0,1:T(4,128)(2,1)S(1)}, u32[]{:S(2)}, u32[]{:S(2)}) collective-permute-start(bf16[4,96,128]{2,0,1:T(4,128)(2,1)S(1)} %pad_maximum_fusion.29), channel_id=1, source_target_pairs={{0,480},{16,496},{32,0},{48,16},{64,32},{80,48},{96,64},{112,80},{... | collective-permute-start | bytes 294920 | tf_op jit(solution)/shard_map/ppermute | solution.py:21
  200.3 3.9 %collective-permute-start.22 = (bf16[4,96,128]{2,0,1:T(4,128)(2,1)S(1)}, bf16[4,96,128]{2,0,1:T(4,128)(2,1)S(1)}, u32[]{:S(2)}, u32[]{:S(2)}) collective-permute-start(bf16[4,96,128]{2,0,1:T(4,128)(2,1)S(1)} %pad_maximum_fusion.28), channel_id=1, source_target_pairs={{0,496},{16,0},{32,16},{48,32},{64,48},{80,64},{96,80},{112,96},{1... | collective-permute-start | bytes 294920 | tf_op jit(solution)/shard_map/ppermute | solution.py:21
  206.1 4.4 %collective-permute-done.22 = bf16[4,96,128]{2,0,1:T(4,128)(2,1)S(1)} collective-permute-done((bf16[4,96,128]{2,0,1:T(4,128)(2,1)S(1)}, bf16[4,96,128]{2,0,1:T(4,128)(2,1)S(1)}, u32[]{:S(2)}, u32[]{:S(2)}) %collective-permute-start.22) | collective-permute-done | bytes 98336 | tf_op jit(solution)/shard_map/ppermute | solution.py:21
  211.2 1.8 concatenate.143
  213.0 1.2 fusion.135
  216.1 1.2 fusion.24
  (201 shorter events, 36.9 us)
Async XLA Ops:
  0.0 4.1 %copy-start = (bf16[1,1,6,2,96,96]{5,4,3,2,1,0:T(8,128)(2,1)S(1)}, bf16[1,1,6,2,96,96]{5,4,3,2,1,0:T(8,128)(2,1)}, u32[]{:S(2)}) copy-start(bf16[1,1,6,2,96,96]{5,4,3,2,1,0:T(8,128)(2,1)} %param.11) | copy-start | bytes 663556
  4.4 21.8 %copy-start.11 = (bf16[1,8,4,96,96]{4,3,2,1,0:T(8,128)(2,1)S(1)}, bf16[1,8,4,96,96]{4,3,2,1,0:T(8,128)(2,1)}, u32[]{:S(2)}) copy-start(bf16[1,8,4,96,96]{4,3,2,1,0:T(8,128)(2,1)} %param.8) | copy-start | bytes 1769476
  5.7 98.4 %collective-permute-start.5 = (bf16[11,96,128]{2,1,0:T(8,128)(2,1)}, bf16[11,96,128]{2,1,0:T(8,128)(2,1)}, u32[]{:S(2)}, u32[]{:S(2)}) collective-permute-start(bf16[11,96,128]{2,1,0:T(8,128)(2,1)} %get-tuple-element.59), channel_id=1, source_target_pairs={{0,16},{16,32},{32,48},{48,64},{64,80},{80,96},{96,112},{112,128},... | collective-permute-start | bytes 811016 | tf_op jit(solution)/shard_map/ppermute | solution.py:21
  9.7 85.2 %collective-permute-start.4 = (bf16[11,96,128]{2,1,0:T(8,128)(2,1)}, bf16[11,96,128]{2,1,0:T(8,128)(2,1)}, u32[]{:S(2)}, u32[]{:S(2)}) collective-permute-start(bf16[11,96,128]{2,1,0:T(8,128)(2,1)} %get-tuple-element.58), channel_id=1, source_target_pairs={{0,32},{16,48},{32,64},{48,80},{64,96},{80,112},{96,128},{112,144}... | collective-permute-start | bytes 811016 | tf_op jit(solution)/shard_map/ppermute | solution.py:21
  12.8 82.7 %collective-permute-start.3 = (bf16[11,96,128]{2,1,0:T(8,128)(2,1)}, bf16[11,96,128]{2,1,0:T(8,128)(2,1)}, u32[]{:S(2)}, u32[]{:S(2)}) collective-permute-start(bf16[11,96,128]{2,1,0:T(8,128)(2,1)} %get-tuple-element.57), channel_id=1, source_target_pairs={{0,48},{16,64},{32,80},{48,96},{64,112},{80,128},{96,144},{112,160... | collective-permute-start | bytes 811016 | tf_op jit(solution)/shard_map/ppermute | solution.py:21
  16.0 80.3 %collective-permute-start.8 = (bf16[11,96,128]{2,1,0:T(8,128)(2,1)}, bf16[11,96,128]{2,1,0:T(8,128)(2,1)}, u32[]{:S(2)}, u32[]{:S(2)}) collective-permute-start(bf16[11,96,128]{2,1,0:T(8,128)(2,1)} %get-tuple-element.61), channel_id=1, source_target_pairs={{0,464},{16,480},{32,496},{48,0},{64,16},{80,32},{96,48},{112,64},... | collective-permute-start | bytes 811016 | tf_op jit(solution)/shard_map/ppermute | solution.py:21
  18.4 10.0 %collective-permute-start = (bf16[3,96,128]{2,1,0:T(8,128)(2,1)S(1)}, bf16[3,96,128]{2,1,0:T(8,128)(2,1)S(1)}, u32[]{:S(2)}, u32[]{:S(2)}) collective-permute-start(bf16[3,96,128]{2,1,0:T(8,128)(2,1)S(1)} %get-tuple-element.62), channel_id=1, source_target_pairs={{1,0},{2,1},{3,2},{4,3},{5,4},{6,5},{7,6},{8,7},{9,8},{10,9},{11,1... | collective-permute-start | bytes 221192 | tf_op jit(solution)/shard_map/ppermute | solution.py:16
  28.4 34.4 %collective-permute-start.1 = (bf16[3,4,96,96]{3,2,0,1:T(8,128)(2,1)S(1)}, bf16[3,4,96,96]{3,2,0,1:T(8,128)(2,1)S(1)}, u32[]{:S(2)}, u32[]{:S(2)}) collective-permute-start(bf16[3,4,96,96]{3,2,0,1:T(8,128)(2,1)S(1)} %slice_bitcast_fusion), channel_id=1, source_target_pairs={{0,1},{1,2},{2,3},{3,4},{4,5},{5,6},{6,7},{7,8},{8,9},{9,10},{10,1... | collective-permute-start | bytes 663560 | tf_op jit(solution)/shard_map/ppermute | solution.py:16
  62.9 11.2 %copy-start.13 = (bf16[11,96,128]{2,1,0:T(8,128)(2,1)S(1)}, bf16[11,96,128]{2,1,0:T(8,128)(2,1)}, u32[]{:S(2)}) copy-start(bf16[11,96,128]{2,1,0:T(8,128)(2,1)} %get-tuple-element.56) | copy-start | bytes 811012
  62.9 11.2 %collective-permute-start.2 = (bf16[3,96,128]{2,1,0:T(8,128)(2,1)S(1)}, bf16[3,96,128]{2,1,0:T(8,128)(2,1)S(1)}, u32[]{:S(2)}, u32[]{:S(2)}) collective-permute-start(bf16[3,96,128]{2,1,0:T(8,128)(2,1)S(1)} %get-tuple-element.63), channel_id=1, source_target_pairs={{0,1},{1,2},{2,3},{3,4},{4,5},{5,6},{6,7},{7,8},{8,9},{9,10},{10,1... | collective-permute-start | bytes 221192 | tf_op jit(solution)/shard_map/ppermute | solution.py:16
  74.1 18.9 %collective-permute-start.6 = (bf16[11,96,128]{2,1,0:T(8,128)(2,1)S(1)}, bf16[11,96,128]{2,1,0:T(8,128)(2,1)S(1)}, u32[]{:S(2)}, u32[]{:S(2)}) collective-permute-start(bf16[11,96,128]{2,1,0:T(8,128)(2,1)S(1)} %copy-done.13), channel_id=1, source_target_pairs={{0,496},{16,0},{32,16},{48,32},{64,48},{80,64},{96,80},{112,96},{1... | collective-permute-start | bytes 811016 | tf_op jit(solution)/shard_map/ppermute | solution.py:21
  78.7 14.3 %copy-start.12 = (bf16[11,96,128]{2,1,0:T(8,128)(2,1)S(1)}, bf16[11,96,128]{2,1,0:T(8,128)(2,1)}, u32[]{:S(2)}) copy-start(bf16[11,96,128]{2,1,0:T(8,128)(2,1)} %get-tuple-element.60) | copy-start | bytes 811012
  93.0 15.4 %copy-start.14 = (bf16[11,96,128]{2,1,0:T(8,128)(2,1)}, bf16[11,96,128]{2,1,0:T(8,128)(2,1)S(1)}, u32[]{:S(2)}) copy-start(bf16[11,96,128]{2,1,0:T(8,128)(2,1)S(1)} %collective-permute-done.6) | copy-start | bytes 811012
  93.0 11.1 %collective-permute-start.7 = (bf16[11,96,128]{2,1,0:T(8,128)(2,1)S(1)}, bf16[11,96,128]{2,1,0:T(8,128)(2,1)S(1)}, u32[]{:S(2)}, u32[]{:S(2)}) collective-permute-start(bf16[11,96,128]{2,1,0:T(8,128)(2,1)S(1)} %copy-done.12), channel_id=1, source_target_pairs={{0,480},{16,496},{32,0},{48,16},{64,32},{80,48},{96,64},{112,80},{... | collective-permute-start | bytes 811016 | tf_op jit(solution)/shard_map/ppermute | solution.py:21
  104.1 4.5 %copy-start.15 = (bf16[11,96,128]{2,1,0:T(8,128)(2,1)}, bf16[11,96,128]{2,1,0:T(8,128)(2,1)S(1)}, u32[]{:S(2)}) copy-start(bf16[11,96,128]{2,1,0:T(8,128)(2,1)S(1)} %collective-permute-done.7) | copy-start | bytes 811012
  111.7 6.0 %copy-start.1 = (f32[1,8,96,128]{3,2,1,0:T(8,128)S(1)}, f32[1,8,96,128]{3,2,1,0:T(8,128)}, u32[]{:S(2)}) copy-start(f32[1,8,96,128]{3,2,1,0:T(8,128)} %param.7) | copy-start | bytes 1179652
  121.5 31.6 %collective-permute-start.13 = (bf16[4,96,128]{2,0,1:T(4,128)(2,1)S(1)}, bf16[4,96,128]{2,0,1:T(4,128)(2,1)S(1)}, u32[]{:S(2)}, u32[]{:S(2)}) collective-permute-start(bf16[4,96,128]{2,0,1:T(4,128)(2,1)S(1)} %pad_maximum_fusion.21), channel_id=1, source_target_pairs={{0,16},{16,32},{32,48},{48,64},{64,80},{80,96},{96,112},{112,128},... | collective-permute-start | bytes 294920 | tf_op jit(solution)/shard_map/ppermute | solution.py:21
  123.5 37.0 %collective-permute-start.12 = (bf16[4,96,128]{2,0,1:T(4,128)(2,1)S(1)}, bf16[4,96,128]{2,0,1:T(4,128)(2,1)S(1)}, u32[]{:S(2)}, u32[]{:S(2)}) collective-permute-start(bf16[4,96,128]{2,0,1:T(4,128)(2,1)S(1)} %pad_maximum_fusion.20), channel_id=1, source_target_pairs={{0,32},{16,48},{32,64},{48,80},{64,96},{80,112},{96,128},{112,144}... | collective-permute-start | bytes 294920 | tf_op jit(solution)/shard_map/ppermute | solution.py:21
  125.6 35.1 %collective-permute-start.11 = (bf16[4,96,128]{2,0,1:T(4,128)(2,1)S(1)}, bf16[4,96,128]{2,0,1:T(4,128)(2,1)S(1)}, u32[]{:S(2)}, u32[]{:S(2)}) collective-permute-start(bf16[4,96,128]{2,0,1:T(4,128)(2,1)S(1)} %pad_maximum_fusion.19), channel_id=1, source_target_pairs={{0,48},{16,64},{32,80},{48,96},{64,112},{80,128},{96,144},{112,160... | collective-permute-start | bytes 294920 | tf_op jit(solution)/shard_map/ppermute | solution.py:21
  127.6 33.1 %collective-permute-start.16 = (bf16[4,96,128]{2,0,1:T(4,128)(2,1)S(1)}, bf16[4,96,128]{2,0,1:T(4,128)(2,1)S(1)}, u32[]{:S(2)}, u32[]{:S(2)}) collective-permute-start(bf16[4,96,128]{2,0,1:T(4,128)(2,1)S(1)} %pad_maximum_fusion.24), channel_id=1, source_target_pairs={{0,464},{16,480},{32,496},{48,0},{64,16},{80,32},{96,48},{112,64},... | collective-permute-start | bytes 294920 | tf_op jit(solution)/shard_map/ppermute | solution.py:21
  131.6 11.1 %collective-permute-start.10 = (bf16[3,96,128]{2,1,0:T(8,128)(2,1)S(1)}, bf16[3,96,128]{2,1,0:T(8,128)(2,1)S(1)}, u32[]{:S(2)}, u32[]{:S(2)}) collective-permute-start(bf16[3,96,128]{2,1,0:T(8,128)(2,1)S(1)} %get-tuple-element.55), channel_id=1, source_target_pairs={{0,1},{1,2},{2,3},{3,4},{4,5},{5,6},{6,7},{7,8},{8,9},{9,10},{10,1... | collective-permute-start | bytes 221192 | tf_op jit(solution)/shard_map/ppermute | solution.py:16
  142.7 5.1 %collective-permute-start.9 = (bf16[3,96,128]{2,1,0:T(8,128)(2,1)S(1)}, bf16[3,96,128]{2,1,0:T(8,128)(2,1)S(1)}, u32[]{:S(2)}, u32[]{:S(2)}) collective-permute-start(bf16[3,96,128]{2,1,0:T(8,128)(2,1)S(1)} %get-tuple-element.54), channel_id=1, source_target_pairs={{1,0},{2,1},{3,2},{4,3},{5,4},{6,5},{7,6},{8,7},{9,8},{10,9},{11,1... | collective-permute-start | bytes 221192 | tf_op jit(solution)/shard_map/ppermute | solution.py:16
  147.8 13.4 %collective-permute-start.15 = (bf16[4,96,128]{2,0,1:T(4,128)(2,1)S(1)}, bf16[4,96,128]{2,0,1:T(4,128)(2,1)S(1)}, u32[]{:S(2)}, u32[]{:S(2)}) collective-permute-start(bf16[4,96,128]{2,0,1:T(4,128)(2,1)S(1)} %pad_maximum_fusion.23), channel_id=1, source_target_pairs={{0,480},{16,496},{32,0},{48,16},{64,32},{80,48},{96,64},{112,80},{... | collective-permute-start | bytes 294920 | tf_op jit(solution)/shard_map/ppermute | solution.py:21
  153.1 12.3 %collective-permute-start.14 = (bf16[4,96,128]{2,0,1:T(4,128)(2,1)S(1)}, bf16[4,96,128]{2,0,1:T(4,128)(2,1)S(1)}, u32[]{:S(2)}, u32[]{:S(2)}) collective-permute-start(bf16[4,96,128]{2,0,1:T(4,128)(2,1)S(1)} %pad_maximum_fusion.22), channel_id=1, source_target_pairs={{0,496},{16,0},{32,16},{48,32},{64,48},{80,64},{96,80},{112,96},{1... | collective-permute-start | bytes 294920 | tf_op jit(solution)/shard_map/ppermute | solution.py:21
  160.6 4.7 %copy-start.20 = (bf16[4,96,128]{2,0,1:T(4,128)(2,1)}, bf16[4,96,128]{2,0,1:T(4,128)(2,1)S(1)}, u32[]{:S(2)}) copy-start(bf16[4,96,128]{2,0,1:T(4,128)(2,1)S(1)} %collective-permute-done.11) | copy-start | bytes 294916
  160.7 4.6 %copy-start.18 = (bf16[4,96,128]{2,0,1:T(4,128)(2,1)}, bf16[4,96,128]{2,0,1:T(4,128)(2,1)S(1)}, u32[]{:S(2)}) copy-start(bf16[4,96,128]{2,0,1:T(4,128)(2,1)S(1)} %collective-permute-done.16) | copy-start | bytes 294916
  161.2 4.2 %copy-start.26 = (bf16[4,96,128]{2,0,1:T(4,128)(2,1)}, bf16[4,96,128]{2,0,1:T(4,128)(2,1)S(1)}, u32[]{:S(2)}) copy-start(bf16[4,96,128]{2,0,1:T(4,128)(2,1)S(1)} %collective-permute-done.15) | copy-start | bytes 294916
  166.7 1.1 copy-start.27
  166.7 1.1 copy-start.19
  167.9 1.1 copy-start.10
  168.2 1.1 copy-start.2
  168.2 1.2 copy-start.5
  168.2 1.3 copy-start.6
  170.7 19.3 %collective-permute-start.18 = (bf16[3,96,128]{2,1,0:T(8,128)(2,1)S(1)}, bf16[3,96,128]{2,1,0:T(8,128)(2,1)S(1)}, u32[]{:S(2)}, u32[]{:S(2)}) collective-permute-start(bf16[3,96,128]{2,1,0:T(8,128)(2,1)S(1)} %get-tuple-element.53), channel_id=1, source_target_pairs={{0,1},{1,2},{2,3},{3,4},{4,5},{5,6},{6,7},{7,8},{8,9},{9,10},{10,1... | collective-permute-start | bytes 221192 | tf_op jit(solution)/shard_map/ppermute | solution.py:16
  172.7 23.1 %collective-permute-start.17 = (bf16[3,96,128]{2,1,0:T(8,128)(2,1)S(1)}, bf16[3,96,128]{2,1,0:T(8,128)(2,1)S(1)}, u32[]{:S(2)}, u32[]{:S(2)}) collective-permute-start(bf16[3,96,128]{2,1,0:T(8,128)(2,1)S(1)} %get-tuple-element.52), channel_id=1, source_target_pairs={{1,0},{2,1},{3,2},{4,3},{5,4},{6,5},{7,6},{8,7},{9,8},{10,9},{11,1... | collective-permute-start | bytes 221192 | tf_op jit(solution)/shard_map/ppermute | solution.py:16
  183.2 17.2 %collective-permute-start.21 = (bf16[4,96,128]{2,0,1:T(4,128)(2,1)S(1)}, bf16[4,96,128]{2,0,1:T(4,128)(2,1)S(1)}, u32[]{:S(2)}, u32[]{:S(2)}) collective-permute-start(bf16[4,96,128]{2,0,1:T(4,128)(2,1)S(1)} %pad_maximum_fusion.27), channel_id=1, source_target_pairs={{0,16},{16,32},{32,48},{48,64},{64,80},{80,96},{96,112},{112,128},... | collective-permute-start | bytes 294920 | tf_op jit(solution)/shard_map/ppermute | solution.py:21
  185.8 19.5 %collective-permute-start.20 = (bf16[4,96,128]{2,0,1:T(4,128)(2,1)S(1)}, bf16[4,96,128]{2,0,1:T(4,128)(2,1)S(1)}, u32[]{:S(2)}, u32[]{:S(2)}) collective-permute-start(bf16[4,96,128]{2,0,1:T(4,128)(2,1)S(1)} %pad_maximum_fusion.26), channel_id=1, source_target_pairs={{0,32},{16,48},{32,64},{48,80},{64,96},{80,112},{96,128},{112,144}... | collective-permute-start | bytes 294920 | tf_op jit(solution)/shard_map/ppermute | solution.py:21
  187.8 17.6 %collective-permute-start.19 = (bf16[4,96,128]{2,0,1:T(4,128)(2,1)S(1)}, bf16[4,96,128]{2,0,1:T(4,128)(2,1)S(1)}, u32[]{:S(2)}, u32[]{:S(2)}) collective-permute-start(bf16[4,96,128]{2,0,1:T(4,128)(2,1)S(1)} %pad_maximum_fusion.25), channel_id=1, source_target_pairs={{0,48},{16,64},{32,80},{48,96},{64,112},{80,128},{96,144},{112,160... | collective-permute-start | bytes 294920 | tf_op jit(solution)/shard_map/ppermute | solution.py:21
  190.1 15.4 %collective-permute-start.24 = (bf16[4,96,128]{2,0,1:T(4,128)(2,1)S(1)}, bf16[4,96,128]{2,0,1:T(4,128)(2,1)S(1)}, u32[]{:S(2)}, u32[]{:S(2)}) collective-permute-start(bf16[4,96,128]{2,0,1:T(4,128)(2,1)S(1)} %pad_maximum_fusion.30), channel_id=1, source_target_pairs={{0,464},{16,480},{32,496},{48,0},{64,16},{80,32},{96,48},{112,64},... | collective-permute-start | bytes 294920 | tf_op jit(solution)/shard_map/ppermute | solution.py:21
  195.8 9.8 %collective-permute-start.23 = (bf16[4,96,128]{2,0,1:T(4,128)(2,1)S(1)}, bf16[4,96,128]{2,0,1:T(4,128)(2,1)S(1)}, u32[]{:S(2)}, u32[]{:S(2)}) collective-permute-start(bf16[4,96,128]{2,0,1:T(4,128)(2,1)S(1)} %pad_maximum_fusion.29), channel_id=1, source_target_pairs={{0,480},{16,496},{32,0},{48,16},{64,32},{80,48},{96,64},{112,80},{... | collective-permute-start | bytes 294920 | tf_op jit(solution)/shard_map/ppermute | solution.py:21
  200.3 10.2 %collective-permute-start.22 = (bf16[4,96,128]{2,0,1:T(4,128)(2,1)S(1)}, bf16[4,96,128]{2,0,1:T(4,128)(2,1)S(1)}, u32[]{:S(2)}, u32[]{:S(2)}) collective-permute-start(bf16[4,96,128]{2,0,1:T(4,128)(2,1)S(1)} %pad_maximum_fusion.28), channel_id=1, source_target_pairs={{0,496},{16,0},{32,16},{48,32},{64,48},{80,64},{96,80},{112,96},{1... | collective-permute-start | bytes 294920 | tf_op jit(solution)/shard_map/ppermute | solution.py:21
  205.5 5.0 %copy-start.24 = (bf16[4,96,128]{2,0,1:T(4,128)(2,1)}, bf16[4,96,128]{2,0,1:T(4,128)(2,1)S(1)}, u32[]{:S(2)}) copy-start(bf16[4,96,128]{2,0,1:T(4,128)(2,1)S(1)} %collective-permute-done.23) | copy-start | bytes 294916
  213.0 1.4 copy-start.29
  213.0 1.4 copy-start.25
  213.0 1.5 copy-start.23
  214.8 1.0 copy-start.3
  214.8 1.1 copy-start.4
  214.8 1.2 copy-start.7
  (9 other events, 7.4 us)

commit v3 on v2

--- a/solution.py
+++ b/solution.py
@@ -49,6 +49,25 @@
     index_rows = jnp.zeros((buckets, 1, params, probes), jnp.bfloat16)
     index_rows = index_rows.at[:, 0, 0, :slots].set(far_knot.astype(jnp.bfloat16))
     knot_vals = knot_ids.astype(jnp.float32)
+    ext_knots = knots + 6
+    ext_ids = jnp.arange(ext_knots, dtype=jnp.int32)
+    band_weight = None
+    for step in range(4):
+        place = (ext_ids[None, :] == knot_ids[:, None] + 3 + step).astype(jnp.float32)
+        term = jnp.einsum("km,kab->kamb", place, blocks[:, step].astype(jnp.float32))
+        band_weight = term if band_weight is None else band_weight + term
+    for step in range(1, 4):
+        place = (ext_ids[None, :] == knot_ids[:, None] + 3 - step).astype(jnp.float32)
+        band_weight = band_weight + jnp.einsum(
+            "km,kba->kamb", place, lower_blocks[3 - step : 3 - step + knots, step].astype(jnp.float32)
+        )
+    fetch_order = [bucket_of[-s] for s in shifts]
+    fetch_place = jnp.concatenate(
+        [own_place.reshape(knots, buckets, slots)[:, b] for b in fetch_order], axis=1
+    )
+    fetch_blocks = jnp.concatenate([couplings[b] for b in fetch_order], axis=0).astype(jnp.float32)
+    fetch_weight = jnp.einsum("kf,fab->kafb", fetch_place, fetch_blocks)
+    weight = jnp.concatenate([band_weight, fetch_weight], axis=2).astype(jnp.bfloat16)
     answer_pick = None
     land_place = None
 
@@ -111,30 +130,14 @@
             ).astype(jnp.bfloat16)
         low = shifted_open(probe_bf[knots - 3 :], "seg", 1)
         high = shifted_open(probe_bf[:3], "seg", -1)
-        extended = jnp.concatenate([low, probe_bf, high], axis=0)
-        summed = jnp.zeros(probe_bf.shape, jnp.float32)
-        for step in range(4):
-            summed = summed + jnp.einsum(
-                "kab,kbr->kar",
-                blocks[:, step],
-                extended[3 + step : 3 + step + knots],
-                preferred_element_type=jnp.float32,
-            )
-        for step in range(1, 4):
-            summed = summed + jnp.einsum(
-                "kba,kbr->kar",
-                lower_blocks[3 - step : 3 - step + knots, step],
-                extended[3 - step : 3 - step + knots],
-                preferred_element_type=jnp.float32,
-            )
-        fetched = jnp.stack(fetched)
-        forward = jnp.einsum(
-            "bsqp,bspr->bsqr", couplings, fetched, preferred_element_type=jnp.float32
-        ).reshape(own_rows, params, probes)
+        stacked = jnp.concatenate(
+            [low, probe_bf, high] + [fetched[b] for b in fetch_order], axis=0
+        )
+        summed = jnp.einsum(
+            "kamb,mbr->kar", weight, stacked, preferred_element_type=jnp.float32
+        )
         landed = jnp.concatenate(landed, axis=0)
-        cross = jnp.einsum(
-            "ks,spr->kpr", own_place, forward, precision=lax.Precision.HIGHEST
-        ) + jnp.einsum("ks,spr->kpr", land_place, landed, preferred_element_type=jnp.float32)
+        cross = jnp.einsum("ks,spr->kpr", land_place, landed, preferred_element_type=jnp.float32)
         residual = residual - (summed + cross)
         coeff_next = 1.0 / (2.0 * center / radius - coeff)
         direction = coeff_next * coeff * direction + 2.0 * coeff_next / radius * residual

time: 219 us -> 182 us (0.83)
  the two profiles are of different devices: /device:TPU:487 before, /device:TPU:287 now
where the time goes in v3:
time: 182 us; the launch traced here: 180 us
  starting transfers between devices  110 us (60%)
  local copies, waits for them, and re-layouts  20.2 us (11%)
  waiting for transfers between devices  16.8 us (9%)
  other arithmetic  16.6 us (9%)
  matrix products  14.9 us (8%)
    ppermute x18, starting transfers between devices, shifted_ring(): lax.ppermute(value, axis, [(i, (i + steps) % count) for i in range(count)])  60.8 us
    ppermute x7, starting transfers between devices, shifted_open(): lax.ppermute(value, axis, [(source, source + steps) for source in range(i...  49.7 us
    dot_general x3, matrix products, body(): jnp.einsum('kamb,mbr->kar', weight, stacked, preferred_element_type=jnp.f...  10.3 us
    ppermute x18, waiting for transfers between devices, shifted_ring(): lax.ppermute(value, axis, [(i, (i + steps) % count) for i in range(count)])  9.96 us
    unnamed x65, local copies, waits for them, and re-layouts  8.22 us
    ppermute x7, waiting for transfers between devices, shifted_open(): lax.ppermute(value, axis, [(source, source + steps) for source in range(i...  6.87 us
    another operation x7, other arithmetic  6.27 us
    slice x6, local copies, waits for them, and re-layouts, body(): got[:knots]  4.72 us
  transfers between devices with their start and end apart: 25, of which 4 were waited for; matrix products, arithmetic and copies ran while one was open for 12% of the time, Pallas kernels for 0%

profile of v3, /device:TPU:287, one launch (start us, length us, event | category | flops | bytes accessed | tf_op | source)
XLA Modules:
  0.0 180.0 jit_solution(11234380442187700356)
XLA Ops:
  0.0 1.1 fusion.30
  1.1 2.4 %collective-permute-start.2 = (bf16[3,96,128]{2,1,0:T(8,128)(2,1)S(1)}, bf16[3,96,128]{2,1,0:T(8,128)(2,1)S(1)}, u32[]{:S(2)}, u32[]{:S(2)}) collective-permute-start(bf16[3,96,128]{2,1,0:T(8,128)(2,1)S(1)} %get-tuple-element.66), channel_id=1, source_target_pairs={{1,0},{2,1},{3,2},{4,3},{5,4},{6,5},{7,6},{8,7},{9,8},{10,9},{11,1... | collective-permute-start | bytes 221192 | tf_op jit(solution)/shard_map/ppermute | solution.py:16
  3.5 8.9 %collective-permute-start.1 = (bf16[3,96,128]{2,1,0:T(8,128)(2,1)S(1)}, bf16[3,96,128]{2,1,0:T(8,128)(2,1)S(1)}, u32[]{:S(2)}, u32[]{:S(2)}) collective-permute-start(bf16[3,96,128]{2,1,0:T(8,128)(2,1)S(1)} %get-tuple-element.67), channel_id=1, source_target_pairs={{0,1},{1,2},{2,3},{3,4},{4,5},{5,6},{6,7},{7,8},{8,9},{9,10},{10,1... | collective-permute-start | bytes 221192 | tf_op jit(solution)/shard_map/ppermute | solution.py:16
  12.4 1.0 slice_bitcast_fusion
  13.4 1.9 %collective-permute-start = (bf16[3,4,96,96]{3,2,1,0:T(8,128)(2,1)S(1)}, bf16[3,4,96,96]{3,2,1,0:T(8,128)(2,1)S(1)}, u32[]{:S(2)}, u32[]{:S(2)}) collective-permute-start(bf16[3,4,96,96]{3,2,1,0:T(8,128)(2,1)S(1)} %slice_bitcast_fusion), channel_id=1, source_target_pairs={{0,1},{1,2},{2,3},{3,4},{4,5},{5,6},{6,7},{7,8},{8,9},{9,10},{10,1... | collective-permute-start | bytes 663560 | tf_op jit(solution)/shard_map/ppermute | solution.py:16
  18.8 1.3 fusion.40
  20.1 3.3 %collective-permute-start.8 = (bf16[11,96,128]{2,1,0:T(8,128)(2,1)}, bf16[11,96,128]{2,1,0:T(8,128)(2,1)}, u32[]{:S(2)}, u32[]{:S(2)}) collective-permute-start(bf16[11,96,128]{2,1,0:T(8,128)(2,1)} %get-tuple-element.60), channel_id=1, source_target_pairs={{0,496},{16,0},{32,16},{48,32},{64,48},{80,64},{96,80},{112,96},{1... | collective-permute-start | bytes 811016 | tf_op jit(solution)/shard_map/ppermute | solution.py:21
  23.3 2.6 %collective-permute-start.4 = (bf16[11,96,128]{2,1,0:T(8,128)(2,1)}, bf16[11,96,128]{2,1,0:T(8,128)(2,1)}, u32[]{:S(2)}, u32[]{:S(2)}) collective-permute-start(bf16[11,96,128]{2,1,0:T(8,128)(2,1)} %get-tuple-element.61), channel_id=1, source_target_pairs={{0,32},{16,48},{32,64},{48,80},{64,96},{80,112},{96,128},{112,144}... | collective-permute-start | bytes 811016 | tf_op jit(solution)/shard_map/ppermute | solution.py:21
  26.9 1.9 %fusion.1 = bf16[8,96,12,96]{3,1,2,0:T(8,128)(2,1)} fusion(f32[12,8]{0,1:T(8,128)S(1)} %copy.34, f32[12,96,96]{2,1,0:T(8,128)S(1)} %convert.88), kind=kLoop, calls=%fused_computation.6 | loop fusion | flops 1769472 | bytes 2212224 | tf_op jit(solution)/shard_map/kf,fab->kafb/transpose | solution.py:69
  28.7 4.2 %collective-permute-start.5 = (bf16[11,96,128]{2,1,0:T(8,128)(2,1)}, bf16[11,96,128]{2,1,0:T(8,128)(2,1)}, u32[]{:S(2)}, u32[]{:S(2)}) collective-permute-start(bf16[11,96,128]{2,1,0:T(8,128)(2,1)} %get-tuple-element.62), channel_id=1, source_target_pairs={{0,48},{16,64},{32,80},{48,96},{64,112},{80,128},{96,144},{112,160... | collective-permute-start | bytes 811016 | tf_op jit(solution)/shard_map/ppermute | solution.py:21
  33.0 1.9 %collective-permute-start.6 = (bf16[11,96,128]{2,1,0:T(8,128)(2,1)}, bf16[11,96,128]{2,1,0:T(8,128)(2,1)}, u32[]{:S(2)}, u32[]{:S(2)}) collective-permute-start(bf16[11,96,128]{2,1,0:T(8,128)(2,1)} %get-tuple-element.63), channel_id=1, source_target_pairs={{0,464},{16,480},{32,496},{48,0},{64,16},{80,32},{96,48},{112,64},... | collective-permute-start | bytes 811016 | tf_op jit(solution)/shard_map/ppermute | solution.py:21
  35.0 6.9 %collective-permute-done = bf16[3,4,96,96]{3,2,1,0:T(8,128)(2,1)S(1)} collective-permute-done((bf16[3,4,96,96]{3,2,1,0:T(8,128)(2,1)S(1)}, bf16[3,4,96,96]{3,2,1,0:T(8,128)(2,1)S(1)}, u32[]{:S(2)}, u32[]{:S(2)}) %collective-permute-start) | collective-permute-done | bytes 221216 | tf_op jit(solution)/shard_map/ppermute | solution.py:16
  41.9 2.4 %collective-permute-start.7 = (bf16[11,96,128]{2,1,0:T(8,128)(2,1)}, bf16[11,96,128]{2,1,0:T(8,128)(2,1)}, u32[]{:S(2)}, u32[]{:S(2)}) collective-permute-start(bf16[11,96,128]{2,1,0:T(8,128)(2,1)} %get-tuple-element.64), channel_id=1, source_target_pairs={{0,480},{16,496},{32,0},{48,16},{64,32},{80,48},{96,64},{112,80},{... | collective-permute-start | bytes 811016 | tf_op jit(solution)/shard_map/ppermute | solution.py:21
  44.3 1.2 fusion.44
  45.5 0.9 copy.30
  46.4 0.9 copy.31
  47.4 0.9 copy.32
  48.3 4.8 %fusion = bf16[8,96,14,96]{3,1,2,0:T(8,128)(2,1)S(1)} fusion(f32[8,14]{1,0:T(8,128)S(1)} %fusion.78, f32[8,96,96]{1,2,0:T(8,128)} %copy.32, f32[8,14]{1,0:T(8,128)S(1)} %get-tuple-element.127, f32[8,96,96]{1,2,0:T(8,128)} %copy.31, f32[8,14]{1,0:T(8,128)S(1)} %get-tuple-element.126, f32[8,96,96]{1,2,0:T(8,128)} %copy.30, f32[8,96,96]{2,1,0:T(8,128)} %get-tuple-element.25, ...), kind=kLoop, calls=%fused_computation.1 | loop fusion | flops 14450688 | bytes 4131904 | tf_op jit(solution)/shard_map/convert.36
  53.1 8.9 %collective-permute-start.3 = (bf16[11,96,128]{2,1,0:T(8,128)(2,1)S(1)}, bf16[11,96,128]{2,1,0:T(8,128)(2,1)S(1)}, u32[]{:S(2)}, u32[]{:S(2)}) collective-permute-start(bf16[11,96,128]{2,1,0:T(8,128)(2,1)S(1)} %copy-done.9), channel_id=1, source_target_pairs={{0,16},{16,32},{32,48},{48,64},{64,80},{80,96},{96,112},{112,128},... | collective-permute-start | bytes 811016 | tf_op jit(solution)/shard_map/ppermute | solution.py:21
  65.6 0.9 slice.551
  66.8 0.9 slice.539
  67.9 0.9 slice.542
  69.0 0.9 slice.545
  70.2 0.9 slice.548
  77.0 0.8 constant_dynamic-update-slice_fusion.18
  80.4 4.9 %fusion.95 = (bf16[8,96,128]{2,1,0:T(8,128)(2,1)S(1)}, f32[8,96,128]{2,1,0:T(8,128)}, f32[8,96,128]{2,1,0:T(8,128)}) fusion(f32[8,96,128]{2,0,1:T(8,128)S(1)} %fusion.28, f32[1,8,96,128]{3,2,1,0:T(8,128)S(1)} %copy-done.4, bf16[26,96,128]{2,1,0:T(8,128)(2,1)} %constant_dynamic-update-slice_fusion.6, bf16[8,96,12,96]{3,1,2,0:T(8,128)(2,1)} %fusion.1, ...), kind=kOutput, calls=%fused_computation.270 | convolution fusion | flops 493240320 | bytes 6242304 | tf_op jit(solution)/shard_map/kamb,mbr->kar/dot_general | solution.py:136
  86.8 1.3 fusion.63
  88.3 2.2 %collective-permute-start.10 = (bf16[3,96,128]{2,1,0:T(8,128)(2,1)S(1)}, bf16[3,96,128]{2,1,0:T(8,128)(2,1)S(1)}, u32[]{:S(2)}, u32[]{:S(2)}) collective-permute-start(bf16[3,96,128]{2,1,0:T(8,128)(2,1)S(1)} %get-tuple-element.58), channel_id=1, source_target_pairs={{1,0},{2,1},{3,2},{4,3},{5,4},{6,5},{7,6},{8,7},{9,8},{10,9},{11,1... | collective-permute-start | bytes 221192 | tf_op jit(solution)/shard_map/ppermute | solution.py:16
  90.5 22.9 %collective-permute-start.9 = (bf16[3,96,128]{2,1,0:T(8,128)(2,1)S(1)}, bf16[3,96,128]{2,1,0:T(8,128)(2,1)S(1)}, u32[]{:S(2)}, u32[]{:S(2)}) collective-permute-start(bf16[3,96,128]{2,1,0:T(8,128)(2,1)S(1)} %copy-done.11), channel_id=1, source_target_pairs={{0,1},{1,2},{2,3},{3,4},{4,5},{5,6},{6,7},{7,8},{8,9},{9,10},{10,1... | collective-permute-start | bytes 221192 | tf_op jit(solution)/shard_map/ppermute | solution.py:16
  113.8 6.8 %collective-permute-start.11 = (bf16[4,96,128]{2,1,0:T(8,128)(2,1)S(1)}, bf16[4,96,128]{2,1,0:T(8,128)(2,1)S(1)}, u32[]{:S(2)}, u32[]{:S(2)}) collective-permute-start(bf16[4,96,128]{2,1,0:T(8,128)(2,1)S(1)} %pad_maximum_fusion.33), channel_id=1, source_target_pairs={{0,16},{16,32},{32,48},{48,64},{64,80},{80,96},{96,112},{112,128},... | collective-permute-start | bytes 294920 | tf_op jit(solution)/shard_map/ppermute | solution.py:21
  120.6 1.9 %collective-permute-start.12 = (bf16[4,96,128]{2,1,0:T(8,128)(2,1)S(1)}, bf16[4,96,128]{2,1,0:T(8,128)(2,1)S(1)}, u32[]{:S(2)}, u32[]{:S(2)}) collective-permute-start(bf16[4,96,128]{2,1,0:T(8,128)(2,1)S(1)} %pad_maximum_fusion.34), channel_id=1, source_target_pairs={{0,32},{16,48},{32,64},{48,80},{64,96},{80,112},{96,128},{112,144}... | collective-permute-start | bytes 294920 | tf_op jit(solution)/shard_map/ppermute | solution.py:21
  122.6 1.9 %collective-permute-start.13 = (bf16[4,96,128]{2,1,0:T(8,128)(2,1)S(1)}, bf16[4,96,128]{2,1,0:T(8,128)(2,1)S(1)}, u32[]{:S(2)}, u32[]{:S(2)}) collective-permute-start(bf16[4,96,128]{2,1,0:T(8,128)(2,1)S(1)} %pad_maximum_fusion.35), channel_id=1, source_target_pairs={{0,48},{16,64},{32,80},{48,96},{64,112},{80,128},{96,144},{112,160... | collective-permute-start | bytes 294920 | tf_op jit(solution)/shard_map/ppermute | solution.py:21
  124.6 3.6 %collective-permute-start.14 = (bf16[4,96,128]{2,1,0:T(8,128)(2,1)S(1)}, bf16[4,96,128]{2,1,0:T(8,128)(2,1)S(1)}, u32[]{:S(2)}, u32[]{:S(2)}) collective-permute-start(bf16[4,96,128]{2,1,0:T(8,128)(2,1)S(1)} %pad_maximum_fusion.36), channel_id=1, source_target_pairs={{0,464},{16,480},{32,496},{48,0},{64,16},{80,32},{96,48},{112,64},... | collective-permute-start | bytes 294920 | tf_op jit(solution)/shard_map/ppermute | solution.py:21
  128.3 3.4 %collective-permute-start.15 = (bf16[4,96,128]{2,1,0:T(8,128)(2,1)S(1)}, bf16[4,96,128]{2,1,0:T(8,128)(2,1)S(1)}, u32[]{:S(2)}, u32[]{:S(2)}) collective-permute-start(bf16[4,96,128]{2,1,0:T(8,128)(2,1)S(1)} %pad_maximum_fusion.37), channel_id=1, source_target_pairs={{0,480},{16,496},{32,0},{48,16},{64,32},{80,48},{96,64},{112,80},{... | collective-permute-start | bytes 294920 | tf_op jit(solution)/shard_map/ppermute | solution.py:21
  131.7 2.5 %collective-permute-start.16 = (bf16[4,96,128]{2,1,0:T(8,128)(2,1)S(1)}, bf16[4,96,128]{2,1,0:T(8,128)(2,1)S(1)}, u32[]{:S(2)}, u32[]{:S(2)}) collective-permute-start(bf16[4,96,128]{2,1,0:T(8,128)(2,1)S(1)} %pad_maximum_fusion.38), channel_id=1, source_target_pairs={{0,496},{16,0},{32,16},{48,32},{64,48},{80,64},{96,80},{112,96},{1... | collective-permute-start | bytes 294920 | tf_op jit(solution)/shard_map/ppermute | solution.py:21
  134.4 1.4 collective-permute-done.15
  135.8 4.3 %collective-permute-done.16 = bf16[4,96,128]{2,1,0:T(8,128)(2,1)S(1)} collective-permute-done((bf16[4,96,128]{2,1,0:T(8,128)(2,1)S(1)}, bf16[4,96,128]{2,1,0:T(8,128)(2,1)S(1)}, u32[]{:S(2)}, u32[]{:S(2)}) %collective-permute-start.16) | collective-permute-done | bytes 98336 | tf_op jit(solution)/shard_map/ppermute | solution.py:21
  140.3 2.3 %fusion.31 = (bf16[8,96,128]{2,1,0:T(8,128)(2,1)S(1)}, f32[8,96,128]{2,1,0:T(8,128)S(1)}) fusion(f32[8,96,128]{2,1,0:T(8,128)S(1)} %copy-done.14, f32[8,96,128]{2,0,1:T(8,128)S(1)} %fusion.25, bf16[26,96,128]{2,1,0:T(8,128)(2,1)S(1)} %get-tuple-element.81, bf16[8,96,12,96]{3,1,2,0:T(8,128)(2,1)S(1)} %copy-done.2, bf16[8,96,14,96]{3,1,2,0:T(8,128)(2,1)S(1)} %fusion, ...), kind=kOutput, calls=%fused_computation.53 | convolution fusion | flops 493436928 | bytes 7028736 | tf_op jit(solution)/shard_map/kamb,mbr->kar/dot_general | solution.py:136
  143.2 1.9 %collective-permute-start.18 = (bf16[3,96,128]{2,1,0:T(8,128)(2,1)S(1)}, bf16[3,96,128]{2,1,0:T(8,128)(2,1)S(1)}, u32[]{:S(2)}, u32[]{:S(2)}) collective-permute-start(bf16[3,96,128]{2,1,0:T(8,128)(2,1)S(1)} %get-tuple-element.56), channel_id=1, source_target_pairs={{1,0},{2,1},{3,2},{4,3},{5,4},{6,5},{7,6},{8,7},{9,8},{10,9},{11,1... | collective-permute-start | bytes 221192 | tf_op jit(solution)/shard_map/ppermute | solution.py:16
  145.1 9.4 %collective-permute-start.17 = (bf16[3,96,128]{2,1,0:T(8,128)(2,1)S(1)}, bf16[3,96,128]{2,1,0:T(8,128)(2,1)S(1)}, u32[]{:S(2)}, u32[]{:S(2)}) collective-permute-start(bf16[3,96,128]{2,1,0:T(8,128)(2,1)S(1)} %get-tuple-element.57), channel_id=1, source_target_pairs={{0,1},{1,2},{2,3},{3,4},{4,5},{5,6},{6,7},{7,8},{8,9},{9,10},{10,1... | collective-permute-start | bytes 221192 | tf_op jit(solution)/shard_map/ppermute | solution.py:16
  154.8 2.4 %collective-permute-start.19 = (bf16[4,96,128]{2,1,0:T(8,128)(2,1)S(1)}, bf16[4,96,128]{2,1,0:T(8,128)(2,1)S(1)}, u32[]{:S(2)}, u32[]{:S(2)}) collective-permute-start(bf16[4,96,128]{2,1,0:T(8,128)(2,1)S(1)} %pad_maximum_fusion.39), channel_id=1, source_target_pairs={{0,16},{16,32},{32,48},{48,64},{64,80},{80,96},{96,112},{112,128},... | collective-permute-start | bytes 294920 | tf_op jit(solution)/shard_map/ppermute | solution.py:21
  157.3 1.9 %collective-permute-start.20 = (bf16[4,96,128]{2,1,0:T(8,128)(2,1)S(1)}, bf16[4,96,128]{2,1,0:T(8,128)(2,1)S(1)}, u32[]{:S(2)}, u32[]{:S(2)}) collective-permute-start(bf16[4,96,128]{2,1,0:T(8,128)(2,1)S(1)} %pad_maximum_fusion.40), channel_id=1, source_target_pairs={{0,32},{16,48},{32,64},{48,80},{64,96},{80,112},{96,128},{112,144}... | collective-permute-start | bytes 294920 | tf_op jit(solution)/shard_map/ppermute | solution.py:21
  159.2 1.9 %collective-permute-start.21 = (bf16[4,96,128]{2,1,0:T(8,128)(2,1)S(1)}, bf16[4,96,128]{2,1,0:T(8,128)(2,1)S(1)}, u32[]{:S(2)}, u32[]{:S(2)}) collective-permute-start(bf16[4,96,128]{2,1,0:T(8,128)(2,1)S(1)} %pad_maximum_fusion.41), channel_id=1, source_target_pairs={{0,48},{16,64},{32,80},{48,96},{64,112},{80,128},{96,144},{112,160... | collective-permute-start | bytes 294920 | tf_op jit(solution)/shard_map/ppermute | solution.py:21
  161.2 3.6 %collective-permute-start.22 = (bf16[4,96,128]{2,1,0:T(8,128)(2,1)S(1)}, bf16[4,96,128]{2,1,0:T(8,128)(2,1)S(1)}, u32[]{:S(2)}, u32[]{:S(2)}) collective-permute-start(bf16[4,96,128]{2,1,0:T(8,128)(2,1)S(1)} %pad_maximum_fusion.42), channel_id=1, source_target_pairs={{0,464},{16,480},{32,496},{48,0},{64,16},{80,32},{96,48},{112,64},... | collective-permute-start | bytes 294920 | tf_op jit(solution)/shard_map/ppermute | solution.py:21
  164.9 3.4 %collective-permute-start.23 = (bf16[4,96,128]{2,1,0:T(8,128)(2,1)S(1)}, bf16[4,96,128]{2,1,0:T(8,128)(2,1)S(1)}, u32[]{:S(2)}, u32[]{:S(2)}) collective-permute-start(bf16[4,96,128]{2,1,0:T(8,128)(2,1)S(1)} %pad_maximum_fusion.43), channel_id=1, source_target_pairs={{0,480},{16,496},{32,0},{48,16},{64,32},{80,48},{96,64},{112,80},{... | collective-permute-start | bytes 294920 | tf_op jit(solution)/shard_map/ppermute | solution.py:21
  168.3 4.0 %collective-permute-start.24 = (bf16[4,96,128]{2,1,0:T(8,128)(2,1)S(1)}, bf16[4,96,128]{2,1,0:T(8,128)(2,1)S(1)}, u32[]{:S(2)}, u32[]{:S(2)}) collective-permute-start(bf16[4,96,128]{2,1,0:T(8,128)(2,1)S(1)} %pad_maximum_fusion.44), channel_id=1, source_target_pairs={{0,496},{16,0},{32,16},{48,32},{64,48},{80,64},{96,80},{112,96},{1... | collective-permute-start | bytes 294920 | tf_op jit(solution)/shard_map/ppermute | solution.py:21
  172.5 4.2 %collective-permute-done.24 = bf16[4,96,128]{2,1,0:T(8,128)(2,1)S(1)} collective-permute-done((bf16[4,96,128]{2,1,0:T(8,128)(2,1)S(1)}, bf16[4,96,128]{2,1,0:T(8,128)(2,1)S(1)}, u32[]{:S(2)}, u32[]{:S(2)}) %collective-permute-start.24) | collective-permute-done | bytes 98336 | tf_op jit(solution)/shard_map/ppermute | solution.py:21
  176.9 3.1 %fusion.15 = f32[1,8,96,128]{3,2,1,0:T(8,128)} fusion(f32[8,96,128]{2,1,0:T(8,128)S(1)} %get-tuple-element.121, bf16[8,96,12,96]{3,1,2,0:T(8,128)(2,1)S(1)} %copy-done.2, bf16[8,96,14,96]{3,1,2,0:T(8,128)(2,1)S(1)} %fusion, bf16[26,96,128]{2,1,0:T(8,128)(2,1)S(1)} %get-tuple-element.69, f32[8,96,128]{2,0,1:T(8,128)S(1)} %fusion.23, ...), kind=kOutput, calls=%fused_computation.24 | convolution fusion | flops 493830144 | bytes 6438912 | tf_op jit(solution)/shard_map/kamb,mbr->kar/dot_general | solution.py:136
  (172 shorter events, 20.6 us)
Async XLA Ops:
  0.0 18.4 %copy-start = (bf16[1,1,6,2,96,96]{5,4,3,2,1,0:T(8,128)(2,1)S(1)}, bf16[1,1,6,2,96,96]{5,4,3,2,1,0:T(8,128)(2,1)}, u32[]{:S(2)}) copy-start(bf16[1,1,6,2,96,96]{5,4,3,2,1,0:T(8,128)(2,1)} %param.11) | copy-start | bytes 663556
  1.1 31.9 %collective-permute-start.2 = (bf16[3,96,128]{2,1,0:T(8,128)(2,1)S(1)}, bf16[3,96,128]{2,1,0:T(8,128)(2,1)S(1)}, u32[]{:S(2)}, u32[]{:S(2)}) collective-permute-start(bf16[3,96,128]{2,1,0:T(8,128)(2,1)S(1)} %get-tuple-element.66), channel_id=1, source_target_pairs={{1,0},{2,1},{3,2},{4,3},{5,4},{6,5},{7,6},{8,7},{9,8},{10,9},{11,1... | collective-permute-start | bytes 221192 | tf_op jit(solution)/shard_map/ppermute | solution.py:16
  3.5 25.2 %collective-permute-start.1 = (bf16[3,96,128]{2,1,0:T(8,128)(2,1)S(1)}, bf16[3,96,128]{2,1,0:T(8,128)(2,1)S(1)}, u32[]{:S(2)}, u32[]{:S(2)}) collective-permute-start(bf16[3,96,128]{2,1,0:T(8,128)(2,1)S(1)} %get-tuple-element.67), channel_id=1, source_target_pairs={{0,1},{1,2},{2,3},{3,4},{4,5},{5,6},{6,7},{7,8},{8,9},{9,10},{10,1... | collective-permute-start | bytes 221192 | tf_op jit(solution)/shard_map/ppermute | solution.py:16
  13.4 12.6 %copy-start.13 = (s32[1,1,6]{2,1,0:T(1,128)S(1)}, s32[1,1,6]{2,1,0:T(1,128)}, u32[]{:S(2)}) copy-start(s32[1,1,6]{2,1,0:T(1,128)} %param.10) | copy-start | bytes 76
  13.4 28.4 %collective-permute-start = (bf16[3,4,96,96]{3,2,1,0:T(8,128)(2,1)S(1)}, bf16[3,4,96,96]{3,2,1,0:T(8,128)(2,1)S(1)}, u32[]{:S(2)}, u32[]{:S(2)}) collective-permute-start(bf16[3,4,96,96]{3,2,1,0:T(8,128)(2,1)S(1)} %slice_bitcast_fusion), channel_id=1, source_target_pairs={{0,1},{1,2},{2,3},{3,4},{4,5},{5,6},{6,7},{7,8},{8,9},{9,10},{10,1... | collective-permute-start | bytes 663560 | tf_op jit(solution)/shard_map/ppermute | solution.py:16
  20.1 12.9 %copy-start.3 = (f32[1,8,96,128]{3,2,1,0:T(8,128)S(1)}, f32[1,8,96,128]{3,2,1,0:T(8,128)}, u32[]{:S(2)}) copy-start(f32[1,8,96,128]{3,2,1,0:T(8,128)} %param.7) | copy-start | bytes 1179652
  20.1 24.3 %copy-start.1 = (bf16[1,8,4,96,96]{4,3,2,1,0:T(8,128)(2,1)S(1)}, bf16[1,8,4,96,96]{4,3,2,1,0:T(8,128)(2,1)}, u32[]{:S(2)}) copy-start(bf16[1,8,4,96,96]{4,3,2,1,0:T(8,128)(2,1)} %param.8) | copy-start | bytes 1769476
  20.1 33.0 %collective-permute-start.8 = (bf16[11,96,128]{2,1,0:T(8,128)(2,1)}, bf16[11,96,128]{2,1,0:T(8,128)(2,1)}, u32[]{:S(2)}, u32[]{:S(2)}) collective-permute-start(bf16[11,96,128]{2,1,0:T(8,128)(2,1)} %get-tuple-element.60), channel_id=1, source_target_pairs={{0,496},{16,0},{32,16},{48,32},{64,48},{80,64},{96,80},{112,96},{1... | collective-permute-start | bytes 811016 | tf_op jit(solution)/shard_map/ppermute | solution.py:21
  23.3 39.4 %collective-permute-start.4 = (bf16[11,96,128]{2,1,0:T(8,128)(2,1)}, bf16[11,96,128]{2,1,0:T(8,128)(2,1)}, u32[]{:S(2)}, u32[]{:S(2)}) collective-permute-start(bf16[11,96,128]{2,1,0:T(8,128)(2,1)} %get-tuple-element.61), channel_id=1, source_target_pairs={{0,32},{16,48},{32,64},{48,80},{64,96},{80,112},{96,128},{112,144}... | collective-permute-start | bytes 811016 | tf_op jit(solution)/shard_map/ppermute | solution.py:21
  28.7 34.7 %collective-permute-start.5 = (bf16[11,96,128]{2,1,0:T(8,128)(2,1)}, bf16[11,96,128]{2,1,0:T(8,128)(2,1)}, u32[]{:S(2)}, u32[]{:S(2)}) collective-permute-start(bf16[11,96,128]{2,1,0:T(8,128)(2,1)} %get-tuple-element.62), channel_id=1, source_target_pairs={{0,48},{16,64},{32,80},{48,96},{64,112},{80,128},{96,144},{112,160... | collective-permute-start | bytes 811016 | tf_op jit(solution)/shard_map/ppermute | solution.py:21
  33.0 31.0 %collective-permute-start.6 = (bf16[11,96,128]{2,1,0:T(8,128)(2,1)}, bf16[11,96,128]{2,1,0:T(8,128)(2,1)}, u32[]{:S(2)}, u32[]{:S(2)}) collective-permute-start(bf16[11,96,128]{2,1,0:T(8,128)(2,1)} %get-tuple-element.63), channel_id=1, source_target_pairs={{0,464},{16,480},{32,496},{48,0},{64,16},{80,32},{96,48},{112,64},... | collective-permute-start | bytes 811016 | tf_op jit(solution)/shard_map/ppermute | solution.py:21
  35.0 9.3 %copy-start.12 = (bf16[26,96,128]{2,1,0:T(8,128)(2,1)}, bf16[26,96,128]{2,1,0:T(8,128)(2,1)S(1)}, u32[]{:S(2)}) copy-start(bf16[26,96,128]{2,1,0:T(8,128)(2,1)S(1)} %constant_dynamic-update-slice_fusion.12) | copy-start | bytes 1916932
  41.9 22.9 %collective-permute-start.7 = (bf16[11,96,128]{2,1,0:T(8,128)(2,1)}, bf16[11,96,128]{2,1,0:T(8,128)(2,1)}, u32[]{:S(2)}, u32[]{:S(2)}) collective-permute-start(bf16[11,96,128]{2,1,0:T(8,128)(2,1)} %get-tuple-element.64), channel_id=1, source_target_pairs={{0,480},{16,496},{32,0},{48,16},{64,32},{80,48},{96,64},{112,80},{... | collective-permute-start | bytes 811016 | tf_op jit(solution)/shard_map/ppermute | solution.py:21
  48.3 4.8 %copy-start.9 = (bf16[11,96,128]{2,1,0:T(8,128)(2,1)S(1)}, bf16[11,96,128]{2,1,0:T(8,128)(2,1)}, u32[]{:S(2)}) copy-start(bf16[11,96,128]{2,1,0:T(8,128)(2,1)} %get-tuple-element.65) | copy-start | bytes 811012
  53.1 12.3 %collective-permute-start.3 = (bf16[11,96,128]{2,1,0:T(8,128)(2,1)S(1)}, bf16[11,96,128]{2,1,0:T(8,128)(2,1)S(1)}, u32[]{:S(2)}, u32[]{:S(2)}) collective-permute-start(bf16[11,96,128]{2,1,0:T(8,128)(2,1)S(1)} %copy-done.9), channel_id=1, source_target_pairs={{0,16},{16,32},{32,48},{48,64},{64,80},{80,96},{96,112},{112,128},... | collective-permute-start | bytes 811016 | tf_op jit(solution)/shard_map/ppermute | solution.py:21
  65.5 6.1 %copy-start.10 = (bf16[11,96,128]{2,1,0:T(8,128)(2,1)}, bf16[11,96,128]{2,1,0:T(8,128)(2,1)S(1)}, u32[]{:S(2)}) copy-start(bf16[11,96,128]{2,1,0:T(8,128)(2,1)S(1)} %collective-permute-done.3) | copy-start | bytes 811012
  66.6 13.9 %copy-start.4 = (f32[1,8,96,128]{3,2,1,0:T(8,128)S(1)}, f32[1,8,96,128]{3,2,1,0:T(8,128)}, u32[]{:S(2)}) copy-start(f32[1,8,96,128]{3,2,1,0:T(8,128)} %param.7) | copy-start | bytes 1179652
  80.4 4.9 %copy-start.7 = (f32[8,96,128]{2,0,1:T(8,128)}, f32[8,96,128]{2,0,1:T(8,128)S(1)}, u32[]{:S(2)}) copy-start(f32[8,96,128]{2,0,1:T(8,128)S(1)} %fusion.28) | copy-start | bytes 1179652
  85.4 0.7 copy-start.5
  86.8 3.7 %copy-start.11 = (bf16[3,96,128]{2,1,0:T(8,128)(2,1)S(1)}, bf16[3,96,128]{2,1,0:T(8,128)(2,1)}, u32[]{:S(2)}) copy-start(bf16[3,96,128]{2,1,0:T(8,128)(2,1)} %get-tuple-element.59) | copy-start | bytes 221188
  88.1 40.1 %copy-start.6 = (bf16[8,96,128]{2,1,0:T(8,128)(2,1)S(1)}, bf16[8,96,128]{2,1,0:T(8,128)(2,1)}, u32[]{:S(2)}) copy-start(bf16[8,96,128]{2,1,0:T(8,128)(2,1)} %copy-done.5) | copy-start | bytes 589828
  88.3 52.0 %copy-start.2 = (bf16[8,96,12,96]{3,1,2,0:T(8,128)(2,1)S(1)}, bf16[8,96,12,96]{3,1,2,0:T(8,128)(2,1)}, u32[]{:S(2)}) copy-start(bf16[8,96,12,96]{3,1,2,0:T(8,128)(2,1)} %fusion.1) | copy-start | bytes 5308420
  88.3 52.0 %copy-start.8 = (f32[8,96,128]{2,0,1:T(8,128)S(1)}, f32[8,96,128]{2,0,1:T(8,128)}, u32[]{:S(2)}) copy-start(f32[8,96,128]{2,0,1:T(8,128)} %copy-done.7) | copy-start | bytes 1179652
  88.3 52.0 %copy-start.14 = (f32[8,96,128]{2,1,0:T(8,128)S(1)}, f32[8,96,128]{2,1,0:T(8,128)}, u32[]{:S(2)}) copy-start(f32[8,96,128]{2,1,0:T(8,128)} %get-tuple-element.18) | copy-start | bytes 1179652
  88.3 52.0 %copy-start.15 = (f32[8,96,128]{2,1,0:T(8,128)S(1)}, f32[8,96,128]{2,1,0:T(8,128)}, u32[]{:S(2)}) copy-start(f32[8,96,128]{2,1,0:T(8,128)} %get-tuple-element.119) | copy-start | bytes 1179652
  88.3 40.0 %collective-permute-start.10 = (bf16[3,96,128]{2,1,0:T(8,128)(2,1)S(1)}, bf16[3,96,128]{2,1,0:T(8,128)(2,1)S(1)}, u32[]{:S(2)}, u32[]{:S(2)}) collective-permute-start(bf16[3,96,128]{2,1,0:T(8,128)(2,1)S(1)} %get-tuple-element.58), channel_id=1, source_target_pairs={{1,0},{2,1},{3,2},{4,3},{5,4},{6,5},{7,6},{8,7},{9,8},{10,9},{11,1... | collective-permute-start | bytes 221192 | tf_op jit(solution)/shard_map/ppermute | solution.py:16
  90.5 34.0 %collective-permute-start.9 = (bf16[3,96,128]{2,1,0:T(8,128)(2,1)S(1)}, bf16[3,96,128]{2,1,0:T(8,128)(2,1)S(1)}, u32[]{:S(2)}, u32[]{:S(2)}) collective-permute-start(bf16[3,96,128]{2,1,0:T(8,128)(2,1)S(1)} %copy-done.11), channel_id=1, source_target_pairs={{0,1},{1,2},{2,3},{3,4},{4,5},{5,6},{6,7},{7,8},{8,9},{9,10},{10,1... | collective-permute-start | bytes 221192 | tf_op jit(solution)/shard_map/ppermute | solution.py:16
  113.8 17.9 %collective-permute-start.11 = (bf16[4,96,128]{2,1,0:T(8,128)(2,1)S(1)}, bf16[4,96,128]{2,1,0:T(8,128)(2,1)S(1)}, u32[]{:S(2)}, u32[]{:S(2)}) collective-permute-start(bf16[4,96,128]{2,1,0:T(8,128)(2,1)S(1)} %pad_maximum_fusion.33), channel_id=1, source_target_pairs={{0,16},{16,32},{32,48},{48,64},{64,80},{80,96},{96,112},{112,128},... | collective-permute-start | bytes 294920 | tf_op jit(solution)/shard_map/ppermute | solution.py:21
  120.6 13.6 %collective-permute-start.12 = (bf16[4,96,128]{2,1,0:T(8,128)(2,1)S(1)}, bf16[4,96,128]{2,1,0:T(8,128)(2,1)S(1)}, u32[]{:S(2)}, u32[]{:S(2)}) collective-permute-start(bf16[4,96,128]{2,1,0:T(8,128)(2,1)S(1)} %pad_maximum_fusion.34), channel_id=1, source_target_pairs={{0,32},{16,48},{32,64},{48,80},{64,96},{80,112},{96,128},{112,144}... | collective-permute-start | bytes 294920 | tf_op jit(solution)/shard_map/ppermute | solution.py:21
  122.6 11.7 %collective-permute-start.13 = (bf16[4,96,128]{2,1,0:T(8,128)(2,1)S(1)}, bf16[4,96,128]{2,1,0:T(8,128)(2,1)S(1)}, u32[]{:S(2)}, u32[]{:S(2)}) collective-permute-start(bf16[4,96,128]{2,1,0:T(8,128)(2,1)S(1)} %pad_maximum_fusion.35), channel_id=1, source_target_pairs={{0,48},{16,64},{32,80},{48,96},{64,112},{80,128},{96,144},{112,160... | collective-permute-start | bytes 294920 | tf_op jit(solution)/shard_map/ppermute | solution.py:21
  124.6 9.8 %collective-permute-start.14 = (bf16[4,96,128]{2,1,0:T(8,128)(2,1)S(1)}, bf16[4,96,128]{2,1,0:T(8,128)(2,1)S(1)}, u32[]{:S(2)}, u32[]{:S(2)}) collective-permute-start(bf16[4,96,128]{2,1,0:T(8,128)(2,1)S(1)} %pad_maximum_fusion.36), channel_id=1, source_target_pairs={{0,464},{16,480},{32,496},{48,0},{64,16},{80,32},{96,48},{112,64},... | collective-permute-start | bytes 294920 | tf_op jit(solution)/shard_map/ppermute | solution.py:21
  128.3 7.5 %collective-permute-start.15 = (bf16[4,96,128]{2,1,0:T(8,128)(2,1)S(1)}, bf16[4,96,128]{2,1,0:T(8,128)(2,1)S(1)}, u32[]{:S(2)}, u32[]{:S(2)}) collective-permute-start(bf16[4,96,128]{2,1,0:T(8,128)(2,1)S(1)} %pad_maximum_fusion.37), channel_id=1, source_target_pairs={{0,480},{16,496},{32,0},{48,16},{64,32},{80,48},{96,64},{112,80},{... | collective-permute-start | bytes 294920 | tf_op jit(solution)/shard_map/ppermute | solution.py:21
  131.7 8.4 %collective-permute-start.16 = (bf16[4,96,128]{2,1,0:T(8,128)(2,1)S(1)}, bf16[4,96,128]{2,1,0:T(8,128)(2,1)S(1)}, u32[]{:S(2)}, u32[]{:S(2)}) collective-permute-start(bf16[4,96,128]{2,1,0:T(8,128)(2,1)S(1)} %pad_maximum_fusion.38), channel_id=1, source_target_pairs={{0,496},{16,0},{32,16},{48,32},{64,48},{80,64},{96,80},{112,96},{1... | collective-permute-start | bytes 294920 | tf_op jit(solution)/shard_map/ppermute | solution.py:21
  143.2 21.7 %collective-permute-start.18 = (bf16[3,96,128]{2,1,0:T(8,128)(2,1)S(1)}, bf16[3,96,128]{2,1,0:T(8,128)(2,1)S(1)}, u32[]{:S(2)}, u32[]{:S(2)}) collective-permute-start(bf16[3,96,128]{2,1,0:T(8,128)(2,1)S(1)} %get-tuple-element.56), channel_id=1, source_target_pairs={{1,0},{2,1},{3,2},{4,3},{5,4},{6,5},{7,6},{8,7},{9,8},{10,9},{11,1... | collective-permute-start | bytes 221192 | tf_op jit(solution)/shard_map/ppermute | solution.py:16
  145.1 16.1 %collective-permute-start.17 = (bf16[3,96,128]{2,1,0:T(8,128)(2,1)S(1)}, bf16[3,96,128]{2,1,0:T(8,128)(2,1)S(1)}, u32[]{:S(2)}, u32[]{:S(2)}) collective-permute-start(bf16[3,96,128]{2,1,0:T(8,128)(2,1)S(1)} %get-tuple-element.57), channel_id=1, source_target_pairs={{0,1},{1,2},{2,3},{3,4},{4,5},{5,6},{6,7},{7,8},{8,9},{9,10},{10,1... | collective-permute-start | bytes 221192 | tf_op jit(solution)/shard_map/ppermute | solution.py:16
  154.8 13.5 %collective-permute-start.19 = (bf16[4,96,128]{2,1,0:T(8,128)(2,1)S(1)}, bf16[4,96,128]{2,1,0:T(8,128)(2,1)S(1)}, u32[]{:S(2)}, u32[]{:S(2)}) collective-permute-start(bf16[4,96,128]{2,1,0:T(8,128)(2,1)S(1)} %pad_maximum_fusion.39), channel_id=1, source_target_pairs={{0,16},{16,32},{32,48},{48,64},{64,80},{80,96},{96,112},{112,128},... | collective-permute-start | bytes 294920 | tf_op jit(solution)/shard_map/ppermute | solution.py:21
  157.3 15.1 %collective-permute-start.20 = (bf16[4,96,128]{2,1,0:T(8,128)(2,1)S(1)}, bf16[4,96,128]{2,1,0:T(8,128)(2,1)S(1)}, u32[]{:S(2)}, u32[]{:S(2)}) collective-permute-start(bf16[4,96,128]{2,1,0:T(8,128)(2,1)S(1)} %pad_maximum_fusion.40), channel_id=1, source_target_pairs={{0,32},{16,48},{32,64},{48,80},{64,96},{80,112},{96,128},{112,144}... | collective-permute-start | bytes 294920 | tf_op jit(solution)/shard_map/ppermute | solution.py:21
  159.2 13.2 %collective-permute-start.21 = (bf16[4,96,128]{2,1,0:T(8,128)(2,1)S(1)}, bf16[4,96,128]{2,1,0:T(8,128)(2,1)S(1)}, u32[]{:S(2)}, u32[]{:S(2)}) collective-permute-start(bf16[4,96,128]{2,1,0:T(8,128)(2,1)S(1)} %pad_maximum_fusion.41), channel_id=1, source_target_pairs={{0,48},{16,64},{32,80},{48,96},{64,112},{80,128},{96,144},{112,160... | collective-permute-start | bytes 294920 | tf_op jit(solution)/shard_map/ppermute | solution.py:21
  161.2 11.2 %collective-permute-start.22 = (bf16[4,96,128]{2,1,0:T(8,128)(2,1)S(1)}, bf16[4,96,128]{2,1,0:T(8,128)(2,1)S(1)}, u32[]{:S(2)}, u32[]{:S(2)}) collective-permute-start(bf16[4,96,128]{2,1,0:T(8,128)(2,1)S(1)} %pad_maximum_fusion.42), channel_id=1, source_target_pairs={{0,464},{16,480},{32,496},{48,0},{64,16},{80,32},{96,48},{112,64},... | collective-permute-start | bytes 294920 | tf_op jit(solution)/shard_map/ppermute | solution.py:21
  164.9 7.5 %collective-permute-start.23 = (bf16[4,96,128]{2,1,0:T(8,128)(2,1)S(1)}, bf16[4,96,128]{2,1,0:T(8,128)(2,1)S(1)}, u32[]{:S(2)}, u32[]{:S(2)}) collective-permute-start(bf16[4,96,128]{2,1,0:T(8,128)(2,1)S(1)} %pad_maximum_fusion.43), channel_id=1, source_target_pairs={{0,480},{16,496},{32,0},{48,16},{64,32},{80,48},{96,64},{112,80},{... | collective-permute-start | bytes 294920 | tf_op jit(solution)/shard_map/ppermute | solution.py:21
  168.3 8.4 %collective-permute-start.24 = (bf16[4,96,128]{2,1,0:T(8,128)(2,1)S(1)}, bf16[4,96,128]{2,1,0:T(8,128)(2,1)S(1)}, u32[]{:S(2)}, u32[]{:S(2)}) collective-permute-start(bf16[4,96,128]{2,1,0:T(8,128)(2,1)S(1)} %pad_maximum_fusion.44), channel_id=1, source_target_pairs={{0,496},{16,0},{32,16},{48,32},{64,48},{80,64},{96,80},{112,96},{1... | collective-permute-start | bytes 294920 | tf_op jit(solution)/shard_map/ppermute | solution.py:21

commit v4 on v1

--- a/solution.py
+++ b/solution.py
@@ -35,8 +35,6 @@
     ]
     bucket_of = {o: b for b, o in enumerate(offsets)}
     shifts = [o for o in offsets if o > 0] + [o for o in offsets if o < 0]
-    lines = lax.axis_size("line")
-    me = lax.axis_index("line")
 
     boundary_blocks = shifted_open(blocks[knots - 3 :], "seg", 1)
     lower_blocks = jnp.concatenate([boundary_blocks, blocks], axis=0)
@@ -44,18 +42,38 @@
     used = jnp.arange(slots, dtype=jnp.int32)[None, :] < used_count[:, None]
     own_knot = jnp.where(used, my_pairs[:, :, 0], -1)
     far_knot = jnp.where(used, my_pairs[:, :, 1], -1)
-    table = lax.all_gather(far_knot, "line")
+    knot_ids = jnp.arange(knots, dtype=jnp.int32)
+    answer_knots = [None] * len(shifts)
+    landing_knots = [None] * len(shifts)
+    for t, s in enumerate(shifts):
+        got = shifted_ring(far_knot[bucket_of[s]], "line", s)
+        landing_knots[t] = got
+        answer_knots[shifts.index(-s)] = got
+    own_pick = (own_knot.reshape(-1)[:, None] == knot_ids[None, :]).astype(jnp.bfloat16)
+    answer_pick = (jnp.concatenate(answer_knots)[:, None] == knot_ids[None, :]).astype(jnp.bfloat16)
+    pick = jnp.concatenate([own_pick, answer_pick], axis=0)
+    land_place = (jnp.concatenate(landing_knots)[None, :] == knot_ids[:, None]).astype(jnp.bfloat16)
 
-    answer_knots = []
-    landing_knots = []
-    for s in shifts:
-        answer_knots.append(lax.dynamic_index_in_dim(table, (me + s) % lines, 0, False)[bucket_of[-s]])
-        landing_knots.append(lax.dynamic_index_in_dim(table, (me - s + lines) % lines, 0, False)[bucket_of[s]])
-    knot_ids = jnp.arange(knots, dtype=jnp.int32)
-    pick_index = jnp.concatenate([own_knot.reshape(-1)] + answer_knots)
-    pick = (pick_index[:, None] == knot_ids[None, :]).astype(jnp.bfloat16)
-    own_place = (own_knot.reshape(-1)[None, :] == knot_ids[:, None]).astype(jnp.float32)
-    land_place = (jnp.concatenate(landing_knots)[None, :] == knot_ids[:, None]).astype(jnp.bfloat16)
+    ext_knots = knots + 6
+    band_col = jnp.arange(ext_knots, dtype=jnp.int32)[None, None, :, None]
+    band_row = knot_ids[:, None, None, None]
+    band_weight = jnp.zeros((knots, params, ext_knots, params), jnp.bfloat16)
+    for step in range(4):
+        band_weight = jnp.where(
+            band_col == band_row + 3 + step, blocks[:, step][:, :, None, :], band_weight
+        )
+    for step in range(1, 4):
+        flipped = jnp.swapaxes(lower_blocks[3 - step : 3 - step + knots, step], -1, -2)
+        band_weight = jnp.where(band_col == band_row + 3 - step, flipped[:, :, None, :], band_weight)
+    fetch_order = [bucket_of[-s] for s in shifts]
+    fetch_knot = jnp.concatenate([own_knot[b] for b in fetch_order])
+    fetch_blocks = jnp.concatenate([couplings[b] for b in fetch_order], axis=0)
+    fetch_weight = jnp.where(
+        fetch_knot[None, None, :, None] == knot_ids[:, None, None, None],
+        jnp.swapaxes(fetch_blocks, 0, 1)[None],
+        jnp.zeros((), jnp.bfloat16),
+    )
+    weight = jnp.concatenate([band_weight, fetch_weight], axis=2)
 
     center = (HI_BOUND + LO_BOUND) / 2.0
     radius = (HI_BOUND - LO_BOUND) / 2.0
@@ -84,30 +102,14 @@
             landed.append(got[slots:])
         low = shifted_open(probe_bf[knots - 3 :], "seg", 1)
         high = shifted_open(probe_bf[:3], "seg", -1)
-        extended = jnp.concatenate([low, probe_bf, high], axis=0)
-        summed = jnp.zeros(probe_bf.shape, jnp.float32)
-        for step in range(4):
-            summed = summed + jnp.einsum(
-                "kab,kbr->kar",
-                blocks[:, step],
-                extended[3 + step : 3 + step + knots],
-                preferred_element_type=jnp.float32,
-            )
-        for step in range(1, 4):
-            summed = summed + jnp.einsum(
-                "kba,kbr->kar",
-                lower_blocks[3 - step : 3 - step + knots, step],
-                extended[3 - step : 3 - step + knots],
-                preferred_element_type=jnp.float32,
-            )
-        fetched = jnp.stack(fetched)
-        forward = jnp.einsum(
-            "bsqp,bspr->bsqr", couplings, fetched, preferred_element_type=jnp.float32
-        ).reshape(own_rows, params, probes)
+        stacked = jnp.concatenate(
+            [low, probe_bf, high] + [fetched[b] for b in fetch_order], axis=0
+        )
+        summed = jnp.einsum(
+            "kamb,mbr->kar", weight, stacked, preferred_element_type=jnp.float32
+        )
         landed = jnp.concatenate(landed, axis=0)
-        cross = jnp.einsum(
-            "ks,spr->kpr", own_place, forward, precision=lax.Precision.HIGHEST
-        ) + jnp.einsum("ks,spr->kpr", land_place, landed, preferred_element_type=jnp.float32)
+        cross = jnp.einsum("ks,spr->kpr", land_place, landed, preferred_element_type=jnp.float32)
         residual = residual - (summed + cross)
         coeff_next = 1.0 / (2.0 * center / radius - coeff)
         direction = coeff_next * coeff * direction + 2.0 * coeff_next / radius * residual

time: 219 us -> 200 us (0.913)
  the two profiles are of different devices: /device:TPU:359 before, /device:TPU:24 now
where the time goes in v4:
time: 200 us; the launch traced here: 197 us
  starting transfers between devices  131 us (66%)
  local copies, waits for them, and re-layouts  34.2 us (17%)
  other arithmetic  15.3 us (8%)
  matrix products  12.2 us (6%)
  waiting for transfers between devices  3.98 us (2%)
    ppermute x24, starting transfers between devices, shifted_ring(): lax.ppermute(value, axis, [(i, (i + steps) % count) for i in range(count)])  91.7 us
    ppermute x7, starting transfers between devices, shifted_open(): lax.ppermute(value, axis, [(source, source + steps) for source in range(i...  39 us
    unnamed x53, local copies, waits for them, and re-layouts  12.7 us
    dot_general x3, matrix products, body(): jnp.einsum('kamb,mbr->kar', weight, stacked, preferred_element_type=jnp.f...  7.63 us
    slice x6, local copies, waits for them, and re-layouts, body(): landed.append(got[slots:])  6.2 us
  transfers between devices with their start and end apart: 31, of which 3 were waited for; matrix products, arithmetic and copies ran while one was open for 21% of the time, Pallas kernels for 0%

profile of v4, /device:TPU:24, one launch (start us, length us, event | category | flops | bytes accessed | tf_op | source)
XLA Modules:
  0.0 197.3 jit_solution(16776729807483759876)
XLA Ops:
  1.7 1.9 collective-permute-start.8
  3.6 3.4 %collective-permute-start.7 = (s32[2]{0:T(128)S(1)}, s32[2]{0:T(128)S(1)}, u32[]{:S(2)}, u32[]{:S(2)}) collective-permute-start(s32[2]{0:T(128)S(1)} %get-tuple-element.6), channel_id=1, source_target_pairs={{0,32},{16,48},{32,64},{48,80},{64,96},{80,112},{96,128},{112,144}... | collective-permute-start | bytes 32 | tf_op jit(solution)/shard_map/ppermute | solution.py:21
  7.0 4.0 %collective-permute-start.6 = (s32[2]{0:T(128)S(1)}, s32[2]{0:T(128)S(1)}, u32[]{:S(2)}, u32[]{:S(2)}) collective-permute-start(s32[2]{0:T(128)S(1)} %get-tuple-element.7), channel_id=1, source_target_pairs={{0,48},{16,64},{32,80},{48,96},{64,112},{80,128},{96,144},{112,160... | collective-permute-start | bytes 32 | tf_op jit(solution)/shard_map/ppermute | solution.py:21
  11.0 6.3 %collective-permute-start.5 = (s32[2]{0:T(128)S(1)}, s32[2]{0:T(128)S(1)}, u32[]{:S(2)}, u32[]{:S(2)}) collective-permute-start(s32[2]{0:T(128)S(1)} %get-tuple-element.8), channel_id=1, source_target_pairs={{0,464},{16,480},{32,496},{48,0},{64,16},{80,32},{96,48},{112,64},... | collective-permute-start | bytes 32 | tf_op jit(solution)/shard_map/ppermute | solution.py:21
  17.4 4.2 %collective-permute-start.4 = (s32[2]{0:T(128)S(1)}, s32[2]{0:T(128)S(1)}, u32[]{:S(2)}, u32[]{:S(2)}) collective-permute-start(s32[2]{0:T(128)S(1)} %get-tuple-element.9), channel_id=1, source_target_pairs={{0,480},{16,496},{32,0},{48,16},{64,32},{80,48},{96,64},{112,80},{... | collective-permute-start | bytes 32 | tf_op jit(solution)/shard_map/ppermute | solution.py:21
  25.4 1.7 slice_bitcast_fusion
  34.1 1.9 collective-permute-start.3
  36.1 2.7 %collective-permute-start.2 = (bf16[3,96,128]{2,1,0:T(8,128)(2,1)}, bf16[3,96,128]{2,1,0:T(8,128)(2,1)}, u32[]{:S(2)}, u32[]{:S(2)}) collective-permute-start(bf16[3,96,128]{2,1,0:T(8,128)(2,1)} %get-tuple-element.64), channel_id=1, source_target_pairs={{1,0},{2,1},{3,2},{4,3},{5,4},{6,5},{7,6},{8,7},{9,8},{10,9},{11,1... | collective-permute-start | bytes 221192 | tf_op jit(solution)/shard_map/ppermute | solution.py:16
  38.7 9.2 %collective-permute-start.1 = (bf16[3,96,128]{2,1,0:T(8,128)(2,1)}, bf16[3,96,128]{2,1,0:T(8,128)(2,1)}, u32[]{:S(2)}, u32[]{:S(2)}) collective-permute-start(bf16[3,96,128]{2,1,0:T(8,128)(2,1)} %get-tuple-element.65), channel_id=1, source_target_pairs={{0,1},{1,2},{2,3},{3,4},{4,5},{5,6},{6,7},{7,8},{8,9},{9,10},{10,1... | collective-permute-start | bytes 221192 | tf_op jit(solution)/shard_map/ppermute | solution.py:16
  48.0 2.7 %collective-permute-start = (bf16[3,4,96,96]{3,2,1,0:T(8,128)(2,1)}, bf16[3,4,96,96]{3,2,1,0:T(8,128)(2,1)}, u32[]{:S(2)}, u32[]{:S(2)}) collective-permute-start(bf16[3,4,96,96]{3,2,1,0:T(8,128)(2,1)} %slice_bitcast_fusion), channel_id=1, source_target_pairs={{0,1},{1,2},{2,3},{3,4},{4,5},{5,6},{6,7},{7,8},{8,9},{9,10},{10,1... | collective-permute-start | bytes 663560 | tf_op jit(solution)/shard_map/ppermute | solution.py:16
  53.2 1.9 collective-permute-start.9
  55.9 1.9 collective-permute-start.10
  60.9 3.1 %collective-permute-start.11 = (bf16[4,96,128]{2,0,1:T(4,128)(2,1)S(1)}, bf16[4,96,128]{2,0,1:T(4,128)(2,1)S(1)}, u32[]{:S(2)}, u32[]{:S(2)}) collective-permute-start(bf16[4,96,128]{2,0,1:T(4,128)(2,1)S(1)} %pad_maximum_fusion.33), channel_id=1, source_target_pairs={{0,48},{16,64},{32,80},{48,96},{64,112},{80,128},{96,144},{112,160... | collective-permute-start | bytes 294920 | tf_op jit(solution)/shard_map/ppermute | solution.py:21
  66.0 15.2 %collective-permute-start.12 = (bf16[4,96,128]{2,0,1:T(4,128)(2,1)}, bf16[4,96,128]{2,0,1:T(4,128)(2,1)S(1)}, u32[]{:S(2)}, u32[]{:S(2)}) collective-permute-start(bf16[4,96,128]{2,0,1:T(4,128)(2,1)} %pad_maximum_fusion.34), channel_id=1, source_target_pairs={{0,464},{16,480},{32,496},{48,0},{64,16},{80,32},{96,48},{112,64},... | collective-permute-start | bytes 294920 | tf_op jit(solution)/shard_map/ppermute | solution.py:21
  82.9 4.1 %collective-permute-start.13 = (bf16[4,96,128]{2,0,1:T(4,128)(2,1)}, bf16[4,96,128]{2,0,1:T(4,128)(2,1)S(1)}, u32[]{:S(2)}, u32[]{:S(2)}) collective-permute-start(bf16[4,96,128]{2,0,1:T(4,128)(2,1)} %pad_maximum_fusion.35), channel_id=1, source_target_pairs={{0,480},{16,496},{32,0},{48,16},{64,32},{80,48},{96,64},{112,80},{... | collective-permute-start | bytes 294920 | tf_op jit(solution)/shard_map/ppermute | solution.py:21
  87.1 1.7 fusion.60
  88.7 1.9 collective-permute-start.14
  90.7 1.7 fusion.59
  95.2 3.3 %concatenate.111 = bf16[12,96,128]{2,0,1:T(8,128)(2,1)} concatenate(bf16[2,96,128]{2,0,1:T(2,128)(2,1)} %get-tuple-element.100, bf16[2,96,128]{2,0,1:T(2,128)(2,1)} %get-tuple-element.98, bf16[2,96,128]{2,0,1:T(2,128)(2,1)} %get-tuple-element.96, bf16[2,96,128]{2,0,1:T(2,128)(2,1)} %get-tuple-element.94, bf16[2,96,128]{2,0,1:T(2,128)(2,1)} %get-tuple-element.92, ...), dimensions={0} | concatenate | bytes 589824 | tf_op jit(solution)/shard_map/concatenate | solution.py:111
  98.5 2.0 fusion.41
  101.7 1.4 constant_dynamic-update-slice_fusion.9
  103.1 1.4 constant_dynamic-update-slice_fusion.8
  104.5 1.4 constant_dynamic-update-slice_fusion.7
  106.0 1.4 constant_dynamic-update-slice_fusion.6
  107.4 2.0 %maximum_bitcast_fusion.1 = (bf16[8,96,96]{1,2,0:T(8,128)(2,1)}, bf16[8,96,96]{1,2,0:T(8,128)(2,1)}, bf16[8,96,96]{1,2,0:T(8,128)(2,1)}, bf16[8,96,96]{2,1,0:T(8...) fusion(bf16[8,4,96,96]{3,2,1,0:T(8,128)(2,1)S(1)} %bitcast.171, ...), kind=kLoop, calls=%fused_computation.52 | loop fusion | flops 221184 | bytes 2826240 | tf_op jit(solution)/shard_map/transpose | solution.py:66
  111.6 1.7 copy.34
  113.3 3.1 %select_select_fusion = bf16[8,96,14,96]{3,1,2,0:T(8,128)(2,1)S(1)} fusion(pred[8,14]{1,0:T(8,128)(4,1)S(1)} %get-tuple-element.110, pred[8,14]{1,0:T(8,128)(4,1)} %get-tuple-element.111, pred[8,14]{1,0:T(8,128)(4,1)} %get-tuple-element.112, pred[8,14]{1,0:T(8,128)(4,1)} %get-tuple-element.113, pred[8,14]{1,0:T(8,128)(4,1)} %get-tuple-element.114, ...), kind=kLoop, calls=%fused_computation.1 | loop fusion | flops 7225344 | bytes 3097360 | tf_op jit(solution)/shard_map/jit(_where)/select_n | solution.py:67
  116.4 2.2 %fusion.37 = (bf16[8,96,128]{2,1,0:T(8,128)(2,1)S(1)}, f32[8,96,128]{2,1,0:T(8,128)S(1)}) fusion(f32[1,8,96,128]{3,2,1,0:T(8,128)S(1)} %copy-done.2, f32[8,96,128]{2,0,1:T(8,128)S(1)} %copy-done.3, bf16[26,96,128]{2,1,0:T(8,128)(2,1)S(1)} %copy-done.5, bf16[8,96,12,96]{3,1,2,0:T(8,128)(2,1)S(1)} %broadcast_select_fusion, ...), kind=kOutput, calls=%fused_computation.121 | convolution fusion | flops 493240320 | bytes 5849088 | tf_op jit(solution)/shard_map/kamb,mbr->kar/dot_general | solution.py:108
  119.3 1.9 collective-permute-start.16
  121.2 10.6 %collective-permute-start.15 = (bf16[3,96,128]{2,1,0:T(8,128)(2,1)S(1)}, bf16[3,96,128]{2,1,0:T(8,128)(2,1)S(1)}, u32[]{:S(2)}, u32[]{:S(2)}) collective-permute-start(bf16[3,96,128]{2,1,0:T(8,128)(2,1)S(1)} %get-tuple-element.63), channel_id=1, source_target_pairs={{0,1},{1,2},{2,3},{3,4},{4,5},{5,6},{6,7},{7,8},{8,9},{9,10},{10,1... | collective-permute-start | bytes 221192 | tf_op jit(solution)/shard_map/ppermute | solution.py:16
  132.2 2.1 %collective-permute-start.17 = (bf16[4,96,128]{2,1,0:T(8,128)(2,1)S(1)}, bf16[4,96,128]{2,1,0:T(8,128)(2,1)S(1)}, u32[]{:S(2)}, u32[]{:S(2)}) collective-permute-start(bf16[4,96,128]{2,1,0:T(8,128)(2,1)S(1)} %pad_maximum_fusion.37), channel_id=1, source_target_pairs={{0,16},{16,32},{32,48},{48,64},{64,80},{80,96},{96,112},{112,128},... | collective-permute-start | bytes 294920 | tf_op jit(solution)/shard_map/ppermute | solution.py:21
  134.4 2.1 %collective-permute-start.18 = (bf16[4,96,128]{2,1,0:T(8,128)(2,1)S(1)}, bf16[4,96,128]{2,1,0:T(8,128)(2,1)S(1)}, u32[]{:S(2)}, u32[]{:S(2)}) collective-permute-start(bf16[4,96,128]{2,1,0:T(8,128)(2,1)S(1)} %pad_maximum_fusion.38), channel_id=1, source_target_pairs={{0,32},{16,48},{32,64},{48,80},{64,96},{80,112},{96,128},{112,144}... | collective-permute-start | bytes 294920 | tf_op jit(solution)/shard_map/ppermute | solution.py:21
  136.5 1.9 collective-permute-start.19
  138.5 8.3 %collective-permute-start.20 = (bf16[4,96,128]{2,1,0:T(8,128)(2,1)S(1)}, bf16[4,96,128]{2,1,0:T(8,128)(2,1)S(1)}, u32[]{:S(2)}, u32[]{:S(2)}) collective-permute-start(bf16[4,96,128]{2,1,0:T(8,128)(2,1)S(1)} %pad_maximum_fusion.40), channel_id=1, source_target_pairs={{0,464},{16,480},{32,496},{48,0},{64,16},{80,32},{96,48},{112,64},... | collective-permute-start | bytes 294920 | tf_op jit(solution)/shard_map/ppermute | solution.py:21
  146.9 4.5 %collective-permute-start.21 = (bf16[4,96,128]{2,1,0:T(8,128)(2,1)S(1)}, bf16[4,96,128]{2,1,0:T(8,128)(2,1)S(1)}, u32[]{:S(2)}, u32[]{:S(2)}) collective-permute-start(bf16[4,96,128]{2,1,0:T(8,128)(2,1)S(1)} %pad_maximum_fusion.41), channel_id=1, source_target_pairs={{0,480},{16,496},{32,0},{48,16},{64,32},{80,48},{96,64},{112,80},{... | collective-permute-start | bytes 294920 | tf_op jit(solution)/shard_map/ppermute | solution.py:21
  151.4 2.1 %collective-permute-start.22 = (bf16[4,96,128]{2,1,0:T(8,128)(2,1)S(1)}, bf16[4,96,128]{2,1,0:T(8,128)(2,1)S(1)}, u32[]{:S(2)}, u32[]{:S(2)}) collective-permute-start(bf16[4,96,128]{2,1,0:T(8,128)(2,1)S(1)} %pad_maximum_fusion.42), channel_id=1, source_target_pairs={{0,496},{16,0},{32,16},{48,32},{64,48},{80,64},{96,80},{112,96},{1... | collective-permute-start | bytes 294920 | tf_op jit(solution)/shard_map/ppermute | solution.py:21
  153.7 1.9 collective-permute-done.22
  155.7 2.3 %fusion.27 = (bf16[8,96,128]{2,1,0:T(8,128)(2,1)S(1)}, f32[8,96,128]{2,1,0:T(8,128)S(1)}) fusion(f32[8,96,128]{2,1,0:T(8,128)S(1)} %get-tuple-element.107, f32[1,8,96,128]{3,2,1,0:T(8,128)S(1)} %copy-done.2, f32[8,96,128]{2,0,1:T(8,128)S(1)} %fusion.24, bf16[26,96,128]{2,1,0:T(8,128)(2,1)S(1)} %get-tuple-element.79, ...), kind=kOutput, calls=%fused_computation.39 | convolution fusion | flops 493535232 | bytes 6242304 | tf_op jit(solution)/shard_map/kamb,mbr->kar/dot_general | solution.py:108
  158.6 1.9 collective-permute-start.24
  160.5 9.9 %collective-permute-start.23 = (bf16[3,96,128]{2,1,0:T(8,128)(2,1)S(1)}, bf16[3,96,128]{2,1,0:T(8,128)(2,1)S(1)}, u32[]{:S(2)}, u32[]{:S(2)}) collective-permute-start(bf16[3,96,128]{2,1,0:T(8,128)(2,1)S(1)} %get-tuple-element.61), channel_id=1, source_target_pairs={{0,1},{1,2},{2,3},{3,4},{4,5},{5,6},{6,7},{7,8},{8,9},{9,10},{10,1... | collective-permute-start | bytes 221192 | tf_op jit(solution)/shard_map/ppermute | solution.py:16
  170.8 1.9 collective-permute-start.25
  172.8 1.9 collective-permute-start.26
  174.7 1.9 collective-permute-start.27
  176.7 8.7 %collective-permute-start.28 = (bf16[4,96,128]{2,1,0:T(8,128)(2,1)S(1)}, bf16[4,96,128]{2,1,0:T(8,128)(2,1)S(1)}, u32[]{:S(2)}, u32[]{:S(2)}) collective-permute-start(bf16[4,96,128]{2,1,0:T(8,128)(2,1)S(1)} %pad_maximum_fusion.46), channel_id=1, source_target_pairs={{0,464},{16,480},{32,496},{48,0},{64,16},{80,32},{96,48},{112,64},... | collective-permute-start | bytes 294920 | tf_op jit(solution)/shard_map/ppermute | solution.py:21
  185.5 4.3 %collective-permute-start.29 = (bf16[4,96,128]{2,1,0:T(8,128)(2,1)S(1)}, bf16[4,96,128]{2,1,0:T(8,128)(2,1)S(1)}, u32[]{:S(2)}, u32[]{:S(2)}) collective-permute-start(bf16[4,96,128]{2,1,0:T(8,128)(2,1)S(1)} %pad_maximum_fusion.47), channel_id=1, source_target_pairs={{0,480},{16,496},{32,0},{48,16},{64,32},{80,48},{96,64},{112,80},{... | collective-permute-start | bytes 294920 | tf_op jit(solution)/shard_map/ppermute | solution.py:21
  189.8 1.9 collective-permute-start.30
  192.0 1.9 collective-permute-done.30
  194.2 3.1 %fusion.15 = f32[1,8,96,128]{3,2,1,0:T(8,128)} fusion(f32[8,96,128]{2,1,0:T(8,128)S(1)} %get-tuple-element.109, bf16[8,96,12,96]{3,1,2,0:T(8,128)(2,1)S(1)} %broadcast_select_fusion, bf16[8,96,14,96]{3,1,2,0:T(8,128)(2,1)S(1)} %select_select_fusion, bf16[26,96,128]{2,1,0:T(8,128)(2,1)S(1)} %get-tuple-element.67, f32[8,96,128]{2,0,1:T(8,128)S(1)} %fusion.22, ...), kind=kOutput, calls=%fused_computation.22 | convolution fusion | flops 494125056 | bytes 6438912 | tf_op jit(solution)/shard_map/kamb,mbr->kar/dot_general | solution.py:108
  (158 shorter events, 31.4 us)
Async XLA Ops:
  1.7 32.4 %collective-permute-start.8 = (s32[2]{0:T(128)S(1)}, s32[2]{0:T(128)S(1)}, u32[]{:S(2)}, u32[]{:S(2)}) collective-permute-start(s32[2]{0:T(128)S(1)} %get-tuple-element.5), channel_id=1, source_target_pairs={{0,16},{16,32},{32,48},{48,64},{64,80},{80,96},{96,112},{112,128},... | collective-permute-start | bytes 32 | tf_op jit(solution)/shard_map/ppermute | solution.py:21
  3.6 32.4 %collective-permute-start.7 = (s32[2]{0:T(128)S(1)}, s32[2]{0:T(128)S(1)}, u32[]{:S(2)}, u32[]{:S(2)}) collective-permute-start(s32[2]{0:T(128)S(1)} %get-tuple-element.6), channel_id=1, source_target_pairs={{0,32},{16,48},{32,64},{48,80},{64,96},{80,112},{96,128},{112,144}... | collective-permute-start | bytes 32 | tf_op jit(solution)/shard_map/ppermute | solution.py:21
  7.0 31.7 %collective-permute-start.6 = (s32[2]{0:T(128)S(1)}, s32[2]{0:T(128)S(1)}, u32[]{:S(2)}, u32[]{:S(2)}) collective-permute-start(s32[2]{0:T(128)S(1)} %get-tuple-element.7), channel_id=1, source_target_pairs={{0,48},{16,64},{32,80},{48,96},{64,112},{80,128},{96,144},{112,160... | collective-permute-start | bytes 32 | tf_op jit(solution)/shard_map/ppermute | solution.py:21
  11.0 36.9 %collective-permute-start.5 = (s32[2]{0:T(128)S(1)}, s32[2]{0:T(128)S(1)}, u32[]{:S(2)}, u32[]{:S(2)}) collective-permute-start(s32[2]{0:T(128)S(1)} %get-tuple-element.8), channel_id=1, source_target_pairs={{0,464},{16,480},{32,496},{48,0},{64,16},{80,32},{96,48},{112,64},... | collective-permute-start | bytes 32 | tf_op jit(solution)/shard_map/ppermute | solution.py:21
  17.4 33.4 %collective-permute-start.4 = (s32[2]{0:T(128)S(1)}, s32[2]{0:T(128)S(1)}, u32[]{:S(2)}, u32[]{:S(2)}) collective-permute-start(s32[2]{0:T(128)S(1)} %get-tuple-element.9), channel_id=1, source_target_pairs={{0,480},{16,496},{32,0},{48,16},{64,32},{80,48},{96,64},{112,80},{... | collective-permute-start | bytes 32 | tf_op jit(solution)/shard_map/ppermute | solution.py:21
  33.8 17.9 %copy-start = (bf16[1,1,6,2,96,96]{5,4,3,2,1,0:T(8,128)(2,1)S(1)}, bf16[1,1,6,2,96,96]{5,4,3,2,1,0:T(8,128)(2,1)}, u32[]{:S(2)}) copy-start(bf16[1,1,6,2,96,96]{5,4,3,2,1,0:T(8,128)(2,1)} %param.9) | copy-start | bytes 663556
  34.1 16.7 %copy-start.6 = (s32[2]{0:T(128)}, s32[2]{0:T(128)S(1)}, u32[]{:S(2)}) copy-start(s32[2]{0:T(128)S(1)} %collective-permute-done.8) | copy-start | bytes 28
  34.1 16.6 %collective-permute-start.3 = (s32[2]{0:T(128)S(1)}, s32[2]{0:T(128)S(1)}, u32[]{:S(2)}, u32[]{:S(2)}) collective-permute-start(s32[2]{0:T(128)S(1)} %get-tuple-element.10), channel_id=1, source_target_pairs={{0,496},{16,0},{32,16},{48,32},{64,48},{80,64},{96,80},{112,96},{1... | collective-permute-start | bytes 32 | tf_op jit(solution)/shard_map/ppermute | solution.py:21
  36.1 22.5 %copy-start.7 = (s32[2]{0:T(128)}, s32[2]{0:T(128)S(1)}, u32[]{:S(2)}) copy-start(s32[2]{0:T(128)S(1)} %collective-permute-done.7) | copy-start | bytes 28
  36.1 29.9 %collective-permute-start.2 = (bf16[3,96,128]{2,1,0:T(8,128)(2,1)}, bf16[3,96,128]{2,1,0:T(8,128)(2,1)}, u32[]{:S(2)}, u32[]{:S(2)}) collective-permute-start(bf16[3,96,128]{2,1,0:T(8,128)(2,1)} %get-tuple-element.64), channel_id=1, source_target_pairs={{1,0},{2,1},{3,2},{4,3},{5,4},{6,5},{7,6},{8,7},{9,8},{10,9},{11,1... | collective-permute-start | bytes 221192 | tf_op jit(solution)/shard_map/ppermute | solution.py:16
  38.7 13.5 %copy-start.8 = (s32[2]{0:T(128)}, s32[2]{0:T(128)S(1)}, u32[]{:S(2)}) copy-start(s32[2]{0:T(128)S(1)} %collective-permute-done.6) | copy-start | bytes 28
  38.7 22.2 %collective-permute-start.1 = (bf16[3,96,128]{2,1,0:T(8,128)(2,1)}, bf16[3,96,128]{2,1,0:T(8,128)(2,1)}, u32[]{:S(2)}, u32[]{:S(2)}) collective-permute-start(bf16[3,96,128]{2,1,0:T(8,128)(2,1)} %get-tuple-element.65), channel_id=1, source_target_pairs={{0,1},{1,2},{2,3},{3,4},{4,5},{5,6},{6,7},{7,8},{8,9},{9,10},{10,1... | collective-permute-start | bytes 221192 | tf_op jit(solution)/shard_map/ppermute | solution.py:16
  48.0 4.3 %copy-start.9 = (s32[2]{0:T(128)}, s32[2]{0:T(128)S(1)}, u32[]{:S(2)}) copy-start(s32[2]{0:T(128)S(1)} %collective-permute-done.5) | copy-start | bytes 28
  48.0 59.4 %collective-permute-start = (bf16[3,4,96,96]{3,2,1,0:T(8,128)(2,1)}, bf16[3,4,96,96]{3,2,1,0:T(8,128)(2,1)}, u32[]{:S(2)}, u32[]{:S(2)}) collective-permute-start(bf16[3,4,96,96]{3,2,1,0:T(8,128)(2,1)} %slice_bitcast_fusion), channel_id=1, source_target_pairs={{0,1},{1,2},{2,3},{3,4},{4,5},{5,6},{6,7},{7,8},{8,9},{9,10},{10,1... | collective-permute-start | bytes 663560 | tf_op jit(solution)/shard_map/ppermute | solution.py:16
  50.7 1.5 copy-start.10
  50.8 1.5 copy-start.11
  52.5 54.9 %copy-start.1 = (bf16[1,8,4,96,96]{4,3,2,1,0:T(8,128)(2,1)S(1)}, bf16[1,8,4,96,96]{4,3,2,1,0:T(8,128)(2,1)}, u32[]{:S(2)}) copy-start(bf16[1,8,4,96,96]{4,3,2,1,0:T(8,128)(2,1)} %param.6) | copy-start | bytes 1769476
  53.2 29.7 %collective-permute-start.9 = (bf16[4,96,128]{2,0,1:T(4,128)(2,1)}, bf16[4,96,128]{2,0,1:T(4,128)(2,1)}, u32[]{:S(2)}, u32[]{:S(2)}) collective-permute-start(bf16[4,96,128]{2,0,1:T(4,128)(2,1)} %pad_maximum_fusion.31), channel_id=1, source_target_pairs={{0,16},{16,32},{32,48},{48,64},{64,80},{80,96},{96,112},{112,128},... | collective-permute-start | bytes 294920 | tf_op jit(solution)/shard_map/ppermute | solution.py:21
  55.9 32.8 %collective-permute-start.10 = (bf16[4,96,128]{2,0,1:T(4,128)(2,1)}, bf16[4,96,128]{2,0,1:T(4,128)(2,1)}, u32[]{:S(2)}, u32[]{:S(2)}) collective-permute-start(bf16[4,96,128]{2,0,1:T(4,128)(2,1)} %pad_maximum_fusion.32), channel_id=1, source_target_pairs={{0,32},{16,48},{32,64},{48,80},{64,96},{80,112},{96,128},{112,144}... | collective-permute-start | bytes 294920 | tf_op jit(solution)/shard_map/ppermute | solution.py:21
  60.9 31.4 %collective-permute-start.11 = (bf16[4,96,128]{2,0,1:T(4,128)(2,1)S(1)}, bf16[4,96,128]{2,0,1:T(4,128)(2,1)S(1)}, u32[]{:S(2)}, u32[]{:S(2)}) collective-permute-start(bf16[4,96,128]{2,0,1:T(4,128)(2,1)S(1)} %pad_maximum_fusion.33), channel_id=1, source_target_pairs={{0,48},{16,64},{32,80},{48,96},{64,112},{80,128},{96,144},{112,160... | collective-permute-start | bytes 294920 | tf_op jit(solution)/shard_map/ppermute | solution.py:21
  66.0 27.1 %collective-permute-start.12 = (bf16[4,96,128]{2,0,1:T(4,128)(2,1)}, bf16[4,96,128]{2,0,1:T(4,128)(2,1)S(1)}, u32[]{:S(2)}, u32[]{:S(2)}) collective-permute-start(bf16[4,96,128]{2,0,1:T(4,128)(2,1)} %pad_maximum_fusion.34), channel_id=1, source_target_pairs={{0,464},{16,480},{32,496},{48,0},{64,16},{80,32},{96,48},{112,64},... | collective-permute-start | bytes 294920 | tf_op jit(solution)/shard_map/ppermute | solution.py:21
  82.1 0.8 copy-start.4
  82.9 10.8 %collective-permute-start.13 = (bf16[4,96,128]{2,0,1:T(4,128)(2,1)}, bf16[4,96,128]{2,0,1:T(4,128)(2,1)S(1)}, u32[]{:S(2)}, u32[]{:S(2)}) collective-permute-start(bf16[4,96,128]{2,0,1:T(4,128)(2,1)} %pad_maximum_fusion.35), channel_id=1, source_target_pairs={{0,480},{16,496},{32,0},{48,16},{64,32},{80,48},{96,64},{112,80},{... | collective-permute-start | bytes 294920 | tf_op jit(solution)/shard_map/ppermute | solution.py:21
  88.7 5.7 %collective-permute-start.14 = (bf16[4,96,128]{2,0,1:T(4,128)(2,1)}, bf16[4,96,128]{2,0,1:T(4,128)(2,1)S(1)}, u32[]{:S(2)}, u32[]{:S(2)}) collective-permute-start(bf16[4,96,128]{2,0,1:T(4,128)(2,1)} %pad_maximum_fusion.36), channel_id=1, source_target_pairs={{0,496},{16,0},{32,16},{48,32},{64,48},{80,64},{96,80},{112,96},{1... | collective-permute-start | bytes 294920 | tf_op jit(solution)/shard_map/ppermute | solution.py:21
  109.4 7.0 %copy-start.2 = (f32[1,8,96,128]{3,2,1,0:T(8,128)S(1)}, f32[1,8,96,128]{3,2,1,0:T(8,128)}, u32[]{:S(2)}) copy-start(f32[1,8,96,128]{3,2,1,0:T(8,128)} %param.5) | copy-start | bytes 1179652
  113.3 3.1 %copy-start.3 = (f32[8,96,128]{2,0,1:T(8,128)S(1)}, f32[8,96,128]{2,0,1:T(8,128)}, u32[]{:S(2)}) copy-start(f32[8,96,128]{2,0,1:T(8,128)} %fusion.41) | copy-start | bytes 1179652
  113.3 3.1 %copy-start.5 = (bf16[26,96,128]{2,1,0:T(8,128)(2,1)S(1)}, bf16[26,96,128]{2,1,0:T(8,128)(2,1)}, u32[]{:S(2)}) copy-start(bf16[26,96,128]{2,1,0:T(8,128)(2,1)} %constant_dynamic-update-slice_fusion.6) | copy-start | bytes 1916932
  119.3 27.6 %collective-permute-start.16 = (bf16[3,96,128]{2,1,0:T(8,128)(2,1)S(1)}, bf16[3,96,128]{2,1,0:T(8,128)(2,1)S(1)}, u32[]{:S(2)}, u32[]{:S(2)}) collective-permute-start(bf16[3,96,128]{2,1,0:T(8,128)(2,1)S(1)} %get-tuple-element.62), channel_id=1, source_target_pairs={{1,0},{2,1},{3,2},{4,3},{5,4},{6,5},{7,6},{8,7},{9,8},{10,9},{11,1... | collective-permute-start | bytes 221192 | tf_op jit(solution)/shard_map/ppermute | solution.py:16
  121.2 17.3 %collective-permute-start.15 = (bf16[3,96,128]{2,1,0:T(8,128)(2,1)S(1)}, bf16[3,96,128]{2,1,0:T(8,128)(2,1)S(1)}, u32[]{:S(2)}, u32[]{:S(2)}) collective-permute-start(bf16[3,96,128]{2,1,0:T(8,128)(2,1)S(1)} %get-tuple-element.63), channel_id=1, source_target_pairs={{0,1},{1,2},{2,3},{3,4},{4,5},{5,6},{6,7},{7,8},{8,9},{9,10},{10,1... | collective-permute-start | bytes 221192 | tf_op jit(solution)/shard_map/ppermute | solution.py:16
  132.2 19.2 %collective-permute-start.17 = (bf16[4,96,128]{2,1,0:T(8,128)(2,1)S(1)}, bf16[4,96,128]{2,1,0:T(8,128)(2,1)S(1)}, u32[]{:S(2)}, u32[]{:S(2)}) collective-permute-start(bf16[4,96,128]{2,1,0:T(8,128)(2,1)S(1)} %pad_maximum_fusion.37), channel_id=1, source_target_pairs={{0,16},{16,32},{32,48},{48,64},{64,80},{80,96},{96,112},{112,128},... | collective-permute-start | bytes 294920 | tf_op jit(solution)/shard_map/ppermute | solution.py:21
  134.4 19.2 %collective-permute-start.18 = (bf16[4,96,128]{2,1,0:T(8,128)(2,1)S(1)}, bf16[4,96,128]{2,1,0:T(8,128)(2,1)S(1)}, u32[]{:S(2)}, u32[]{:S(2)}) collective-permute-start(bf16[4,96,128]{2,1,0:T(8,128)(2,1)S(1)} %pad_maximum_fusion.38), channel_id=1, source_target_pairs={{0,32},{16,48},{32,64},{48,80},{64,96},{80,112},{96,128},{112,144}... | collective-permute-start | bytes 294920 | tf_op jit(solution)/shard_map/ppermute | solution.py:21
  136.5 17.0 %collective-permute-start.19 = (bf16[4,96,128]{2,1,0:T(8,128)(2,1)S(1)}, bf16[4,96,128]{2,1,0:T(8,128)(2,1)S(1)}, u32[]{:S(2)}, u32[]{:S(2)}) collective-permute-start(bf16[4,96,128]{2,1,0:T(8,128)(2,1)S(1)} %pad_maximum_fusion.39), channel_id=1, source_target_pairs={{0,48},{16,64},{32,80},{48,96},{64,112},{80,128},{96,144},{112,160... | collective-permute-start | bytes 294920 | tf_op jit(solution)/shard_map/ppermute | solution.py:21
  138.5 15.1 %collective-permute-start.20 = (bf16[4,96,128]{2,1,0:T(8,128)(2,1)S(1)}, bf16[4,96,128]{2,1,0:T(8,128)(2,1)S(1)}, u32[]{:S(2)}, u32[]{:S(2)}) collective-permute-start(bf16[4,96,128]{2,1,0:T(8,128)(2,1)S(1)} %pad_maximum_fusion.40), channel_id=1, source_target_pairs={{0,464},{16,480},{32,496},{48,0},{64,16},{80,32},{96,48},{112,64},... | collective-permute-start | bytes 294920 | tf_op jit(solution)/shard_map/ppermute | solution.py:21
  146.9 6.7 %collective-permute-start.21 = (bf16[4,96,128]{2,1,0:T(8,128)(2,1)S(1)}, bf16[4,96,128]{2,1,0:T(8,128)(2,1)S(1)}, u32[]{:S(2)}, u32[]{:S(2)}) collective-permute-start(bf16[4,96,128]{2,1,0:T(8,128)(2,1)S(1)} %pad_maximum_fusion.41), channel_id=1, source_target_pairs={{0,480},{16,496},{32,0},{48,16},{64,32},{80,48},{96,64},{112,80},{... | collective-permute-start | bytes 294920 | tf_op jit(solution)/shard_map/ppermute | solution.py:21
  151.4 4.1 %collective-permute-start.22 = (bf16[4,96,128]{2,1,0:T(8,128)(2,1)S(1)}, bf16[4,96,128]{2,1,0:T(8,128)(2,1)S(1)}, u32[]{:S(2)}, u32[]{:S(2)}) collective-permute-start(bf16[4,96,128]{2,1,0:T(8,128)(2,1)S(1)} %pad_maximum_fusion.42), channel_id=1, source_target_pairs={{0,496},{16,0},{32,16},{48,32},{64,48},{80,64},{96,80},{112,96},{1... | collective-permute-start | bytes 294920 | tf_op jit(solution)/shard_map/ppermute | solution.py:21
  158.6 26.9 %collective-permute-start.24 = (bf16[3,96,128]{2,1,0:T(8,128)(2,1)S(1)}, bf16[3,96,128]{2,1,0:T(8,128)(2,1)S(1)}, u32[]{:S(2)}, u32[]{:S(2)}) collective-permute-start(bf16[3,96,128]{2,1,0:T(8,128)(2,1)S(1)} %get-tuple-element.60), channel_id=1, source_target_pairs={{1,0},{2,1},{3,2},{4,3},{5,4},{6,5},{7,6},{8,7},{9,8},{10,9},{11,1... | collective-permute-start | bytes 221192 | tf_op jit(solution)/shard_map/ppermute | solution.py:16
  160.5 16.2 %collective-permute-start.23 = (bf16[3,96,128]{2,1,0:T(8,128)(2,1)S(1)}, bf16[3,96,128]{2,1,0:T(8,128)(2,1)S(1)}, u32[]{:S(2)}, u32[]{:S(2)}) collective-permute-start(bf16[3,96,128]{2,1,0:T(8,128)(2,1)S(1)} %get-tuple-element.61), channel_id=1, source_target_pairs={{0,1},{1,2},{2,3},{3,4},{4,5},{5,6},{6,7},{7,8},{8,9},{9,10},{10,1... | collective-permute-start | bytes 221192 | tf_op jit(solution)/shard_map/ppermute | solution.py:16
  170.8 19.0 %collective-permute-start.25 = (bf16[4,96,128]{2,1,0:T(8,128)(2,1)S(1)}, bf16[4,96,128]{2,1,0:T(8,128)(2,1)S(1)}, u32[]{:S(2)}, u32[]{:S(2)}) collective-permute-start(bf16[4,96,128]{2,1,0:T(8,128)(2,1)S(1)} %pad_maximum_fusion.43), channel_id=1, source_target_pairs={{0,16},{16,32},{32,48},{48,64},{64,80},{80,96},{96,112},{112,128},... | collective-permute-start | bytes 294920 | tf_op jit(solution)/shard_map/ppermute | solution.py:21
  172.8 19.0 %collective-permute-start.26 = (bf16[4,96,128]{2,1,0:T(8,128)(2,1)S(1)}, bf16[4,96,128]{2,1,0:T(8,128)(2,1)S(1)}, u32[]{:S(2)}, u32[]{:S(2)}) collective-permute-start(bf16[4,96,128]{2,1,0:T(8,128)(2,1)S(1)} %pad_maximum_fusion.44), channel_id=1, source_target_pairs={{0,32},{16,48},{32,64},{48,80},{64,96},{80,112},{96,128},{112,144}... | collective-permute-start | bytes 294920 | tf_op jit(solution)/shard_map/ppermute | solution.py:21
  174.7 17.1 %collective-permute-start.27 = (bf16[4,96,128]{2,1,0:T(8,128)(2,1)S(1)}, bf16[4,96,128]{2,1,0:T(8,128)(2,1)S(1)}, u32[]{:S(2)}, u32[]{:S(2)}) collective-permute-start(bf16[4,96,128]{2,1,0:T(8,128)(2,1)S(1)} %pad_maximum_fusion.45), channel_id=1, source_target_pairs={{0,48},{16,64},{32,80},{48,96},{64,112},{80,128},{96,144},{112,160... | collective-permute-start | bytes 294920 | tf_op jit(solution)/shard_map/ppermute | solution.py:21
  176.7 15.1 %collective-permute-start.28 = (bf16[4,96,128]{2,1,0:T(8,128)(2,1)S(1)}, bf16[4,96,128]{2,1,0:T(8,128)(2,1)S(1)}, u32[]{:S(2)}, u32[]{:S(2)}) collective-permute-start(bf16[4,96,128]{2,1,0:T(8,128)(2,1)S(1)} %pad_maximum_fusion.46), channel_id=1, source_target_pairs={{0,464},{16,480},{32,496},{48,0},{64,16},{80,32},{96,48},{112,64},... | collective-permute-start | bytes 294920 | tf_op jit(solution)/shard_map/ppermute | solution.py:21
  185.5 6.5 %collective-permute-start.29 = (bf16[4,96,128]{2,1,0:T(8,128)(2,1)S(1)}, bf16[4,96,128]{2,1,0:T(8,128)(2,1)S(1)}, u32[]{:S(2)}, u32[]{:S(2)}) collective-permute-start(bf16[4,96,128]{2,1,0:T(8,128)(2,1)S(1)} %pad_maximum_fusion.47), channel_id=1, source_target_pairs={{0,480},{16,496},{32,0},{48,16},{64,32},{80,48},{96,64},{112,80},{... | collective-permute-start | bytes 294920 | tf_op jit(solution)/shard_map/ppermute | solution.py:21
  189.8 4.1 %collective-permute-start.30 = (bf16[4,96,128]{2,1,0:T(8,128)(2,1)S(1)}, bf16[4,96,128]{2,1,0:T(8,128)(2,1)S(1)}, u32[]{:S(2)}, u32[]{:S(2)}) collective-permute-start(bf16[4,96,128]{2,1,0:T(8,128)(2,1)S(1)} %pad_maximum_fusion.48), channel_id=1, source_target_pairs={{0,496},{16,0},{32,16},{48,32},{64,48},{80,64},{96,80},{112,96},{1... | collective-permute-start | bytes 294920 | tf_op jit(solution)/shard_map/ppermute | solution.py:21

commit v5 on v3

--- a/solution.py
+++ b/solution.py
@@ -36,7 +36,16 @@
     bucket_of = {o: b for b, o in enumerate(offsets)}
     shifts = [o for o in offsets if o > 0] + [o for o in offsets if o < 0]
 
-    boundary_blocks = shifted_open(blocks[knots - 3 :], "seg", 1)
+    center = (HI_BOUND + LO_BOUND) / 2.0
+    first_direction = right_rows / center
+    first_probe = first_direction.astype(jnp.bfloat16)
+    tail_blocks = blocks[knots - 3 :]
+    tail_probe = first_probe[knots - 3 :]
+    sent_down = shifted_open(
+        jnp.concatenate([tail_blocks.reshape(-1), tail_probe.reshape(-1)]), "seg", 1
+    )
+    boundary_blocks = sent_down[: tail_blocks.size].reshape(tail_blocks.shape)
+    first_low = sent_down[tail_blocks.size :].reshape(tail_probe.shape)
     lower_blocks = jnp.concatenate([boundary_blocks, blocks], axis=0)
 
     used = jnp.arange(slots, dtype=jnp.int32)[None, :] < used_count[:, None]
@@ -76,10 +85,10 @@
     coeff = radius / center
     solution = jnp.zeros(right_rows.shape, jnp.float32)
     residual = right_rows
-    direction = right_rows / center
+    direction = first_direction
     own_rows = buckets * slots
     for turn in range(ITERS):
-        probe_bf = direction.astype(jnp.bfloat16)
+        probe_bf = first_probe if turn == 0 else direction.astype(jnp.bfloat16)
         solution = solution + direction
         if answer_pick is None:
             picked = jnp.einsum(
@@ -128,7 +137,7 @@
             land_place = jnp.concatenate(
                 [(got_index[s][None, :] == knot_vals[:, None]) for s in shifts], axis=1
             ).astype(jnp.bfloat16)
-        low = shifted_open(probe_bf[knots - 3 :], "seg", 1)
+        low = first_low if turn == 0 else shifted_open(probe_bf[knots - 3 :], "seg", 1)
         high = shifted_open(probe_bf[:3], "seg", -1)
         stacked = jnp.concatenate(
             [low, probe_bf, high] + [fetched[b] for b in fetch_order], axis=0

time: 182 us -> 190 us (1.044)
  the two profiles are of different devices: /device:TPU:287 before, /device:TPU:383 now
where the time goes in v5:
time: 190 us; the launch traced here: 188 us
  starting transfers between devices  86 us (45%)
  waiting for transfers between devices  36 us (19%)
  local copies, waits for them, and re-layouts  32.9 us (17%)
  other arithmetic  16.7 us (9%)
  matrix products  15.9 us (8%)
    ppermute x18, starting transfers between devices, shifted_ring(): lax.ppermute(value, axis, [(i, (i + steps) % count) for i in range(count)])  51.9 us
    ppermute x18, waiting for transfers between devices, shifted_ring(): lax.ppermute(value, axis, [(i, (i + steps) % count) for i in range(count)])  36 us
    ppermute x6, starting transfers between devices, shifted_open(): lax.ppermute(value, axis, [(source, source + steps) for source in range(i...  34 us
    unnamed x57, local copies, waits for them, and re-layouts  14.5 us
    another operation x7, other arithmetic  7.51 us
    dot_general x3, matrix products, body(): jnp.einsum('kamb,mbr->kar', weight, stacked, preferred_element_type=jnp.f...  7.5 us
    another operation x3, local copies, waits for them, and re-layouts  5.74 us
    dot_general x6, matrix products, body(): jnp.einsum('sk,kpr->spr', far_pick[bucket_of[-s]], got[:knots], preferred...  4.22 us
  transfers between devices with their start and end apart: 24, of which 9 were waited for; matrix products, arithmetic and copies ran while one was open for 21% of the time, Pallas kernels for 0%

profile of v5, /device:TPU:383, one launch (start us, length us, event | category | flops | bytes accessed | tf_op | source)
XLA Modules:
  0.0 188.5 jit_solution(7930452987427003679)
XLA Ops:
  1.7 2.4 %collective-permute-start.1 = (bf16[3,96,128]{2,1,0:T(8,128)(2,1)}, bf16[3,96,128]{2,1,0:T(8,128)(2,1)}, u32[]{:S(2)}, u32[]{:S(2)}) collective-permute-start(bf16[3,96,128]{2,1,0:T(8,128)(2,1)} %get-tuple-element.66), channel_id=1, source_target_pairs={{1,0},{2,1},{3,2},{4,3},{5,4},{6,5},{7,6},{8,7},{9,8},{10,9},{11,1... | collective-permute-start | bytes 221192 | tf_op jit(solution)/shard_map/ppermute | solution.py:16
  6.2 9.0 %collective-permute-start = (bf16[147456]{0:T(1024)(128)(2,1)}, bf16[147456]{0:T(1024)(128)(2,1)}, u32[]{:S(2)}, u32[]{:S(2)}) collective-permute-start(bf16[147456]{0:T(1024)(128)(2,1)} %pad_maximum_fusion.26), channel_id=1, source_target_pairs={{0,1},{1,2},{2,3},{3,4},{4,5},{5,6},{6,7},{7,8},{8,9},{9,10},{10,1... | collective-permute-start | bytes 884744 | tf_op jit(solution)/shard_map/ppermute | solution.py:16
  19.8 3.1 %collective-permute-start.7 = (bf16[11,96,128]{2,1,0:T(8,128)(2,1)S(1)}, bf16[11,96,128]{2,1,0:T(8,128)(2,1)S(1)}, u32[]{:S(2)}, u32[]{:S(2)}) collective-permute-start(bf16[11,96,128]{2,1,0:T(8,128)(2,1)S(1)} %get-tuple-element.60), channel_id=1, source_target_pairs={{0,496},{16,0},{32,16},{48,32},{64,48},{80,64},{96,80},{112,96},{1... | collective-permute-start | bytes 811016 | tf_op jit(solution)/shard_map/ppermute | solution.py:21
  22.9 3.4 %collective-permute-start.3 = (bf16[11,96,128]{2,1,0:T(8,128)(2,1)S(1)}, bf16[11,96,128]{2,1,0:T(8,128)(2,1)}, u32[]{:S(2)}, u32[]{:S(2)}) collective-permute-start(bf16[11,96,128]{2,1,0:T(8,128)(2,1)S(1)} %get-tuple-element.61), channel_id=1, source_target_pairs={{0,32},{16,48},{32,64},{48,80},{64,96},{80,112},{96,128},{112,144}... | collective-permute-start | bytes 811016 | tf_op jit(solution)/shard_map/ppermute | solution.py:21
  26.4 4.2 %collective-permute-start.4 = (bf16[11,96,128]{2,1,0:T(8,128)(2,1)}, bf16[11,96,128]{2,1,0:T(8,128)(2,1)}, u32[]{:S(2)}, u32[]{:S(2)}) collective-permute-start(bf16[11,96,128]{2,1,0:T(8,128)(2,1)} %get-tuple-element.62), channel_id=1, source_target_pairs={{0,48},{16,64},{32,80},{48,96},{64,112},{80,128},{96,144},{112,160... | collective-permute-start | bytes 811016 | tf_op jit(solution)/shard_map/ppermute | solution.py:21
  32.6 16.2 %collective-permute-done.7 = bf16[11,96,128]{2,1,0:T(8,128)(2,1)S(1)} collective-permute-done((bf16[11,96,128]{2,1,0:T(8,128)(2,1)S(1)}, bf16[11,96,128]{2,1,0:T(8,128)(2,1)S(1)}, u32[]{:S(2)}, u32[]{:S(2)}) %collective-permute-start.7) | collective-permute-done | bytes 270368 | tf_op jit(solution)/shard_map/ppermute | solution.py:21
  48.8 1.9 %collective-permute-start.5 = (bf16[11,96,128]{2,1,0:T(8,128)(2,1)}, bf16[11,96,128]{2,1,0:T(8,128)(2,1)S(1)}, u32[]{:S(2)}, u32[]{:S(2)}) collective-permute-start(bf16[11,96,128]{2,1,0:T(8,128)(2,1)} %get-tuple-element.63), channel_id=1, source_target_pairs={{0,464},{16,480},{32,496},{48,0},{64,16},{80,32},{96,48},{112,64},... | collective-permute-start | bytes 811016 | tf_op jit(solution)/shard_map/ppermute | solution.py:21
  51.0 1.9 %collective-permute-start.6 = (bf16[11,96,128]{2,1,0:T(8,128)(2,1)}, bf16[11,96,128]{2,1,0:T(8,128)(2,1)S(1)}, u32[]{:S(2)}, u32[]{:S(2)}) collective-permute-start(bf16[11,96,128]{2,1,0:T(8,128)(2,1)} %get-tuple-element.64), channel_id=1, source_target_pairs={{0,480},{16,496},{32,0},{48,16},{64,32},{80,48},{96,64},{112,80},{... | collective-permute-start | bytes 811016 | tf_op jit(solution)/shard_map/ppermute | solution.py:21
  54.7 1.9 %collective-permute-start.2 = (bf16[11,96,128]{2,1,0:T(8,128)(2,1)S(1)}, bf16[11,96,128]{2,1,0:T(8,128)(2,1)S(1)}, u32[]{:S(2)}, u32[]{:S(2)}) collective-permute-start(bf16[11,96,128]{2,1,0:T(8,128)(2,1)S(1)} %copy-done.7), channel_id=1, source_target_pairs={{0,16},{16,32},{32,48},{48,64},{64,80},{80,96},{96,112},{112,128},... | collective-permute-start | bytes 811016 | tf_op jit(solution)/shard_map/ppermute | solution.py:21
  58.3 4.4 %collective-permute-done.5 = bf16[11,96,128]{2,1,0:T(8,128)(2,1)S(1)} collective-permute-done((bf16[11,96,128]{2,1,0:T(8,128)(2,1)}, bf16[11,96,128]{2,1,0:T(8,128)(2,1)S(1)}, u32[]{:S(2)}, u32[]{:S(2)}) %collective-permute-start.5) | collective-permute-done | bytes 270368 | tf_op jit(solution)/shard_map/ppermute | solution.py:21
  68.9 1.4 constant_dynamic-update-slice_fusion.19
  75.4 1.9 %fusion.28 = f32[8,96,128]{2,0,1:T(8,128)} fusion(bf16[12,96,128]{2,1,0:T(8,128)(2,1)} %constant_dynamic-update-slice_fusion.15, pred[8,12]{1,0:T(8,128)(4,1)S(1)} %concatenate.117), kind=kOutput, calls=%fused_computation.49 | convolution fusion | flops 2359296 | bytes 688224 | tf_op jit(solution)/shard_map/ks,spr->kpr/dot_general | solution.py:149
  77.3 1.6 slice.549
  78.9 1.9 %reshape.379 = bf16[3,4,96,96]{3,2,1,0:T(8,128)(2,1)} reshape(bf16[110592]{0:T(1024)(128)(2,1)} %slice.549) | data formatting | bytes 442368 | tf_op jit(solution)/shard_map/reshape | solution.py:47
  81.8 2.5 %fusion.44 = (f32[8,96,96]{2,1,0:T(8,128)}, f32[8,96,96]{2,1,0:T(8,128)}, f32[8,96,96]{2,1,0:T(8,128)}, f32[8,96,96]{2,1,0:T(8,128)}, f32[8,96,96]{2,1,0:T(8,128...) fusion(bf16[8,4,96,96]{3,2,1,0:T(8,128)(2,1)S(1)} %bitcast.283, bf16[3,4,96,96]{3,2,1,0:T(8,128)(2,1)} %reshape.379), kind=kLoop, calls=%fused_computation.76 | loop fusion | flops 737280 | bytes 3858432 | tf_op jit(solution)/shard_map/convert.26
  85.2 1.9 %copy.30 = f32[8,96,96]{1,2,0:T(8,128)} copy(f32[8,96,96]{2,1,0:T(8,128)} %get-tuple-element.19) | data formatting | bytes 589824 | tf_op jit(solution)/shard_map/convert.26
  87.1 1.9 %copy.31 = f32[8,96,96]{1,2,0:T(8,128)} copy(f32[8,96,96]{2,1,0:T(8,128)} %get-tuple-element.20) | data formatting | bytes 589824 | tf_op jit(solution)/shard_map/convert.27
  89.0 1.9 %copy.32 = f32[8,96,96]{1,2,0:T(8,128)} copy(f32[8,96,96]{2,1,0:T(8,128)} %get-tuple-element.21) | data formatting | bytes 589824 | tf_op jit(solution)/shard_map/convert.28
  90.9 1.5 constant_dynamic-update-slice_fusion.12
  92.5 1.4 constant_dynamic-update-slice_fusion.11
  93.9 1.4 constant_dynamic-update-slice_fusion.10
  96.7 1.4 constant_dynamic-update-slice_fusion.8
  98.1 1.4 constant_dynamic-update-slice_fusion.7
  100.2 4.8 %fusion = bf16[8,96,14,96]{3,1,2,0:T(8,128)(2,1)S(1)} fusion(f32[8,14]{1,0:T(8,128)S(1)} %fusion.78, f32[8,96,96]{1,2,0:T(8,128)} %copy.32, f32[8,14]{1,0:T(8,128)S(1)} %get-tuple-element.127, f32[8,96,96]{1,2,0:T(8,128)} %copy.31, f32[8,14]{1,0:T(8,128)S(1)} %get-tuple-element.126, f32[8,96,96]{1,2,0:T(8,128)} %copy.30, f32[8,96,96]{2,1,0:T(8,128)} %get-tuple-element.25, ...), kind=kLoop, calls=%fused_computation.1 | loop fusion | flops 14450688 | bytes 4131904 | tf_op jit(solution)/shard_map/convert.36
  105.0 2.1 %fusion.95 = (bf16[8,96,128]{2,1,0:T(8,128)(2,1)S(1)}, f32[8,96,128]{2,1,0:T(8,128)S(1)}, f32[8,96,128]{2,1,0:T(8,128)S(1)}) fusion(f32[8,96,128]{2,0,1:T(8,128)S(1)} %copy-done.6, f32[1,8,96,128]{3,2,1,0:T(8,128)S(1)} %copy-done.5, bf16[26,96,128]{2,1,0:T(8,128)(2,1)S(1)} %copy-done.10, bf16[8,96,12,96]{3,1,2,0:T(8,128)(2,1)S(1)} %fusion.1, ...), kind=kOutput, calls=%fused_computation.270 | convolution fusion | flops 493240320 | bytes 6242304 | tf_op jit(solution)/shard_map/kamb,mbr->kar/dot_general | solution.py:145
  107.7 1.9 %collective-permute-start.9 = (bf16[3,96,128]{2,1,0:T(8,128)(2,1)S(1)}, bf16[3,96,128]{2,1,0:T(8,128)(2,1)S(1)}, u32[]{:S(2)}, u32[]{:S(2)}) collective-permute-start(bf16[3,96,128]{2,1,0:T(8,128)(2,1)S(1)} %get-tuple-element.58), channel_id=1, source_target_pairs={{1,0},{2,1},{3,2},{4,3},{5,4},{6,5},{7,6},{8,7},{9,8},{10,9},{11,1... | collective-permute-start | bytes 221192 | tf_op jit(solution)/shard_map/ppermute | solution.py:16
  109.6 9.4 %collective-permute-start.8 = (bf16[3,96,128]{2,1,0:T(8,128)(2,1)S(1)}, bf16[3,96,128]{2,1,0:T(8,128)(2,1)S(1)}, u32[]{:S(2)}, u32[]{:S(2)}) collective-permute-start(bf16[3,96,128]{2,1,0:T(8,128)(2,1)S(1)} %get-tuple-element.59), channel_id=1, source_target_pairs={{0,1},{1,2},{2,3},{3,4},{4,5},{5,6},{6,7},{7,8},{8,9},{9,10},{10,1... | collective-permute-start | bytes 221192 | tf_op jit(solution)/shard_map/ppermute | solution.py:16
  119.3 4.0 %collective-permute-start.10 = (bf16[4,96,128]{2,1,0:T(8,128)(2,1)S(1)}, bf16[4,96,128]{2,1,0:T(8,128)(2,1)S(1)}, u32[]{:S(2)}, u32[]{:S(2)}) collective-permute-start(bf16[4,96,128]{2,1,0:T(8,128)(2,1)S(1)} %pad_maximum_fusion.34), channel_id=1, source_target_pairs={{0,16},{16,32},{32,48},{48,64},{64,80},{80,96},{96,112},{112,128},... | collective-permute-start | bytes 294920 | tf_op jit(solution)/shard_map/ppermute | solution.py:21
  123.4 4.2 %collective-permute-start.11 = (bf16[4,96,128]{2,1,0:T(8,128)(2,1)S(1)}, bf16[4,96,128]{2,1,0:T(8,128)(2,1)S(1)}, u32[]{:S(2)}, u32[]{:S(2)}) collective-permute-start(bf16[4,96,128]{2,1,0:T(8,128)(2,1)S(1)} %pad_maximum_fusion.35), channel_id=1, source_target_pairs={{0,32},{16,48},{32,64},{48,80},{64,96},{80,112},{96,128},{112,144}... | collective-permute-start | bytes 294920 | tf_op jit(solution)/shard_map/ppermute | solution.py:21
  127.6 3.7 %collective-permute-start.12 = (bf16[4,96,128]{2,1,0:T(8,128)(2,1)S(1)}, bf16[4,96,128]{2,1,0:T(8,128)(2,1)S(1)}, u32[]{:S(2)}, u32[]{:S(2)}) collective-permute-start(bf16[4,96,128]{2,1,0:T(8,128)(2,1)S(1)} %pad_maximum_fusion.36), channel_id=1, source_target_pairs={{0,48},{16,64},{32,80},{48,96},{64,112},{80,128},{96,144},{112,160... | collective-permute-start | bytes 294920 | tf_op jit(solution)/shard_map/ppermute | solution.py:21
  131.3 1.9 %collective-permute-start.13 = (bf16[4,96,128]{2,1,0:T(8,128)(2,1)S(1)}, bf16[4,96,128]{2,1,0:T(8,128)(2,1)S(1)}, u32[]{:S(2)}, u32[]{:S(2)}) collective-permute-start(bf16[4,96,128]{2,1,0:T(8,128)(2,1)S(1)} %pad_maximum_fusion.37), channel_id=1, source_target_pairs={{0,464},{16,480},{32,496},{48,0},{64,16},{80,32},{96,48},{112,64},... | collective-permute-start | bytes 294920 | tf_op jit(solution)/shard_map/ppermute | solution.py:21
  133.3 1.9 %collective-permute-start.14 = (bf16[4,96,128]{2,1,0:T(8,128)(2,1)S(1)}, bf16[4,96,128]{2,1,0:T(8,128)(2,1)S(1)}, u32[]{:S(2)}, u32[]{:S(2)}) collective-permute-start(bf16[4,96,128]{2,1,0:T(8,128)(2,1)S(1)} %pad_maximum_fusion.38), channel_id=1, source_target_pairs={{0,480},{16,496},{32,0},{48,16},{64,32},{80,48},{96,64},{112,80},{... | collective-permute-start | bytes 294920 | tf_op jit(solution)/shard_map/ppermute | solution.py:21
  135.3 2.5 %collective-permute-start.15 = (bf16[4,96,128]{2,1,0:T(8,128)(2,1)S(1)}, bf16[4,96,128]{2,1,0:T(8,128)(2,1)S(1)}, u32[]{:S(2)}, u32[]{:S(2)}) collective-permute-start(bf16[4,96,128]{2,1,0:T(8,128)(2,1)S(1)} %pad_maximum_fusion.39), channel_id=1, source_target_pairs={{0,496},{16,0},{32,16},{48,32},{64,48},{80,64},{96,80},{112,96},{1... | collective-permute-start | bytes 294920 | tf_op jit(solution)/shard_map/ppermute | solution.py:21
  137.9 4.3 %collective-permute-done.13 = bf16[4,96,128]{2,1,0:T(8,128)(2,1)S(1)} collective-permute-done((bf16[4,96,128]{2,1,0:T(8,128)(2,1)S(1)}, bf16[4,96,128]{2,1,0:T(8,128)(2,1)S(1)}, u32[]{:S(2)}, u32[]{:S(2)}) %collective-permute-start.13) | collective-permute-done | bytes 98336 | tf_op jit(solution)/shard_map/ppermute | solution.py:21
  142.2 1.6 collective-permute-done.14
  143.7 1.7 collective-permute-done.15
  145.6 2.3 %fusion.31 = (bf16[8,96,128]{2,1,0:T(8,128)(2,1)S(1)}, f32[8,96,128]{2,1,0:T(8,128)S(1)}) fusion(f32[8,96,128]{2,1,0:T(8,128)S(1)} %get-tuple-element.18, f32[8,96,128]{2,0,1:T(8,128)S(1)} %fusion.25, bf16[26,96,128]{2,1,0:T(8,128)(2,1)S(1)} %get-tuple-element.81, bf16[8,96,12,96]{3,1,2,0:T(8,128)(2,1)S(1)} %fusion.1, bf16[8,96,14,96]{3,1,2,0:T(8,128)(2,1)S(1)} %fusion, ...), kind=kOutput, calls=%fused_computation.53 | convolution fusion | flops 493436928 | bytes 7028736 | tf_op jit(solution)/shard_map/kamb,mbr->kar/dot_general | solution.py:145
  148.5 1.9 %collective-permute-start.17 = (bf16[3,96,128]{2,1,0:T(8,128)(2,1)S(1)}, bf16[3,96,128]{2,1,0:T(8,128)(2,1)S(1)}, u32[]{:S(2)}, u32[]{:S(2)}) collective-permute-start(bf16[3,96,128]{2,1,0:T(8,128)(2,1)S(1)} %get-tuple-element.56), channel_id=1, source_target_pairs={{1,0},{2,1},{3,2},{4,3},{5,4},{6,5},{7,6},{8,7},{9,8},{10,9},{11,1... | collective-permute-start | bytes 221192 | tf_op jit(solution)/shard_map/ppermute | solution.py:16
  150.4 9.4 %collective-permute-start.16 = (bf16[3,96,128]{2,1,0:T(8,128)(2,1)S(1)}, bf16[3,96,128]{2,1,0:T(8,128)(2,1)S(1)}, u32[]{:S(2)}, u32[]{:S(2)}) collective-permute-start(bf16[3,96,128]{2,1,0:T(8,128)(2,1)S(1)} %get-tuple-element.57), channel_id=1, source_target_pairs={{0,1},{1,2},{2,3},{3,4},{4,5},{5,6},{6,7},{7,8},{8,9},{9,10},{10,1... | collective-permute-start | bytes 221192 | tf_op jit(solution)/shard_map/ppermute | solution.py:16
  160.1 2.4 %collective-permute-start.18 = (bf16[4,96,128]{2,1,0:T(8,128)(2,1)S(1)}, bf16[4,96,128]{2,1,0:T(8,128)(2,1)S(1)}, u32[]{:S(2)}, u32[]{:S(2)}) collective-permute-start(bf16[4,96,128]{2,1,0:T(8,128)(2,1)S(1)} %pad_maximum_fusion.40), channel_id=1, source_target_pairs={{0,16},{16,32},{32,48},{48,64},{64,80},{80,96},{96,112},{112,128},... | collective-permute-start | bytes 294920 | tf_op jit(solution)/shard_map/ppermute | solution.py:21
  162.5 3.4 %collective-permute-start.19 = (bf16[4,96,128]{2,1,0:T(8,128)(2,1)S(1)}, bf16[4,96,128]{2,1,0:T(8,128)(2,1)S(1)}, u32[]{:S(2)}, u32[]{:S(2)}) collective-permute-start(bf16[4,96,128]{2,1,0:T(8,128)(2,1)S(1)} %pad_maximum_fusion.41), channel_id=1, source_target_pairs={{0,32},{16,48},{32,64},{48,80},{64,96},{80,112},{96,128},{112,144}... | collective-permute-start | bytes 294920 | tf_op jit(solution)/shard_map/ppermute | solution.py:21
  165.9 3.4 %collective-permute-start.20 = (bf16[4,96,128]{2,1,0:T(8,128)(2,1)S(1)}, bf16[4,96,128]{2,1,0:T(8,128)(2,1)S(1)}, u32[]{:S(2)}, u32[]{:S(2)}) collective-permute-start(bf16[4,96,128]{2,1,0:T(8,128)(2,1)S(1)} %pad_maximum_fusion.42), channel_id=1, source_target_pairs={{0,48},{16,64},{32,80},{48,96},{64,112},{80,128},{96,144},{112,160... | collective-permute-start | bytes 294920 | tf_op jit(solution)/shard_map/ppermute | solution.py:21
  169.4 2.2 %collective-permute-start.21 = (bf16[4,96,128]{2,1,0:T(8,128)(2,1)S(1)}, bf16[4,96,128]{2,1,0:T(8,128)(2,1)S(1)}, u32[]{:S(2)}, u32[]{:S(2)}) collective-permute-start(bf16[4,96,128]{2,1,0:T(8,128)(2,1)S(1)} %pad_maximum_fusion.43), channel_id=1, source_target_pairs={{0,464},{16,480},{32,496},{48,0},{64,16},{80,32},{96,48},{112,64},... | collective-permute-start | bytes 294920 | tf_op jit(solution)/shard_map/ppermute | solution.py:21
  171.6 2.4 %collective-permute-start.22 = (bf16[4,96,128]{2,1,0:T(8,128)(2,1)S(1)}, bf16[4,96,128]{2,1,0:T(8,128)(2,1)S(1)}, u32[]{:S(2)}, u32[]{:S(2)}) collective-permute-start(bf16[4,96,128]{2,1,0:T(8,128)(2,1)S(1)} %pad_maximum_fusion.44), channel_id=1, source_target_pairs={{0,480},{16,496},{32,0},{48,16},{64,32},{80,48},{96,64},{112,80},{... | collective-permute-start | bytes 294920 | tf_op jit(solution)/shard_map/ppermute | solution.py:21
  174.1 3.5 %collective-permute-start.23 = (bf16[4,96,128]{2,1,0:T(8,128)(2,1)S(1)}, bf16[4,96,128]{2,1,0:T(8,128)(2,1)S(1)}, u32[]{:S(2)}, u32[]{:S(2)}) collective-permute-start(bf16[4,96,128]{2,1,0:T(8,128)(2,1)S(1)} %pad_maximum_fusion.45), channel_id=1, source_target_pairs={{0,496},{16,0},{32,16},{48,32},{64,48},{80,64},{96,80},{112,96},{1... | collective-permute-start | bytes 294920 | tf_op jit(solution)/shard_map/ppermute | solution.py:21
  177.7 2.3 %collective-permute-done.21 = bf16[4,96,128]{2,1,0:T(8,128)(2,1)S(1)} collective-permute-done((bf16[4,96,128]{2,1,0:T(8,128)(2,1)S(1)}, bf16[4,96,128]{2,1,0:T(8,128)(2,1)S(1)}, u32[]{:S(2)}, u32[]{:S(2)}) %collective-permute-start.21) | collective-permute-done | bytes 98336 | tf_op jit(solution)/shard_map/ppermute | solution.py:21
  181.0 4.1 %collective-permute-done.23 = bf16[4,96,128]{2,1,0:T(8,128)(2,1)S(1)} collective-permute-done((bf16[4,96,128]{2,1,0:T(8,128)(2,1)S(1)}, bf16[4,96,128]{2,1,0:T(8,128)(2,1)S(1)}, u32[]{:S(2)}, u32[]{:S(2)}) %collective-permute-start.23) | collective-permute-done | bytes 98336 | tf_op jit(solution)/shard_map/ppermute | solution.py:21
  185.4 3.1 %fusion.15 = f32[1,8,96,128]{3,2,1,0:T(8,128)} fusion(f32[8,96,128]{2,1,0:T(8,128)S(1)} %get-tuple-element.121, bf16[8,96,12,96]{3,1,2,0:T(8,128)(2,1)S(1)} %fusion.1, bf16[8,96,14,96]{3,1,2,0:T(8,128)(2,1)S(1)} %fusion, bf16[26,96,128]{2,1,0:T(8,128)(2,1)S(1)} %get-tuple-element.69, f32[8,96,128]{2,0,1:T(8,128)S(1)} %fusion.23, ...), kind=kOutput, calls=%fused_computation.24 | convolution fusion | flops 493830144 | bytes 6438912 | tf_op jit(solution)/shard_map/kamb,mbr->kar/dot_general | solution.py:145
  (167 shorter events, 32.5 us)
Async XLA Ops:
  0.0 18.4 %copy-start = (bf16[1,1,6,2,96,96]{5,4,3,2,1,0:T(8,128)(2,1)S(1)}, bf16[1,1,6,2,96,96]{5,4,3,2,1,0:T(8,128)(2,1)}, u32[]{:S(2)}) copy-start(bf16[1,1,6,2,96,96]{5,4,3,2,1,0:T(8,128)(2,1)} %param.11) | copy-start | bytes 663556
  1.7 89.2 %collective-permute-start.1 = (bf16[3,96,128]{2,1,0:T(8,128)(2,1)}, bf16[3,96,128]{2,1,0:T(8,128)(2,1)}, u32[]{:S(2)}, u32[]{:S(2)}) collective-permute-start(bf16[3,96,128]{2,1,0:T(8,128)(2,1)} %get-tuple-element.66), channel_id=1, source_target_pairs={{1,0},{2,1},{3,2},{4,3},{5,4},{6,5},{7,6},{8,7},{9,8},{10,9},{11,1... | collective-permute-start | bytes 221192 | tf_op jit(solution)/shard_map/ppermute | solution.py:16
  6.2 24.4 %copy-start.11 = (s32[1,1,6]{2,1,0:T(1,128)S(1)}, s32[1,1,6]{2,1,0:T(1,128)}, u32[]{:S(2)}) copy-start(s32[1,1,6]{2,1,0:T(1,128)} %param.10) | copy-start | bytes 76
  6.2 71.0 %collective-permute-start = (bf16[147456]{0:T(1024)(128)(2,1)}, bf16[147456]{0:T(1024)(128)(2,1)}, u32[]{:S(2)}, u32[]{:S(2)}) collective-permute-start(bf16[147456]{0:T(1024)(128)(2,1)} %pad_maximum_fusion.26), channel_id=1, source_target_pairs={{0,1},{1,2},{2,3},{3,4},{4,5},{5,6},{6,7},{7,8},{8,9},{9,10},{10,1... | collective-permute-start | bytes 884744 | tf_op jit(solution)/shard_map/ppermute | solution.py:16
  19.8 29.0 %collective-permute-start.7 = (bf16[11,96,128]{2,1,0:T(8,128)(2,1)S(1)}, bf16[11,96,128]{2,1,0:T(8,128)(2,1)S(1)}, u32[]{:S(2)}, u32[]{:S(2)}) collective-permute-start(bf16[11,96,128]{2,1,0:T(8,128)(2,1)S(1)} %get-tuple-element.60), channel_id=1, source_target_pairs={{0,496},{16,0},{32,16},{48,32},{64,48},{80,64},{96,80},{112,96},{1... | collective-permute-start | bytes 811016 | tf_op jit(solution)/shard_map/ppermute | solution.py:21
  22.9 28.0 %collective-permute-start.3 = (bf16[11,96,128]{2,1,0:T(8,128)(2,1)S(1)}, bf16[11,96,128]{2,1,0:T(8,128)(2,1)}, u32[]{:S(2)}, u32[]{:S(2)}) collective-permute-start(bf16[11,96,128]{2,1,0:T(8,128)(2,1)S(1)} %get-tuple-element.61), channel_id=1, source_target_pairs={{0,32},{16,48},{32,64},{48,80},{64,96},{80,112},{96,128},{112,144}... | collective-permute-start | bytes 811016 | tf_op jit(solution)/shard_map/ppermute | solution.py:21
  26.4 28.3 %collective-permute-start.4 = (bf16[11,96,128]{2,1,0:T(8,128)(2,1)}, bf16[11,96,128]{2,1,0:T(8,128)(2,1)}, u32[]{:S(2)}, u32[]{:S(2)}) collective-permute-start(bf16[11,96,128]{2,1,0:T(8,128)(2,1)} %get-tuple-element.62), channel_id=1, source_target_pairs={{0,48},{16,64},{32,80},{48,96},{64,112},{80,128},{96,144},{112,160... | collective-permute-start | bytes 811016 | tf_op jit(solution)/shard_map/ppermute | solution.py:21
  31.2 23.5 %copy-start.7 = (bf16[11,96,128]{2,1,0:T(8,128)(2,1)S(1)}, bf16[11,96,128]{2,1,0:T(8,128)(2,1)}, u32[]{:S(2)}) copy-start(bf16[11,96,128]{2,1,0:T(8,128)(2,1)} %get-tuple-element.65) | copy-start | bytes 811012
  48.8 4.1 %copy-start.8 = (bf16[11,96,128]{2,1,0:T(8,128)(2,1)}, bf16[11,96,128]{2,1,0:T(8,128)(2,1)S(1)}, u32[]{:S(2)}) copy-start(bf16[11,96,128]{2,1,0:T(8,128)(2,1)S(1)} %collective-permute-done.7) | copy-start | bytes 811012
  48.8 13.9 %collective-permute-start.5 = (bf16[11,96,128]{2,1,0:T(8,128)(2,1)}, bf16[11,96,128]{2,1,0:T(8,128)(2,1)S(1)}, u32[]{:S(2)}, u32[]{:S(2)}) collective-permute-start(bf16[11,96,128]{2,1,0:T(8,128)(2,1)} %get-tuple-element.63), channel_id=1, source_target_pairs={{0,464},{16,480},{32,496},{48,0},{64,16},{80,32},{96,48},{112,64},... | collective-permute-start | bytes 811016 | tf_op jit(solution)/shard_map/ppermute | solution.py:21
  51.0 13.0 %collective-permute-start.6 = (bf16[11,96,128]{2,1,0:T(8,128)(2,1)}, bf16[11,96,128]{2,1,0:T(8,128)(2,1)S(1)}, u32[]{:S(2)}, u32[]{:S(2)}) collective-permute-start(bf16[11,96,128]{2,1,0:T(8,128)(2,1)} %get-tuple-element.64), channel_id=1, source_target_pairs={{0,480},{16,496},{32,0},{48,16},{64,32},{80,48},{96,64},{112,80},{... | collective-permute-start | bytes 811016 | tf_op jit(solution)/shard_map/ppermute | solution.py:21
  53.8 27.9 %copy-start.1 = (bf16[1,8,4,96,96]{4,3,2,1,0:T(8,128)(2,1)S(1)}, bf16[1,8,4,96,96]{4,3,2,1,0:T(8,128)(2,1)}, u32[]{:S(2)}) copy-start(bf16[1,8,4,96,96]{4,3,2,1,0:T(8,128)(2,1)} %param.8) | copy-start | bytes 1769476
  54.7 10.2 %collective-permute-start.2 = (bf16[11,96,128]{2,1,0:T(8,128)(2,1)S(1)}, bf16[11,96,128]{2,1,0:T(8,128)(2,1)S(1)}, u32[]{:S(2)}, u32[]{:S(2)}) collective-permute-start(bf16[11,96,128]{2,1,0:T(8,128)(2,1)S(1)} %copy-done.7), channel_id=1, source_target_pairs={{0,16},{16,32},{32,48},{48,64},{64,80},{80,96},{96,112},{112,128},... | collective-permute-start | bytes 811016 | tf_op jit(solution)/shard_map/ppermute | solution.py:21
  80.8 3.4 %copy-start.4 = (f32[1,8,96,128]{3,2,1,0:T(8,128)S(1)}, f32[1,8,96,128]{3,2,1,0:T(8,128)}, u32[]{:S(2)}) copy-start(f32[1,8,96,128]{3,2,1,0:T(8,128)} %param.7) | copy-start | bytes 1179652
  84.2 15.9 %copy-start.2 = (f32[8,96,96]{2,1,0:T(8,128)S(1)}, f32[8,96,96]{2,1,0:T(8,128)}, u32[]{:S(2)}) copy-start(f32[8,96,96]{2,1,0:T(8,128)} %get-tuple-element.22) | copy-start | bytes 884740
  84.2 15.9 %copy-start.3 = (f32[8,96,96]{2,1,0:T(8,128)S(1)}, f32[8,96,96]{2,1,0:T(8,128)}, u32[]{:S(2)}) copy-start(f32[8,96,96]{2,1,0:T(8,128)} %get-tuple-element.23) | copy-start | bytes 884740
  84.3 0.9 copy-start.9
  100.2 4.8 %copy-start.5 = (f32[1,8,96,128]{3,2,1,0:T(8,128)S(1)}, f32[1,8,96,128]{3,2,1,0:T(8,128)}, u32[]{:S(2)}) copy-start(f32[1,8,96,128]{3,2,1,0:T(8,128)} %param.7) | copy-start | bytes 1179652
  100.2 4.8 %copy-start.6 = (f32[8,96,128]{2,0,1:T(8,128)S(1)}, f32[8,96,128]{2,0,1:T(8,128)}, u32[]{:S(2)}) copy-start(f32[8,96,128]{2,0,1:T(8,128)} %fusion.28) | copy-start | bytes 1179652
  100.2 4.8 %copy-start.10 = (bf16[26,96,128]{2,1,0:T(8,128)(2,1)S(1)}, bf16[26,96,128]{2,1,0:T(8,128)(2,1)}, u32[]{:S(2)}) copy-start(bf16[26,96,128]{2,1,0:T(8,128)(2,1)} %constant_dynamic-update-slice_fusion.6) | copy-start | bytes 1916932
  107.7 25.6 %collective-permute-start.9 = (bf16[3,96,128]{2,1,0:T(8,128)(2,1)S(1)}, bf16[3,96,128]{2,1,0:T(8,128)(2,1)S(1)}, u32[]{:S(2)}, u32[]{:S(2)}) collective-permute-start(bf16[3,96,128]{2,1,0:T(8,128)(2,1)S(1)} %get-tuple-element.58), channel_id=1, source_target_pairs={{1,0},{2,1},{3,2},{4,3},{5,4},{6,5},{7,6},{8,7},{9,8},{10,9},{11,1... | collective-permute-start | bytes 221192 | tf_op jit(solution)/shard_map/ppermute | solution.py:16
  109.6 21.7 %collective-permute-start.8 = (bf16[3,96,128]{2,1,0:T(8,128)(2,1)S(1)}, bf16[3,96,128]{2,1,0:T(8,128)(2,1)S(1)}, u32[]{:S(2)}, u32[]{:S(2)}) collective-permute-start(bf16[3,96,128]{2,1,0:T(8,128)(2,1)S(1)} %get-tuple-element.59), channel_id=1, source_target_pairs={{0,1},{1,2},{2,3},{3,4},{4,5},{5,6},{6,7},{7,8},{8,9},{9,10},{10,1... | collective-permute-start | bytes 221192 | tf_op jit(solution)/shard_map/ppermute | solution.py:16
  119.3 15.9 %collective-permute-start.10 = (bf16[4,96,128]{2,1,0:T(8,128)(2,1)S(1)}, bf16[4,96,128]{2,1,0:T(8,128)(2,1)S(1)}, u32[]{:S(2)}, u32[]{:S(2)}) collective-permute-start(bf16[4,96,128]{2,1,0:T(8,128)(2,1)S(1)} %pad_maximum_fusion.34), channel_id=1, source_target_pairs={{0,16},{16,32},{32,48},{48,64},{64,80},{80,96},{96,112},{112,128},... | collective-permute-start | bytes 294920 | tf_op jit(solution)/shard_map/ppermute | solution.py:21
  123.4 14.4 %collective-permute-start.11 = (bf16[4,96,128]{2,1,0:T(8,128)(2,1)S(1)}, bf16[4,96,128]{2,1,0:T(8,128)(2,1)S(1)}, u32[]{:S(2)}, u32[]{:S(2)}) collective-permute-start(bf16[4,96,128]{2,1,0:T(8,128)(2,1)S(1)} %pad_maximum_fusion.35), channel_id=1, source_target_pairs={{0,32},{16,48},{32,64},{48,80},{64,96},{80,112},{96,128},{112,144}... | collective-permute-start | bytes 294920 | tf_op jit(solution)/shard_map/ppermute | solution.py:21
  127.6 10.2 %collective-permute-start.12 = (bf16[4,96,128]{2,1,0:T(8,128)(2,1)S(1)}, bf16[4,96,128]{2,1,0:T(8,128)(2,1)S(1)}, u32[]{:S(2)}, u32[]{:S(2)}) collective-permute-start(bf16[4,96,128]{2,1,0:T(8,128)(2,1)S(1)} %pad_maximum_fusion.36), channel_id=1, source_target_pairs={{0,48},{16,64},{32,80},{48,96},{64,112},{80,128},{96,144},{112,160... | collective-permute-start | bytes 294920 | tf_op jit(solution)/shard_map/ppermute | solution.py:21
  131.3 10.8 %collective-permute-start.13 = (bf16[4,96,128]{2,1,0:T(8,128)(2,1)S(1)}, bf16[4,96,128]{2,1,0:T(8,128)(2,1)S(1)}, u32[]{:S(2)}, u32[]{:S(2)}) collective-permute-start(bf16[4,96,128]{2,1,0:T(8,128)(2,1)S(1)} %pad_maximum_fusion.37), channel_id=1, source_target_pairs={{0,464},{16,480},{32,496},{48,0},{64,16},{80,32},{96,48},{112,64},... | collective-permute-start | bytes 294920 | tf_op jit(solution)/shard_map/ppermute | solution.py:21
  133.3 10.4 %collective-permute-start.14 = (bf16[4,96,128]{2,1,0:T(8,128)(2,1)S(1)}, bf16[4,96,128]{2,1,0:T(8,128)(2,1)S(1)}, u32[]{:S(2)}, u32[]{:S(2)}) collective-permute-start(bf16[4,96,128]{2,1,0:T(8,128)(2,1)S(1)} %pad_maximum_fusion.38), channel_id=1, source_target_pairs={{0,480},{16,496},{32,0},{48,16},{64,32},{80,48},{96,64},{112,80},{... | collective-permute-start | bytes 294920 | tf_op jit(solution)/shard_map/ppermute | solution.py:21
  135.3 10.1 %collective-permute-start.15 = (bf16[4,96,128]{2,1,0:T(8,128)(2,1)S(1)}, bf16[4,96,128]{2,1,0:T(8,128)(2,1)S(1)}, u32[]{:S(2)}, u32[]{:S(2)}) collective-permute-start(bf16[4,96,128]{2,1,0:T(8,128)(2,1)S(1)} %pad_maximum_fusion.39), channel_id=1, source_target_pairs={{0,496},{16,0},{32,16},{48,32},{64,48},{80,64},{96,80},{112,96},{1... | collective-permute-start | bytes 294920 | tf_op jit(solution)/shard_map/ppermute | solution.py:21
  148.5 23.2 %collective-permute-start.17 = (bf16[3,96,128]{2,1,0:T(8,128)(2,1)S(1)}, bf16[3,96,128]{2,1,0:T(8,128)(2,1)S(1)}, u32[]{:S(2)}, u32[]{:S(2)}) collective-permute-start(bf16[3,96,128]{2,1,0:T(8,128)(2,1)S(1)} %get-tuple-element.56), channel_id=1, source_target_pairs={{1,0},{2,1},{3,2},{4,3},{5,4},{6,5},{7,6},{8,7},{9,8},{10,9},{11,1... | collective-permute-start | bytes 221192 | tf_op jit(solution)/shard_map/ppermute | solution.py:16
  150.4 19.0 %collective-permute-start.16 = (bf16[3,96,128]{2,1,0:T(8,128)(2,1)S(1)}, bf16[3,96,128]{2,1,0:T(8,128)(2,1)S(1)}, u32[]{:S(2)}, u32[]{:S(2)}) collective-permute-start(bf16[3,96,128]{2,1,0:T(8,128)(2,1)S(1)} %get-tuple-element.57), channel_id=1, source_target_pairs={{0,1},{1,2},{2,3},{3,4},{4,5},{5,6},{6,7},{7,8},{8,9},{9,10},{10,1... | collective-permute-start | bytes 221192 | tf_op jit(solution)/shard_map/ppermute | solution.py:16
  160.1 13.9 %collective-permute-start.18 = (bf16[4,96,128]{2,1,0:T(8,128)(2,1)S(1)}, bf16[4,96,128]{2,1,0:T(8,128)(2,1)S(1)}, u32[]{:S(2)}, u32[]{:S(2)}) collective-permute-start(bf16[4,96,128]{2,1,0:T(8,128)(2,1)S(1)} %pad_maximum_fusion.40), channel_id=1, source_target_pairs={{0,16},{16,32},{32,48},{48,64},{64,80},{80,96},{96,112},{112,128},... | collective-permute-start | bytes 294920 | tf_op jit(solution)/shard_map/ppermute | solution.py:21
  162.5 15.1 %collective-permute-start.19 = (bf16[4,96,128]{2,1,0:T(8,128)(2,1)S(1)}, bf16[4,96,128]{2,1,0:T(8,128)(2,1)S(1)}, u32[]{:S(2)}, u32[]{:S(2)}) collective-permute-start(bf16[4,96,128]{2,1,0:T(8,128)(2,1)S(1)} %pad_maximum_fusion.41), channel_id=1, source_target_pairs={{0,32},{16,48},{32,64},{48,80},{64,96},{80,112},{96,128},{112,144}... | collective-permute-start | bytes 294920 | tf_op jit(solution)/shard_map/ppermute | solution.py:21
  165.9 11.7 %collective-permute-start.20 = (bf16[4,96,128]{2,1,0:T(8,128)(2,1)S(1)}, bf16[4,96,128]{2,1,0:T(8,128)(2,1)S(1)}, u32[]{:S(2)}, u32[]{:S(2)}) collective-permute-start(bf16[4,96,128]{2,1,0:T(8,128)(2,1)S(1)} %pad_maximum_fusion.42), channel_id=1, source_target_pairs={{0,48},{16,64},{32,80},{48,96},{64,112},{80,128},{96,144},{112,160... | collective-permute-start | bytes 294920 | tf_op jit(solution)/shard_map/ppermute | solution.py:21
  169.4 10.6 %collective-permute-start.21 = (bf16[4,96,128]{2,1,0:T(8,128)(2,1)S(1)}, bf16[4,96,128]{2,1,0:T(8,128)(2,1)S(1)}, u32[]{:S(2)}, u32[]{:S(2)}) collective-permute-start(bf16[4,96,128]{2,1,0:T(8,128)(2,1)S(1)} %pad_maximum_fusion.43), channel_id=1, source_target_pairs={{0,464},{16,480},{32,496},{48,0},{64,16},{80,32},{96,48},{112,64},... | collective-permute-start | bytes 294920 | tf_op jit(solution)/shard_map/ppermute | solution.py:21
  171.6 9.4 %collective-permute-start.22 = (bf16[4,96,128]{2,1,0:T(8,128)(2,1)S(1)}, bf16[4,96,128]{2,1,0:T(8,128)(2,1)S(1)}, u32[]{:S(2)}, u32[]{:S(2)}) collective-permute-start(bf16[4,96,128]{2,1,0:T(8,128)(2,1)S(1)} %pad_maximum_fusion.44), channel_id=1, source_target_pairs={{0,480},{16,496},{32,0},{48,16},{64,32},{80,48},{96,64},{112,80},{... | collective-permute-start | bytes 294920 | tf_op jit(solution)/shard_map/ppermute | solution.py:21
  174.1 11.1 %collective-permute-start.23 = (bf16[4,96,128]{2,1,0:T(8,128)(2,1)S(1)}, bf16[4,96,128]{2,1,0:T(8,128)(2,1)S(1)}, u32[]{:S(2)}, u32[]{:S(2)}) collective-permute-start(bf16[4,96,128]{2,1,0:T(8,128)(2,1)S(1)} %pad_maximum_fusion.45), channel_id=1, source_target_pairs={{0,496},{16,0},{32,16},{48,32},{64,48},{80,64},{96,80},{112,96},{1... | collective-permute-start | bytes 294920 | tf_op jit(solution)/shard_map/ppermute | solution.py:21

commit v6 on v3

--- a/solution.py
+++ b/solution.py
@@ -2,6 +2,8 @@
 import jax.numpy as jnp
 from jax import lax
 from jax.sharding import PartitionSpec as P
+from jax.experimental import pallas as pl
+from jax.experimental.pallas import tpu as pltpu
 
 ITERS = 3
 
@@ -19,6 +21,42 @@
 def shifted_ring(value, axis, steps):
     count = lax.axis_size(axis)
     return lax.ppermute(value, axis, [(i, (i + steps) % count) for i in range(count)])
+
+
+def unpack_first(pick_ref, low_ref, probe_ref, high_ref, *refs):
+    messages = refs[:-3]
+    stacked_ref, landed_ref, index_ref = refs[-3:]
+    edge = low_ref.shape[0]
+    knots = probe_ref.shape[0]
+    slots = pick_ref.shape[1]
+    stacked_ref[:edge] = low_ref[...]
+    stacked_ref[edge : edge + knots] = probe_ref[...]
+    stacked_ref[edge + knots : 2 * edge + knots] = high_ref[...]
+    base = 2 * edge + knots
+    for t, message in enumerate(messages):
+        for slot in range(slots):
+            knot = pick_ref[t, slot]
+            row = message[jnp.minimum(jnp.maximum(knot, 0), knots - 1)]
+            stacked_ref[base + t * slots + slot] = jnp.where(knot >= 0, row, jnp.zeros_like(row))
+            landed_ref[t * slots + slot] = message[knots + slot]
+        index_ref[t] = message[knots + slots, 0, :]
+
+
+def unpack_call(pick, low, probe, high, messages):
+    knots, params, probes = probe.shape
+    slots = pick.shape[1]
+    count = len(messages)
+    vmem = pl.BlockSpec(memory_space=pltpu.VMEM)
+    return pl.pallas_call(
+        unpack_first,
+        out_shape=(
+            jax.ShapeDtypeStruct((knots + 2 * low.shape[0] + count * slots, params, probes), probe.dtype),
+            jax.ShapeDtypeStruct((count * slots, params, probes), probe.dtype),
+            jax.ShapeDtypeStruct((count, probes), probe.dtype),
+        ),
+        in_specs=[pl.BlockSpec(memory_space=pltpu.SMEM)] + [vmem] * (3 + count),
+        out_specs=(vmem, vmem, vmem),
+    )(pick, low, probe, high, *messages)
 
 
 def body(right_side, band_blocks, knot_pairs, pair_counts, cross_blocks):
@@ -68,6 +106,7 @@
     fetch_blocks = jnp.concatenate([couplings[b] for b in fetch_order], axis=0).astype(jnp.float32)
     fetch_weight = jnp.einsum("kf,fab->kafb", fetch_place, fetch_blocks)
     weight = jnp.concatenate([band_weight, fetch_weight], axis=2).astype(jnp.bfloat16)
+    first_pick = jnp.stack([far_knot[bucket_of[-s]] for s in shifts])
     answer_pick = None
     land_place = None
 
@@ -100,7 +139,7 @@
         ).astype(jnp.bfloat16)
         fetched = [None] * buckets
         landed = []
-        got_index = {}
+        received = []
         for t, s in enumerate(shifts):
             if answer_pick is None:
                 message = jnp.concatenate(
@@ -109,34 +148,26 @@
             else:
                 message = jnp.concatenate([answers[t], product[bucket_of[s]]], axis=0)
             got = shifted_ring(message, "line", s)
-            if answer_pick is None:
-                fetched[bucket_of[-s]] = jnp.einsum(
-                    "sk,kpr->spr",
-                    far_pick[bucket_of[-s]],
-                    got[:knots],
-                    preferred_element_type=jnp.float32,
-                ).astype(jnp.bfloat16)
-                landed.append(got[knots : knots + slots])
-                got_index[s] = got[knots + slots, 0, :slots].astype(jnp.float32)
-            else:
-                fetched[bucket_of[-s]] = got[:slots]
-                landed.append(got[slots:])
-        if answer_pick is None:
-            answer_pick = jnp.concatenate(
-                [(got_index[-s][:, None] == knot_vals[None, :]) for s in shifts], axis=0
-            ).astype(jnp.bfloat16)
-            land_place = jnp.concatenate(
-                [(got_index[s][None, :] == knot_vals[:, None]) for s in shifts], axis=1
-            ).astype(jnp.bfloat16)
+            received.append(got)
+            fetched[bucket_of[-s]] = got[:slots]
+            landed.append(got[slots:])
         low = shifted_open(probe_bf[knots - 3 :], "seg", 1)
         high = shifted_open(probe_bf[:3], "seg", -1)
-        stacked = jnp.concatenate(
-            [low, probe_bf, high] + [fetched[b] for b in fetch_order], axis=0
-        )
+        if answer_pick is None:
+            stacked, landed, heard = unpack_call(first_pick, low, probe_bf, high, received)
+            heard = heard[:, :slots].astype(jnp.float32)
+            answer_pick = jnp.concatenate(
+                [(heard[shifts.index(-s)][:, None] == knot_vals[None, :]) for s in shifts], axis=0
+            ).astype(jnp.bfloat16)
+            land_place = (heard.reshape(-1)[None, :] == knot_vals[:, None]).astype(jnp.bfloat16)
+        else:
+            stacked = jnp.concatenate(
+                [low, probe_bf, high] + [fetched[b] for b in fetch_order], axis=0
+            )
+            landed = jnp.concatenate(landed, axis=0)
         summed = jnp.einsum(
             "kamb,mbr->kar", weight, stacked, preferred_element_type=jnp.float32
         )
-        landed = jnp.concatenate(landed, axis=0)
         cross = jnp.einsum("ks,spr->kpr", land_place, landed, preferred_element_type=jnp.float32)
         residual = residual - (summed + cross)
         coeff_next = 1.0 / (2.0 * center / radius - coeff)

time: 182 us -> 165 us (0.907)
  the two profiles are of different devices: /device:TPU:287 before, /device:TPU:24 now
where the time goes in v6:
time: 165 us; the launch traced here: 164 us
  starting transfers between devices  117 us (71%)
  matrix products  13.9 us (8%)
  other arithmetic  12.8 us (8%)
  waiting for transfers between devices  9.39 us (6%)
  local copies, waits for them, and re-layouts  7.78 us (5%)
  Pallas kernels  2.47 us (1%)
    ppermute x18, starting transfers between devices, shifted_ring(): lax.ppermute(value, axis, [(i, (i + steps) % count) for i in range(count)])  77.3 us
    ppermute x7, starting transfers between devices, shifted_open(): lax.ppermute(value, axis, [(source, source + steps) for source in range(i...  39.2 us
    dot_general x3, matrix products, body(): jnp.einsum('kamb,mbr->kar', weight, stacked, preferred_element_type=jnp.f...  10.3 us
    ppermute x18, waiting for transfers between devices, shifted_ring(): lax.ppermute(value, axis, [(i, (i + steps) % count) for i in range(count)])  9.37 us
    another operation x7, other arithmetic  6.25 us
  transfers between devices with their start and end apart: 25, of which 6 were waited for; matrix products, arithmetic and copies ran while one was open for 11% of the time, Pallas kernels for 0%

profile of v6, /device:TPU:24, one launch (start us, length us, event | category | flops | bytes accessed | tf_op | source)
XLA Modules:
  0.0 163.8 jit_solution(5111023562813891089)
XLA Ops:
  0.0 1.1 fusion.31.probe_ref
  1.1 0.7 fusion.92
  1.8 2.6 %collective-permute-start.2 = (bf16[3,96,128]{2,1,0:T(8,128)(2,1)}, bf16[3,96,128]{2,1,0:T(8,128)(2,1)S(1)}, u32[]{:S(2)}, u32[]{:S(2)}) collective-permute-start(bf16[3,96,128]{2,1,0:T(8,128)(2,1)} %get-tuple-element.70), channel_id=1, source_target_pairs={{1,0},{2,1},{3,2},{4,3},{5,4},{6,5},{7,6},{8,7},{9,8},{10,9},{11,1... | collective-permute-start | bytes 221192 | tf_op jit(solution)/shard_map/ppermute | solution.py:18
  4.5 9.2 %collective-permute-start.1 = (bf16[3,96,128]{2,1,0:T(8,128)(2,1)}, bf16[3,96,128]{2,1,0:T(8,128)(2,1)}, u32[]{:S(2)}, u32[]{:S(2)}) collective-permute-start(bf16[3,96,128]{2,1,0:T(8,128)(2,1)} %get-tuple-element.71), channel_id=1, source_target_pairs={{0,1},{1,2},{2,3},{3,4},{4,5},{5,6},{6,7},{7,8},{8,9},{9,10},{10,1... | collective-permute-start | bytes 221192 | tf_op jit(solution)/shard_map/ppermute | solution.py:18
  13.7 1.0 slice_bitcast_fusion
  14.7 2.7 %collective-permute-start = (bf16[3,4,96,96]{3,2,1,0:T(8,128)(2,1)S(1)}, bf16[3,4,96,96]{3,2,1,0:T(8,128)(2,1)S(1)}, u32[]{:S(2)}, u32[]{:S(2)}) collective-permute-start(bf16[3,4,96,96]{3,2,1,0:T(8,128)(2,1)S(1)} %slice_bitcast_fusion), channel_id=1, source_target_pairs={{0,1},{1,2},{2,3},{3,4},{4,5},{5,6},{6,7},{7,8},{8,9},{9,10},{10,1... | collective-permute-start | bytes 663560 | tf_op jit(solution)/shard_map/ppermute | solution.py:18
  17.4 0.7 iota_compare_fusion.8
  18.3 0.8 fusion.93
  19.1 0.7 fusion.78
  20.8 1.2 fusion.41
  22.0 7.4 %collective-permute-start.8 = (bf16[11,96,128]{2,1,0:T(8,128)(2,1)S(1)}, bf16[11,96,128]{2,1,0:T(8,128)(2,1)}, u32[]{:S(2)}, u32[]{:S(2)}) collective-permute-start(bf16[11,96,128]{2,1,0:T(8,128)(2,1)S(1)} %get-tuple-element.64), channel_id=1, source_target_pairs={{0,496},{16,0},{32,16},{48,32},{64,48},{80,64},{96,80},{112,96},{1... | collective-permute-start | bytes 811016 | tf_op jit(solution)/shard_map/ppermute | solution.py:23
  29.5 1.9 %collective-permute-start.4 = (bf16[11,96,128]{2,1,0:T(8,128)(2,1)}, bf16[11,96,128]{2,1,0:T(8,128)(2,1)}, u32[]{:S(2)}, u32[]{:S(2)}) collective-permute-start(bf16[11,96,128]{2,1,0:T(8,128)(2,1)} %get-tuple-element.65), channel_id=1, source_target_pairs={{0,32},{16,48},{32,64},{48,80},{64,96},{80,112},{96,128},{112,144}... | collective-permute-start | bytes 811016 | tf_op jit(solution)/shard_map/ppermute | solution.py:23
  32.0 0.7 copy.63.pick_ref
  33.1 1.9 %fusion.1 = bf16[8,96,12,96]{3,1,2,0:T(8,128)(2,1)} fusion(f32[12,8]{0,1:T(8,128)S(1)} %copy.56, f32[12,96,96]{2,1,0:T(8,128)S(1)} %convert.82), kind=kLoop, calls=%fused_computation.6 | loop fusion | flops 1769472 | bytes 2212224 | tf_op jit(solution)/shard_map/kf,fab->kafb/transpose | solution.py:107
  34.9 1.9 %collective-permute-start.5 = (bf16[11,96,128]{2,1,0:T(8,128)(2,1)}, bf16[11,96,128]{2,1,0:T(8,128)(2,1)}, u32[]{:S(2)}, u32[]{:S(2)}) collective-permute-start(bf16[11,96,128]{2,1,0:T(8,128)(2,1)} %get-tuple-element.66), channel_id=1, source_target_pairs={{0,48},{16,64},{32,80},{48,96},{64,112},{80,128},{96,144},{112,160... | collective-permute-start | bytes 811016 | tf_op jit(solution)/shard_map/ppermute | solution.py:23
  36.9 1.2 fusion.45
  38.1 0.9 copy.52
  39.0 0.9 copy.53
  39.9 0.9 copy.54
  40.8 17.6 %collective-permute-start.6 = (bf16[11,96,128]{2,1,0:T(8,128)(2,1)}, bf16[11,96,128]{2,1,0:T(8,128)(2,1)}, u32[]{:S(2)}, u32[]{:S(2)}) collective-permute-start(bf16[11,96,128]{2,1,0:T(8,128)(2,1)} %get-tuple-element.67), channel_id=1, source_target_pairs={{0,464},{16,480},{32,496},{48,0},{64,16},{80,32},{96,48},{112,64},... | collective-permute-start | bytes 811016 | tf_op jit(solution)/shard_map/ppermute | solution.py:23
  58.4 5.3 %collective-permute-start.7 = (bf16[11,96,128]{2,1,0:T(8,128)(2,1)}, bf16[11,96,128]{2,1,0:T(8,128)(2,1)}, u32[]{:S(2)}, u32[]{:S(2)}) collective-permute-start(bf16[11,96,128]{2,1,0:T(8,128)(2,1)} %get-tuple-element.68), channel_id=1, source_target_pairs={{0,480},{16,496},{32,0},{48,16},{64,32},{80,48},{96,64},{112,80},{... | collective-permute-start | bytes 811016 | tf_op jit(solution)/shard_map/ppermute | solution.py:23
  63.7 1.9 %collective-permute-start.3 = (bf16[11,96,128]{2,1,0:T(8,128)(2,1)}, bf16[11,96,128]{2,1,0:T(8,128)(2,1)}, u32[]{:S(2)}, u32[]{:S(2)}) collective-permute-start(bf16[11,96,128]{2,1,0:T(8,128)(2,1)} %get-tuple-element.69), channel_id=1, source_target_pairs={{0,16},{16,32},{32,48},{48,64},{64,80},{80,96},{96,112},{112,128},... | collective-permute-start | bytes 811016 | tf_op jit(solution)/shard_map/ppermute | solution.py:23
  65.6 4.8 %fusion = bf16[8,96,14,96]{3,1,2,0:T(8,128)(2,1)S(1)} fusion(f32[8,14]{1,0:T(8,128)S(1)} %fusion.68, f32[8,96,96]{1,2,0:T(8,128)} %copy.54, f32[8,14]{1,0:T(8,128)S(1)} %get-tuple-element.139, f32[8,96,96]{1,2,0:T(8,128)} %copy.53, f32[8,14]{1,0:T(8,128)S(1)} %get-tuple-element.138, f32[8,96,96]{1,2,0:T(8,128)} %copy.52, f32[8,96,96]{2,1,0:T(8,128)} %get-tuple-element.29, ...), kind=kLoop, calls=%fused_computation.1 | loop fusion | flops 14450688 | bytes 4131904 | tf_op jit(solution)/shard_map/convert.30
  70.9 4.7 %collective-permute-done.3.refs_0_ = bf16[11,96,128]{2,1,0:T(8,128)(2,1)} collective-permute-done((bf16[11,96,128]{2,1,0:T(8,128)(2,1)}, bf16[11,96,128]{2,1,0:T(8,128)(2,1)}, u32[]{:S(2)}, u32[]{:S(2)}) %collective-permute-start.3) | collective-permute-done | bytes 270368 | tf_op jit(solution)/shard_map/ppermute | solution.py:23
  75.7 2.5 %shard_map.55 = (bf16[26,96,128]{2,1,0:T(8,128)(2,1)}, bf16[12,96,128]{2,1,0:T(8,128)(2,1)}, bf16[6,128]{1,0:T(8,128)(2,1)}) custom-call(s32[6,2]{1,0:T(8,128)} %copy.63.pick_ref, bf16[3,96,128]{2,1,0:T(8,128)(2,1)} %collective-permute-done.1.low_ref, bf16[8,96,128]{2,1,0:T(8,128)(2,1)} %copy-done.2, bf16[3,96,128]{2,1,0:T(8,128)(2,1)} %copy-done.5, ...), custom_call_target="tpu_custom_call" | custom-call | tf_op jit(solution)/shard_map/pallas_call | solution.py:50
  78.2 0.7 slice_convert_fusion
  78.9 1.2 fusion.29
  80.1 4.9 %fusion.55 = (bf16[8,96,128]{2,1,0:T(8,128)(2,1)S(1)}, f32[8,96,128]{2,1,0:T(8,128)}) fusion(f32[1,8,96,128]{3,2,1,0:T(8,128)} %param.7, f32[8,96,128]{2,0,1:T(8,128)S(1)} %fusion.29, bf16[26,96,128]{2,1,0:T(8,128)(2,1)} %get-tuple-element.20, bf16[8,96,12,96]{3,1,2,0:T(8,128)(2,1)} %fusion.1, bf16[8,96,14,96]{3,1,2,0:T(8,128)(2,1)S(1)} %fusion), kind=kOutput, calls=%fused_computation.137 | convolution fusion | flops 493240320 | bytes 5849088 | tf_op jit(solution)/shard_map/kamb,mbr->kar/dot_general | solution.py:168
  85.8 2.2 %collective-permute-start.10 = (bf16[3,96,128]{2,1,0:T(8,128)(2,1)S(1)}, bf16[3,96,128]{2,1,0:T(8,128)(2,1)S(1)}, u32[]{:S(2)}, u32[]{:S(2)}) collective-permute-start(bf16[3,96,128]{2,1,0:T(8,128)(2,1)S(1)} %get-tuple-element.62), channel_id=1, source_target_pairs={{1,0},{2,1},{3,2},{4,3},{5,4},{6,5},{7,6},{8,7},{9,8},{10,9},{11,1... | collective-permute-start | bytes 221192 | tf_op jit(solution)/shard_map/ppermute | solution.py:18
  88.0 10.6 %collective-permute-start.9 = (bf16[3,96,128]{2,1,0:T(8,128)(2,1)S(1)}, bf16[3,96,128]{2,1,0:T(8,128)(2,1)S(1)}, u32[]{:S(2)}, u32[]{:S(2)}) collective-permute-start(bf16[3,96,128]{2,1,0:T(8,128)(2,1)S(1)} %get-tuple-element.63), channel_id=1, source_target_pairs={{0,1},{1,2},{2,3},{3,4},{4,5},{5,6},{6,7},{7,8},{8,9},{9,10},{10,1... | collective-permute-start | bytes 221192 | tf_op jit(solution)/shard_map/ppermute | solution.py:18
  98.9 1.9 %collective-permute-start.11 = (bf16[4,96,128]{2,1,0:T(8,128)(2,1)S(1)}, bf16[4,96,128]{2,1,0:T(8,128)(2,1)S(1)}, u32[]{:S(2)}, u32[]{:S(2)}) collective-permute-start(bf16[4,96,128]{2,1,0:T(8,128)(2,1)S(1)} %pad_maximum_fusion.37), channel_id=1, source_target_pairs={{0,16},{16,32},{32,48},{48,64},{64,80},{80,96},{96,112},{112,128},... | collective-permute-start | bytes 294920 | tf_op jit(solution)/shard_map/ppermute | solution.py:23
  100.8 1.9 %collective-permute-start.12 = (bf16[4,96,128]{2,1,0:T(8,128)(2,1)S(1)}, bf16[4,96,128]{2,1,0:T(8,128)(2,1)S(1)}, u32[]{:S(2)}, u32[]{:S(2)}) collective-permute-start(bf16[4,96,128]{2,1,0:T(8,128)(2,1)S(1)} %pad_maximum_fusion.38), channel_id=1, source_target_pairs={{0,32},{16,48},{32,64},{48,80},{64,96},{80,112},{96,128},{112,144}... | collective-permute-start | bytes 294920 | tf_op jit(solution)/shard_map/ppermute | solution.py:23
  102.8 1.9 %collective-permute-start.13 = (bf16[4,96,128]{2,1,0:T(8,128)(2,1)S(1)}, bf16[4,96,128]{2,1,0:T(8,128)(2,1)S(1)}, u32[]{:S(2)}, u32[]{:S(2)}) collective-permute-start(bf16[4,96,128]{2,1,0:T(8,128)(2,1)S(1)} %pad_maximum_fusion.39), channel_id=1, source_target_pairs={{0,48},{16,64},{32,80},{48,96},{64,112},{80,128},{96,144},{112,160... | collective-permute-start | bytes 294920 | tf_op jit(solution)/shard_map/ppermute | solution.py:23
  104.8 8.7 %collective-permute-start.14 = (bf16[4,96,128]{2,1,0:T(8,128)(2,1)S(1)}, bf16[4,96,128]{2,1,0:T(8,128)(2,1)S(1)}, u32[]{:S(2)}, u32[]{:S(2)}) collective-permute-start(bf16[4,96,128]{2,1,0:T(8,128)(2,1)S(1)} %pad_maximum_fusion.40), channel_id=1, source_target_pairs={{0,464},{16,480},{32,496},{48,0},{64,16},{80,32},{96,48},{112,64},... | collective-permute-start | bytes 294920 | tf_op jit(solution)/shard_map/ppermute | solution.py:23
  113.6 4.3 %collective-permute-start.15 = (bf16[4,96,128]{2,1,0:T(8,128)(2,1)S(1)}, bf16[4,96,128]{2,1,0:T(8,128)(2,1)S(1)}, u32[]{:S(2)}, u32[]{:S(2)}) collective-permute-start(bf16[4,96,128]{2,1,0:T(8,128)(2,1)S(1)} %pad_maximum_fusion.41), channel_id=1, source_target_pairs={{0,480},{16,496},{32,0},{48,16},{64,32},{80,48},{96,64},{112,80},{... | collective-permute-start | bytes 294920 | tf_op jit(solution)/shard_map/ppermute | solution.py:23
  117.9 1.9 %collective-permute-start.16 = (bf16[4,96,128]{2,1,0:T(8,128)(2,1)S(1)}, bf16[4,96,128]{2,1,0:T(8,128)(2,1)S(1)}, u32[]{:S(2)}, u32[]{:S(2)}) collective-permute-start(bf16[4,96,128]{2,1,0:T(8,128)(2,1)S(1)} %pad_maximum_fusion.42), channel_id=1, source_target_pairs={{0,496},{16,0},{32,16},{48,32},{64,48},{80,64},{96,80},{112,96},{1... | collective-permute-start | bytes 294920 | tf_op jit(solution)/shard_map/ppermute | solution.py:23
  120.1 1.9 %collective-permute-done.16 = bf16[4,96,128]{2,1,0:T(8,128)(2,1)S(1)} collective-permute-done((bf16[4,96,128]{2,1,0:T(8,128)(2,1)S(1)}, bf16[4,96,128]{2,1,0:T(8,128)(2,1)S(1)}, u32[]{:S(2)}, u32[]{:S(2)}) %collective-permute-start.16) | collective-permute-done | bytes 98336 | tf_op jit(solution)/shard_map/ppermute | solution.py:23
  122.3 2.3 %fusion.32 = (bf16[8,96,128]{2,1,0:T(8,128)(2,1)S(1)}, f32[8,96,128]{2,1,0:T(8,128)S(1)}) fusion(f32[8,96,128]{2,1,0:T(8,128)S(1)} %copy-done.7, f32[1,8,96,128]{3,2,1,0:T(8,128)S(1)} %copy-done.4, f32[8,96,128]{2,0,1:T(8,128)S(1)} %fusion.27, bf16[26,96,128]{2,1,0:T(8,128)(2,1)S(1)} %get-tuple-element.85, bf16[8,96,12,96]{3,1,2,0:T(8,128)(2,1)S(1)} %copy-done.3, ...), kind=kOutput, calls=%fused_computation.52 | convolution fusion | flops 493535232 | bytes 6242304 | tf_op jit(solution)/shard_map/kamb,mbr->kar/dot_general | solution.py:168
  125.1 1.9 %collective-permute-start.18 = (bf16[3,96,128]{2,1,0:T(8,128)(2,1)S(1)}, bf16[3,96,128]{2,1,0:T(8,128)(2,1)S(1)}, u32[]{:S(2)}, u32[]{:S(2)}) collective-permute-start(bf16[3,96,128]{2,1,0:T(8,128)(2,1)S(1)} %get-tuple-element.60), channel_id=1, source_target_pairs={{1,0},{2,1},{3,2},{4,3},{5,4},{6,5},{7,6},{8,7},{9,8},{10,9},{11,1... | collective-permute-start | bytes 221192 | tf_op jit(solution)/shard_map/ppermute | solution.py:18
  127.0 9.9 %collective-permute-start.17 = (bf16[3,96,128]{2,1,0:T(8,128)(2,1)S(1)}, bf16[3,96,128]{2,1,0:T(8,128)(2,1)S(1)}, u32[]{:S(2)}, u32[]{:S(2)}) collective-permute-start(bf16[3,96,128]{2,1,0:T(8,128)(2,1)S(1)} %get-tuple-element.61), channel_id=1, source_target_pairs={{0,1},{1,2},{2,3},{3,4},{4,5},{5,6},{6,7},{7,8},{8,9},{9,10},{10,1... | collective-permute-start | bytes 221192 | tf_op jit(solution)/shard_map/ppermute | solution.py:18
  137.3 1.9 %collective-permute-start.19 = (bf16[4,96,128]{2,1,0:T(8,128)(2,1)S(1)}, bf16[4,96,128]{2,1,0:T(8,128)(2,1)S(1)}, u32[]{:S(2)}, u32[]{:S(2)}) collective-permute-start(bf16[4,96,128]{2,1,0:T(8,128)(2,1)S(1)} %pad_maximum_fusion.43), channel_id=1, source_target_pairs={{0,16},{16,32},{32,48},{48,64},{64,80},{80,96},{96,112},{112,128},... | collective-permute-start | bytes 294920 | tf_op jit(solution)/shard_map/ppermute | solution.py:23
  139.3 1.9 %collective-permute-start.20 = (bf16[4,96,128]{2,1,0:T(8,128)(2,1)S(1)}, bf16[4,96,128]{2,1,0:T(8,128)(2,1)S(1)}, u32[]{:S(2)}, u32[]{:S(2)}) collective-permute-start(bf16[4,96,128]{2,1,0:T(8,128)(2,1)S(1)} %pad_maximum_fusion.44), channel_id=1, source_target_pairs={{0,32},{16,48},{32,64},{48,80},{64,96},{80,112},{96,128},{112,144}... | collective-permute-start | bytes 294920 | tf_op jit(solution)/shard_map/ppermute | solution.py:23
  141.2 1.9 %collective-permute-start.21 = (bf16[4,96,128]{2,1,0:T(8,128)(2,1)S(1)}, bf16[4,96,128]{2,1,0:T(8,128)(2,1)S(1)}, u32[]{:S(2)}, u32[]{:S(2)}) collective-permute-start(bf16[4,96,128]{2,1,0:T(8,128)(2,1)S(1)} %pad_maximum_fusion.45), channel_id=1, source_target_pairs={{0,48},{16,64},{32,80},{48,96},{64,112},{80,128},{96,144},{112,160... | collective-permute-start | bytes 294920 | tf_op jit(solution)/shard_map/ppermute | solution.py:23
  143.2 8.7 %collective-permute-start.22 = (bf16[4,96,128]{2,1,0:T(8,128)(2,1)S(1)}, bf16[4,96,128]{2,1,0:T(8,128)(2,1)S(1)}, u32[]{:S(2)}, u32[]{:S(2)}) collective-permute-start(bf16[4,96,128]{2,1,0:T(8,128)(2,1)S(1)} %pad_maximum_fusion.46), channel_id=1, source_target_pairs={{0,464},{16,480},{32,496},{48,0},{64,16},{80,32},{96,48},{112,64},... | collective-permute-start | bytes 294920 | tf_op jit(solution)/shard_map/ppermute | solution.py:23
  152.0 4.3 %collective-permute-start.23 = (bf16[4,96,128]{2,1,0:T(8,128)(2,1)S(1)}, bf16[4,96,128]{2,1,0:T(8,128)(2,1)S(1)}, u32[]{:S(2)}, u32[]{:S(2)}) collective-permute-start(bf16[4,96,128]{2,1,0:T(8,128)(2,1)S(1)} %pad_maximum_fusion.47), channel_id=1, source_target_pairs={{0,480},{16,496},{32,0},{48,16},{64,32},{80,48},{96,64},{112,80},{... | collective-permute-start | bytes 294920 | tf_op jit(solution)/shard_map/ppermute | solution.py:23
  156.3 1.9 %collective-permute-start.24 = (bf16[4,96,128]{2,1,0:T(8,128)(2,1)S(1)}, bf16[4,96,128]{2,1,0:T(8,128)(2,1)S(1)}, u32[]{:S(2)}, u32[]{:S(2)}) collective-permute-start(bf16[4,96,128]{2,1,0:T(8,128)(2,1)S(1)} %pad_maximum_fusion.48), channel_id=1, source_target_pairs={{0,496},{16,0},{32,16},{48,32},{64,48},{80,64},{96,80},{112,96},{1... | collective-permute-start | bytes 294920 | tf_op jit(solution)/shard_map/ppermute | solution.py:23
  158.5 1.9 %collective-permute-done.24 = bf16[4,96,128]{2,1,0:T(8,128)(2,1)S(1)} collective-permute-done((bf16[4,96,128]{2,1,0:T(8,128)(2,1)S(1)}, bf16[4,96,128]{2,1,0:T(8,128)(2,1)S(1)}, u32[]{:S(2)}, u32[]{:S(2)}) %collective-permute-start.24) | collective-permute-done | bytes 98336 | tf_op jit(solution)/shard_map/ppermute | solution.py:23
  160.7 3.1 %fusion.17 = f32[1,8,96,128]{3,2,1,0:T(8,128)} fusion(f32[8,96,128]{2,1,0:T(8,128)S(1)} %get-tuple-element.133, bf16[8,96,12,96]{3,1,2,0:T(8,128)(2,1)S(1)} %copy-done.3, bf16[8,96,14,96]{3,1,2,0:T(8,128)(2,1)S(1)} %fusion, bf16[26,96,128]{2,1,0:T(8,128)(2,1)S(1)} %get-tuple-element.73, f32[8,96,128]{2,0,1:T(8,128)S(1)} %fusion.25, ...), kind=kOutput, calls=%fused_computation.26 | convolution fusion | flops 494125056 | bytes 6438912 | tf_op jit(solution)/shard_map/kamb,mbr->kar/dot_general | solution.py:168
  (126 shorter events, 5.8 us)
Async XLA Ops:
  0.0 20.5 %copy-start = (bf16[1,1,6,2,96,96]{5,4,3,2,1,0:T(8,128)(2,1)S(1)}, bf16[1,1,6,2,96,96]{5,4,3,2,1,0:T(8,128)(2,1)}, u32[]{:S(2)}) copy-start(bf16[1,1,6,2,96,96]{5,4,3,2,1,0:T(8,128)(2,1)} %param.11) | copy-start | bytes 663556
  1.1 21.0 %copy-start.2 = (bf16[8,96,128]{2,1,0:T(8,128)(2,1)}, bf16[8,96,128]{2,1,0:T(8,128)(2,1)S(1)}, u32[]{:S(2)}) copy-start(bf16[8,96,128]{2,1,0:T(8,128)(2,1)S(1)} %fusion.31.probe_ref) | copy-start | bytes 589828
  1.8 39.0 %collective-permute-start.2 = (bf16[3,96,128]{2,1,0:T(8,128)(2,1)}, bf16[3,96,128]{2,1,0:T(8,128)(2,1)S(1)}, u32[]{:S(2)}, u32[]{:S(2)}) collective-permute-start(bf16[3,96,128]{2,1,0:T(8,128)(2,1)} %get-tuple-element.70), channel_id=1, source_target_pairs={{1,0},{2,1},{3,2},{4,3},{5,4},{6,5},{7,6},{8,7},{9,8},{10,9},{11,1... | collective-permute-start | bytes 221192 | tf_op jit(solution)/shard_map/ppermute | solution.py:18
  4.5 53.9 %collective-permute-start.1 = (bf16[3,96,128]{2,1,0:T(8,128)(2,1)}, bf16[3,96,128]{2,1,0:T(8,128)(2,1)}, u32[]{:S(2)}, u32[]{:S(2)}) collective-permute-start(bf16[3,96,128]{2,1,0:T(8,128)(2,1)} %get-tuple-element.71), channel_id=1, source_target_pairs={{0,1},{1,2},{2,3},{3,4},{4,5},{5,6},{6,7},{7,8},{8,9},{9,10},{10,1... | collective-permute-start | bytes 221192 | tf_op jit(solution)/shard_map/ppermute | solution.py:18
  14.7 16.9 %copy-start.6 = (s32[1,1,6]{2,1,0:T(1,128)S(1)}, s32[1,1,6]{2,1,0:T(1,128)}, u32[]{:S(2)}) copy-start(s32[1,1,6]{2,1,0:T(1,128)} %param.10) | copy-start | bytes 76
  14.7 20.3 %collective-permute-start = (bf16[3,4,96,96]{3,2,1,0:T(8,128)(2,1)S(1)}, bf16[3,4,96,96]{3,2,1,0:T(8,128)(2,1)S(1)}, u32[]{:S(2)}, u32[]{:S(2)}) collective-permute-start(bf16[3,4,96,96]{3,2,1,0:T(8,128)(2,1)S(1)} %slice_bitcast_fusion), channel_id=1, source_target_pairs={{0,1},{1,2},{2,3},{3,4},{4,5},{5,6},{6,7},{7,8},{8,9},{9,10},{10,1... | collective-permute-start | bytes 663560 | tf_op jit(solution)/shard_map/ppermute | solution.py:18
  22.0 14.8 %copy-start.1 = (bf16[1,8,4,96,96]{4,3,2,1,0:T(8,128)(2,1)S(1)}, bf16[1,8,4,96,96]{4,3,2,1,0:T(8,128)(2,1)}, u32[]{:S(2)}) copy-start(bf16[1,8,4,96,96]{4,3,2,1,0:T(8,128)(2,1)} %param.8) | copy-start | bytes 1769476
  22.0 41.6 %collective-permute-start.8 = (bf16[11,96,128]{2,1,0:T(8,128)(2,1)S(1)}, bf16[11,96,128]{2,1,0:T(8,128)(2,1)}, u32[]{:S(2)}, u32[]{:S(2)}) collective-permute-start(bf16[11,96,128]{2,1,0:T(8,128)(2,1)S(1)} %get-tuple-element.64), channel_id=1, source_target_pairs={{0,496},{16,0},{32,16},{48,32},{64,48},{80,64},{96,80},{112,96},{1... | collective-permute-start | bytes 811016 | tf_op jit(solution)/shard_map/ppermute | solution.py:23
  29.5 40.9 %collective-permute-start.4 = (bf16[11,96,128]{2,1,0:T(8,128)(2,1)}, bf16[11,96,128]{2,1,0:T(8,128)(2,1)}, u32[]{:S(2)}, u32[]{:S(2)}) collective-permute-start(bf16[11,96,128]{2,1,0:T(8,128)(2,1)} %get-tuple-element.65), channel_id=1, source_target_pairs={{0,32},{16,48},{32,64},{48,80},{64,96},{80,112},{96,128},{112,144}... | collective-permute-start | bytes 811016 | tf_op jit(solution)/shard_map/ppermute | solution.py:23
  34.9 35.5 %collective-permute-start.5 = (bf16[11,96,128]{2,1,0:T(8,128)(2,1)}, bf16[11,96,128]{2,1,0:T(8,128)(2,1)}, u32[]{:S(2)}, u32[]{:S(2)}) collective-permute-start(bf16[11,96,128]{2,1,0:T(8,128)(2,1)} %get-tuple-element.66), channel_id=1, source_target_pairs={{0,48},{16,64},{32,80},{48,96},{64,112},{80,128},{96,144},{112,160... | collective-permute-start | bytes 811016 | tf_op jit(solution)/shard_map/ppermute | solution.py:23
  40.8 29.6 %copy-start.5 = (bf16[3,96,128]{2,1,0:T(8,128)(2,1)}, bf16[3,96,128]{2,1,0:T(8,128)(2,1)S(1)}, u32[]{:S(2)}) copy-start(bf16[3,96,128]{2,1,0:T(8,128)(2,1)S(1)} %collective-permute-done.2.high_ref) | copy-start | bytes 221188
  40.8 29.6 %collective-permute-start.6 = (bf16[11,96,128]{2,1,0:T(8,128)(2,1)}, bf16[11,96,128]{2,1,0:T(8,128)(2,1)}, u32[]{:S(2)}, u32[]{:S(2)}) collective-permute-start(bf16[11,96,128]{2,1,0:T(8,128)(2,1)} %get-tuple-element.67), channel_id=1, source_target_pairs={{0,464},{16,480},{32,496},{48,0},{64,16},{80,32},{96,48},{112,64},... | collective-permute-start | bytes 811016 | tf_op jit(solution)/shard_map/ppermute | solution.py:23
  58.4 12.5 %collective-permute-start.7 = (bf16[11,96,128]{2,1,0:T(8,128)(2,1)}, bf16[11,96,128]{2,1,0:T(8,128)(2,1)}, u32[]{:S(2)}, u32[]{:S(2)}) collective-permute-start(bf16[11,96,128]{2,1,0:T(8,128)(2,1)} %get-tuple-element.68), channel_id=1, source_target_pairs={{0,480},{16,496},{32,0},{48,16},{64,32},{80,48},{96,64},{112,80},{... | collective-permute-start | bytes 811016 | tf_op jit(solution)/shard_map/ppermute | solution.py:23
  63.7 12.0 %collective-permute-start.3 = (bf16[11,96,128]{2,1,0:T(8,128)(2,1)}, bf16[11,96,128]{2,1,0:T(8,128)(2,1)}, u32[]{:S(2)}, u32[]{:S(2)}) collective-permute-start(bf16[11,96,128]{2,1,0:T(8,128)(2,1)} %get-tuple-element.69), channel_id=1, source_target_pairs={{0,16},{16,32},{32,48},{48,64},{64,80},{80,96},{96,112},{112,128},... | collective-permute-start | bytes 811016 | tf_op jit(solution)/shard_map/ppermute | solution.py:23
  85.7 36.5 %copy-start.3 = (bf16[8,96,12,96]{3,1,2,0:T(8,128)(2,1)S(1)}, bf16[8,96,12,96]{3,1,2,0:T(8,128)(2,1)}, u32[]{:S(2)}) copy-start(bf16[8,96,12,96]{3,1,2,0:T(8,128)(2,1)} %fusion.1) | copy-start | bytes 5308420
  85.7 36.5 %copy-start.4 = (f32[1,8,96,128]{3,2,1,0:T(8,128)S(1)}, f32[1,8,96,128]{3,2,1,0:T(8,128)}, u32[]{:S(2)}) copy-start(f32[1,8,96,128]{3,2,1,0:T(8,128)} %param.7) | copy-start | bytes 1179652
  85.8 36.5 %copy-start.7 = (f32[8,96,128]{2,1,0:T(8,128)S(1)}, f32[8,96,128]{2,1,0:T(8,128)}, u32[]{:S(2)}) copy-start(f32[8,96,128]{2,1,0:T(8,128)} %get-tuple-element.131) | copy-start | bytes 1179652
  85.8 27.8 %collective-permute-start.10 = (bf16[3,96,128]{2,1,0:T(8,128)(2,1)S(1)}, bf16[3,96,128]{2,1,0:T(8,128)(2,1)S(1)}, u32[]{:S(2)}, u32[]{:S(2)}) collective-permute-start(bf16[3,96,128]{2,1,0:T(8,128)(2,1)S(1)} %get-tuple-element.62), channel_id=1, source_target_pairs={{1,0},{2,1},{3,2},{4,3},{5,4},{6,5},{7,6},{8,7},{9,8},{10,9},{11,1... | collective-permute-start | bytes 221192 | tf_op jit(solution)/shard_map/ppermute | solution.py:18
  88.0 16.8 %collective-permute-start.9 = (bf16[3,96,128]{2,1,0:T(8,128)(2,1)S(1)}, bf16[3,96,128]{2,1,0:T(8,128)(2,1)S(1)}, u32[]{:S(2)}, u32[]{:S(2)}) collective-permute-start(bf16[3,96,128]{2,1,0:T(8,128)(2,1)S(1)} %get-tuple-element.63), channel_id=1, source_target_pairs={{0,1},{1,2},{2,3},{3,4},{4,5},{5,6},{6,7},{7,8},{8,9},{9,10},{10,1... | collective-permute-start | bytes 221192 | tf_op jit(solution)/shard_map/ppermute | solution.py:18
  98.9 19.0 %collective-permute-start.11 = (bf16[4,96,128]{2,1,0:T(8,128)(2,1)S(1)}, bf16[4,96,128]{2,1,0:T(8,128)(2,1)S(1)}, u32[]{:S(2)}, u32[]{:S(2)}) collective-permute-start(bf16[4,96,128]{2,1,0:T(8,128)(2,1)S(1)} %pad_maximum_fusion.37), channel_id=1, source_target_pairs={{0,16},{16,32},{32,48},{48,64},{64,80},{80,96},{96,112},{112,128},... | collective-permute-start | bytes 294920 | tf_op jit(solution)/shard_map/ppermute | solution.py:23
  100.8 19.0 %collective-permute-start.12 = (bf16[4,96,128]{2,1,0:T(8,128)(2,1)S(1)}, bf16[4,96,128]{2,1,0:T(8,128)(2,1)S(1)}, u32[]{:S(2)}, u32[]{:S(2)}) collective-permute-start(bf16[4,96,128]{2,1,0:T(8,128)(2,1)S(1)} %pad_maximum_fusion.38), channel_id=1, source_target_pairs={{0,32},{16,48},{32,64},{48,80},{64,96},{80,112},{96,128},{112,144}... | collective-permute-start | bytes 294920 | tf_op jit(solution)/shard_map/ppermute | solution.py:23
  102.8 17.1 %collective-permute-start.13 = (bf16[4,96,128]{2,1,0:T(8,128)(2,1)S(1)}, bf16[4,96,128]{2,1,0:T(8,128)(2,1)S(1)}, u32[]{:S(2)}, u32[]{:S(2)}) collective-permute-start(bf16[4,96,128]{2,1,0:T(8,128)(2,1)S(1)} %pad_maximum_fusion.39), channel_id=1, source_target_pairs={{0,48},{16,64},{32,80},{48,96},{64,112},{80,128},{96,144},{112,160... | collective-permute-start | bytes 294920 | tf_op jit(solution)/shard_map/ppermute | solution.py:23
  104.8 15.1 %collective-permute-start.14 = (bf16[4,96,128]{2,1,0:T(8,128)(2,1)S(1)}, bf16[4,96,128]{2,1,0:T(8,128)(2,1)S(1)}, u32[]{:S(2)}, u32[]{:S(2)}) collective-permute-start(bf16[4,96,128]{2,1,0:T(8,128)(2,1)S(1)} %pad_maximum_fusion.40), channel_id=1, source_target_pairs={{0,464},{16,480},{32,496},{48,0},{64,16},{80,32},{96,48},{112,64},... | collective-permute-start | bytes 294920 | tf_op jit(solution)/shard_map/ppermute | solution.py:23
  113.6 6.5 %collective-permute-start.15 = (bf16[4,96,128]{2,1,0:T(8,128)(2,1)S(1)}, bf16[4,96,128]{2,1,0:T(8,128)(2,1)S(1)}, u32[]{:S(2)}, u32[]{:S(2)}) collective-permute-start(bf16[4,96,128]{2,1,0:T(8,128)(2,1)S(1)} %pad_maximum_fusion.41), channel_id=1, source_target_pairs={{0,480},{16,496},{32,0},{48,16},{64,32},{80,48},{96,64},{112,80},{... | collective-permute-start | bytes 294920 | tf_op jit(solution)/shard_map/ppermute | solution.py:23
  117.9 4.1 %collective-permute-start.16 = (bf16[4,96,128]{2,1,0:T(8,128)(2,1)S(1)}, bf16[4,96,128]{2,1,0:T(8,128)(2,1)S(1)}, u32[]{:S(2)}, u32[]{:S(2)}) collective-permute-start(bf16[4,96,128]{2,1,0:T(8,128)(2,1)S(1)} %pad_maximum_fusion.42), channel_id=1, source_target_pairs={{0,496},{16,0},{32,16},{48,32},{64,48},{80,64},{96,80},{112,96},{1... | collective-permute-start | bytes 294920 | tf_op jit(solution)/shard_map/ppermute | solution.py:23
  125.1 26.9 %collective-permute-start.18 = (bf16[3,96,128]{2,1,0:T(8,128)(2,1)S(1)}, bf16[3,96,128]{2,1,0:T(8,128)(2,1)S(1)}, u32[]{:S(2)}, u32[]{:S(2)}) collective-permute-start(bf16[3,96,128]{2,1,0:T(8,128)(2,1)S(1)} %get-tuple-element.60), channel_id=1, source_target_pairs={{1,0},{2,1},{3,2},{4,3},{5,4},{6,5},{7,6},{8,7},{9,8},{10,9},{11,1... | collective-permute-start | bytes 221192 | tf_op jit(solution)/shard_map/ppermute | solution.py:18
  127.0 16.2 %collective-permute-start.17 = (bf16[3,96,128]{2,1,0:T(8,128)(2,1)S(1)}, bf16[3,96,128]{2,1,0:T(8,128)(2,1)S(1)}, u32[]{:S(2)}, u32[]{:S(2)}) collective-permute-start(bf16[3,96,128]{2,1,0:T(8,128)(2,1)S(1)} %get-tuple-element.61), channel_id=1, source_target_pairs={{0,1},{1,2},{2,3},{3,4},{4,5},{5,6},{6,7},{7,8},{8,9},{9,10},{10,1... | collective-permute-start | bytes 221192 | tf_op jit(solution)/shard_map/ppermute | solution.py:18
  137.3 19.0 %collective-permute-start.19 = (bf16[4,96,128]{2,1,0:T(8,128)(2,1)S(1)}, bf16[4,96,128]{2,1,0:T(8,128)(2,1)S(1)}, u32[]{:S(2)}, u32[]{:S(2)}) collective-permute-start(bf16[4,96,128]{2,1,0:T(8,128)(2,1)S(1)} %pad_maximum_fusion.43), channel_id=1, source_target_pairs={{0,16},{16,32},{32,48},{48,64},{64,80},{80,96},{96,112},{112,128},... | collective-permute-start | bytes 294920 | tf_op jit(solution)/shard_map/ppermute | solution.py:23
  139.3 19.0 %collective-permute-start.20 = (bf16[4,96,128]{2,1,0:T(8,128)(2,1)S(1)}, bf16[4,96,128]{2,1,0:T(8,128)(2,1)S(1)}, u32[]{:S(2)}, u32[]{:S(2)}) collective-permute-start(bf16[4,96,128]{2,1,0:T(8,128)(2,1)S(1)} %pad_maximum_fusion.44), channel_id=1, source_target_pairs={{0,32},{16,48},{32,64},{48,80},{64,96},{80,112},{96,128},{112,144}... | collective-permute-start | bytes 294920 | tf_op jit(solution)/shard_map/ppermute | solution.py:23
  141.2 17.1 %collective-permute-start.21 = (bf16[4,96,128]{2,1,0:T(8,128)(2,1)S(1)}, bf16[4,96,128]{2,1,0:T(8,128)(2,1)S(1)}, u32[]{:S(2)}, u32[]{:S(2)}) collective-permute-start(bf16[4,96,128]{2,1,0:T(8,128)(2,1)S(1)} %pad_maximum_fusion.45), channel_id=1, source_target_pairs={{0,48},{16,64},{32,80},{48,96},{64,112},{80,128},{96,144},{112,160... | collective-permute-start | bytes 294920 | tf_op jit(solution)/shard_map/ppermute | solution.py:23
  143.2 15.1 %collective-permute-start.22 = (bf16[4,96,128]{2,1,0:T(8,128)(2,1)S(1)}, bf16[4,96,128]{2,1,0:T(8,128)(2,1)S(1)}, u32[]{:S(2)}, u32[]{:S(2)}) collective-permute-start(bf16[4,96,128]{2,1,0:T(8,128)(2,1)S(1)} %pad_maximum_fusion.46), channel_id=1, source_target_pairs={{0,464},{16,480},{32,496},{48,0},{64,16},{80,32},{96,48},{112,64},... | collective-permute-start | bytes 294920 | tf_op jit(solution)/shard_map/ppermute | solution.py:23
  152.0 6.5 %collective-permute-start.23 = (bf16[4,96,128]{2,1,0:T(8,128)(2,1)S(1)}, bf16[4,96,128]{2,1,0:T(8,128)(2,1)S(1)}, u32[]{:S(2)}, u32[]{:S(2)}) collective-permute-start(bf16[4,96,128]{2,1,0:T(8,128)(2,1)S(1)} %pad_maximum_fusion.47), channel_id=1, source_target_pairs={{0,480},{16,496},{32,0},{48,16},{64,32},{80,48},{96,64},{112,80},{... | collective-permute-start | bytes 294920 | tf_op jit(solution)/shard_map/ppermute | solution.py:23
  156.3 4.1 %collective-permute-start.24 = (bf16[4,96,128]{2,1,0:T(8,128)(2,1)S(1)}, bf16[4,96,128]{2,1,0:T(8,128)(2,1)S(1)}, u32[]{:S(2)}, u32[]{:S(2)}) collective-permute-start(bf16[4,96,128]{2,1,0:T(8,128)(2,1)S(1)} %pad_maximum_fusion.48), channel_id=1, source_target_pairs={{0,496},{16,0},{32,16},{48,32},{64,48},{80,64},{96,80},{112,96},{1... | collective-permute-start | bytes 294920 | tf_op jit(solution)/shard_map/ppermute | solution.py:23

commit v7 on v6

--- a/solution.py
+++ b/solution.py
@@ -72,7 +72,7 @@
         b - (group_span - 1) if b < group_span - 1 else b - group_span + 2 for b in range(buckets)
     ]
     bucket_of = {o: b for b, o in enumerate(offsets)}
-    shifts = [o for o in offsets if o > 0] + [o for o in offsets if o < 0]
+    shifts = [o for o in offsets if o < 0][::-1] + [o for o in offsets if o > 0]
 
     boundary_blocks = shifted_open(blocks[knots - 3 :], "seg", 1)
     lower_blocks = jnp.concatenate([boundary_blocks, blocks], axis=0)
@@ -96,9 +96,8 @@
         band_weight = term if band_weight is None else band_weight + term
     for step in range(1, 4):
         place = (ext_ids[None, :] == knot_ids[:, None] + 3 - step).astype(jnp.float32)
-        band_weight = band_weight + jnp.einsum(
-            "km,kba->kamb", place, lower_blocks[3 - step : 3 - step + knots, step].astype(jnp.float32)
-        )
+        flipped = jnp.swapaxes(lower_blocks[3 - step : 3 - step + knots, step], -1, -2)
+        band_weight = band_weight + jnp.einsum("km,kab->kamb", place, flipped.astype(jnp.float32))
     fetch_order = [bucket_of[-s] for s in shifts]
     fetch_place = jnp.concatenate(
         [own_place.reshape(knots, buckets, slots)[:, b] for b in fetch_order], axis=1

time: 165 us -> 171 us (1.036)
  the two profiles are of different devices: /device:TPU:24 before, /device:TPU:449 now
where the time goes in v7:
time: 171 us; the launch traced here: 170 us
  starting transfers between devices  95.3 us (56%)
  waiting for transfers between devices  37.5 us (22%)
  matrix products  13.9 us (8%)
  other arithmetic  12.9 us (8%)
  local copies, waits for them, and re-layouts  7.06 us (4%)
  Pallas kernels  2.49 us (1%)
    ppermute x18, starting transfers between devices, shifted_ring(): lax.ppermute(value, axis, [(i, (i + steps) % count) for i in range(count)])  68.4 us
    ppermute x7, starting transfers between devices, shifted_open(): lax.ppermute(value, axis, [(source, source + steps) for source in range(i...  26.9 us
    ppermute x18, waiting for transfers between devices, shifted_ring(): lax.ppermute(value, axis, [(i, (i + steps) % count) for i in range(count)])  22.5 us
    ppermute x7, waiting for transfers between devices, shifted_open(): lax.ppermute(value, axis, [(source, source + steps) for source in range(i...  15.1 us
    dot_general x3, matrix products, body(): jnp.einsum('kamb,mbr->kar', weight, stacked, preferred_element_type=jnp.f...  10.3 us
    another operation x7, other arithmetic  6.25 us
  transfers between devices with their start and end apart: 25, of which 7 were waited for; matrix products, arithmetic and copies ran while one was open for 11% of the time, Pallas kernels for 0%

profile of v7, /device:TPU:449, one launch (start us, length us, event | category | flops | bytes accessed | tf_op | source)
XLA Modules:
  0.0 170.1 jit_solution(3288339678650961624)
XLA Ops:
  0.0 1.1 fusion.31.probe_ref
  1.1 7.6 %collective-permute-start.2 = (bf16[3,96,128]{2,1,0:T(8,128)(2,1)S(1)}, bf16[3,96,128]{2,1,0:T(8,128)(2,1)S(1)}, u32[]{:S(2)}, u32[]{:S(2)}) collective-permute-start(bf16[3,96,128]{2,1,0:T(8,128)(2,1)S(1)} %get-tuple-element.70), channel_id=1, source_target_pairs={{1,0},{2,1},{3,2},{4,3},{5,4},{6,5},{7,6},{8,7},{9,8},{10,9},{11,1... | collective-permute-start | bytes 221192 | tf_op jit(solution)/shard_map/ppermute | solution.py:18
  8.8 1.9 %collective-permute-start.1 = (bf16[3,96,128]{2,1,0:T(8,128)(2,1)S(1)}, bf16[3,96,128]{2,1,0:T(8,128)(2,1)S(1)}, u32[]{:S(2)}, u32[]{:S(2)}) collective-permute-start(bf16[3,96,128]{2,1,0:T(8,128)(2,1)S(1)} %get-tuple-element.71), channel_id=1, source_target_pairs={{0,1},{1,2},{2,3},{3,4},{4,5},{5,6},{6,7},{7,8},{8,9},{9,10},{10,1... | collective-permute-start | bytes 221192 | tf_op jit(solution)/shard_map/ppermute | solution.py:18
  10.7 1.0 slice_bitcast_fusion
  11.7 1.9 %collective-permute-start = (bf16[3,4,96,96]{3,2,1,0:T(8,128)(2,1)S(1)}, bf16[3,4,96,96]{3,2,1,0:T(8,128)(2,1)S(1)}, u32[]{:S(2)}, u32[]{:S(2)}) collective-permute-start(bf16[3,4,96,96]{3,2,1,0:T(8,128)(2,1)S(1)} %slice_bitcast_fusion), channel_id=1, source_target_pairs={{0,1},{1,2},{2,3},{3,4},{4,5},{5,6},{6,7},{7,8},{8,9},{9,10},{10,1... | collective-permute-start | bytes 663560 | tf_op jit(solution)/shard_map/ppermute | solution.py:18
  14.5 0.8 fusion.90
  15.3 0.7 fusion.75
  17.0 1.2 fusion.41
  18.2 5.6 %collective-permute-start.8 = (bf16[11,96,128]{2,1,0:T(8,128)(2,1)S(1)}, bf16[11,96,128]{2,1,0:T(8,128)(2,1)}, u32[]{:S(2)}, u32[]{:S(2)}) collective-permute-start(bf16[11,96,128]{2,1,0:T(8,128)(2,1)S(1)} %get-tuple-element.64), channel_id=1, source_target_pairs={{0,48},{16,64},{32,80},{48,96},{64,112},{80,128},{96,144},{112,160... | collective-permute-start | bytes 811016 | tf_op jit(solution)/shard_map/ppermute | solution.py:23
  23.9 3.7 %collective-permute-start.4 = (bf16[11,96,128]{2,1,0:T(8,128)(2,1)}, bf16[11,96,128]{2,1,0:T(8,128)(2,1)}, u32[]{:S(2)}, u32[]{:S(2)}) collective-permute-start(bf16[11,96,128]{2,1,0:T(8,128)(2,1)} %get-tuple-element.65), channel_id=1, source_target_pairs={{0,480},{16,496},{32,0},{48,16},{64,32},{80,48},{96,64},{112,80},{... | collective-permute-start | bytes 811016 | tf_op jit(solution)/shard_map/ppermute | solution.py:23
  29.2 1.9 %fusion.1 = bf16[8,96,12,96]{3,1,2,0:T(8,128)(2,1)} fusion(f32[12,8]{0,1:T(8,128)S(1)} %copy.56, f32[12,96,96]{2,1,0:T(8,128)S(1)} %convert.88), kind=kLoop, calls=%fused_computation.6 | loop fusion | flops 1769472 | bytes 2212224 | tf_op jit(solution)/shard_map/kf,fab->kafb/transpose | solution.py:106
  31.1 15.1 %collective-permute-done = bf16[3,4,96,96]{3,2,1,0:T(8,128)(2,1)S(1)} collective-permute-done((bf16[3,4,96,96]{3,2,1,0:T(8,128)(2,1)S(1)}, bf16[3,4,96,96]{3,2,1,0:T(8,128)(2,1)S(1)}, u32[]{:S(2)}, u32[]{:S(2)}) %collective-permute-start) | collective-permute-done | bytes 221216 | tf_op jit(solution)/shard_map/ppermute | solution.py:18
  46.2 9.2 %collective-permute-start.5 = (bf16[11,96,128]{2,1,0:T(8,128)(2,1)}, bf16[11,96,128]{2,1,0:T(8,128)(2,1)}, u32[]{:S(2)}, u32[]{:S(2)}) collective-permute-start(bf16[11,96,128]{2,1,0:T(8,128)(2,1)} %get-tuple-element.66), channel_id=1, source_target_pairs={{0,464},{16,480},{32,496},{48,0},{64,16},{80,32},{96,48},{112,64},... | collective-permute-start | bytes 811016 | tf_op jit(solution)/shard_map/ppermute | solution.py:23
  55.4 1.2 convert_bitcast_fusion.2
  56.6 0.9 copy.52
  57.5 0.9 copy.53
  58.5 0.9 copy.54
  59.4 1.9 %collective-permute-start.6 = (bf16[11,96,128]{2,1,0:T(8,128)(2,1)}, bf16[11,96,128]{2,1,0:T(8,128)(2,1)}, u32[]{:S(2)}, u32[]{:S(2)}) collective-permute-start(bf16[11,96,128]{2,1,0:T(8,128)(2,1)} %get-tuple-element.67), channel_id=1, source_target_pairs={{0,16},{16,32},{32,48},{48,64},{64,80},{80,96},{96,112},{112,128},... | collective-permute-start | bytes 811016 | tf_op jit(solution)/shard_map/ppermute | solution.py:23
  61.3 1.9 %collective-permute-start.7 = (bf16[11,96,128]{2,1,0:T(8,128)(2,1)}, bf16[11,96,128]{2,1,0:T(8,128)(2,1)}, u32[]{:S(2)}, u32[]{:S(2)}) collective-permute-start(bf16[11,96,128]{2,1,0:T(8,128)(2,1)} %get-tuple-element.68), channel_id=1, source_target_pairs={{0,32},{16,48},{32,64},{48,80},{64,96},{80,112},{96,128},{112,144}... | collective-permute-start | bytes 811016 | tf_op jit(solution)/shard_map/ppermute | solution.py:23
  63.3 2.4 %collective-permute-start.3 = (bf16[11,96,128]{2,1,0:T(8,128)(2,1)}, bf16[11,96,128]{2,1,0:T(8,128)(2,1)}, u32[]{:S(2)}, u32[]{:S(2)}) collective-permute-start(bf16[11,96,128]{2,1,0:T(8,128)(2,1)} %get-tuple-element.69), channel_id=1, source_target_pairs={{0,496},{16,0},{32,16},{48,32},{64,48},{80,64},{96,80},{112,96},{1... | collective-permute-start | bytes 811016 | tf_op jit(solution)/shard_map/ppermute | solution.py:23
  65.7 4.8 %fusion = bf16[8,96,14,96]{3,1,2,0:T(8,128)(2,1)S(1)} fusion(f32[8,14]{1,0:T(8,128)S(1)} %fusion.65, f32[8,96,96]{2,1,0:T(8,128)} %copy.54, f32[8,14]{1,0:T(8,128)S(1)} %get-tuple-element.136, f32[8,96,96]{2,1,0:T(8,128)} %copy.53, f32[8,14]{1,0:T(8,128)S(1)} %get-tuple-element.135, f32[8,96,96]{2,1,0:T(8,128)} %copy.52, f32[8,96,96]{2,1,0:T(8,128)} %get-tuple-element.29, ...), kind=kLoop, calls=%fused_computation.1 | loop fusion | flops 14450688 | bytes 4131904 | tf_op jit(solution)/shard_map/convert.36
  70.5 2.7 %collective-permute-done.7.refs_4_ = bf16[11,96,128]{2,1,0:T(8,128)(2,1)} collective-permute-done((bf16[11,96,128]{2,1,0:T(8,128)(2,1)}, bf16[11,96,128]{2,1,0:T(8,128)(2,1)}, u32[]{:S(2)}, u32[]{:S(2)}) %collective-permute-start.7) | collective-permute-done | bytes 270368 | tf_op jit(solution)/shard_map/ppermute | solution.py:23
  73.2 2.5 %shard_map.55 = (bf16[26,96,128]{2,1,0:T(8,128)(2,1)}, bf16[12,96,128]{2,1,0:T(8,128)(2,1)}, bf16[6,128]{1,0:T(8,128)(2,1)}) custom-call(s32[6,2]{1,0:T(8,128)} %copy.63.pick_ref, bf16[3,96,128]{2,1,0:T(8,128)(2,1)} %copy-done.6, bf16[8,96,128]{2,1,0:T(8,128)(2,1)} %copy-done.2, bf16[3,96,128]{2,1,0:T(8,128)(2,1)} %copy-done.5, ...), custom_call_target="tpu_custom_call" | custom-call | tf_op jit(solution)/shard_map/pallas_call | solution.py:50
  76.4 1.2 fusion.29
  77.7 4.9 %fusion.52 = (bf16[8,96,128]{2,1,0:T(8,128)(2,1)S(1)}, f32[8,96,128]{2,1,0:T(8,128)}) fusion(f32[1,8,96,128]{3,2,1,0:T(8,128)} %param.7, f32[8,96,128]{2,0,1:T(8,128)S(1)} %fusion.29, bf16[26,96,128]{2,1,0:T(8,128)(2,1)} %get-tuple-element.20, bf16[8,96,12,96]{3,1,2,0:T(8,128)(2,1)} %fusion.1, bf16[8,96,14,96]{3,1,2,0:T(8,128)(2,1)S(1)} %fusion), kind=kOutput, calls=%fused_computation.137 | convolution fusion | flops 493240320 | bytes 5849088 | tf_op jit(solution)/shard_map/kamb,mbr->kar/dot_general | solution.py:167
  83.3 2.2 %collective-permute-start.10 = (bf16[3,96,128]{2,1,0:T(8,128)(2,1)S(1)}, bf16[3,96,128]{2,1,0:T(8,128)(2,1)S(1)}, u32[]{:S(2)}, u32[]{:S(2)}) collective-permute-start(bf16[3,96,128]{2,1,0:T(8,128)(2,1)S(1)} %get-tuple-element.62), channel_id=1, source_target_pairs={{1,0},{2,1},{3,2},{4,3},{5,4},{6,5},{7,6},{8,7},{9,8},{10,9},{11,1... | collective-permute-start | bytes 221192 | tf_op jit(solution)/shard_map/ppermute | solution.py:18
  85.5 3.4 %collective-permute-start.9 = (bf16[3,96,128]{2,1,0:T(8,128)(2,1)S(1)}, bf16[3,96,128]{2,1,0:T(8,128)(2,1)S(1)}, u32[]{:S(2)}, u32[]{:S(2)}) collective-permute-start(bf16[3,96,128]{2,1,0:T(8,128)(2,1)S(1)} %get-tuple-element.63), channel_id=1, source_target_pairs={{0,1},{1,2},{2,3},{3,4},{4,5},{5,6},{6,7},{7,8},{8,9},{9,10},{10,1... | collective-permute-start | bytes 221192 | tf_op jit(solution)/shard_map/ppermute | solution.py:18
  89.2 3.8 %collective-permute-start.11 = (bf16[4,96,128]{2,1,0:T(8,128)(2,1)S(1)}, bf16[4,96,128]{2,1,0:T(8,128)(2,1)S(1)}, u32[]{:S(2)}, u32[]{:S(2)}) collective-permute-start(bf16[4,96,128]{2,1,0:T(8,128)(2,1)S(1)} %pad_maximum_fusion.37), channel_id=1, source_target_pairs={{0,496},{16,0},{32,16},{48,32},{64,48},{80,64},{96,80},{112,96},{1... | collective-permute-start | bytes 294920 | tf_op jit(solution)/shard_map/ppermute | solution.py:23
  93.0 3.8 %collective-permute-start.12 = (bf16[4,96,128]{2,1,0:T(8,128)(2,1)S(1)}, bf16[4,96,128]{2,1,0:T(8,128)(2,1)S(1)}, u32[]{:S(2)}, u32[]{:S(2)}) collective-permute-start(bf16[4,96,128]{2,1,0:T(8,128)(2,1)S(1)} %pad_maximum_fusion.38), channel_id=1, source_target_pairs={{0,480},{16,496},{32,0},{48,16},{64,32},{80,48},{96,64},{112,80},{... | collective-permute-start | bytes 294920 | tf_op jit(solution)/shard_map/ppermute | solution.py:23
  96.9 11.5 %collective-permute-start.13 = (bf16[4,96,128]{2,1,0:T(8,128)(2,1)S(1)}, bf16[4,96,128]{2,1,0:T(8,128)(2,1)S(1)}, u32[]{:S(2)}, u32[]{:S(2)}) collective-permute-start(bf16[4,96,128]{2,1,0:T(8,128)(2,1)S(1)} %pad_maximum_fusion.39), channel_id=1, source_target_pairs={{0,464},{16,480},{32,496},{48,0},{64,16},{80,32},{96,48},{112,64},... | collective-permute-start | bytes 294920 | tf_op jit(solution)/shard_map/ppermute | solution.py:23
  108.5 2.6 %collective-permute-start.14 = (bf16[4,96,128]{2,1,0:T(8,128)(2,1)S(1)}, bf16[4,96,128]{2,1,0:T(8,128)(2,1)S(1)}, u32[]{:S(2)}, u32[]{:S(2)}) collective-permute-start(bf16[4,96,128]{2,1,0:T(8,128)(2,1)S(1)} %pad_maximum_fusion.40), channel_id=1, source_target_pairs={{0,16},{16,32},{32,48},{48,64},{64,80},{80,96},{96,112},{112,128},... | collective-permute-start | bytes 294920 | tf_op jit(solution)/shard_map/ppermute | solution.py:23
  111.1 2.1 %collective-permute-start.15 = (bf16[4,96,128]{2,1,0:T(8,128)(2,1)S(1)}, bf16[4,96,128]{2,1,0:T(8,128)(2,1)S(1)}, u32[]{:S(2)}, u32[]{:S(2)}) collective-permute-start(bf16[4,96,128]{2,1,0:T(8,128)(2,1)S(1)} %pad_maximum_fusion.41), channel_id=1, source_target_pairs={{0,32},{16,48},{32,64},{48,80},{64,96},{80,112},{96,128},{112,144}... | collective-permute-start | bytes 294920 | tf_op jit(solution)/shard_map/ppermute | solution.py:23
  113.3 1.9 %collective-permute-start.16 = (bf16[4,96,128]{2,1,0:T(8,128)(2,1)S(1)}, bf16[4,96,128]{2,1,0:T(8,128)(2,1)S(1)}, u32[]{:S(2)}, u32[]{:S(2)}) collective-permute-start(bf16[4,96,128]{2,1,0:T(8,128)(2,1)S(1)} %pad_maximum_fusion.42), channel_id=1, source_target_pairs={{0,48},{16,64},{32,80},{48,96},{64,112},{80,128},{96,144},{112,160... | collective-permute-start | bytes 294920 | tf_op jit(solution)/shard_map/ppermute | solution.py:23
  115.4 4.2 %collective-permute-done.15 = bf16[4,96,128]{2,1,0:T(8,128)(2,1)S(1)} collective-permute-done((bf16[4,96,128]{2,1,0:T(8,128)(2,1)S(1)}, bf16[4,96,128]{2,1,0:T(8,128)(2,1)S(1)}, u32[]{:S(2)}, u32[]{:S(2)}) %collective-permute-start.15) | collective-permute-done | bytes 98336 | tf_op jit(solution)/shard_map/ppermute | solution.py:23
  119.6 2.9 %collective-permute-done.16 = bf16[4,96,128]{2,1,0:T(8,128)(2,1)S(1)} collective-permute-done((bf16[4,96,128]{2,1,0:T(8,128)(2,1)S(1)}, bf16[4,96,128]{2,1,0:T(8,128)(2,1)S(1)}, u32[]{:S(2)}, u32[]{:S(2)}) %collective-permute-start.16) | collective-permute-done | bytes 98336 | tf_op jit(solution)/shard_map/ppermute | solution.py:23
  122.9 2.3 %fusion.32 = (bf16[8,96,128]{2,1,0:T(8,128)(2,1)S(1)}, f32[8,96,128]{2,1,0:T(8,128)S(1)}) fusion(f32[8,96,128]{2,1,0:T(8,128)S(1)} %copy-done.8, f32[1,8,96,128]{3,2,1,0:T(8,128)S(1)} %copy-done.4, f32[8,96,128]{2,0,1:T(8,128)S(1)} %fusion.27, bf16[26,96,128]{2,1,0:T(8,128)(2,1)S(1)} %get-tuple-element.85, bf16[8,96,12,96]{3,1,2,0:T(8,128)(2,1)S(1)} %copy-done.3, ...), kind=kOutput, calls=%fused_computation.55 | convolution fusion | flops 493535232 | bytes 6242304 | tf_op jit(solution)/shard_map/kamb,mbr->kar/dot_general | solution.py:167
  125.7 7.9 %collective-permute-start.18 = (bf16[3,96,128]{2,1,0:T(8,128)(2,1)S(1)}, bf16[3,96,128]{2,1,0:T(8,128)(2,1)S(1)}, u32[]{:S(2)}, u32[]{:S(2)}) collective-permute-start(bf16[3,96,128]{2,1,0:T(8,128)(2,1)S(1)} %get-tuple-element.60), channel_id=1, source_target_pairs={{1,0},{2,1},{3,2},{4,3},{5,4},{6,5},{7,6},{8,7},{9,8},{10,9},{11,1... | collective-permute-start | bytes 221192 | tf_op jit(solution)/shard_map/ppermute | solution.py:18
  133.6 1.9 %collective-permute-start.17 = (bf16[3,96,128]{2,1,0:T(8,128)(2,1)S(1)}, bf16[3,96,128]{2,1,0:T(8,128)(2,1)S(1)}, u32[]{:S(2)}, u32[]{:S(2)}) collective-permute-start(bf16[3,96,128]{2,1,0:T(8,128)(2,1)S(1)} %get-tuple-element.61), channel_id=1, source_target_pairs={{0,1},{1,2},{2,3},{3,4},{4,5},{5,6},{6,7},{7,8},{8,9},{9,10},{10,1... | collective-permute-start | bytes 221192 | tf_op jit(solution)/shard_map/ppermute | solution.py:18
  135.9 2.7 %collective-permute-start.19 = (bf16[4,96,128]{2,1,0:T(8,128)(2,1)S(1)}, bf16[4,96,128]{2,1,0:T(8,128)(2,1)S(1)}, u32[]{:S(2)}, u32[]{:S(2)}) collective-permute-start(bf16[4,96,128]{2,1,0:T(8,128)(2,1)S(1)} %pad_maximum_fusion.43), channel_id=1, source_target_pairs={{0,496},{16,0},{32,16},{48,32},{64,48},{80,64},{96,80},{112,96},{1... | collective-permute-start | bytes 294920 | tf_op jit(solution)/shard_map/ppermute | solution.py:23
  138.6 2.9 %collective-permute-start.20 = (bf16[4,96,128]{2,1,0:T(8,128)(2,1)S(1)}, bf16[4,96,128]{2,1,0:T(8,128)(2,1)S(1)}, u32[]{:S(2)}, u32[]{:S(2)}) collective-permute-start(bf16[4,96,128]{2,1,0:T(8,128)(2,1)S(1)} %pad_maximum_fusion.44), channel_id=1, source_target_pairs={{0,480},{16,496},{32,0},{48,16},{64,32},{80,48},{96,64},{112,80},{... | collective-permute-start | bytes 294920 | tf_op jit(solution)/shard_map/ppermute | solution.py:23
  141.6 4.4 %collective-permute-start.21 = (bf16[4,96,128]{2,1,0:T(8,128)(2,1)S(1)}, bf16[4,96,128]{2,1,0:T(8,128)(2,1)S(1)}, u32[]{:S(2)}, u32[]{:S(2)}) collective-permute-start(bf16[4,96,128]{2,1,0:T(8,128)(2,1)S(1)} %pad_maximum_fusion.45), channel_id=1, source_target_pairs={{0,464},{16,480},{32,496},{48,0},{64,16},{80,32},{96,48},{112,64},... | collective-permute-start | bytes 294920 | tf_op jit(solution)/shard_map/ppermute | solution.py:23
  146.1 3.7 %collective-permute-start.22 = (bf16[4,96,128]{2,1,0:T(8,128)(2,1)S(1)}, bf16[4,96,128]{2,1,0:T(8,128)(2,1)S(1)}, u32[]{:S(2)}, u32[]{:S(2)}) collective-permute-start(bf16[4,96,128]{2,1,0:T(8,128)(2,1)S(1)} %pad_maximum_fusion.46), channel_id=1, source_target_pairs={{0,16},{16,32},{32,48},{48,64},{64,80},{80,96},{96,112},{112,128},... | collective-permute-start | bytes 294920 | tf_op jit(solution)/shard_map/ppermute | solution.py:23
  149.9 1.9 %collective-permute-start.23 = (bf16[4,96,128]{2,1,0:T(8,128)(2,1)S(1)}, bf16[4,96,128]{2,1,0:T(8,128)(2,1)S(1)}, u32[]{:S(2)}, u32[]{:S(2)}) collective-permute-start(bf16[4,96,128]{2,1,0:T(8,128)(2,1)S(1)} %pad_maximum_fusion.47), channel_id=1, source_target_pairs={{0,32},{16,48},{32,64},{48,80},{64,96},{80,112},{96,128},{112,144}... | collective-permute-start | bytes 294920 | tf_op jit(solution)/shard_map/ppermute | solution.py:23
  151.8 2.1 %collective-permute-start.24 = (bf16[4,96,128]{2,1,0:T(8,128)(2,1)S(1)}, bf16[4,96,128]{2,1,0:T(8,128)(2,1)S(1)}, u32[]{:S(2)}, u32[]{:S(2)}) collective-permute-start(bf16[4,96,128]{2,1,0:T(8,128)(2,1)S(1)} %pad_maximum_fusion.48), channel_id=1, source_target_pairs={{0,48},{16,64},{32,80},{48,96},{64,112},{80,128},{96,144},{112,160... | collective-permute-start | bytes 294920 | tf_op jit(solution)/shard_map/ppermute | solution.py:23
  154.1 2.1 %collective-permute-done.22 = bf16[4,96,128]{2,1,0:T(8,128)(2,1)S(1)} collective-permute-done((bf16[4,96,128]{2,1,0:T(8,128)(2,1)S(1)}, bf16[4,96,128]{2,1,0:T(8,128)(2,1)S(1)}, u32[]{:S(2)}, u32[]{:S(2)}) %collective-permute-start.22) | collective-permute-done | bytes 98336 | tf_op jit(solution)/shard_map/ppermute | solution.py:23
  156.2 7.5 %collective-permute-done.23 = bf16[4,96,128]{2,1,0:T(8,128)(2,1)S(1)} collective-permute-done((bf16[4,96,128]{2,1,0:T(8,128)(2,1)S(1)}, bf16[4,96,128]{2,1,0:T(8,128)(2,1)S(1)}, u32[]{:S(2)}, u32[]{:S(2)}) %collective-permute-start.23) | collective-permute-done | bytes 98336 | tf_op jit(solution)/shard_map/ppermute | solution.py:23
  163.7 3.0 %collective-permute-done.24 = bf16[4,96,128]{2,1,0:T(8,128)(2,1)S(1)} collective-permute-done((bf16[4,96,128]{2,1,0:T(8,128)(2,1)S(1)}, bf16[4,96,128]{2,1,0:T(8,128)(2,1)S(1)}, u32[]{:S(2)}, u32[]{:S(2)}) %collective-permute-start.24) | collective-permute-done | bytes 98336 | tf_op jit(solution)/shard_map/ppermute | solution.py:23
  167.0 3.1 %fusion.17 = f32[1,8,96,128]{3,2,1,0:T(8,128)} fusion(f32[8,96,128]{2,1,0:T(8,128)S(1)} %get-tuple-element.130, bf16[8,96,12,96]{3,1,2,0:T(8,128)(2,1)S(1)} %copy-done.3, bf16[8,96,14,96]{3,1,2,0:T(8,128)(2,1)S(1)} %fusion, bf16[26,96,128]{2,1,0:T(8,128)(2,1)S(1)} %get-tuple-element.73, f32[8,96,128]{2,0,1:T(8,128)S(1)} %fusion.25, ...), kind=kOutput, calls=%fused_computation.26 | convolution fusion | flops 494125056 | bytes 6438912 | tf_op jit(solution)/shard_map/kamb,mbr->kar/dot_general | solution.py:167
  (129 shorter events, 7.0 us)
Async XLA Ops:
  0.0 16.7 %copy-start = (bf16[1,1,6,2,96,96]{5,4,3,2,1,0:T(8,128)(2,1)S(1)}, bf16[1,1,6,2,96,96]{5,4,3,2,1,0:T(8,128)(2,1)}, u32[]{:S(2)}) copy-start(bf16[1,1,6,2,96,96]{5,4,3,2,1,0:T(8,128)(2,1)} %param.11) | copy-start | bytes 663556
  1.1 17.2 %copy-start.2 = (bf16[8,96,128]{2,1,0:T(8,128)(2,1)}, bf16[8,96,128]{2,1,0:T(8,128)(2,1)S(1)}, u32[]{:S(2)}) copy-start(bf16[8,96,128]{2,1,0:T(8,128)(2,1)S(1)} %fusion.31.probe_ref) | copy-start | bytes 589828
  1.1 58.3 %collective-permute-start.2 = (bf16[3,96,128]{2,1,0:T(8,128)(2,1)S(1)}, bf16[3,96,128]{2,1,0:T(8,128)(2,1)S(1)}, u32[]{:S(2)}, u32[]{:S(2)}) collective-permute-start(bf16[3,96,128]{2,1,0:T(8,128)(2,1)S(1)} %get-tuple-element.70), channel_id=1, source_target_pairs={{1,0},{2,1},{3,2},{4,3},{5,4},{6,5},{7,6},{8,7},{9,8},{10,9},{11,1... | collective-permute-start | bytes 221192 | tf_op jit(solution)/shard_map/ppermute | solution.py:18
  8.8 52.5 %collective-permute-start.1 = (bf16[3,96,128]{2,1,0:T(8,128)(2,1)S(1)}, bf16[3,96,128]{2,1,0:T(8,128)(2,1)S(1)}, u32[]{:S(2)}, u32[]{:S(2)}) collective-permute-start(bf16[3,96,128]{2,1,0:T(8,128)(2,1)S(1)} %get-tuple-element.71), channel_id=1, source_target_pairs={{0,1},{1,2},{2,3},{3,4},{4,5},{5,6},{6,7},{7,8},{8,9},{9,10},{10,1... | collective-permute-start | bytes 221192 | tf_op jit(solution)/shard_map/ppermute | solution.py:18
  11.7 16.0 %copy-start.7 = (s32[1,1,6]{2,1,0:T(1,128)S(1)}, s32[1,1,6]{2,1,0:T(1,128)}, u32[]{:S(2)}) copy-start(s32[1,1,6]{2,1,0:T(1,128)} %param.10) | copy-start | bytes 76
  11.7 34.5 %collective-permute-start = (bf16[3,4,96,96]{3,2,1,0:T(8,128)(2,1)S(1)}, bf16[3,4,96,96]{3,2,1,0:T(8,128)(2,1)S(1)}, u32[]{:S(2)}, u32[]{:S(2)}) collective-permute-start(bf16[3,4,96,96]{3,2,1,0:T(8,128)(2,1)S(1)} %slice_bitcast_fusion), channel_id=1, source_target_pairs={{0,1},{1,2},{2,3},{3,4},{4,5},{5,6},{6,7},{7,8},{8,9},{9,10},{10,1... | collective-permute-start | bytes 663560 | tf_op jit(solution)/shard_map/ppermute | solution.py:18
  18.2 37.2 %copy-start.1 = (bf16[1,8,4,96,96]{4,3,2,1,0:T(8,128)(2,1)S(1)}, bf16[1,8,4,96,96]{4,3,2,1,0:T(8,128)(2,1)}, u32[]{:S(2)}) copy-start(bf16[1,8,4,96,96]{4,3,2,1,0:T(8,128)(2,1)} %param.8) | copy-start | bytes 1769476
  18.2 45.0 %collective-permute-start.8 = (bf16[11,96,128]{2,1,0:T(8,128)(2,1)S(1)}, bf16[11,96,128]{2,1,0:T(8,128)(2,1)}, u32[]{:S(2)}, u32[]{:S(2)}) collective-permute-start(bf16[11,96,128]{2,1,0:T(8,128)(2,1)S(1)} %get-tuple-element.64), channel_id=1, source_target_pairs={{0,48},{16,64},{32,80},{48,96},{64,112},{80,128},{96,144},{112,160... | collective-permute-start | bytes 811016 | tf_op jit(solution)/shard_map/ppermute | solution.py:23
  23.9 46.6 %collective-permute-start.4 = (bf16[11,96,128]{2,1,0:T(8,128)(2,1)}, bf16[11,96,128]{2,1,0:T(8,128)(2,1)}, u32[]{:S(2)}, u32[]{:S(2)}) collective-permute-start(bf16[11,96,128]{2,1,0:T(8,128)(2,1)} %get-tuple-element.65), channel_id=1, source_target_pairs={{0,480},{16,496},{32,0},{48,16},{64,32},{80,48},{96,64},{112,80},{... | collective-permute-start | bytes 811016 | tf_op jit(solution)/shard_map/ppermute | solution.py:23
  46.2 24.3 %collective-permute-start.5 = (bf16[11,96,128]{2,1,0:T(8,128)(2,1)}, bf16[11,96,128]{2,1,0:T(8,128)(2,1)}, u32[]{:S(2)}, u32[]{:S(2)}) collective-permute-start(bf16[11,96,128]{2,1,0:T(8,128)(2,1)} %get-tuple-element.66), channel_id=1, source_target_pairs={{0,464},{16,480},{32,496},{48,0},{64,16},{80,32},{96,48},{112,64},... | collective-permute-start | bytes 811016 | tf_op jit(solution)/shard_map/ppermute | solution.py:23
  59.4 11.1 %copy-start.5 = (bf16[3,96,128]{2,1,0:T(8,128)(2,1)}, bf16[3,96,128]{2,1,0:T(8,128)(2,1)S(1)}, u32[]{:S(2)}) copy-start(bf16[3,96,128]{2,1,0:T(8,128)(2,1)S(1)} %collective-permute-done.2.high_ref) | copy-start | bytes 221188
  59.4 11.1 %collective-permute-start.6 = (bf16[11,96,128]{2,1,0:T(8,128)(2,1)}, bf16[11,96,128]{2,1,0:T(8,128)(2,1)}, u32[]{:S(2)}, u32[]{:S(2)}) collective-permute-start(bf16[11,96,128]{2,1,0:T(8,128)(2,1)} %get-tuple-element.67), channel_id=1, source_target_pairs={{0,16},{16,32},{32,48},{48,64},{64,80},{80,96},{96,112},{112,128},... | collective-permute-start | bytes 811016 | tf_op jit(solution)/shard_map/ppermute | solution.py:23
  61.3 4.4 %copy-start.6 = (bf16[3,96,128]{2,1,0:T(8,128)(2,1)}, bf16[3,96,128]{2,1,0:T(8,128)(2,1)S(1)}, u32[]{:S(2)}) copy-start(bf16[3,96,128]{2,1,0:T(8,128)(2,1)S(1)} %collective-permute-done.1.low_ref) | copy-start | bytes 221188
  61.3 11.9 %collective-permute-start.7 = (bf16[11,96,128]{2,1,0:T(8,128)(2,1)}, bf16[11,96,128]{2,1,0:T(8,128)(2,1)}, u32[]{:S(2)}, u32[]{:S(2)}) collective-permute-start(bf16[11,96,128]{2,1,0:T(8,128)(2,1)} %get-tuple-element.68), channel_id=1, source_target_pairs={{0,32},{16,48},{32,64},{48,80},{64,96},{80,112},{96,128},{112,144}... | collective-permute-start | bytes 811016 | tf_op jit(solution)/shard_map/ppermute | solution.py:23
  63.3 9.9 %collective-permute-start.3 = (bf16[11,96,128]{2,1,0:T(8,128)(2,1)}, bf16[11,96,128]{2,1,0:T(8,128)(2,1)}, u32[]{:S(2)}, u32[]{:S(2)}) collective-permute-start(bf16[11,96,128]{2,1,0:T(8,128)(2,1)} %get-tuple-element.69), channel_id=1, source_target_pairs={{0,496},{16,0},{32,16},{48,32},{64,48},{80,64},{96,80},{112,96},{1... | collective-permute-start | bytes 811016 | tf_op jit(solution)/shard_map/ppermute | solution.py:23
  83.2 39.6 %copy-start.3 = (bf16[8,96,12,96]{3,1,2,0:T(8,128)(2,1)S(1)}, bf16[8,96,12,96]{3,1,2,0:T(8,128)(2,1)}, u32[]{:S(2)}) copy-start(bf16[8,96,12,96]{3,1,2,0:T(8,128)(2,1)} %fusion.1) | copy-start | bytes 5308420
  83.3 39.6 %copy-start.4 = (f32[1,8,96,128]{3,2,1,0:T(8,128)S(1)}, f32[1,8,96,128]{3,2,1,0:T(8,128)}, u32[]{:S(2)}) copy-start(f32[1,8,96,128]{3,2,1,0:T(8,128)} %param.7) | copy-start | bytes 1179652
  83.3 39.6 %copy-start.8 = (f32[8,96,128]{2,1,0:T(8,128)S(1)}, f32[8,96,128]{2,1,0:T(8,128)}, u32[]{:S(2)}) copy-start(f32[8,96,128]{2,1,0:T(8,128)} %get-tuple-element.128) | copy-start | bytes 1179652
  83.3 27.9 %collective-permute-start.10 = (bf16[3,96,128]{2,1,0:T(8,128)(2,1)S(1)}, bf16[3,96,128]{2,1,0:T(8,128)(2,1)S(1)}, u32[]{:S(2)}, u32[]{:S(2)}) collective-permute-start(bf16[3,96,128]{2,1,0:T(8,128)(2,1)S(1)} %get-tuple-element.62), channel_id=1, source_target_pairs={{1,0},{2,1},{3,2},{4,3},{5,4},{6,5},{7,6},{8,7},{9,8},{10,9},{11,1... | collective-permute-start | bytes 221192 | tf_op jit(solution)/shard_map/ppermute | solution.py:18
  85.5 23.0 %collective-permute-start.9 = (bf16[3,96,128]{2,1,0:T(8,128)(2,1)S(1)}, bf16[3,96,128]{2,1,0:T(8,128)(2,1)S(1)}, u32[]{:S(2)}, u32[]{:S(2)}) collective-permute-start(bf16[3,96,128]{2,1,0:T(8,128)(2,1)S(1)} %get-tuple-element.63), channel_id=1, source_target_pairs={{0,1},{1,2},{2,3},{3,4},{4,5},{5,6},{6,7},{7,8},{8,9},{9,10},{10,1... | collective-permute-start | bytes 221192 | tf_op jit(solution)/shard_map/ppermute | solution.py:18
  89.2 24.1 %collective-permute-start.11 = (bf16[4,96,128]{2,1,0:T(8,128)(2,1)S(1)}, bf16[4,96,128]{2,1,0:T(8,128)(2,1)S(1)}, u32[]{:S(2)}, u32[]{:S(2)}) collective-permute-start(bf16[4,96,128]{2,1,0:T(8,128)(2,1)S(1)} %pad_maximum_fusion.37), channel_id=1, source_target_pairs={{0,496},{16,0},{32,16},{48,32},{64,48},{80,64},{96,80},{112,96},{1... | collective-permute-start | bytes 294920 | tf_op jit(solution)/shard_map/ppermute | solution.py:23
  93.0 22.2 %collective-permute-start.12 = (bf16[4,96,128]{2,1,0:T(8,128)(2,1)S(1)}, bf16[4,96,128]{2,1,0:T(8,128)(2,1)S(1)}, u32[]{:S(2)}, u32[]{:S(2)}) collective-permute-start(bf16[4,96,128]{2,1,0:T(8,128)(2,1)S(1)} %pad_maximum_fusion.38), channel_id=1, source_target_pairs={{0,480},{16,496},{32,0},{48,16},{64,32},{80,48},{96,64},{112,80},{... | collective-permute-start | bytes 294920 | tf_op jit(solution)/shard_map/ppermute | solution.py:23
  96.9 18.4 %collective-permute-start.13 = (bf16[4,96,128]{2,1,0:T(8,128)(2,1)S(1)}, bf16[4,96,128]{2,1,0:T(8,128)(2,1)S(1)}, u32[]{:S(2)}, u32[]{:S(2)}) collective-permute-start(bf16[4,96,128]{2,1,0:T(8,128)(2,1)S(1)} %pad_maximum_fusion.39), channel_id=1, source_target_pairs={{0,464},{16,480},{32,496},{48,0},{64,16},{80,32},{96,48},{112,64},... | collective-permute-start | bytes 294920 | tf_op jit(solution)/shard_map/ppermute | solution.py:23
  108.5 6.9 %collective-permute-start.14 = (bf16[4,96,128]{2,1,0:T(8,128)(2,1)S(1)}, bf16[4,96,128]{2,1,0:T(8,128)(2,1)S(1)}, u32[]{:S(2)}, u32[]{:S(2)}) collective-permute-start(bf16[4,96,128]{2,1,0:T(8,128)(2,1)S(1)} %pad_maximum_fusion.40), channel_id=1, source_target_pairs={{0,16},{16,32},{32,48},{48,64},{64,80},{80,96},{96,112},{112,128},... | collective-permute-start | bytes 294920 | tf_op jit(solution)/shard_map/ppermute | solution.py:23
  111.1 8.5 %collective-permute-start.15 = (bf16[4,96,128]{2,1,0:T(8,128)(2,1)S(1)}, bf16[4,96,128]{2,1,0:T(8,128)(2,1)S(1)}, u32[]{:S(2)}, u32[]{:S(2)}) collective-permute-start(bf16[4,96,128]{2,1,0:T(8,128)(2,1)S(1)} %pad_maximum_fusion.41), channel_id=1, source_target_pairs={{0,32},{16,48},{32,64},{48,80},{64,96},{80,112},{96,128},{112,144}... | collective-permute-start | bytes 294920 | tf_op jit(solution)/shard_map/ppermute | solution.py:23
  113.3 9.2 %collective-permute-start.16 = (bf16[4,96,128]{2,1,0:T(8,128)(2,1)S(1)}, bf16[4,96,128]{2,1,0:T(8,128)(2,1)S(1)}, u32[]{:S(2)}, u32[]{:S(2)}) collective-permute-start(bf16[4,96,128]{2,1,0:T(8,128)(2,1)S(1)} %pad_maximum_fusion.42), channel_id=1, source_target_pairs={{0,48},{16,64},{32,80},{48,96},{64,112},{80,128},{96,144},{112,160... | collective-permute-start | bytes 294920 | tf_op jit(solution)/shard_map/ppermute | solution.py:23
  125.7 24.2 %collective-permute-start.18 = (bf16[3,96,128]{2,1,0:T(8,128)(2,1)S(1)}, bf16[3,96,128]{2,1,0:T(8,128)(2,1)S(1)}, u32[]{:S(2)}, u32[]{:S(2)}) collective-permute-start(bf16[3,96,128]{2,1,0:T(8,128)(2,1)S(1)} %get-tuple-element.60), channel_id=1, source_target_pairs={{1,0},{2,1},{3,2},{4,3},{5,4},{6,5},{7,6},{8,7},{9,8},{10,9},{11,1... | collective-permute-start | bytes 221192 | tf_op jit(solution)/shard_map/ppermute | solution.py:18
  133.6 12.4 %collective-permute-start.17 = (bf16[3,96,128]{2,1,0:T(8,128)(2,1)S(1)}, bf16[3,96,128]{2,1,0:T(8,128)(2,1)S(1)}, u32[]{:S(2)}, u32[]{:S(2)}) collective-permute-start(bf16[3,96,128]{2,1,0:T(8,128)(2,1)S(1)} %get-tuple-element.61), channel_id=1, source_target_pairs={{0,1},{1,2},{2,3},{3,4},{4,5},{5,6},{6,7},{7,8},{8,9},{9,10},{10,1... | collective-permute-start | bytes 221192 | tf_op jit(solution)/shard_map/ppermute | solution.py:18
  135.9 15.9 %collective-permute-start.19 = (bf16[4,96,128]{2,1,0:T(8,128)(2,1)S(1)}, bf16[4,96,128]{2,1,0:T(8,128)(2,1)S(1)}, u32[]{:S(2)}, u32[]{:S(2)}) collective-permute-start(bf16[4,96,128]{2,1,0:T(8,128)(2,1)S(1)} %pad_maximum_fusion.43), channel_id=1, source_target_pairs={{0,496},{16,0},{32,16},{48,32},{64,48},{80,64},{96,80},{112,96},{1... | collective-permute-start | bytes 294920 | tf_op jit(solution)/shard_map/ppermute | solution.py:23
  138.6 15.4 %collective-permute-start.20 = (bf16[4,96,128]{2,1,0:T(8,128)(2,1)S(1)}, bf16[4,96,128]{2,1,0:T(8,128)(2,1)S(1)}, u32[]{:S(2)}, u32[]{:S(2)}) collective-permute-start(bf16[4,96,128]{2,1,0:T(8,128)(2,1)S(1)} %pad_maximum_fusion.44), channel_id=1, source_target_pairs={{0,480},{16,496},{32,0},{48,16},{64,32},{80,48},{96,64},{112,80},{... | collective-permute-start | bytes 294920 | tf_op jit(solution)/shard_map/ppermute | solution.py:23
  141.6 12.5 %collective-permute-start.21 = (bf16[4,96,128]{2,1,0:T(8,128)(2,1)S(1)}, bf16[4,96,128]{2,1,0:T(8,128)(2,1)S(1)}, u32[]{:S(2)}, u32[]{:S(2)}) collective-permute-start(bf16[4,96,128]{2,1,0:T(8,128)(2,1)S(1)} %pad_maximum_fusion.45), channel_id=1, source_target_pairs={{0,464},{16,480},{32,496},{48,0},{64,16},{80,32},{96,48},{112,64},... | collective-permute-start | bytes 294920 | tf_op jit(solution)/shard_map/ppermute | solution.py:23
  146.1 10.1 %collective-permute-start.22 = (bf16[4,96,128]{2,1,0:T(8,128)(2,1)S(1)}, bf16[4,96,128]{2,1,0:T(8,128)(2,1)S(1)}, u32[]{:S(2)}, u32[]{:S(2)}) collective-permute-start(bf16[4,96,128]{2,1,0:T(8,128)(2,1)S(1)} %pad_maximum_fusion.46), channel_id=1, source_target_pairs={{0,16},{16,32},{32,48},{48,64},{64,80},{80,96},{96,112},{112,128},... | collective-permute-start | bytes 294920 | tf_op jit(solution)/shard_map/ppermute | solution.py:23
  149.9 13.8 %collective-permute-start.23 = (bf16[4,96,128]{2,1,0:T(8,128)(2,1)S(1)}, bf16[4,96,128]{2,1,0:T(8,128)(2,1)S(1)}, u32[]{:S(2)}, u32[]{:S(2)}) collective-permute-start(bf16[4,96,128]{2,1,0:T(8,128)(2,1)S(1)} %pad_maximum_fusion.47), channel_id=1, source_target_pairs={{0,32},{16,48},{32,64},{48,80},{64,96},{80,112},{96,128},{112,144}... | collective-permute-start | bytes 294920 | tf_op jit(solution)/shard_map/ppermute | solution.py:23
  151.8 14.9 %collective-permute-start.24 = (bf16[4,96,128]{2,1,0:T(8,128)(2,1)S(1)}, bf16[4,96,128]{2,1,0:T(8,128)(2,1)S(1)}, u32[]{:S(2)}, u32[]{:S(2)}) collective-permute-start(bf16[4,96,128]{2,1,0:T(8,128)(2,1)S(1)} %pad_maximum_fusion.48), channel_id=1, source_target_pairs={{0,48},{16,64},{32,80},{48,96},{64,112},{80,128},{96,144},{112,160... | collective-permute-start | bytes 294920 | tf_op jit(solution)/shard_map/ppermute | solution.py:23

commit v8 on v6

--- a/solution.py
+++ b/solution.py
@@ -91,21 +91,26 @@
     ext_ids = jnp.arange(ext_knots, dtype=jnp.int32)
     band_weight = None
     for step in range(4):
-        place = (ext_ids[None, :] == knot_ids[:, None] + 3 + step).astype(jnp.float32)
-        term = jnp.einsum("km,kab->kamb", place, blocks[:, step].astype(jnp.float32))
+        place = (ext_ids[None, :] == knot_ids[:, None] + 3 + step).astype(jnp.bfloat16)
+        term = jnp.einsum("km,kab->kamb", place, blocks[:, step], preferred_element_type=jnp.bfloat16)
         band_weight = term if band_weight is None else band_weight + term
     for step in range(1, 4):
-        place = (ext_ids[None, :] == knot_ids[:, None] + 3 - step).astype(jnp.float32)
+        place = (ext_ids[None, :] == knot_ids[:, None] + 3 - step).astype(jnp.bfloat16)
         band_weight = band_weight + jnp.einsum(
-            "km,kba->kamb", place, lower_blocks[3 - step : 3 - step + knots, step].astype(jnp.float32)
+            "km,kba->kamb",
+            place,
+            lower_blocks[3 - step : 3 - step + knots, step],
+            preferred_element_type=jnp.bfloat16,
         )
     fetch_order = [bucket_of[-s] for s in shifts]
     fetch_place = jnp.concatenate(
         [own_place.reshape(knots, buckets, slots)[:, b] for b in fetch_order], axis=1
     )
-    fetch_blocks = jnp.concatenate([couplings[b] for b in fetch_order], axis=0).astype(jnp.float32)
-    fetch_weight = jnp.einsum("kf,fab->kafb", fetch_place, fetch_blocks)
-    weight = jnp.concatenate([band_weight, fetch_weight], axis=2).astype(jnp.bfloat16)
+    fetch_blocks = jnp.concatenate([couplings[b] for b in fetch_order], axis=0)
+    fetch_weight = jnp.einsum(
+        "kf,fab->kafb", fetch_place.astype(jnp.bfloat16), fetch_blocks, preferred_element_type=jnp.bfloat16
+    )
+    weight = jnp.concatenate([band_weight, fetch_weight], axis=2)
     first_pick = jnp.stack([far_knot[bucket_of[-s]] for s in shifts])
     answer_pick = None
     land_place = None

time: 165 us -> 164 us (level)
  other arithmetic: 12.8 us -> 10.5 us
    another operation x7 -> x5, other arithmetic: 6.25 us -> 0.3 us
    add x0 -> x1, other arithmetic: none -> 3.12 us  [body(): band_weight + jnp.einsum('km,kba->kamb', place, lower_blocks[3 - step:3 -...]
    another operation x3 -> x0, local copies, waits for them, and re-layouts: 2.75 us -> none
    squeeze x0 -> x3, local copies, waits for them, and re-layouts: none -> 2.43 us  [body(): lower_blocks[3 - step:3 - step + knots, step]]
    ppermute x18, waiting for transfers between devices: 9.37 us -> 11 us  [shifted_ring(): lax.ppermute(value, axis, [(i, (i + steps) % count) for i in range(count)])]
  transfers between devices with their start and end apart: 25 -> 25, of which waited for: 6 -> 6; matrix products, arithmetic and copies ran while one was open for 11% -> 10% of each run, Pallas kernels for 0% -> 0%
where the time goes in v8:
time: 164 us; the launch traced here: 162 us
  starting transfers between devices  117 us (71%)
  matrix products  13.9 us (8%)
  waiting for transfers between devices  11 us (7%)
  other arithmetic  10.5 us (6%)
  local copies, waits for them, and re-layouts  6.79 us (4%)
  Pallas kernels  2.48 us (2%)
    ppermute x18, starting transfers between devices, shifted_ring(): lax.ppermute(value, axis, [(i, (i + steps) % count) for i in range(count)])  77.4 us
    ppermute x7, starting transfers between devices, shifted_open(): lax.ppermute(value, axis, [(source, source + steps) for source in range(i...  39.2 us
    ppermute x18, waiting for transfers between devices, shifted_ring(): lax.ppermute(value, axis, [(i, (i + steps) % count) for i in range(count)])  11 us
    dot_general x3, matrix products, body(): jnp.einsum('kamb,mbr->kar', weight, stacked, preferred_element_type=jnp.f...  10.3 us
  transfers between devices with their start and end apart: 25, of which 6 were waited for; matrix products, arithmetic and copies ran while one was open for 10% of the time, Pallas kernels for 0%

profile of v8, /device:TPU:24, one launch (start us, length us, event | category | flops | bytes accessed | tf_op | source)
XLA Modules:
  0.0 162.3 jit_solution(8933259569001210343)
XLA Ops:
  0.0 1.1 fusion.29.probe_ref
  1.1 2.7 %collective-permute-start.2 = (bf16[3,96,128]{2,1,0:T(8,128)(2,1)S(1)}, bf16[3,96,128]{2,1,0:T(8,128)(2,1)S(1)}, u32[]{:S(2)}, u32[]{:S(2)}) collective-permute-start(bf16[3,96,128]{2,1,0:T(8,128)(2,1)S(1)} %get-tuple-element.70), channel_id=1, source_target_pairs={{1,0},{2,1},{3,2},{4,3},{5,4},{6,5},{7,6},{8,7},{9,8},{10,9},{11,1... | collective-permute-start | bytes 221192 | tf_op jit(solution)/shard_map/ppermute | solution.py:18
  3.8 9.2 %collective-permute-start.1 = (bf16[3,96,128]{2,1,0:T(8,128)(2,1)S(1)}, bf16[3,96,128]{2,1,0:T(8,128)(2,1)S(1)}, u32[]{:S(2)}, u32[]{:S(2)}) collective-permute-start(bf16[3,96,128]{2,1,0:T(8,128)(2,1)S(1)} %get-tuple-element.71), channel_id=1, source_target_pairs={{0,1},{1,2},{2,3},{3,4},{4,5},{5,6},{6,7},{7,8},{8,9},{9,10},{10,1... | collective-permute-start | bytes 221192 | tf_op jit(solution)/shard_map/ppermute | solution.py:18
  13.0 1.0 slice_bitcast_fusion
  14.0 2.7 %collective-permute-start = (bf16[3,4,96,96]{3,2,1,0:T(8,128)(2,1)S(1)}, bf16[3,4,96,96]{3,2,1,0:T(8,128)(2,1)S(1)}, u32[]{:S(2)}, u32[]{:S(2)}) collective-permute-start(bf16[3,4,96,96]{3,2,1,0:T(8,128)(2,1)S(1)} %slice_bitcast_fusion), channel_id=1, source_target_pairs={{0,1},{1,2},{2,3},{3,4},{4,5},{5,6},{6,7},{7,8},{8,9},{9,10},{10,1... | collective-permute-start | bytes 663560 | tf_op jit(solution)/shard_map/ppermute | solution.py:18
  16.7 0.7 iota_compare_fusion.8
  17.6 0.8 fusion.85
  18.5 0.7 fusion.70
  20.2 1.1 fusion.39
  21.3 7.3 %collective-permute-start.8 = (bf16[11,96,128]{2,1,0:T(8,128)(2,1)S(1)}, bf16[11,96,128]{2,1,0:T(8,128)(2,1)S(1)}, u32[]{:S(2)}, u32[]{:S(2)}) collective-permute-start(bf16[11,96,128]{2,1,0:T(8,128)(2,1)S(1)} %get-tuple-element.64), channel_id=1, source_target_pairs={{0,496},{16,0},{32,16},{48,32},{64,48},{80,64},{96,80},{112,96},{1... | collective-permute-start | bytes 811016 | tf_op jit(solution)/shard_map/ppermute | solution.py:23
  28.6 1.9 %collective-permute-start.4 = (bf16[11,96,128]{2,1,0:T(8,128)(2,1)}, bf16[11,96,128]{2,1,0:T(8,128)(2,1)}, u32[]{:S(2)}, u32[]{:S(2)}) collective-permute-start(bf16[11,96,128]{2,1,0:T(8,128)(2,1)} %get-tuple-element.65), channel_id=1, source_target_pairs={{0,32},{16,48},{32,64},{48,80},{64,96},{80,112},{96,128},{112,144}... | collective-permute-start | bytes 811016 | tf_op jit(solution)/shard_map/ppermute | solution.py:23
  31.4 1.7 %multiply_bitcast_fusion = bf16[8,96,12,96]{3,1,2,0:T(8,128)(2,1)} fusion(bf16[12,8]{0,1:T(8,128)(2,1)S(1)} %copy.56, bf16[12,96,96]{2,1,0:T(8,128)(2,1)S(1)} %constant_dynamic-update-slice_fusion), kind=kLoop, calls=%fused_computation.4 | loop fusion | flops 884736 | bytes 1990848 | tf_op jit(solution)/shard_map/kf,fab->kafb/transpose | solution.py:110
  33.2 0.7 copy.63.pick_ref
  33.8 1.9 %collective-permute-start.5 = (bf16[11,96,128]{2,1,0:T(8,128)(2,1)}, bf16[11,96,128]{2,1,0:T(8,128)(2,1)}, u32[]{:S(2)}, u32[]{:S(2)}) collective-permute-start(bf16[11,96,128]{2,1,0:T(8,128)(2,1)} %get-tuple-element.66), channel_id=1, source_target_pairs={{0,48},{16,64},{32,80},{48,96},{64,112},{80,128},{96,144},{112,160... | collective-permute-start | bytes 811016 | tf_op jit(solution)/shard_map/ppermute | solution.py:23
  35.8 0.9 maximum_bitcast_fusion.1
  36.6 0.8 copy.52
  37.4 0.8 copy.53
  38.3 0.8 copy.54
  39.1 17.8 %collective-permute-start.6 = (bf16[11,96,128]{2,1,0:T(8,128)(2,1)}, bf16[11,96,128]{2,1,0:T(8,128)(2,1)}, u32[]{:S(2)}, u32[]{:S(2)}) collective-permute-start(bf16[11,96,128]{2,1,0:T(8,128)(2,1)} %get-tuple-element.67), channel_id=1, source_target_pairs={{0,464},{16,480},{32,496},{48,0},{64,16},{80,32},{96,48},{112,64},... | collective-permute-start | bytes 811016 | tf_op jit(solution)/shard_map/ppermute | solution.py:23
  56.9 5.3 %collective-permute-start.7 = (bf16[11,96,128]{2,1,0:T(8,128)(2,1)}, bf16[11,96,128]{2,1,0:T(8,128)(2,1)}, u32[]{:S(2)}, u32[]{:S(2)}) collective-permute-start(bf16[11,96,128]{2,1,0:T(8,128)(2,1)} %get-tuple-element.68), channel_id=1, source_target_pairs={{0,480},{16,496},{32,0},{48,16},{64,32},{80,48},{96,64},{112,80},{... | collective-permute-start | bytes 811016 | tf_op jit(solution)/shard_map/ppermute | solution.py:23
  62.2 1.9 %collective-permute-start.3 = (bf16[11,96,128]{2,1,0:T(8,128)(2,1)}, bf16[11,96,128]{2,1,0:T(8,128)(2,1)}, u32[]{:S(2)}, u32[]{:S(2)}) collective-permute-start(bf16[11,96,128]{2,1,0:T(8,128)(2,1)} %get-tuple-element.69), channel_id=1, source_target_pairs={{0,16},{16,32},{32,48},{48,64},{64,80},{80,96},{96,112},{112,128},... | collective-permute-start | bytes 811016 | tf_op jit(solution)/shard_map/ppermute | solution.py:23
  64.1 3.1 %bitcast_add_fusion = bf16[8,96,14,96]{3,1,2,0:T(8,128)(2,1)S(1)} fusion(bf16[8,14]{1,0:T(8,128)(2,1)S(1)} %fusion.60, bf16[8,96,96]{1,2,0:T(8,128)(2,1)} %copy.54, bf16[8,14]{1,0:T(8,128)(2,1)S(1)} %get-tuple-element.139, bf16[8,96,96]{1,2,0:T(8,128)(2,1)} %copy.53, bf16[8,14]{1,0:T(8,128)(2,1)S(1)} %get-tuple-element.138, bf16[8,96,96]{1,2,0:T(8,128)(2,1)} %copy.52, ...), kind=kLoop, calls=%fused_computation.1 | loop fusion | flops 13418496 | bytes 3098144 | tf_op jit(solution)/shard_map/add | solution.py:99
  67.3 2.1 %collective-permute-done.7.refs_4_ = bf16[11,96,128]{2,1,0:T(8,128)(2,1)} collective-permute-done((bf16[11,96,128]{2,1,0:T(8,128)(2,1)}, bf16[11,96,128]{2,1,0:T(8,128)(2,1)}, u32[]{:S(2)}, u32[]{:S(2)}) %collective-permute-start.7) | collective-permute-done | bytes 270368 | tf_op jit(solution)/shard_map/ppermute | solution.py:23
  69.4 4.8 %collective-permute-done.3.refs_0_ = bf16[11,96,128]{2,1,0:T(8,128)(2,1)} collective-permute-done((bf16[11,96,128]{2,1,0:T(8,128)(2,1)}, bf16[11,96,128]{2,1,0:T(8,128)(2,1)}, u32[]{:S(2)}, u32[]{:S(2)}) %collective-permute-start.3) | collective-permute-done | bytes 270368 | tf_op jit(solution)/shard_map/ppermute | solution.py:23
  74.2 2.5 %shard_map.55 = (bf16[26,96,128]{2,1,0:T(8,128)(2,1)}, bf16[12,96,128]{2,1,0:T(8,128)(2,1)}, bf16[6,128]{1,0:T(8,128)(2,1)}) custom-call(s32[6,2]{1,0:T(8,128)} %copy.63.pick_ref, bf16[3,96,128]{2,1,0:T(8,128)(2,1)} %copy-done.7, bf16[8,96,128]{2,1,0:T(8,128)(2,1)} %copy-done.2, bf16[3,96,128]{2,1,0:T(8,128)(2,1)} %copy-done.6, ...), custom_call_target="tpu_custom_call" | custom-call | tf_op jit(solution)/shard_map/pallas_call | solution.py:50
  76.7 0.7 slice_convert_fusion
  77.4 1.2 fusion.27
  78.6 4.9 %fusion.46 = (bf16[8,96,128]{2,1,0:T(8,128)(2,1)S(1)}, f32[8,96,128]{2,1,0:T(8,128)}) fusion(f32[1,8,96,128]{3,2,1,0:T(8,128)} %param.7, f32[8,96,128]{2,0,1:T(8,128)S(1)} %fusion.27, bf16[26,96,128]{2,1,0:T(8,128)(2,1)} %get-tuple-element.20, bf16[8,96,12,96]{3,1,2,0:T(8,128)(2,1)} %multiply_bitcast_fusion, bf16[8,96,14,96]{3,1,2,0:T(8,128)(2,1)S(1)} %bitcast_add_fusion), kind=kOutput, calls=%fused_computation.128 | convolution fusion | flops 493240320 | bytes 5849088 | tf_op jit(solution)/shard_map/kamb,mbr->kar/dot_general | solution.py:173
  84.3 2.2 %collective-permute-start.10 = (bf16[3,96,128]{2,1,0:T(8,128)(2,1)S(1)}, bf16[3,96,128]{2,1,0:T(8,128)(2,1)S(1)}, u32[]{:S(2)}, u32[]{:S(2)}) collective-permute-start(bf16[3,96,128]{2,1,0:T(8,128)(2,1)S(1)} %get-tuple-element.62), channel_id=1, source_target_pairs={{1,0},{2,1},{3,2},{4,3},{5,4},{6,5},{7,6},{8,7},{9,8},{10,9},{11,1... | collective-permute-start | bytes 221192 | tf_op jit(solution)/shard_map/ppermute | solution.py:18
  86.5 10.6 %collective-permute-start.9 = (bf16[3,96,128]{2,1,0:T(8,128)(2,1)S(1)}, bf16[3,96,128]{2,1,0:T(8,128)(2,1)S(1)}, u32[]{:S(2)}, u32[]{:S(2)}) collective-permute-start(bf16[3,96,128]{2,1,0:T(8,128)(2,1)S(1)} %get-tuple-element.63), channel_id=1, source_target_pairs={{0,1},{1,2},{2,3},{3,4},{4,5},{5,6},{6,7},{7,8},{8,9},{9,10},{10,1... | collective-permute-start | bytes 221192 | tf_op jit(solution)/shard_map/ppermute | solution.py:18
  97.4 1.9 %collective-permute-start.11 = (bf16[4,96,128]{2,1,0:T(8,128)(2,1)S(1)}, bf16[4,96,128]{2,1,0:T(8,128)(2,1)S(1)}, u32[]{:S(2)}, u32[]{:S(2)}) collective-permute-start(bf16[4,96,128]{2,1,0:T(8,128)(2,1)S(1)} %pad_maximum_fusion.37), channel_id=1, source_target_pairs={{0,16},{16,32},{32,48},{48,64},{64,80},{80,96},{96,112},{112,128},... | collective-permute-start | bytes 294920 | tf_op jit(solution)/shard_map/ppermute | solution.py:23
  99.3 1.9 %collective-permute-start.12 = (bf16[4,96,128]{2,1,0:T(8,128)(2,1)S(1)}, bf16[4,96,128]{2,1,0:T(8,128)(2,1)S(1)}, u32[]{:S(2)}, u32[]{:S(2)}) collective-permute-start(bf16[4,96,128]{2,1,0:T(8,128)(2,1)S(1)} %pad_maximum_fusion.38), channel_id=1, source_target_pairs={{0,32},{16,48},{32,64},{48,80},{64,96},{80,112},{96,128},{112,144}... | collective-permute-start | bytes 294920 | tf_op jit(solution)/shard_map/ppermute | solution.py:23
  101.3 1.9 %collective-permute-start.13 = (bf16[4,96,128]{2,1,0:T(8,128)(2,1)S(1)}, bf16[4,96,128]{2,1,0:T(8,128)(2,1)S(1)}, u32[]{:S(2)}, u32[]{:S(2)}) collective-permute-start(bf16[4,96,128]{2,1,0:T(8,128)(2,1)S(1)} %pad_maximum_fusion.39), channel_id=1, source_target_pairs={{0,48},{16,64},{32,80},{48,96},{64,112},{80,128},{96,144},{112,160... | collective-permute-start | bytes 294920 | tf_op jit(solution)/shard_map/ppermute | solution.py:23
  103.3 8.7 %collective-permute-start.14 = (bf16[4,96,128]{2,1,0:T(8,128)(2,1)S(1)}, bf16[4,96,128]{2,1,0:T(8,128)(2,1)S(1)}, u32[]{:S(2)}, u32[]{:S(2)}) collective-permute-start(bf16[4,96,128]{2,1,0:T(8,128)(2,1)S(1)} %pad_maximum_fusion.40), channel_id=1, source_target_pairs={{0,464},{16,480},{32,496},{48,0},{64,16},{80,32},{96,48},{112,64},... | collective-permute-start | bytes 294920 | tf_op jit(solution)/shard_map/ppermute | solution.py:23
  112.1 4.3 %collective-permute-start.15 = (bf16[4,96,128]{2,1,0:T(8,128)(2,1)S(1)}, bf16[4,96,128]{2,1,0:T(8,128)(2,1)S(1)}, u32[]{:S(2)}, u32[]{:S(2)}) collective-permute-start(bf16[4,96,128]{2,1,0:T(8,128)(2,1)S(1)} %pad_maximum_fusion.41), channel_id=1, source_target_pairs={{0,480},{16,496},{32,0},{48,16},{64,32},{80,48},{96,64},{112,80},{... | collective-permute-start | bytes 294920 | tf_op jit(solution)/shard_map/ppermute | solution.py:23
  116.4 1.9 %collective-permute-start.16 = (bf16[4,96,128]{2,1,0:T(8,128)(2,1)S(1)}, bf16[4,96,128]{2,1,0:T(8,128)(2,1)S(1)}, u32[]{:S(2)}, u32[]{:S(2)}) collective-permute-start(bf16[4,96,128]{2,1,0:T(8,128)(2,1)S(1)} %pad_maximum_fusion.42), channel_id=1, source_target_pairs={{0,496},{16,0},{32,16},{48,32},{64,48},{80,64},{96,80},{112,96},{1... | collective-permute-start | bytes 294920 | tf_op jit(solution)/shard_map/ppermute | solution.py:23
  118.6 1.9 %collective-permute-done.16 = bf16[4,96,128]{2,1,0:T(8,128)(2,1)S(1)} collective-permute-done((bf16[4,96,128]{2,1,0:T(8,128)(2,1)S(1)}, bf16[4,96,128]{2,1,0:T(8,128)(2,1)S(1)}, u32[]{:S(2)}, u32[]{:S(2)}) %collective-permute-start.16) | collective-permute-done | bytes 98336 | tf_op jit(solution)/shard_map/ppermute | solution.py:23
  120.8 2.3 %fusion.30 = (bf16[8,96,128]{2,1,0:T(8,128)(2,1)S(1)}, f32[8,96,128]{2,1,0:T(8,128)S(1)}) fusion(f32[8,96,128]{2,1,0:T(8,128)S(1)} %copy-done.9, f32[1,8,96,128]{3,2,1,0:T(8,128)S(1)} %copy-done.4, f32[8,96,128]{2,0,1:T(8,128)S(1)} %fusion.25, bf16[26,96,128]{2,1,0:T(8,128)(2,1)S(1)} %get-tuple-element.85, bf16[8,96,12,96]{3,1,2,0:T(8,128)(2,1)S(1)} %copy-done.3, ...), kind=kOutput, calls=%fused_computation.50 | convolution fusion | flops 493535232 | bytes 6242304 | tf_op jit(solution)/shard_map/kamb,mbr->kar/dot_general | solution.py:173
  123.6 1.9 %collective-permute-start.18 = (bf16[3,96,128]{2,1,0:T(8,128)(2,1)S(1)}, bf16[3,96,128]{2,1,0:T(8,128)(2,1)S(1)}, u32[]{:S(2)}, u32[]{:S(2)}) collective-permute-start(bf16[3,96,128]{2,1,0:T(8,128)(2,1)S(1)} %get-tuple-element.60), channel_id=1, source_target_pairs={{1,0},{2,1},{3,2},{4,3},{5,4},{6,5},{7,6},{8,7},{9,8},{10,9},{11,1... | collective-permute-start | bytes 221192 | tf_op jit(solution)/shard_map/ppermute | solution.py:18
  125.5 9.9 %collective-permute-start.17 = (bf16[3,96,128]{2,1,0:T(8,128)(2,1)S(1)}, bf16[3,96,128]{2,1,0:T(8,128)(2,1)S(1)}, u32[]{:S(2)}, u32[]{:S(2)}) collective-permute-start(bf16[3,96,128]{2,1,0:T(8,128)(2,1)S(1)} %get-tuple-element.61), channel_id=1, source_target_pairs={{0,1},{1,2},{2,3},{3,4},{4,5},{5,6},{6,7},{7,8},{8,9},{9,10},{10,1... | collective-permute-start | bytes 221192 | tf_op jit(solution)/shard_map/ppermute | solution.py:18
  135.8 1.9 %collective-permute-start.19 = (bf16[4,96,128]{2,1,0:T(8,128)(2,1)S(1)}, bf16[4,96,128]{2,1,0:T(8,128)(2,1)S(1)}, u32[]{:S(2)}, u32[]{:S(2)}) collective-permute-start(bf16[4,96,128]{2,1,0:T(8,128)(2,1)S(1)} %pad_maximum_fusion.43), channel_id=1, source_target_pairs={{0,16},{16,32},{32,48},{48,64},{64,80},{80,96},{96,112},{112,128},... | collective-permute-start | bytes 294920 | tf_op jit(solution)/shard_map/ppermute | solution.py:23
  137.8 1.9 %collective-permute-start.20 = (bf16[4,96,128]{2,1,0:T(8,128)(2,1)S(1)}, bf16[4,96,128]{2,1,0:T(8,128)(2,1)S(1)}, u32[]{:S(2)}, u32[]{:S(2)}) collective-permute-start(bf16[4,96,128]{2,1,0:T(8,128)(2,1)S(1)} %pad_maximum_fusion.44), channel_id=1, source_target_pairs={{0,32},{16,48},{32,64},{48,80},{64,96},{80,112},{96,128},{112,144}... | collective-permute-start | bytes 294920 | tf_op jit(solution)/shard_map/ppermute | solution.py:23
  139.7 1.9 %collective-permute-start.21 = (bf16[4,96,128]{2,1,0:T(8,128)(2,1)S(1)}, bf16[4,96,128]{2,1,0:T(8,128)(2,1)S(1)}, u32[]{:S(2)}, u32[]{:S(2)}) collective-permute-start(bf16[4,96,128]{2,1,0:T(8,128)(2,1)S(1)} %pad_maximum_fusion.45), channel_id=1, source_target_pairs={{0,48},{16,64},{32,80},{48,96},{64,112},{80,128},{96,144},{112,160... | collective-permute-start | bytes 294920 | tf_op jit(solution)/shard_map/ppermute | solution.py:23
  141.7 8.7 %collective-permute-start.22 = (bf16[4,96,128]{2,1,0:T(8,128)(2,1)S(1)}, bf16[4,96,128]{2,1,0:T(8,128)(2,1)S(1)}, u32[]{:S(2)}, u32[]{:S(2)}) collective-permute-start(bf16[4,96,128]{2,1,0:T(8,128)(2,1)S(1)} %pad_maximum_fusion.46), channel_id=1, source_target_pairs={{0,464},{16,480},{32,496},{48,0},{64,16},{80,32},{96,48},{112,64},... | collective-permute-start | bytes 294920 | tf_op jit(solution)/shard_map/ppermute | solution.py:23
  150.5 4.3 %collective-permute-start.23 = (bf16[4,96,128]{2,1,0:T(8,128)(2,1)S(1)}, bf16[4,96,128]{2,1,0:T(8,128)(2,1)S(1)}, u32[]{:S(2)}, u32[]{:S(2)}) collective-permute-start(bf16[4,96,128]{2,1,0:T(8,128)(2,1)S(1)} %pad_maximum_fusion.47), channel_id=1, source_target_pairs={{0,480},{16,496},{32,0},{48,16},{64,32},{80,48},{96,64},{112,80},{... | collective-permute-start | bytes 294920 | tf_op jit(solution)/shard_map/ppermute | solution.py:23
  154.8 1.9 %collective-permute-start.24 = (bf16[4,96,128]{2,1,0:T(8,128)(2,1)S(1)}, bf16[4,96,128]{2,1,0:T(8,128)(2,1)S(1)}, u32[]{:S(2)}, u32[]{:S(2)}) collective-permute-start(bf16[4,96,128]{2,1,0:T(8,128)(2,1)S(1)} %pad_maximum_fusion.48), channel_id=1, source_target_pairs={{0,496},{16,0},{32,16},{48,32},{64,48},{80,64},{96,80},{112,96},{1... | collective-permute-start | bytes 294920 | tf_op jit(solution)/shard_map/ppermute | solution.py:23
  157.0 1.9 %collective-permute-done.24 = bf16[4,96,128]{2,1,0:T(8,128)(2,1)S(1)} collective-permute-done((bf16[4,96,128]{2,1,0:T(8,128)(2,1)S(1)}, bf16[4,96,128]{2,1,0:T(8,128)(2,1)S(1)}, u32[]{:S(2)}, u32[]{:S(2)}) %collective-permute-start.24) | collective-permute-done | bytes 98336 | tf_op jit(solution)/shard_map/ppermute | solution.py:23
  159.2 3.1 %fusion.15 = f32[1,8,96,128]{3,2,1,0:T(8,128)} fusion(f32[8,96,128]{2,1,0:T(8,128)S(1)} %get-tuple-element.133, bf16[8,96,12,96]{3,1,2,0:T(8,128)(2,1)S(1)} %copy-done.3, bf16[8,96,14,96]{3,1,2,0:T(8,128)(2,1)S(1)} %bitcast_add_fusion, bf16[26,96,128]{2,1,0:T(8,128)(2,1)S(1)} %get-tuple-element.73, f32[8,96,128]{2,0,1:T(8,128)S(1)} %fusion.23, ...), kind=kOutput, calls=%fused_computation.24 | convolution fusion | flops 494125056 | bytes 6438912 | tf_op jit(solution)/shard_map/kamb,mbr->kar/dot_general | solution.py:173
  (129 shorter events, 5.3 us)
Async XLA Ops:
  0.0 19.8 %copy-start = (bf16[1,1,6,2,96,96]{5,4,3,2,1,0:T(8,128)(2,1)S(1)}, bf16[1,1,6,2,96,96]{5,4,3,2,1,0:T(8,128)(2,1)}, u32[]{:S(2)}) copy-start(bf16[1,1,6,2,96,96]{5,4,3,2,1,0:T(8,128)(2,1)} %param.11) | copy-start | bytes 663556
  1.1 20.2 %copy-start.2 = (bf16[8,96,128]{2,1,0:T(8,128)(2,1)}, bf16[8,96,128]{2,1,0:T(8,128)(2,1)S(1)}, u32[]{:S(2)}) copy-start(bf16[8,96,128]{2,1,0:T(8,128)(2,1)S(1)} %fusion.29.probe_ref) | copy-start | bytes 589828
  1.1 37.9 %collective-permute-start.2 = (bf16[3,96,128]{2,1,0:T(8,128)(2,1)S(1)}, bf16[3,96,128]{2,1,0:T(8,128)(2,1)S(1)}, u32[]{:S(2)}, u32[]{:S(2)}) collective-permute-start(bf16[3,96,128]{2,1,0:T(8,128)(2,1)S(1)} %get-tuple-element.70), channel_id=1, source_target_pairs={{1,0},{2,1},{3,2},{4,3},{5,4},{6,5},{7,6},{8,7},{9,8},{10,9},{11,1... | collective-permute-start | bytes 221192 | tf_op jit(solution)/shard_map/ppermute | solution.py:18
  3.8 53.1 %collective-permute-start.1 = (bf16[3,96,128]{2,1,0:T(8,128)(2,1)S(1)}, bf16[3,96,128]{2,1,0:T(8,128)(2,1)S(1)}, u32[]{:S(2)}, u32[]{:S(2)}) collective-permute-start(bf16[3,96,128]{2,1,0:T(8,128)(2,1)S(1)} %get-tuple-element.71), channel_id=1, source_target_pairs={{0,1},{1,2},{2,3},{3,4},{4,5},{5,6},{6,7},{7,8},{8,9},{9,10},{10,1... | collective-permute-start | bytes 221192 | tf_op jit(solution)/shard_map/ppermute | solution.py:18
  14.0 16.7 %copy-start.8 = (s32[1,1,6]{2,1,0:T(1,128)S(1)}, s32[1,1,6]{2,1,0:T(1,128)}, u32[]{:S(2)}) copy-start(s32[1,1,6]{2,1,0:T(1,128)} %param.10) | copy-start | bytes 76
  14.0 19.8 %collective-permute-start = (bf16[3,4,96,96]{3,2,1,0:T(8,128)(2,1)S(1)}, bf16[3,4,96,96]{3,2,1,0:T(8,128)(2,1)S(1)}, u32[]{:S(2)}, u32[]{:S(2)}) collective-permute-start(bf16[3,4,96,96]{3,2,1,0:T(8,128)(2,1)S(1)} %slice_bitcast_fusion), channel_id=1, source_target_pairs={{0,1},{1,2},{2,3},{3,4},{4,5},{5,6},{6,7},{7,8},{8,9},{9,10},{10,1... | collective-permute-start | bytes 663560 | tf_op jit(solution)/shard_map/ppermute | solution.py:18
  20.2 15.6 %copy-start.1 = (bf16[1,8,4,96,96]{4,3,2,1,0:T(8,128)(2,1)S(1)}, bf16[1,8,4,96,96]{4,3,2,1,0:T(8,128)(2,1)}, u32[]{:S(2)}) copy-start(bf16[1,8,4,96,96]{4,3,2,1,0:T(8,128)(2,1)} %param.8) | copy-start | bytes 1769476
  21.3 40.8 %collective-permute-start.8 = (bf16[11,96,128]{2,1,0:T(8,128)(2,1)S(1)}, bf16[11,96,128]{2,1,0:T(8,128)(2,1)S(1)}, u32[]{:S(2)}, u32[]{:S(2)}) collective-permute-start(bf16[11,96,128]{2,1,0:T(8,128)(2,1)S(1)} %get-tuple-element.64), channel_id=1, source_target_pairs={{0,496},{16,0},{32,16},{48,32},{64,48},{80,64},{96,80},{112,96},{1... | collective-permute-start | bytes 811016 | tf_op jit(solution)/shard_map/ppermute | solution.py:23
  28.6 38.6 %collective-permute-start.4 = (bf16[11,96,128]{2,1,0:T(8,128)(2,1)}, bf16[11,96,128]{2,1,0:T(8,128)(2,1)}, u32[]{:S(2)}, u32[]{:S(2)}) collective-permute-start(bf16[11,96,128]{2,1,0:T(8,128)(2,1)} %get-tuple-element.65), channel_id=1, source_target_pairs={{0,32},{16,48},{32,64},{48,80},{64,96},{80,112},{96,128},{112,144}... | collective-permute-start | bytes 811016 | tf_op jit(solution)/shard_map/ppermute | solution.py:23
  33.8 33.4 %collective-permute-start.5 = (bf16[11,96,128]{2,1,0:T(8,128)(2,1)}, bf16[11,96,128]{2,1,0:T(8,128)(2,1)}, u32[]{:S(2)}, u32[]{:S(2)}) collective-permute-start(bf16[11,96,128]{2,1,0:T(8,128)(2,1)} %get-tuple-element.66), channel_id=1, source_target_pairs={{0,48},{16,64},{32,80},{48,96},{64,112},{80,128},{96,144},{112,160... | collective-permute-start | bytes 811016 | tf_op jit(solution)/shard_map/ppermute | solution.py:23
  39.1 35.1 %copy-start.6 = (bf16[3,96,128]{2,1,0:T(8,128)(2,1)}, bf16[3,96,128]{2,1,0:T(8,128)(2,1)S(1)}, u32[]{:S(2)}) copy-start(bf16[3,96,128]{2,1,0:T(8,128)(2,1)S(1)} %collective-permute-done.2.high_ref) | copy-start | bytes 221188
  39.1 28.2 %collective-permute-start.6 = (bf16[11,96,128]{2,1,0:T(8,128)(2,1)}, bf16[11,96,128]{2,1,0:T(8,128)(2,1)}, u32[]{:S(2)}, u32[]{:S(2)}) collective-permute-start(bf16[11,96,128]{2,1,0:T(8,128)(2,1)} %get-tuple-element.67), channel_id=1, source_target_pairs={{0,464},{16,480},{32,496},{48,0},{64,16},{80,32},{96,48},{112,64},... | collective-permute-start | bytes 811016 | tf_op jit(solution)/shard_map/ppermute | solution.py:23
  56.9 7.3 %copy-start.7 = (bf16[3,96,128]{2,1,0:T(8,128)(2,1)}, bf16[3,96,128]{2,1,0:T(8,128)(2,1)S(1)}, u32[]{:S(2)}) copy-start(bf16[3,96,128]{2,1,0:T(8,128)(2,1)S(1)} %collective-permute-done.1.low_ref) | copy-start | bytes 221188
  56.9 12.6 %collective-permute-start.7 = (bf16[11,96,128]{2,1,0:T(8,128)(2,1)}, bf16[11,96,128]{2,1,0:T(8,128)(2,1)}, u32[]{:S(2)}, u32[]{:S(2)}) collective-permute-start(bf16[11,96,128]{2,1,0:T(8,128)(2,1)} %get-tuple-element.68), channel_id=1, source_target_pairs={{0,480},{16,496},{32,0},{48,16},{64,32},{80,48},{96,64},{112,80},{... | collective-permute-start | bytes 811016 | tf_op jit(solution)/shard_map/ppermute | solution.py:23
  62.2 2.0 %copy-start.5 = (bf16[11,96,128]{2,1,0:T(8,128)(2,1)}, bf16[11,96,128]{2,1,0:T(8,128)(2,1)S(1)}, u32[]{:S(2)}) copy-start(bf16[11,96,128]{2,1,0:T(8,128)(2,1)S(1)} %collective-permute-done.8.refs_5_) | copy-start | bytes 811012
  62.2 12.0 %collective-permute-start.3 = (bf16[11,96,128]{2,1,0:T(8,128)(2,1)}, bf16[11,96,128]{2,1,0:T(8,128)(2,1)}, u32[]{:S(2)}, u32[]{:S(2)}) collective-permute-start(bf16[11,96,128]{2,1,0:T(8,128)(2,1)} %get-tuple-element.69), channel_id=1, source_target_pairs={{0,16},{16,32},{32,48},{48,64},{64,80},{80,96},{96,112},{112,128},... | collective-permute-start | bytes 811016 | tf_op jit(solution)/shard_map/ppermute | solution.py:23
  84.2 36.5 %copy-start.3 = (bf16[8,96,12,96]{3,1,2,0:T(8,128)(2,1)S(1)}, bf16[8,96,12,96]{3,1,2,0:T(8,128)(2,1)}, u32[]{:S(2)}) copy-start(bf16[8,96,12,96]{3,1,2,0:T(8,128)(2,1)} %multiply_bitcast_fusion) | copy-start | bytes 5308420
  84.2 36.5 %copy-start.4 = (f32[1,8,96,128]{3,2,1,0:T(8,128)S(1)}, f32[1,8,96,128]{3,2,1,0:T(8,128)}, u32[]{:S(2)}) copy-start(f32[1,8,96,128]{3,2,1,0:T(8,128)} %param.7) | copy-start | bytes 1179652
  84.2 36.5 %copy-start.9 = (f32[8,96,128]{2,1,0:T(8,128)S(1)}, f32[8,96,128]{2,1,0:T(8,128)}, u32[]{:S(2)}) copy-start(f32[8,96,128]{2,1,0:T(8,128)} %get-tuple-element.131) | copy-start | bytes 1179652
  84.3 27.8 %collective-permute-start.10 = (bf16[3,96,128]{2,1,0:T(8,128)(2,1)S(1)}, bf16[3,96,128]{2,1,0:T(8,128)(2,1)S(1)}, u32[]{:S(2)}, u32[]{:S(2)}) collective-permute-start(bf16[3,96,128]{2,1,0:T(8,128)(2,1)S(1)} %get-tuple-element.62), channel_id=1, source_target_pairs={{1,0},{2,1},{3,2},{4,3},{5,4},{6,5},{7,6},{8,7},{9,8},{10,9},{11,1... | collective-permute-start | bytes 221192 | tf_op jit(solution)/shard_map/ppermute | solution.py:18
  86.5 16.8 %collective-permute-start.9 = (bf16[3,96,128]{2,1,0:T(8,128)(2,1)S(1)}, bf16[3,96,128]{2,1,0:T(8,128)(2,1)S(1)}, u32[]{:S(2)}, u32[]{:S(2)}) collective-permute-start(bf16[3,96,128]{2,1,0:T(8,128)(2,1)S(1)} %get-tuple-element.63), channel_id=1, source_target_pairs={{0,1},{1,2},{2,3},{3,4},{4,5},{5,6},{6,7},{7,8},{8,9},{9,10},{10,1... | collective-permute-start | bytes 221192 | tf_op jit(solution)/shard_map/ppermute | solution.py:18
  97.4 19.0 %collective-permute-start.11 = (bf16[4,96,128]{2,1,0:T(8,128)(2,1)S(1)}, bf16[4,96,128]{2,1,0:T(8,128)(2,1)S(1)}, u32[]{:S(2)}, u32[]{:S(2)}) collective-permute-start(bf16[4,96,128]{2,1,0:T(8,128)(2,1)S(1)} %pad_maximum_fusion.37), channel_id=1, source_target_pairs={{0,16},{16,32},{32,48},{48,64},{64,80},{80,96},{96,112},{112,128},... | collective-permute-start | bytes 294920 | tf_op jit(solution)/shard_map/ppermute | solution.py:23
  99.3 19.0 %collective-permute-start.12 = (bf16[4,96,128]{2,1,0:T(8,128)(2,1)S(1)}, bf16[4,96,128]{2,1,0:T(8,128)(2,1)S(1)}, u32[]{:S(2)}, u32[]{:S(2)}) collective-permute-start(bf16[4,96,128]{2,1,0:T(8,128)(2,1)S(1)} %pad_maximum_fusion.38), channel_id=1, source_target_pairs={{0,32},{16,48},{32,64},{48,80},{64,96},{80,112},{96,128},{112,144}... | collective-permute-start | bytes 294920 | tf_op jit(solution)/shard_map/ppermute | solution.py:23
  101.3 17.1 %collective-permute-start.13 = (bf16[4,96,128]{2,1,0:T(8,128)(2,1)S(1)}, bf16[4,96,128]{2,1,0:T(8,128)(2,1)S(1)}, u32[]{:S(2)}, u32[]{:S(2)}) collective-permute-start(bf16[4,96,128]{2,1,0:T(8,128)(2,1)S(1)} %pad_maximum_fusion.39), channel_id=1, source_target_pairs={{0,48},{16,64},{32,80},{48,96},{64,112},{80,128},{96,144},{112,160... | collective-permute-start | bytes 294920 | tf_op jit(solution)/shard_map/ppermute | solution.py:23
  103.3 15.1 %collective-permute-start.14 = (bf16[4,96,128]{2,1,0:T(8,128)(2,1)S(1)}, bf16[4,96,128]{2,1,0:T(8,128)(2,1)S(1)}, u32[]{:S(2)}, u32[]{:S(2)}) collective-permute-start(bf16[4,96,128]{2,1,0:T(8,128)(2,1)S(1)} %pad_maximum_fusion.40), channel_id=1, source_target_pairs={{0,464},{16,480},{32,496},{48,0},{64,16},{80,32},{96,48},{112,64},... | collective-permute-start | bytes 294920 | tf_op jit(solution)/shard_map/ppermute | solution.py:23
  112.1 6.5 %collective-permute-start.15 = (bf16[4,96,128]{2,1,0:T(8,128)(2,1)S(1)}, bf16[4,96,128]{2,1,0:T(8,128)(2,1)S(1)}, u32[]{:S(2)}, u32[]{:S(2)}) collective-permute-start(bf16[4,96,128]{2,1,0:T(8,128)(2,1)S(1)} %pad_maximum_fusion.41), channel_id=1, source_target_pairs={{0,480},{16,496},{32,0},{48,16},{64,32},{80,48},{96,64},{112,80},{... | collective-permute-start | bytes 294920 | tf_op jit(solution)/shard_map/ppermute | solution.py:23
  116.4 4.1 %collective-permute-start.16 = (bf16[4,96,128]{2,1,0:T(8,128)(2,1)S(1)}, bf16[4,96,128]{2,1,0:T(8,128)(2,1)S(1)}, u32[]{:S(2)}, u32[]{:S(2)}) collective-permute-start(bf16[4,96,128]{2,1,0:T(8,128)(2,1)S(1)} %pad_maximum_fusion.42), channel_id=1, source_target_pairs={{0,496},{16,0},{32,16},{48,32},{64,48},{80,64},{96,80},{112,96},{1... | collective-permute-start | bytes 294920 | tf_op jit(solution)/shard_map/ppermute | solution.py:23
  123.6 26.9 %collective-permute-start.18 = (bf16[3,96,128]{2,1,0:T(8,128)(2,1)S(1)}, bf16[3,96,128]{2,1,0:T(8,128)(2,1)S(1)}, u32[]{:S(2)}, u32[]{:S(2)}) collective-permute-start(bf16[3,96,128]{2,1,0:T(8,128)(2,1)S(1)} %get-tuple-element.60), channel_id=1, source_target_pairs={{1,0},{2,1},{3,2},{4,3},{5,4},{6,5},{7,6},{8,7},{9,8},{10,9},{11,1... | collective-permute-start | bytes 221192 | tf_op jit(solution)/shard_map/ppermute | solution.py:18
  125.5 16.2 %collective-permute-start.17 = (bf16[3,96,128]{2,1,0:T(8,128)(2,1)S(1)}, bf16[3,96,128]{2,1,0:T(8,128)(2,1)S(1)}, u32[]{:S(2)}, u32[]{:S(2)}) collective-permute-start(bf16[3,96,128]{2,1,0:T(8,128)(2,1)S(1)} %get-tuple-element.61), channel_id=1, source_target_pairs={{0,1},{1,2},{2,3},{3,4},{4,5},{5,6},{6,7},{7,8},{8,9},{9,10},{10,1... | collective-permute-start | bytes 221192 | tf_op jit(solution)/shard_map/ppermute | solution.py:18
  135.8 19.0 %collective-permute-start.19 = (bf16[4,96,128]{2,1,0:T(8,128)(2,1)S(1)}, bf16[4,96,128]{2,1,0:T(8,128)(2,1)S(1)}, u32[]{:S(2)}, u32[]{:S(2)}) collective-permute-start(bf16[4,96,128]{2,1,0:T(8,128)(2,1)S(1)} %pad_maximum_fusion.43), channel_id=1, source_target_pairs={{0,16},{16,32},{32,48},{48,64},{64,80},{80,96},{96,112},{112,128},... | collective-permute-start | bytes 294920 | tf_op jit(solution)/shard_map/ppermute | solution.py:23
  137.8 19.0 %collective-permute-start.20 = (bf16[4,96,128]{2,1,0:T(8,128)(2,1)S(1)}, bf16[4,96,128]{2,1,0:T(8,128)(2,1)S(1)}, u32[]{:S(2)}, u32[]{:S(2)}) collective-permute-start(bf16[4,96,128]{2,1,0:T(8,128)(2,1)S(1)} %pad_maximum_fusion.44), channel_id=1, source_target_pairs={{0,32},{16,48},{32,64},{48,80},{64,96},{80,112},{96,128},{112,144}... | collective-permute-start | bytes 294920 | tf_op jit(solution)/shard_map/ppermute | solution.py:23
  139.7 17.1 %collective-permute-start.21 = (bf16[4,96,128]{2,1,0:T(8,128)(2,1)S(1)}, bf16[4,96,128]{2,1,0:T(8,128)(2,1)S(1)}, u32[]{:S(2)}, u32[]{:S(2)}) collective-permute-start(bf16[4,96,128]{2,1,0:T(8,128)(2,1)S(1)} %pad_maximum_fusion.45), channel_id=1, source_target_pairs={{0,48},{16,64},{32,80},{48,96},{64,112},{80,128},{96,144},{112,160... | collective-permute-start | bytes 294920 | tf_op jit(solution)/shard_map/ppermute | solution.py:23
  141.7 15.1 %collective-permute-start.22 = (bf16[4,96,128]{2,1,0:T(8,128)(2,1)S(1)}, bf16[4,96,128]{2,1,0:T(8,128)(2,1)S(1)}, u32[]{:S(2)}, u32[]{:S(2)}) collective-permute-start(bf16[4,96,128]{2,1,0:T(8,128)(2,1)S(1)} %pad_maximum_fusion.46), channel_id=1, source_target_pairs={{0,464},{16,480},{32,496},{48,0},{64,16},{80,32},{96,48},{112,64},... | collective-permute-start | bytes 294920 | tf_op jit(solution)/shard_map/ppermute | solution.py:23
  150.5 6.5 %collective-permute-start.23 = (bf16[4,96,128]{2,1,0:T(8,128)(2,1)S(1)}, bf16[4,96,128]{2,1,0:T(8,128)(2,1)S(1)}, u32[]{:S(2)}, u32[]{:S(2)}) collective-permute-start(bf16[4,96,128]{2,1,0:T(8,128)(2,1)S(1)} %pad_maximum_fusion.47), channel_id=1, source_target_pairs={{0,480},{16,496},{32,0},{48,16},{64,32},{80,48},{96,64},{112,80},{... | collective-permute-start | bytes 294920 | tf_op jit(solution)/shard_map/ppermute | solution.py:23
  154.8 4.1 %collective-permute-start.24 = (bf16[4,96,128]{2,1,0:T(8,128)(2,1)S(1)}, bf16[4,96,128]{2,1,0:T(8,128)(2,1)S(1)}, u32[]{:S(2)}, u32[]{:S(2)}) collective-permute-start(bf16[4,96,128]{2,1,0:T(8,128)(2,1)S(1)} %pad_maximum_fusion.48), channel_id=1, source_target_pairs={{0,496},{16,0},{32,16},{48,32},{64,48},{80,64},{96,80},{112,96},{1... | collective-permute-start | bytes 294920 | tf_op jit(solution)/shard_map/ppermute | solution.py:23

commit v9 on v8

--- a/solution.py
+++ b/solution.py
@@ -23,40 +23,35 @@
     return lax.ppermute(value, axis, [(i, (i + steps) % count) for i in range(count)])
 
 
-def unpack_first(pick_ref, low_ref, probe_ref, high_ref, *refs):
+def unpack_first(pick_ref, *refs):
     messages = refs[:-3]
-    stacked_ref, landed_ref, index_ref = refs[-3:]
-    edge = low_ref.shape[0]
-    knots = probe_ref.shape[0]
+    fetched_ref, landed_ref, index_ref = refs[-3:]
     slots = pick_ref.shape[1]
-    stacked_ref[:edge] = low_ref[...]
-    stacked_ref[edge : edge + knots] = probe_ref[...]
-    stacked_ref[edge + knots : 2 * edge + knots] = high_ref[...]
-    base = 2 * edge + knots
+    knots = messages[0].shape[0] - slots - 1
     for t, message in enumerate(messages):
         for slot in range(slots):
             knot = pick_ref[t, slot]
             row = message[jnp.minimum(jnp.maximum(knot, 0), knots - 1)]
-            stacked_ref[base + t * slots + slot] = jnp.where(knot >= 0, row, jnp.zeros_like(row))
+            fetched_ref[t * slots + slot] = jnp.where(knot >= 0, row, jnp.zeros_like(row))
             landed_ref[t * slots + slot] = message[knots + slot]
         index_ref[t] = message[knots + slots, 0, :]
 
 
-def unpack_call(pick, low, probe, high, messages):
-    knots, params, probes = probe.shape
+def unpack_call(pick, messages):
+    rows, params, probes = messages[0].shape
     slots = pick.shape[1]
     count = len(messages)
     vmem = pl.BlockSpec(memory_space=pltpu.VMEM)
     return pl.pallas_call(
         unpack_first,
         out_shape=(
-            jax.ShapeDtypeStruct((knots + 2 * low.shape[0] + count * slots, params, probes), probe.dtype),
-            jax.ShapeDtypeStruct((count * slots, params, probes), probe.dtype),
-            jax.ShapeDtypeStruct((count, probes), probe.dtype),
+            jax.ShapeDtypeStruct((count * slots, params, probes), messages[0].dtype),
+            jax.ShapeDtypeStruct((count * slots, params, probes), messages[0].dtype),
+            jax.ShapeDtypeStruct((count, probes), messages[0].dtype),
         ),
-        in_specs=[pl.BlockSpec(memory_space=pltpu.SMEM)] + [vmem] * (3 + count),
+        in_specs=[pl.BlockSpec(memory_space=pltpu.SMEM)] + [vmem] * count,
         out_specs=(vmem, vmem, vmem),
-    )(pick, low, probe, high, *messages)
+    )(pick, *messages)
 
 
 def body(right_side, band_blocks, knot_pairs, pair_counts, cross_blocks):
@@ -159,7 +154,7 @@
         low = shifted_open(probe_bf[knots - 3 :], "seg", 1)
         high = shifted_open(probe_bf[:3], "seg", -1)
         if answer_pick is None:
-            stacked, landed, heard = unpack_call(first_pick, low, probe_bf, high, received)
+            first_fetched, landed, heard = unpack_call(first_pick, received)
             heard = heard[:, :slots].astype(jnp.float32)
             answer_pick = jnp.concatenate(
                 [(heard[shifts.index(-s)][:, None] == knot_vals[None, :]) for s in shifts], axis=0
@@ -170,9 +165,17 @@
                 [low, probe_bf, high] + [fetched[b] for b in fetch_order], axis=0
             )
             landed = jnp.concatenate(landed, axis=0)
-        summed = jnp.einsum(
-            "kamb,mbr->kar", weight, stacked, preferred_element_type=jnp.float32
-        )
+        if turn == 0:
+            extended = jnp.concatenate([low, probe_bf, high], axis=0)
+            summed = jnp.einsum(
+                "kamb,mbr->kar", band_weight, extended, preferred_element_type=jnp.float32
+            ) + jnp.einsum(
+                "kamb,mbr->kar", fetch_weight, first_fetched, preferred_element_type=jnp.float32
+            )
+        else:
+            summed = jnp.einsum(
+                "kamb,mbr->kar", weight, stacked, preferred_element_type=jnp.float32
+            )
         cross = jnp.einsum("ks,spr->kpr", land_place, landed, preferred_element_type=jnp.float32)
         residual = residual - (summed + cross)
         coeff_next = 1.0 / (2.0 * center / radius - coeff)

time: 164 us -> 157 us (0.957)
  starting transfers between devices: 117 us -> 112 us
  waiting for transfers between devices: 11 us -> 7.8 us
  local copies, waits for them, and re-layouts: 6.79 us -> 8.69 us
    ppermute x18, starting transfers between devices: 77.4 us -> 67.9 us  [shifted_ring(): lax.ppermute(value, axis, [(i, (i + steps) % count) for i in range(count)])]
    ppermute x18, waiting for transfers between devices: 11 us -> 4.14 us  [shifted_ring(): lax.ppermute(value, axis, [(i, (i + steps) % count) for i in range(count)])]
    dot_general x3 -> x2, matrix products: 10.3 us -> 5.39 us  [body(): jnp.einsum('kamb,mbr->kar', weight, stacked, preferred_element_type=jnp.f...]
    dot_general x0 -> x2, matrix products: none -> 4.71 us  [the longest x1 2.56 us: body(): jnp.einsum('kamb,mbr->kar', band_weight, extended, preferred_element_type...]
    ppermute x7, starting transfers between devices: 39.2 us -> 43.7 us  [shifted_open(): lax.ppermute(value, axis, [(source, source + steps) for source in range(i...]
    ppermute x7, waiting for transfers between devices: 0.02 us -> 3.66 us  [shifted_open(): lax.ppermute(value, axis, [(source, source + steps) for source in range(i...]
  transfers between devices with their start and end apart: 25 -> 25, of which waited for: 6 -> 5; matrix products, arithmetic and copies ran while one was open for 10% -> 14% of each run, Pallas kernels for 0% -> 1%
where the time goes in v9:
time: 157 us; the launch traced here: 156 us
  starting transfers between devices  112 us (71%)
  matrix products  13.8 us (9%)
  other arithmetic  10.6 us (7%)
  local copies, waits for them, and re-layouts  8.69 us (6%)
  waiting for transfers between devices  7.8 us (5%)
  Pallas kernels  2.21 us (1%)
    ppermute x18, starting transfers between devices, shifted_ring(): lax.ppermute(value, axis, [(i, (i + steps) % count) for i in range(count)])  67.9 us
    ppermute x7, starting transfers between devices, shifted_open(): lax.ppermute(value, axis, [(source, source + steps) for source in range(i...  43.7 us
    dot_general x2, matrix products, body(): jnp.einsum('kamb,mbr->kar', weight, stacked, preferred_element_type=jnp.f...  5.39 us
    ppermute x18, waiting for transfers between devices, shifted_ring(): lax.ppermute(value, axis, [(i, (i + steps) % count) for i in range(count)])  4.14 us
    ppermute x7, waiting for transfers between devices, shifted_open(): lax.ppermute(value, axis, [(source, source + steps) for source in range(i...  3.66 us
    add x1, other arithmetic, body(): band_weight + jnp.einsum('km,kba->kamb', place, lower_blocks[3 - step:3 -...  3.17 us
  transfers between devices with their start and end apart: 25, of which 5 were waited for; matrix products, arithmetic and copies ran while one was open for 14% of the time, Pallas kernels for 1%

profile of v9, /device:TPU:24, one launch (start us, length us, event | category | flops | bytes accessed | tf_op | source)
XLA Modules:
  0.0 155.6 jit_solution(14058132272705233918)
XLA Ops:
  0.0 1.0 slice_bitcast_fusion
  1.0 8.8 %collective-permute-start = (bf16[3,4,96,96]{3,2,1,0:T(8,128)(2,1)S(1)}, bf16[3,4,96,96]{3,2,1,0:T(8,128)(2,1)S(1)}, u32[]{:S(2)}, u32[]{:S(2)}) collective-permute-start(bf16[3,4,96,96]{3,2,1,0:T(8,128)(2,1)S(1)} %slice_bitcast_fusion), channel_id=1, source_target_pairs={{0,1},{1,2},{2,3},{3,4},{4,5},{5,6},{6,7},{7,8},{8,9},{9,10},{10,1... | collective-permute-start | bytes 663560 | tf_op jit(solution)/shard_map/ppermute | solution.py:18
  9.8 0.7 iota_compare_fusion.8
  10.7 0.8 fusion.88
  11.5 0.7 fusion.73
  12.5 1.0 fusion.27
  14.3 1.1 fusion.42
  15.4 7.9 %collective-permute-start.8 = (bf16[11,96,128]{2,1,0:T(8,128)(2,1)S(1)}, bf16[11,96,128]{2,1,0:T(8,128)(2,1)S(1)}, u32[]{:S(2)}, u32[]{:S(2)}) collective-permute-start(bf16[11,96,128]{2,1,0:T(8,128)(2,1)S(1)} %get-tuple-element.66), channel_id=1, source_target_pairs={{0,496},{16,0},{32,16},{48,32},{64,48},{80,64},{96,80},{112,96},{1... | collective-permute-start | bytes 811016 | tf_op jit(solution)/shard_map/ppermute | solution.py:23
  23.3 1.9 %collective-permute-start.4 = (bf16[11,96,128]{2,1,0:T(8,128)(2,1)}, bf16[11,96,128]{2,1,0:T(8,128)(2,1)}, u32[]{:S(2)}, u32[]{:S(2)}) collective-permute-start(bf16[11,96,128]{2,1,0:T(8,128)(2,1)} %get-tuple-element.67), channel_id=1, source_target_pairs={{0,32},{16,48},{32,64},{48,80},{64,96},{80,112},{96,128},{112,144}... | collective-permute-start | bytes 811016 | tf_op jit(solution)/shard_map/ppermute | solution.py:23
  25.2 1.9 %collective-permute-start.5 = (bf16[11,96,128]{2,1,0:T(8,128)(2,1)}, bf16[11,96,128]{2,1,0:T(8,128)(2,1)}, u32[]{:S(2)}, u32[]{:S(2)}) collective-permute-start(bf16[11,96,128]{2,1,0:T(8,128)(2,1)} %get-tuple-element.68), channel_id=1, source_target_pairs={{0,48},{16,64},{32,80},{48,96},{64,112},{80,128},{96,144},{112,160... | collective-permute-start | bytes 811016 | tf_op jit(solution)/shard_map/ppermute | solution.py:23
  27.2 7.8 %collective-permute-start.6 = (bf16[11,96,128]{2,1,0:T(8,128)(2,1)}, bf16[11,96,128]{2,1,0:T(8,128)(2,1)}, u32[]{:S(2)}, u32[]{:S(2)}) collective-permute-start(bf16[11,96,128]{2,1,0:T(8,128)(2,1)} %get-tuple-element.69), channel_id=1, source_target_pairs={{0,464},{16,480},{32,496},{48,0},{64,16},{80,32},{96,48},{112,64},... | collective-permute-start | bytes 811016 | tf_op jit(solution)/shard_map/ppermute | solution.py:23
  36.5 1.7 %multiply_bitcast_fusion = bf16[8,96,12,96]{3,1,2,0:T(8,128)(2,1)} fusion(bf16[12,8]{0,1:T(8,128)(2,1)S(1)} %copy.56, bf16[12,96,96]{2,1,0:T(8,128)(2,1)S(1)} %constant_dynamic-update-slice_fusion), kind=kLoop, calls=%fused_computation.6 | loop fusion | flops 884736 | bytes 1990848 | tf_op jit(solution)/shard_map/kf,fab->kafb/transpose | solution.py:105
  38.2 0.7 copy.63.pick_ref
  38.9 5.1 %collective-permute-start.7 = (bf16[11,96,128]{2,1,0:T(8,128)(2,1)}, bf16[11,96,128]{2,1,0:T(8,128)(2,1)}, u32[]{:S(2)}, u32[]{:S(2)}) collective-permute-start(bf16[11,96,128]{2,1,0:T(8,128)(2,1)} %get-tuple-element.70), channel_id=1, source_target_pairs={{0,480},{16,496},{32,0},{48,16},{64,32},{80,48},{96,64},{112,80},{... | collective-permute-start | bytes 811016 | tf_op jit(solution)/shard_map/ppermute | solution.py:23
  44.1 0.9 maximum_bitcast_fusion.3
  45.0 0.8 copy.52
  45.8 0.8 copy.53
  46.6 0.8 copy.54
  47.4 1.9 %collective-permute-start.3 = (bf16[11,96,128]{2,1,0:T(8,128)(2,1)}, bf16[11,96,128]{2,1,0:T(8,128)(2,1)}, u32[]{:S(2)}, u32[]{:S(2)}) collective-permute-start(bf16[11,96,128]{2,1,0:T(8,128)(2,1)} %get-tuple-element.71), channel_id=1, source_target_pairs={{0,16},{16,32},{32,48},{48,64},{64,80},{80,96},{96,112},{112,128},... | collective-permute-start | bytes 811016 | tf_op jit(solution)/shard_map/ppermute | solution.py:23
  49.3 3.2 %bitcast_add_fusion = bf16[8,96,14,96]{3,1,2,0:T(8,128)(2,1)S(1)} fusion(bf16[8,14]{1,0:T(8,128)(2,1)S(1)} %fusion.63, bf16[8,96,96]{1,2,0:T(8,128)(2,1)} %copy.54, bf16[8,14]{1,0:T(8,128)(2,1)S(1)} %get-tuple-element.139, bf16[8,96,96]{1,2,0:T(8,128)(2,1)} %copy.53, bf16[8,14]{1,0:T(8,128)(2,1)S(1)} %get-tuple-element.138, bf16[8,96,96]{1,2,0:T(8,128)(2,1)} %copy.52, ...), kind=kLoop, calls=%fused_computation.3 | loop fusion | flops 13418496 | bytes 3098144 | tf_op jit(solution)/shard_map/add | solution.py:94
  52.5 9.0 %collective-permute-start.1 = (bf16[3,96,128]{2,1,0:T(8,128)(2,1)}, bf16[3,96,128]{2,1,0:T(8,128)(2,1)S(1)}, u32[]{:S(2)}, u32[]{:S(2)}) collective-permute-start(bf16[3,96,128]{2,1,0:T(8,128)(2,1)} %get-tuple-element.64), channel_id=1, source_target_pairs={{0,1},{1,2},{2,3},{3,4},{4,5},{5,6},{6,7},{7,8},{8,9},{9,10},{10,1... | collective-permute-start | bytes 221192 | tf_op jit(solution)/shard_map/ppermute | solution.py:18
  61.6 1.9 %collective-permute-start.2 = (bf16[3,96,128]{2,1,0:T(8,128)(2,1)S(1)}, bf16[3,96,128]{2,1,0:T(8,128)(2,1)}, u32[]{:S(2)}, u32[]{:S(2)}) collective-permute-start(bf16[3,96,128]{2,1,0:T(8,128)(2,1)S(1)} %get-tuple-element.65), channel_id=1, source_target_pairs={{1,0},{2,1},{3,2},{4,3},{5,4},{6,5},{7,6},{8,7},{9,8},{10,9},{11,1... | collective-permute-start | bytes 221192 | tf_op jit(solution)/shard_map/ppermute | solution.py:18
  63.5 2.2 %shard_map.55 = (bf16[12,96,128]{2,1,0:T(8,128)(2,1)}, bf16[12,96,128]{2,1,0:T(8,128)(2,1)}, bf16[6,128]{1,0:T(8,128)(2,1)}) custom-call(s32[6,2]{1,0:T(8,128)} %copy.63.pick_ref, bf16[11,96,128]{2,1,0:T(8,128)(2,1)} %collective-permute-done.3.refs_0_, bf16[11,96,128]{2,1,0:T(8,128)(2,1)} %collective-permute-done.4.refs_1_, ...), custom_call_target="tpu_custom_call" | custom-call | tf_op jit(solution)/shard_map/pallas_call | solution.py:45
  65.7 0.7 slice_convert_fusion
  66.5 1.3 fusion.25
  67.8 2.1 %convolution_bitcast_fusion = f32[8,96,128]{2,1,0:T(8,128)S(1)} fusion(bf16[12,96,128]{2,1,0:T(8,128)(2,1)} %get-tuple-element.20, bf16[12,8]{0,1:T(8,128)(2,1)S(1)} %copy.56, bf16[12,96,96]{2,1,0:T(8,128)(2,1)} %copy-done.6), kind=kOutput, calls=%fused_computation.13 | convolution fusion | flops 227377152 | bytes 909504 | tf_op jit(solution)/shard_map/kamb,mbr->kar/dot_general | solution.py:172
  70.6 3.6 %collective-permute-done.2 = bf16[3,96,128]{2,1,0:T(8,128)(2,1)} collective-permute-done((bf16[3,96,128]{2,1,0:T(8,128)(2,1)S(1)}, bf16[3,96,128]{2,1,0:T(8,128)(2,1)}, u32[]{:S(2)}, u32[]{:S(2)}) %collective-permute-start.2) | collective-permute-done | bytes 73760 | tf_op jit(solution)/shard_map/ppermute | solution.py:18
  74.2 2.6 %fusion.49 = (bf16[8,96,128]{2,1,0:T(8,128)(2,1)S(1)}, f32[8,96,128]{2,1,0:T(8,128)}) fusion(f32[1,8,96,128]{3,2,1,0:T(8,128)S(1)} %copy-done.2, f32[8,96,128]{2,0,1:T(8,128)S(1)} %fusion.25, f32[8,96,128]{2,1,0:T(8,128)S(1)} %convolution_bitcast_fusion, bf16[8,96,14,96]{3,1,2,0:T(8,128)(2,1)S(1)} %bitcast_add_fusion, ...), kind=kOutput, calls=%fused_computation.134 | convolution fusion | flops 265273344 | bytes 4177920 | tf_op jit(solution)/shard_map/kamb,mbr->kar/dot_general | solution.py:170
  78.2 2.2 %collective-permute-start.10 = (bf16[3,96,128]{2,1,0:T(8,128)(2,1)S(1)}, bf16[3,96,128]{2,1,0:T(8,128)(2,1)S(1)}, u32[]{:S(2)}, u32[]{:S(2)}) collective-permute-start(bf16[3,96,128]{2,1,0:T(8,128)(2,1)S(1)} %get-tuple-element.62), channel_id=1, source_target_pairs={{1,0},{2,1},{3,2},{4,3},{5,4},{6,5},{7,6},{8,7},{9,8},{10,9},{11,1... | collective-permute-start | bytes 221192 | tf_op jit(solution)/shard_map/ppermute | solution.py:18
  80.4 9.9 %collective-permute-start.9 = (bf16[3,96,128]{2,1,0:T(8,128)(2,1)S(1)}, bf16[3,96,128]{2,1,0:T(8,128)(2,1)S(1)}, u32[]{:S(2)}, u32[]{:S(2)}) collective-permute-start(bf16[3,96,128]{2,1,0:T(8,128)(2,1)S(1)} %copy-done.8), channel_id=1, source_target_pairs={{0,1},{1,2},{2,3},{3,4},{4,5},{5,6},{6,7},{7,8},{8,9},{9,10},{10,1... | collective-permute-start | bytes 221192 | tf_op jit(solution)/shard_map/ppermute | solution.py:18
  90.6 1.9 %collective-permute-start.11 = (bf16[4,96,128]{2,1,0:T(8,128)(2,1)S(1)}, bf16[4,96,128]{2,1,0:T(8,128)(2,1)S(1)}, u32[]{:S(2)}, u32[]{:S(2)}) collective-permute-start(bf16[4,96,128]{2,1,0:T(8,128)(2,1)S(1)} %pad_maximum_fusion.30), channel_id=1, source_target_pairs={{0,16},{16,32},{32,48},{48,64},{64,80},{80,96},{96,112},{112,128},... | collective-permute-start | bytes 294920 | tf_op jit(solution)/shard_map/ppermute | solution.py:23
  92.6 1.9 %collective-permute-start.12 = (bf16[4,96,128]{2,1,0:T(8,128)(2,1)S(1)}, bf16[4,96,128]{2,1,0:T(8,128)(2,1)S(1)}, u32[]{:S(2)}, u32[]{:S(2)}) collective-permute-start(bf16[4,96,128]{2,1,0:T(8,128)(2,1)S(1)} %pad_maximum_fusion.31), channel_id=1, source_target_pairs={{0,32},{16,48},{32,64},{48,80},{64,96},{80,112},{96,128},{112,144}... | collective-permute-start | bytes 294920 | tf_op jit(solution)/shard_map/ppermute | solution.py:23
  94.5 1.9 %collective-permute-start.13 = (bf16[4,96,128]{2,1,0:T(8,128)(2,1)S(1)}, bf16[4,96,128]{2,1,0:T(8,128)(2,1)S(1)}, u32[]{:S(2)}, u32[]{:S(2)}) collective-permute-start(bf16[4,96,128]{2,1,0:T(8,128)(2,1)S(1)} %pad_maximum_fusion.32), channel_id=1, source_target_pairs={{0,48},{16,64},{32,80},{48,96},{64,112},{80,128},{96,144},{112,160... | collective-permute-start | bytes 294920 | tf_op jit(solution)/shard_map/ppermute | solution.py:23
  96.5 8.7 %collective-permute-start.14 = (bf16[4,96,128]{2,1,0:T(8,128)(2,1)S(1)}, bf16[4,96,128]{2,1,0:T(8,128)(2,1)S(1)}, u32[]{:S(2)}, u32[]{:S(2)}) collective-permute-start(bf16[4,96,128]{2,1,0:T(8,128)(2,1)S(1)} %pad_maximum_fusion.33), channel_id=1, source_target_pairs={{0,464},{16,480},{32,496},{48,0},{64,16},{80,32},{96,48},{112,64},... | collective-permute-start | bytes 294920 | tf_op jit(solution)/shard_map/ppermute | solution.py:23
  105.3 4.3 %collective-permute-start.15 = (bf16[4,96,128]{2,1,0:T(8,128)(2,1)S(1)}, bf16[4,96,128]{2,1,0:T(8,128)(2,1)S(1)}, u32[]{:S(2)}, u32[]{:S(2)}) collective-permute-start(bf16[4,96,128]{2,1,0:T(8,128)(2,1)S(1)} %pad_maximum_fusion.34), channel_id=1, source_target_pairs={{0,480},{16,496},{32,0},{48,16},{64,32},{80,48},{96,64},{112,80},{... | collective-permute-start | bytes 294920 | tf_op jit(solution)/shard_map/ppermute | solution.py:23
  109.6 1.9 %collective-permute-start.16 = (bf16[4,96,128]{2,1,0:T(8,128)(2,1)S(1)}, bf16[4,96,128]{2,1,0:T(8,128)(2,1)S(1)}, u32[]{:S(2)}, u32[]{:S(2)}) collective-permute-start(bf16[4,96,128]{2,1,0:T(8,128)(2,1)S(1)} %pad_maximum_fusion.35), channel_id=1, source_target_pairs={{0,496},{16,0},{32,16},{48,32},{64,48},{80,64},{96,80},{112,96},{1... | collective-permute-start | bytes 294920 | tf_op jit(solution)/shard_map/ppermute | solution.py:23
  111.9 1.9 %collective-permute-done.16 = bf16[4,96,128]{2,1,0:T(8,128)(2,1)S(1)} collective-permute-done((bf16[4,96,128]{2,1,0:T(8,128)(2,1)S(1)}, bf16[4,96,128]{2,1,0:T(8,128)(2,1)S(1)}, u32[]{:S(2)}, u32[]{:S(2)}) %collective-permute-start.16) | collective-permute-done | bytes 98336 | tf_op jit(solution)/shard_map/ppermute | solution.py:23
  114.1 2.3 %fusion.32 = (bf16[8,96,128]{2,1,0:T(8,128)(2,1)S(1)}, f32[8,96,128]{2,1,0:T(8,128)S(1)}) fusion(f32[8,96,128]{2,1,0:T(8,128)S(1)} %copy-done.5, f32[1,8,96,128]{3,2,1,0:T(8,128)S(1)} %copy-done.3, f32[8,96,128]{2,0,1:T(8,128)S(1)} %fusion.23, bf16[26,96,128]{2,1,0:T(8,128)(2,1)S(1)} %get-tuple-element.85, bf16[8,96,12,96]{3,1,2,0:T(8,128)(2,1)S(1)} %copy-done.4, ...), kind=kOutput, calls=%fused_computation.55 | convolution fusion | flops 493535232 | bytes 6242304 | tf_op jit(solution)/shard_map/kamb,mbr->kar/dot_general | solution.py:176
  116.9 1.9 %collective-permute-start.18 = (bf16[3,96,128]{2,1,0:T(8,128)(2,1)S(1)}, bf16[3,96,128]{2,1,0:T(8,128)(2,1)S(1)}, u32[]{:S(2)}, u32[]{:S(2)}) collective-permute-start(bf16[3,96,128]{2,1,0:T(8,128)(2,1)S(1)} %get-tuple-element.60), channel_id=1, source_target_pairs={{1,0},{2,1},{3,2},{4,3},{5,4},{6,5},{7,6},{8,7},{9,8},{10,9},{11,1... | collective-permute-start | bytes 221192 | tf_op jit(solution)/shard_map/ppermute | solution.py:18
  118.8 9.9 %collective-permute-start.17 = (bf16[3,96,128]{2,1,0:T(8,128)(2,1)S(1)}, bf16[3,96,128]{2,1,0:T(8,128)(2,1)S(1)}, u32[]{:S(2)}, u32[]{:S(2)}) collective-permute-start(bf16[3,96,128]{2,1,0:T(8,128)(2,1)S(1)} %get-tuple-element.61), channel_id=1, source_target_pairs={{0,1},{1,2},{2,3},{3,4},{4,5},{5,6},{6,7},{7,8},{8,9},{9,10},{10,1... | collective-permute-start | bytes 221192 | tf_op jit(solution)/shard_map/ppermute | solution.py:18
  129.1 1.9 %collective-permute-start.19 = (bf16[4,96,128]{2,1,0:T(8,128)(2,1)S(1)}, bf16[4,96,128]{2,1,0:T(8,128)(2,1)S(1)}, u32[]{:S(2)}, u32[]{:S(2)}) collective-permute-start(bf16[4,96,128]{2,1,0:T(8,128)(2,1)S(1)} %pad_maximum_fusion.36), channel_id=1, source_target_pairs={{0,16},{16,32},{32,48},{48,64},{64,80},{80,96},{96,112},{112,128},... | collective-permute-start | bytes 294920 | tf_op jit(solution)/shard_map/ppermute | solution.py:23
  131.0 1.9 %collective-permute-start.20 = (bf16[4,96,128]{2,1,0:T(8,128)(2,1)S(1)}, bf16[4,96,128]{2,1,0:T(8,128)(2,1)S(1)}, u32[]{:S(2)}, u32[]{:S(2)}) collective-permute-start(bf16[4,96,128]{2,1,0:T(8,128)(2,1)S(1)} %pad_maximum_fusion.37), channel_id=1, source_target_pairs={{0,32},{16,48},{32,64},{48,80},{64,96},{80,112},{96,128},{112,144}... | collective-permute-start | bytes 294920 | tf_op jit(solution)/shard_map/ppermute | solution.py:23
  133.0 1.9 %collective-permute-start.21 = (bf16[4,96,128]{2,1,0:T(8,128)(2,1)S(1)}, bf16[4,96,128]{2,1,0:T(8,128)(2,1)S(1)}, u32[]{:S(2)}, u32[]{:S(2)}) collective-permute-start(bf16[4,96,128]{2,1,0:T(8,128)(2,1)S(1)} %pad_maximum_fusion.38), channel_id=1, source_target_pairs={{0,48},{16,64},{32,80},{48,96},{64,112},{80,128},{96,144},{112,160... | collective-permute-start | bytes 294920 | tf_op jit(solution)/shard_map/ppermute | solution.py:23
  135.0 8.7 %collective-permute-start.22 = (bf16[4,96,128]{2,1,0:T(8,128)(2,1)S(1)}, bf16[4,96,128]{2,1,0:T(8,128)(2,1)S(1)}, u32[]{:S(2)}, u32[]{:S(2)}) collective-permute-start(bf16[4,96,128]{2,1,0:T(8,128)(2,1)S(1)} %pad_maximum_fusion.39), channel_id=1, source_target_pairs={{0,464},{16,480},{32,496},{48,0},{64,16},{80,32},{96,48},{112,64},... | collective-permute-start | bytes 294920 | tf_op jit(solution)/shard_map/ppermute | solution.py:23
  143.8 4.3 %collective-permute-start.23 = (bf16[4,96,128]{2,1,0:T(8,128)(2,1)S(1)}, bf16[4,96,128]{2,1,0:T(8,128)(2,1)S(1)}, u32[]{:S(2)}, u32[]{:S(2)}) collective-permute-start(bf16[4,96,128]{2,1,0:T(8,128)(2,1)S(1)} %pad_maximum_fusion.40), channel_id=1, source_target_pairs={{0,480},{16,496},{32,0},{48,16},{64,32},{80,48},{96,64},{112,80},{... | collective-permute-start | bytes 294920 | tf_op jit(solution)/shard_map/ppermute | solution.py:23
  148.1 1.9 %collective-permute-start.24 = (bf16[4,96,128]{2,1,0:T(8,128)(2,1)S(1)}, bf16[4,96,128]{2,1,0:T(8,128)(2,1)S(1)}, u32[]{:S(2)}, u32[]{:S(2)}) collective-permute-start(bf16[4,96,128]{2,1,0:T(8,128)(2,1)S(1)} %pad_maximum_fusion.41), channel_id=1, source_target_pairs={{0,496},{16,0},{32,16},{48,32},{64,48},{80,64},{96,80},{112,96},{1... | collective-permute-start | bytes 294920 | tf_op jit(solution)/shard_map/ppermute | solution.py:23
  150.3 1.9 %collective-permute-done.24 = bf16[4,96,128]{2,1,0:T(8,128)(2,1)S(1)} collective-permute-done((bf16[4,96,128]{2,1,0:T(8,128)(2,1)S(1)}, bf16[4,96,128]{2,1,0:T(8,128)(2,1)S(1)}, u32[]{:S(2)}, u32[]{:S(2)}) %collective-permute-start.24) | collective-permute-done | bytes 98336 | tf_op jit(solution)/shard_map/ppermute | solution.py:23
  152.5 3.1 %fusion.11 = f32[1,8,96,128]{3,2,1,0:T(8,128)} fusion(f32[8,96,128]{2,1,0:T(8,128)S(1)} %get-tuple-element.133, bf16[8,96,12,96]{3,1,2,0:T(8,128)(2,1)S(1)} %copy-done.4, bf16[8,96,14,96]{3,1,2,0:T(8,128)(2,1)S(1)} %bitcast_add_fusion, bf16[26,96,128]{2,1,0:T(8,128)(2,1)S(1)} %get-tuple-element.73, f32[8,96,128]{2,0,1:T(8,128)S(1)} %fusion.21, ...), kind=kOutput, calls=%fused_computation.22 | convolution fusion | flops 494125056 | bytes 6438912 | tf_op jit(solution)/shard_map/kamb,mbr->kar/dot_general | solution.py:176
  (132 shorter events, 7.2 us)
Async XLA Ops:
  0.0 13.9 %copy-start = (bf16[1,1,6,2,96,96]{5,4,3,2,1,0:T(8,128)(2,1)S(1)}, bf16[1,1,6,2,96,96]{5,4,3,2,1,0:T(8,128)(2,1)}, u32[]{:S(2)}) copy-start(bf16[1,1,6,2,96,96]{5,4,3,2,1,0:T(8,128)(2,1)} %param.11) | copy-start | bytes 663556
  1.0 37.9 %collective-permute-start = (bf16[3,4,96,96]{3,2,1,0:T(8,128)(2,1)S(1)}, bf16[3,4,96,96]{3,2,1,0:T(8,128)(2,1)S(1)}, u32[]{:S(2)}, u32[]{:S(2)}) collective-permute-start(bf16[3,4,96,96]{3,2,1,0:T(8,128)(2,1)S(1)} %slice_bitcast_fusion), channel_id=1, source_target_pairs={{0,1},{1,2},{2,3},{3,4},{4,5},{5,6},{6,7},{7,8},{8,9},{9,10},{10,1... | collective-permute-start | bytes 663560 | tf_op jit(solution)/shard_map/ppermute | solution.py:18
  13.5 22.2 %copy-start.10 = (s32[1,1,6]{2,1,0:T(1,128)S(1)}, s32[1,1,6]{2,1,0:T(1,128)}, u32[]{:S(2)}) copy-start(s32[1,1,6]{2,1,0:T(1,128)} %param.10) | copy-start | bytes 76
  14.3 29.8 %copy-start.1 = (bf16[1,8,4,96,96]{4,3,2,1,0:T(8,128)(2,1)S(1)}, bf16[1,8,4,96,96]{4,3,2,1,0:T(8,128)(2,1)}, u32[]{:S(2)}) copy-start(bf16[1,8,4,96,96]{4,3,2,1,0:T(8,128)(2,1)} %param.8) | copy-start | bytes 1769476
  15.4 32.0 %collective-permute-start.8 = (bf16[11,96,128]{2,1,0:T(8,128)(2,1)S(1)}, bf16[11,96,128]{2,1,0:T(8,128)(2,1)S(1)}, u32[]{:S(2)}, u32[]{:S(2)}) collective-permute-start(bf16[11,96,128]{2,1,0:T(8,128)(2,1)S(1)} %get-tuple-element.66), channel_id=1, source_target_pairs={{0,496},{16,0},{32,16},{48,32},{64,48},{80,64},{96,80},{112,96},{1... | collective-permute-start | bytes 811016 | tf_op jit(solution)/shard_map/ppermute | solution.py:23
  23.3 29.2 %collective-permute-start.4 = (bf16[11,96,128]{2,1,0:T(8,128)(2,1)}, bf16[11,96,128]{2,1,0:T(8,128)(2,1)}, u32[]{:S(2)}, u32[]{:S(2)}) collective-permute-start(bf16[11,96,128]{2,1,0:T(8,128)(2,1)} %get-tuple-element.67), channel_id=1, source_target_pairs={{0,32},{16,48},{32,64},{48,80},{64,96},{80,112},{96,128},{112,144}... | collective-permute-start | bytes 811016 | tf_op jit(solution)/shard_map/ppermute | solution.py:23
  25.2 36.3 %collective-permute-start.5 = (bf16[11,96,128]{2,1,0:T(8,128)(2,1)}, bf16[11,96,128]{2,1,0:T(8,128)(2,1)}, u32[]{:S(2)}, u32[]{:S(2)}) collective-permute-start(bf16[11,96,128]{2,1,0:T(8,128)(2,1)} %get-tuple-element.68), channel_id=1, source_target_pairs={{0,48},{16,64},{32,80},{48,96},{64,112},{80,128},{96,144},{112,160... | collective-permute-start | bytes 811016 | tf_op jit(solution)/shard_map/ppermute | solution.py:23
  27.2 36.3 %collective-permute-start.6 = (bf16[11,96,128]{2,1,0:T(8,128)(2,1)}, bf16[11,96,128]{2,1,0:T(8,128)(2,1)}, u32[]{:S(2)}, u32[]{:S(2)}) collective-permute-start(bf16[11,96,128]{2,1,0:T(8,128)(2,1)} %get-tuple-element.69), channel_id=1, source_target_pairs={{0,464},{16,480},{32,496},{48,0},{64,16},{80,32},{96,48},{112,64},... | collective-permute-start | bytes 811016 | tf_op jit(solution)/shard_map/ppermute | solution.py:23
  36.2 7.8 %copy-start.6 = (bf16[12,96,96]{2,1,0:T(8,128)(2,1)}, bf16[12,96,96]{2,1,0:T(8,128)(2,1)S(1)}, u32[]{:S(2)}) copy-start(bf16[12,96,96]{2,1,0:T(8,128)(2,1)S(1)} %constant_dynamic-update-slice_fusion) | copy-start | bytes 663556
  38.9 24.6 %collective-permute-start.7 = (bf16[11,96,128]{2,1,0:T(8,128)(2,1)}, bf16[11,96,128]{2,1,0:T(8,128)(2,1)}, u32[]{:S(2)}, u32[]{:S(2)}) collective-permute-start(bf16[11,96,128]{2,1,0:T(8,128)(2,1)} %get-tuple-element.70), channel_id=1, source_target_pairs={{0,480},{16,496},{32,0},{48,16},{64,32},{80,48},{96,64},{112,80},{... | collective-permute-start | bytes 811016 | tf_op jit(solution)/shard_map/ppermute | solution.py:23
  47.4 1.9 %copy-start.7 = (bf16[11,96,128]{2,1,0:T(8,128)(2,1)}, bf16[11,96,128]{2,1,0:T(8,128)(2,1)S(1)}, u32[]{:S(2)}) copy-start(bf16[11,96,128]{2,1,0:T(8,128)(2,1)S(1)} %collective-permute-done.8.refs_5_) | copy-start | bytes 811012
  47.4 16.1 %collective-permute-start.3 = (bf16[11,96,128]{2,1,0:T(8,128)(2,1)}, bf16[11,96,128]{2,1,0:T(8,128)(2,1)}, u32[]{:S(2)}, u32[]{:S(2)}) collective-permute-start(bf16[11,96,128]{2,1,0:T(8,128)(2,1)} %get-tuple-element.71), channel_id=1, source_target_pairs={{0,16},{16,32},{32,48},{48,64},{64,80},{80,96},{96,112},{112,128},... | collective-permute-start | bytes 811016 | tf_op jit(solution)/shard_map/ppermute | solution.py:23
  52.5 17.4 %collective-permute-start.1 = (bf16[3,96,128]{2,1,0:T(8,128)(2,1)}, bf16[3,96,128]{2,1,0:T(8,128)(2,1)S(1)}, u32[]{:S(2)}, u32[]{:S(2)}) collective-permute-start(bf16[3,96,128]{2,1,0:T(8,128)(2,1)} %get-tuple-element.64), channel_id=1, source_target_pairs={{0,1},{1,2},{2,3},{3,4},{4,5},{5,6},{6,7},{7,8},{8,9},{9,10},{10,1... | collective-permute-start | bytes 221192 | tf_op jit(solution)/shard_map/ppermute | solution.py:18
  61.6 12.6 %collective-permute-start.2 = (bf16[3,96,128]{2,1,0:T(8,128)(2,1)S(1)}, bf16[3,96,128]{2,1,0:T(8,128)(2,1)}, u32[]{:S(2)}, u32[]{:S(2)}) collective-permute-start(bf16[3,96,128]{2,1,0:T(8,128)(2,1)S(1)} %get-tuple-element.65), channel_id=1, source_target_pairs={{1,0},{2,1},{3,2},{4,3},{5,4},{6,5},{7,6},{8,7},{9,8},{10,9},{11,1... | collective-permute-start | bytes 221192 | tf_op jit(solution)/shard_map/ppermute | solution.py:18
  66.5 7.7 %copy-start.2 = (f32[1,8,96,128]{3,2,1,0:T(8,128)S(1)}, f32[1,8,96,128]{3,2,1,0:T(8,128)}, u32[]{:S(2)}) copy-start(f32[1,8,96,128]{3,2,1,0:T(8,128)} %param.7) | copy-start | bytes 1179652
  70.0 0.6 copy-start.9
  77.6 2.8 %copy-start.8 = (bf16[3,96,128]{2,1,0:T(8,128)(2,1)S(1)}, bf16[3,96,128]{2,1,0:T(8,128)(2,1)}, u32[]{:S(2)}) copy-start(bf16[3,96,128]{2,1,0:T(8,128)(2,1)} %get-tuple-element.63) | copy-start | bytes 221188
  78.1 35.9 %copy-start.3 = (f32[1,8,96,128]{3,2,1,0:T(8,128)S(1)}, f32[1,8,96,128]{3,2,1,0:T(8,128)}, u32[]{:S(2)}) copy-start(f32[1,8,96,128]{3,2,1,0:T(8,128)} %param.7) | copy-start | bytes 1179652
  78.1 35.9 %copy-start.4 = (bf16[8,96,12,96]{3,1,2,0:T(8,128)(2,1)S(1)}, bf16[8,96,12,96]{3,1,2,0:T(8,128)(2,1)}, u32[]{:S(2)}) copy-start(bf16[8,96,12,96]{3,1,2,0:T(8,128)(2,1)} %multiply_bitcast_fusion) | copy-start | bytes 5308420
  78.1 35.9 %copy-start.5 = (f32[8,96,128]{2,1,0:T(8,128)S(1)}, f32[8,96,128]{2,1,0:T(8,128)}, u32[]{:S(2)}) copy-start(f32[8,96,128]{2,1,0:T(8,128)} %get-tuple-element.131) | copy-start | bytes 1179652
  78.2 27.2 %collective-permute-start.10 = (bf16[3,96,128]{2,1,0:T(8,128)(2,1)S(1)}, bf16[3,96,128]{2,1,0:T(8,128)(2,1)S(1)}, u32[]{:S(2)}, u32[]{:S(2)}) collective-permute-start(bf16[3,96,128]{2,1,0:T(8,128)(2,1)S(1)} %get-tuple-element.62), channel_id=1, source_target_pairs={{1,0},{2,1},{3,2},{4,3},{5,4},{6,5},{7,6},{8,7},{9,8},{10,9},{11,1... | collective-permute-start | bytes 221192 | tf_op jit(solution)/shard_map/ppermute | solution.py:18
  80.4 16.2 %collective-permute-start.9 = (bf16[3,96,128]{2,1,0:T(8,128)(2,1)S(1)}, bf16[3,96,128]{2,1,0:T(8,128)(2,1)S(1)}, u32[]{:S(2)}, u32[]{:S(2)}) collective-permute-start(bf16[3,96,128]{2,1,0:T(8,128)(2,1)S(1)} %copy-done.8), channel_id=1, source_target_pairs={{0,1},{1,2},{2,3},{3,4},{4,5},{5,6},{6,7},{7,8},{8,9},{9,10},{10,1... | collective-permute-start | bytes 221192 | tf_op jit(solution)/shard_map/ppermute | solution.py:18
  90.6 19.0 %collective-permute-start.11 = (bf16[4,96,128]{2,1,0:T(8,128)(2,1)S(1)}, bf16[4,96,128]{2,1,0:T(8,128)(2,1)S(1)}, u32[]{:S(2)}, u32[]{:S(2)}) collective-permute-start(bf16[4,96,128]{2,1,0:T(8,128)(2,1)S(1)} %pad_maximum_fusion.30), channel_id=1, source_target_pairs={{0,16},{16,32},{32,48},{48,64},{64,80},{80,96},{96,112},{112,128},... | collective-permute-start | bytes 294920 | tf_op jit(solution)/shard_map/ppermute | solution.py:23
  92.6 19.0 %collective-permute-start.12 = (bf16[4,96,128]{2,1,0:T(8,128)(2,1)S(1)}, bf16[4,96,128]{2,1,0:T(8,128)(2,1)S(1)}, u32[]{:S(2)}, u32[]{:S(2)}) collective-permute-start(bf16[4,96,128]{2,1,0:T(8,128)(2,1)S(1)} %pad_maximum_fusion.31), channel_id=1, source_target_pairs={{0,32},{16,48},{32,64},{48,80},{64,96},{80,112},{96,128},{112,144}... | collective-permute-start | bytes 294920 | tf_op jit(solution)/shard_map/ppermute | solution.py:23
  94.5 17.1 %collective-permute-start.13 = (bf16[4,96,128]{2,1,0:T(8,128)(2,1)S(1)}, bf16[4,96,128]{2,1,0:T(8,128)(2,1)S(1)}, u32[]{:S(2)}, u32[]{:S(2)}) collective-permute-start(bf16[4,96,128]{2,1,0:T(8,128)(2,1)S(1)} %pad_maximum_fusion.32), channel_id=1, source_target_pairs={{0,48},{16,64},{32,80},{48,96},{64,112},{80,128},{96,144},{112,160... | collective-permute-start | bytes 294920 | tf_op jit(solution)/shard_map/ppermute | solution.py:23
  96.5 15.1 %collective-permute-start.14 = (bf16[4,96,128]{2,1,0:T(8,128)(2,1)S(1)}, bf16[4,96,128]{2,1,0:T(8,128)(2,1)S(1)}, u32[]{:S(2)}, u32[]{:S(2)}) collective-permute-start(bf16[4,96,128]{2,1,0:T(8,128)(2,1)S(1)} %pad_maximum_fusion.33), channel_id=1, source_target_pairs={{0,464},{16,480},{32,496},{48,0},{64,16},{80,32},{96,48},{112,64},... | collective-permute-start | bytes 294920 | tf_op jit(solution)/shard_map/ppermute | solution.py:23
  105.3 6.5 %collective-permute-start.15 = (bf16[4,96,128]{2,1,0:T(8,128)(2,1)S(1)}, bf16[4,96,128]{2,1,0:T(8,128)(2,1)S(1)}, u32[]{:S(2)}, u32[]{:S(2)}) collective-permute-start(bf16[4,96,128]{2,1,0:T(8,128)(2,1)S(1)} %pad_maximum_fusion.34), channel_id=1, source_target_pairs={{0,480},{16,496},{32,0},{48,16},{64,32},{80,48},{96,64},{112,80},{... | collective-permute-start | bytes 294920 | tf_op jit(solution)/shard_map/ppermute | solution.py:23
  109.6 4.1 %collective-permute-start.16 = (bf16[4,96,128]{2,1,0:T(8,128)(2,1)S(1)}, bf16[4,96,128]{2,1,0:T(8,128)(2,1)S(1)}, u32[]{:S(2)}, u32[]{:S(2)}) collective-permute-start(bf16[4,96,128]{2,1,0:T(8,128)(2,1)S(1)} %pad_maximum_fusion.35), channel_id=1, source_target_pairs={{0,496},{16,0},{32,16},{48,32},{64,48},{80,64},{96,80},{112,96},{1... | collective-permute-start | bytes 294920 | tf_op jit(solution)/shard_map/ppermute | solution.py:23
  116.9 26.9 %collective-permute-start.18 = (bf16[3,96,128]{2,1,0:T(8,128)(2,1)S(1)}, bf16[3,96,128]{2,1,0:T(8,128)(2,1)S(1)}, u32[]{:S(2)}, u32[]{:S(2)}) collective-permute-start(bf16[3,96,128]{2,1,0:T(8,128)(2,1)S(1)} %get-tuple-element.60), channel_id=1, source_target_pairs={{1,0},{2,1},{3,2},{4,3},{5,4},{6,5},{7,6},{8,7},{9,8},{10,9},{11,1... | collective-permute-start | bytes 221192 | tf_op jit(solution)/shard_map/ppermute | solution.py:18
  118.8 16.2 %collective-permute-start.17 = (bf16[3,96,128]{2,1,0:T(8,128)(2,1)S(1)}, bf16[3,96,128]{2,1,0:T(8,128)(2,1)S(1)}, u32[]{:S(2)}, u32[]{:S(2)}) collective-permute-start(bf16[3,96,128]{2,1,0:T(8,128)(2,1)S(1)} %get-tuple-element.61), channel_id=1, source_target_pairs={{0,1},{1,2},{2,3},{3,4},{4,5},{5,6},{6,7},{7,8},{8,9},{9,10},{10,1... | collective-permute-start | bytes 221192 | tf_op jit(solution)/shard_map/ppermute | solution.py:18
  129.1 19.0 %collective-permute-start.19 = (bf16[4,96,128]{2,1,0:T(8,128)(2,1)S(1)}, bf16[4,96,128]{2,1,0:T(8,128)(2,1)S(1)}, u32[]{:S(2)}, u32[]{:S(2)}) collective-permute-start(bf16[4,96,128]{2,1,0:T(8,128)(2,1)S(1)} %pad_maximum_fusion.36), channel_id=1, source_target_pairs={{0,16},{16,32},{32,48},{48,64},{64,80},{80,96},{96,112},{112,128},... | collective-permute-start | bytes 294920 | tf_op jit(solution)/shard_map/ppermute | solution.py:23
  131.0 19.0 %collective-permute-start.20 = (bf16[4,96,128]{2,1,0:T(8,128)(2,1)S(1)}, bf16[4,96,128]{2,1,0:T(8,128)(2,1)S(1)}, u32[]{:S(2)}, u32[]{:S(2)}) collective-permute-start(bf16[4,96,128]{2,1,0:T(8,128)(2,1)S(1)} %pad_maximum_fusion.37), channel_id=1, source_target_pairs={{0,32},{16,48},{32,64},{48,80},{64,96},{80,112},{96,128},{112,144}... | collective-permute-start | bytes 294920 | tf_op jit(solution)/shard_map/ppermute | solution.py:23
  133.0 17.1 %collective-permute-start.21 = (bf16[4,96,128]{2,1,0:T(8,128)(2,1)S(1)}, bf16[4,96,128]{2,1,0:T(8,128)(2,1)S(1)}, u32[]{:S(2)}, u32[]{:S(2)}) collective-permute-start(bf16[4,96,128]{2,1,0:T(8,128)(2,1)S(1)} %pad_maximum_fusion.38), channel_id=1, source_target_pairs={{0,48},{16,64},{32,80},{48,96},{64,112},{80,128},{96,144},{112,160... | collective-permute-start | bytes 294920 | tf_op jit(solution)/shard_map/ppermute | solution.py:23
  135.0 15.1 %collective-permute-start.22 = (bf16[4,96,128]{2,1,0:T(8,128)(2,1)S(1)}, bf16[4,96,128]{2,1,0:T(8,128)(2,1)S(1)}, u32[]{:S(2)}, u32[]{:S(2)}) collective-permute-start(bf16[4,96,128]{2,1,0:T(8,128)(2,1)S(1)} %pad_maximum_fusion.39), channel_id=1, source_target_pairs={{0,464},{16,480},{32,496},{48,0},{64,16},{80,32},{96,48},{112,64},... | collective-permute-start | bytes 294920 | tf_op jit(solution)/shard_map/ppermute | solution.py:23
  143.8 6.5 %collective-permute-start.23 = (bf16[4,96,128]{2,1,0:T(8,128)(2,1)S(1)}, bf16[4,96,128]{2,1,0:T(8,128)(2,1)S(1)}, u32[]{:S(2)}, u32[]{:S(2)}) collective-permute-start(bf16[4,96,128]{2,1,0:T(8,128)(2,1)S(1)} %pad_maximum_fusion.40), channel_id=1, source_target_pairs={{0,480},{16,496},{32,0},{48,16},{64,32},{80,48},{96,64},{112,80},{... | collective-permute-start | bytes 294920 | tf_op jit(solution)/shard_map/ppermute | solution.py:23
  148.1 4.1 %collective-permute-start.24 = (bf16[4,96,128]{2,1,0:T(8,128)(2,1)S(1)}, bf16[4,96,128]{2,1,0:T(8,128)(2,1)S(1)}, u32[]{:S(2)}, u32[]{:S(2)}) collective-permute-start(bf16[4,96,128]{2,1,0:T(8,128)(2,1)S(1)} %pad_maximum_fusion.41), channel_id=1, source_target_pairs={{0,496},{16,0},{32,16},{48,32},{64,48},{80,64},{96,80},{112,96},{1... | collective-permute-start | bytes 294920 | tf_op jit(solution)/shard_map/ppermute | solution.py:23

commit v10 on v9

--- a/solution.py
+++ b/solution.py
@@ -105,7 +105,6 @@
     fetch_weight = jnp.einsum(
         "kf,fab->kafb", fetch_place.astype(jnp.bfloat16), fetch_blocks, preferred_element_type=jnp.bfloat16
     )
-    weight = jnp.concatenate([band_weight, fetch_weight], axis=2)
     first_pick = jnp.stack([far_knot[bucket_of[-s]] for s in shifts])
     answer_pick = None
     land_place = None
@@ -161,21 +160,17 @@
             ).astype(jnp.bfloat16)
             land_place = (heard.reshape(-1)[None, :] == knot_vals[:, None]).astype(jnp.bfloat16)
         else:
-            stacked = jnp.concatenate(
-                [low, probe_bf, high] + [fetched[b] for b in fetch_order], axis=0
-            )
             landed = jnp.concatenate(landed, axis=0)
         if turn == 0:
-            extended = jnp.concatenate([low, probe_bf, high], axis=0)
-            summed = jnp.einsum(
-                "kamb,mbr->kar", band_weight, extended, preferred_element_type=jnp.float32
-            ) + jnp.einsum(
-                "kamb,mbr->kar", fetch_weight, first_fetched, preferred_element_type=jnp.float32
-            )
+            fetched_rows = first_fetched
         else:
-            summed = jnp.einsum(
-                "kamb,mbr->kar", weight, stacked, preferred_element_type=jnp.float32
-            )
+            fetched_rows = jnp.concatenate([fetched[b] for b in fetch_order], axis=0)
+        extended = jnp.concatenate([low, probe_bf, high], axis=0)
+        summed = jnp.einsum(
+            "kamb,mbr->kar", band_weight, extended, preferred_element_type=jnp.float32
+        ) + jnp.einsum(
+            "kamb,mbr->kar", fetch_weight, fetched_rows, preferred_element_type=jnp.float32
+        )
         cross = jnp.einsum("ks,spr->kpr", land_place, landed, preferred_element_type=jnp.float32)
         residual = residual - (summed + cross)
         coeff_next = 1.0 / (2.0 * center / radius - coeff)

time: 157 us -> 193 us (1.23)
  the two profiles are of different devices: /device:TPU:24 before, /device:TPU:357 now
where the time goes in v10:
time: 193 us; the launch traced here: 191 us
  starting transfers between devices  94.1 us (49%)
  local copies, waits for them, and re-layouts  29.6 us (15%)
  waiting for transfers between devices  29.4 us (15%)
  matrix products  24.7 us (13%)
  other arithmetic  10.6 us (5%)
  Pallas kernels  2.24 us (1%)
    ppermute x18, starting transfers between devices, shifted_ring(): lax.ppermute(value, axis, [(i, (i + steps) % count) for i in range(count)])  62.8 us
    ppermute x7, starting transfers between devices, shifted_open(): lax.ppermute(value, axis, [(source, source + steps) for source in range(i...  31.4 us
    ppermute x7, waiting for transfers between devices, shifted_open(): lax.ppermute(value, axis, [(source, source + steps) for source in range(i...  29.3 us
    dot_general x3, matrix products, body(): jnp.einsum('kamb,mbr->kar', band_weight, extended, preferred_element_type...  8.37 us
    slice x12, local copies, waits for them, and re-layouts, body(): landed.append(got[slots:])  7.78 us
    dot_general x3, matrix products, body(): jnp.einsum('kamb,mbr->kar', fetch_weight, fetched_rows, preferred_element...  7.48 us
    concatenate x2, local copies, waits for them, and re-layouts, body(): landed = jnp.concatenate(landed, axis=0)  6.62 us
    dot_general x3, matrix products, body(): jnp.einsum('ks,spr->kpr', land_place, landed, preferred_element_type=jnp....  5.99 us
  transfers between devices with their start and end apart: 25, of which 2 were waited for; matrix products, arithmetic and copies ran while one was open for 24% of the time, Pallas kernels for 1%

profile of v10, /device:TPU:357, one launch (start us, length us, event | category | flops | bytes accessed | tf_op | source)
XLA Modules:
  0.0 191.4 jit_solution(4058756516929804980)
XLA Ops:
  1.8 1.0 fusion.41
  3.3 1.2 fusion.37
  4.8 1.2 fusion.68
  5.9 3.4 %collective-permute-start.3 = (bf16[11,96,128]{2,1,0:T(8,128)(2,1)S(1)}, bf16[11,96,128]{2,1,0:T(8,128)(2,1)S(1)}, u32[]{:S(2)}, u32[]{:S(2)}) collective-permute-start(bf16[11,96,128]{2,1,0:T(8,128)(2,1)S(1)} %get-tuple-element.71), channel_id=1, source_target_pairs={{0,16},{16,32},{32,48},{48,64},{64,80},{80,96},{96,112},{112,128},... | collective-permute-start | bytes 811016 | tf_op jit(solution)/shard_map/ppermute | solution.py:23
  9.3 3.4 %collective-permute-start.4 = (bf16[11,96,128]{2,1,0:T(8,128)(2,1)}, bf16[11,96,128]{2,1,0:T(8,128)(2,1)}, u32[]{:S(2)}, u32[]{:S(2)}) collective-permute-start(bf16[11,96,128]{2,1,0:T(8,128)(2,1)} %get-tuple-element.67), channel_id=1, source_target_pairs={{0,32},{16,48},{32,64},{48,80},{64,96},{80,112},{96,128},{112,144}... | collective-permute-start | bytes 811016 | tf_op jit(solution)/shard_map/ppermute | solution.py:23
  12.8 2.5 %collective-permute-start.5 = (bf16[11,96,128]{2,1,0:T(8,128)(2,1)}, bf16[11,96,128]{2,1,0:T(8,128)(2,1)}, u32[]{:S(2)}, u32[]{:S(2)}) collective-permute-start(bf16[11,96,128]{2,1,0:T(8,128)(2,1)} %get-tuple-element.68), channel_id=1, source_target_pairs={{0,48},{16,64},{32,80},{48,96},{64,112},{80,128},{96,144},{112,160... | collective-permute-start | bytes 811016 | tf_op jit(solution)/shard_map/ppermute | solution.py:23
  15.3 3.0 %collective-permute-start.6 = (bf16[11,96,128]{2,1,0:T(8,128)(2,1)}, bf16[11,96,128]{2,1,0:T(8,128)(2,1)}, u32[]{:S(2)}, u32[]{:S(2)}) collective-permute-start(bf16[11,96,128]{2,1,0:T(8,128)(2,1)} %get-tuple-element.69), channel_id=1, source_target_pairs={{0,464},{16,480},{32,496},{48,0},{64,16},{80,32},{96,48},{112,64},... | collective-permute-start | bytes 811016 | tf_op jit(solution)/shard_map/ppermute | solution.py:23
  18.4 3.2 %collective-permute-start = (bf16[3,4,96,96]{3,2,1,0:T(8,128)(2,1)S(1)}, bf16[3,4,96,96]{3,2,1,0:T(8,128)(2,1)S(1)}, u32[]{:S(2)}, u32[]{:S(2)}) collective-permute-start(bf16[3,4,96,96]{3,2,1,0:T(8,128)(2,1)S(1)} %slice_bitcast_fusion), channel_id=1, source_target_pairs={{0,1},{1,2},{2,3},{3,4},{4,5},{5,6},{6,7},{7,8},{8,9},{9,10},{10,1... | collective-permute-start | bytes 663560 | tf_op jit(solution)/shard_map/ppermute | solution.py:18
  24.5 28.7 %collective-permute-done = bf16[3,4,96,96]{3,2,1,0:T(8,128)(2,1)S(1)} collective-permute-done((bf16[3,4,96,96]{3,2,1,0:T(8,128)(2,1)S(1)}, bf16[3,4,96,96]{3,2,1,0:T(8,128)(2,1)S(1)}, u32[]{:S(2)}, u32[]{:S(2)}) %collective-permute-start) | collective-permute-done | bytes 221216 | tf_op jit(solution)/shard_map/ppermute | solution.py:18
  53.2 1.9 collective-permute-start.7
  55.1 0.9 maximum_bitcast_fusion.7
  56.0 0.8 copy.56
  56.8 0.8 copy.57
  57.6 0.8 copy.58
  58.4 2.4 %collective-permute-start.8 = (bf16[11,96,128]{2,1,0:T(8,128)(2,1)}, bf16[11,96,128]{2,1,0:T(8,128)(2,1)}, u32[]{:S(2)}, u32[]{:S(2)}) collective-permute-start(bf16[11,96,128]{2,1,0:T(8,128)(2,1)} %get-tuple-element.66), channel_id=1, source_target_pairs={{0,496},{16,0},{32,16},{48,32},{64,48},{80,64},{96,80},{112,96},{1... | collective-permute-start | bytes 811016 | tf_op jit(solution)/shard_map/ppermute | solution.py:23
  60.8 3.1 %bitcast_add_fusion = bf16[8,96,14,96]{3,1,2,0:T(8,128)(2,1)S(1)} fusion(bf16[8,14]{1,0:T(8,128)(2,1)S(1)} %fusion.87, bf16[8,96,96]{1,2,0:T(8,128)(2,1)} %copy.58, bf16[8,14]{1,0:T(8,128)(2,1)S(1)} %get-tuple-element.139, bf16[8,96,96]{1,2,0:T(8,128)(2,1)} %copy.57, bf16[8,14]{1,0:T(8,128)(2,1)S(1)} %get-tuple-element.138, bf16[8,96,96]{1,2,0:T(8,128)(2,1)} %copy.56, ...), kind=kLoop, calls=%fused_computation | loop fusion | flops 13418496 | bytes 3098144 | tf_op jit(solution)/shard_map/add | solution.py:94
  64.0 1.9 %collective-permute-start.1 = (bf16[3,96,128]{2,1,0:T(8,128)(2,1)}, bf16[3,96,128]{2,1,0:T(8,128)(2,1)}, u32[]{:S(2)}, u32[]{:S(2)}) collective-permute-start(bf16[3,96,128]{2,1,0:T(8,128)(2,1)} %get-tuple-element.64), channel_id=1, source_target_pairs={{0,1},{1,2},{2,3},{3,4},{4,5},{5,6},{6,7},{7,8},{8,9},{9,10},{10,1... | collective-permute-start | bytes 221192 | tf_op jit(solution)/shard_map/ppermute | solution.py:18
  65.9 9.5 %collective-permute-start.2 = (bf16[3,96,128]{2,1,0:T(8,128)(2,1)S(1)}, bf16[3,96,128]{2,1,0:T(8,128)(2,1)}, u32[]{:S(2)}, u32[]{:S(2)}) collective-permute-start(bf16[3,96,128]{2,1,0:T(8,128)(2,1)S(1)} %get-tuple-element.65), channel_id=1, source_target_pairs={{1,0},{2,1},{3,2},{4,3},{5,4},{6,5},{7,6},{8,7},{9,8},{10,9},{11,1... | collective-permute-start | bytes 221192 | tf_op jit(solution)/shard_map/ppermute | solution.py:18
  75.5 2.2 %shard_map.55 = (bf16[12,96,128]{2,1,0:T(8,128)(2,1)}, bf16[12,96,128]{2,1,0:T(8,128)(2,1)}, bf16[6,128]{1,0:T(8,128)(2,1)}) custom-call(s32[6,2]{1,0:T(8,128)} %copy.67.pick_ref, bf16[11,96,128]{2,1,0:T(8,128)(2,1)} %copy-done.12, bf16[11,96,128]{2,1,0:T(8,128)(2,1)} %collective-permute-done.4.refs_1_, bf16[11,96,128]{2,1,0:T(8,128)(2,1)} %collective-permute-done.5.refs_2_, ...), custom_call_target="tpu_custom_call" | custom-call | tf_op jit(solution)/shard_map/pallas_call | solution.py:45
  79.1 2.0 %fusion.39 = f32[8,96,128]{2,0,1:T(8,128)} fusion(bf16[12,96,128]{2,1,0:T(8,128)(2,1)} %get-tuple-element.22, f32[12]{0:T(128)S(1)} %eq.250, f32[8]{0:T(128)S(1)} %iota_convert_fusion), kind=kOutput, calls=%fused_computation.53 | convolution fusion | flops 2359392 | bytes 688208 | tf_op jit(solution)/shard_map/ks,spr->kpr/dot_general | solution.py:174
  81.8 2.9 %fusion.9 = f32[8,96,128]{2,1,0:T(8,128)} fusion(bf16[12,8]{0,1:T(8,128)(2,1)S(1)} %copy.60, bf16[12,96,96]{2,1,0:T(8,128)(2,1)} %copy-done.13, bf16[12,96,128]{2,1,0:T(8,128)(2,1)} %get-tuple-element.20), kind=kOutput, calls=%fused_computation.18 | convolution fusion | flops 227377152 | bytes 909504 | tf_op jit(solution)/shard_map/kamb,mbr->kar/dot_general | solution.py:171
  85.5 3.0 %fusion.73 = (bf16[8,96,128]{2,1,0:T(8,128)(2,1)S(1)}, f32[8,96,128]{2,1,0:T(8,128)}) fusion(f32[1,8,96,128]{3,2,1,0:T(8,128)S(1)} %copy-done, f32[8,96,128]{2,0,1:T(8,128)} %fusion.39, f32[8,96,128]{2,1,0:T(8,128)} %fusion.9, bf16[8,96,14,96]{3,1,2,0:T(8,128)(2,1)S(1)} %bitcast_add_fusion, bf16[3,96,128]{2,1,0:T(8,128)(2,1)} %collective-permute-done.2, ...), kind=kOutput, calls=%fused_computation.119 | convolution fusion | flops 265273344 | bytes 4177920 | tf_op jit(solution)/shard_map/kamb,mbr->kar/dot_general | solution.py:169
  90.7 4.6 %collective-permute-start.16 = (bf16[4,96,128]{2,0,1:T(4,128)(2,1)S(1)}, bf16[4,96,128]{2,0,1:T(4,128)(2,1)S(1)}, u32[]{:S(2)}, u32[]{:S(2)}) collective-permute-start(bf16[4,96,128]{2,0,1:T(4,128)(2,1)S(1)} %pad_maximum_fusion.12), channel_id=1, source_target_pairs={{0,496},{16,0},{32,16},{48,32},{64,48},{80,64},{96,80},{112,96},{1... | collective-permute-start | bytes 294920 | tf_op jit(solution)/shard_map/ppermute | solution.py:23
  95.5 5.9 %collective-permute-start.15 = (bf16[4,96,128]{2,0,1:T(4,128)(2,1)S(1)}, bf16[4,96,128]{2,0,1:T(4,128)(2,1)S(1)}, u32[]{:S(2)}, u32[]{:S(2)}) collective-permute-start(bf16[4,96,128]{2,0,1:T(4,128)(2,1)S(1)} %pad_maximum_fusion.11), channel_id=1, source_target_pairs={{0,480},{16,496},{32,0},{48,16},{64,32},{80,48},{96,64},{112,80},{... | collective-permute-start | bytes 294920 | tf_op jit(solution)/shard_map/ppermute | solution.py:23
  101.5 2.1 %collective-permute-start.14 = (bf16[4,96,128]{2,0,1:T(4,128)(2,1)S(1)}, bf16[4,96,128]{2,0,1:T(4,128)(2,1)S(1)}, u32[]{:S(2)}, u32[]{:S(2)}) collective-permute-start(bf16[4,96,128]{2,0,1:T(4,128)(2,1)S(1)} %pad_maximum_fusion.10), channel_id=1, source_target_pairs={{0,464},{16,480},{32,496},{48,0},{64,16},{80,32},{96,48},{112,64},... | collective-permute-start | bytes 294920 | tf_op jit(solution)/shard_map/ppermute | solution.py:23
  103.7 7.7 %collective-permute-start.13 = (bf16[4,96,128]{2,0,1:T(4,128)(2,1)S(1)}, bf16[4,96,128]{2,0,1:T(4,128)(2,1)S(1)}, u32[]{:S(2)}, u32[]{:S(2)}) collective-permute-start(bf16[4,96,128]{2,0,1:T(4,128)(2,1)S(1)} %pad_maximum_fusion.9), channel_id=1, source_target_pairs={{0,48},{16,64},{32,80},{48,96},{64,112},{80,128},{96,144},{112,160... | collective-permute-start | bytes 294920 | tf_op jit(solution)/shard_map/ppermute | solution.py:23
  111.5 1.9 %collective-permute-start.12 = (bf16[4,96,128]{2,0,1:T(4,128)(2,1)S(1)}, bf16[4,96,128]{2,0,1:T(4,128)(2,1)S(1)}, u32[]{:S(2)}, u32[]{:S(2)}) collective-permute-start(bf16[4,96,128]{2,0,1:T(4,128)(2,1)S(1)} %pad_maximum_fusion.8), channel_id=1, source_target_pairs={{0,32},{16,48},{32,64},{48,80},{64,96},{80,112},{96,128},{112,144}... | collective-permute-start | bytes 294920 | tf_op jit(solution)/shard_map/ppermute | solution.py:23
  113.5 3.1 %collective-permute-start.11 = (bf16[4,96,128]{2,0,1:T(4,128)(2,1)S(1)}, bf16[4,96,128]{2,0,1:T(4,128)(2,1)S(1)}, u32[]{:S(2)}, u32[]{:S(2)}) collective-permute-start(bf16[4,96,128]{2,0,1:T(4,128)(2,1)S(1)} %pad_maximum_fusion.7), channel_id=1, source_target_pairs={{0,16},{16,32},{32,48},{48,64},{64,80},{80,96},{96,112},{112,128},... | collective-permute-start | bytes 294920 | tf_op jit(solution)/shard_map/ppermute | solution.py:23
  117.3 2.0 %collective-permute-start.10 = (bf16[3,96,128]{2,1,0:T(8,128)(2,1)}, bf16[3,96,128]{2,1,0:T(8,128)(2,1)}, u32[]{:S(2)}, u32[]{:S(2)}) collective-permute-start(bf16[3,96,128]{2,1,0:T(8,128)(2,1)} %get-tuple-element.63), channel_id=1, source_target_pairs={{1,0},{2,1},{3,2},{4,3},{5,4},{6,5},{7,6},{8,7},{9,8},{10,9},{11,1... | collective-permute-start | bytes 221192 | tf_op jit(solution)/shard_map/ppermute | solution.py:18
  120.0 3.5 %collective-permute-start.9 = (bf16[3,96,128]{2,1,0:T(8,128)(2,1)}, bf16[3,96,128]{2,1,0:T(8,128)(2,1)}, u32[]{:S(2)}, u32[]{:S(2)}) collective-permute-start(bf16[3,96,128]{2,1,0:T(8,128)(2,1)} %get-tuple-element.62), channel_id=1, source_target_pairs={{0,1},{1,2},{2,3},{3,4},{4,5},{5,6},{6,7},{7,8},{8,9},{9,10},{10,1... | collective-permute-start | bytes 221192 | tf_op jit(solution)/shard_map/ppermute | solution.py:18
  126.3 3.3 %concatenate.116 = bf16[12,96,128]{2,0,1:T(8,128)(2,1)} concatenate(bf16[2,96,128]{2,0,1:T(2,128)(2,1)} %get-tuple-element.94, bf16[2,96,128]{2,0,1:T(2,128)(2,1)} %get-tuple-element.92, bf16[2,96,128]{2,0,1:T(2,128)(2,1)} %get-tuple-element.90, bf16[2,96,128]{2,0,1:T(2,128)(2,1)} %get-tuple-element.88, bf16[2,96,128]{2,0,1:T(2,128)(2,1)} %get-tuple-element.86, ...), dimensions={0} | concatenate | bytes 589824 | tf_op jit(solution)/shard_map/concatenate | solution.py:163
  129.6 2.0 %fusion.92 = f32[8,96,128]{2,0,1:T(8,128)} fusion(bf16[12,96,128]{2,0,1:T(8,128)(2,1)} %concatenate.116, f32[12]{0:T(128)S(1)} %eq.250, f32[8]{0:T(128)S(1)} %iota_convert_fusion), kind=kOutput, calls=%fused_computation.172 | convolution fusion | flops 2359392 | bytes 688208 | tf_op jit(solution)/shard_map/ks,spr->kpr/dot_general | solution.py:174
  131.6 2.5 %concatenate.115 = bf16[12,96,128]{2,0,1:T(8,128)(2,1)} concatenate(bf16[2,96,128]{2,0,1:T(2,128)(2,1)} %get-tuple-element.95, bf16[2,96,128]{2,0,1:T(2,128)(2,1)} %get-tuple-element.93, bf16[2,96,128]{2,0,1:T(2,128)(2,1)} %get-tuple-element.91, bf16[2,96,128]{2,0,1:T(2,128)(2,1)} %get-tuple-element.89, bf16[2,96,128]{2,0,1:T(2,128)(2,1)S(1)} %get-tuple-element.87, ...), dimensions={0} | concatenate | bytes 589824 | tf_op jit(solution)/shard_map/concatenate | solution.py:167
  134.2 2.3 %fusion.12 = f32[8,96,128]{2,1,0:T(8,128)S(1)} fusion(bf16[12,8]{0,1:T(8,128)(2,1)S(1)} %copy.60, bf16[12,96,96]{2,1,0:T(8,128)(2,1)} %copy-done.13, bf16[12,96,128]{2,0,1:T(8,128)(2,1)} %concatenate.115), kind=kOutput, calls=%fused_computation.19 | convolution fusion | flops 227377152 | bytes 909504 | tf_op jit(solution)/shard_map/kamb,mbr->kar/dot_general | solution.py:171
  137.1 2.6 %fusion.54 = (bf16[8,96,128]{2,1,0:T(8,128)(2,1)S(1)}, f32[8,96,128]{2,1,0:T(8,128)}) fusion(f32[8,96,128]{2,1,0:T(8,128)S(1)} %copy-done.6, f32[1,8,96,128]{3,2,1,0:T(8,128)S(1)} %copy-done, f32[8,96,128]{2,0,1:T(8,128)S(1)} %copy-done.7, f32[8,96,128]{2,1,0:T(8,128)S(1)} %fusion.12, bf16[8,96,14,96]{3,1,2,0:T(8,128)(2,1)S(1)} %bitcast_add_fusion, ...), kind=kOutput, calls=%fused_computation.72 | convolution fusion | flops 265568256 | bytes 4571136 | tf_op jit(solution)/shard_map/kamb,mbr->kar/dot_general | solution.py:169
  142.0 2.4 %collective-permute-start.24 = (bf16[4,96,128]{2,0,1:T(4,128)(2,1)S(1)}, bf16[4,96,128]{2,0,1:T(4,128)(2,1)S(1)}, u32[]{:S(2)}, u32[]{:S(2)}) collective-permute-start(bf16[4,96,128]{2,0,1:T(4,128)(2,1)S(1)} %pad_maximum_fusion.18), channel_id=1, source_target_pairs={{0,496},{16,0},{32,16},{48,32},{64,48},{80,64},{96,80},{112,96},{1... | collective-permute-start | bytes 294920 | tf_op jit(solution)/shard_map/ppermute | solution.py:23
  144.5 2.4 %collective-permute-start.23 = (bf16[4,96,128]{2,0,1:T(4,128)(2,1)S(1)}, bf16[4,96,128]{2,0,1:T(4,128)(2,1)S(1)}, u32[]{:S(2)}, u32[]{:S(2)}) collective-permute-start(bf16[4,96,128]{2,0,1:T(4,128)(2,1)S(1)} %pad_maximum_fusion.17), channel_id=1, source_target_pairs={{0,480},{16,496},{32,0},{48,16},{64,32},{80,48},{96,64},{112,80},{... | collective-permute-start | bytes 294920 | tf_op jit(solution)/shard_map/ppermute | solution.py:23
  147.0 1.9 %collective-permute-start.22 = (bf16[4,96,128]{2,0,1:T(4,128)(2,1)S(1)}, bf16[4,96,128]{2,0,1:T(4,128)(2,1)S(1)}, u32[]{:S(2)}, u32[]{:S(2)}) collective-permute-start(bf16[4,96,128]{2,0,1:T(4,128)(2,1)S(1)} %pad_maximum_fusion.16), channel_id=1, source_target_pairs={{0,464},{16,480},{32,496},{48,0},{64,16},{80,32},{96,48},{112,64},... | collective-permute-start | bytes 294920 | tf_op jit(solution)/shard_map/ppermute | solution.py:23
  149.0 7.8 %collective-permute-start.21 = (bf16[4,96,128]{2,0,1:T(4,128)(2,1)S(1)}, bf16[4,96,128]{2,0,1:T(4,128)(2,1)S(1)}, u32[]{:S(2)}, u32[]{:S(2)}) collective-permute-start(bf16[4,96,128]{2,0,1:T(4,128)(2,1)S(1)} %pad_maximum_fusion.15), channel_id=1, source_target_pairs={{0,48},{16,64},{32,80},{48,96},{64,112},{80,128},{96,144},{112,160... | collective-permute-start | bytes 294920 | tf_op jit(solution)/shard_map/ppermute | solution.py:23
  157.0 2.9 %collective-permute-start.20 = (bf16[4,96,128]{2,0,1:T(4,128)(2,1)S(1)}, bf16[4,96,128]{2,0,1:T(4,128)(2,1)S(1)}, u32[]{:S(2)}, u32[]{:S(2)}) collective-permute-start(bf16[4,96,128]{2,0,1:T(4,128)(2,1)S(1)} %pad_maximum_fusion.14), channel_id=1, source_target_pairs={{0,32},{16,48},{32,64},{48,80},{64,96},{80,112},{96,128},{112,144}... | collective-permute-start | bytes 294920 | tf_op jit(solution)/shard_map/ppermute | solution.py:23
  160.0 3.4 %collective-permute-start.19 = (bf16[4,96,128]{2,0,1:T(4,128)(2,1)S(1)}, bf16[4,96,128]{2,0,1:T(4,128)(2,1)S(1)}, u32[]{:S(2)}, u32[]{:S(2)}) collective-permute-start(bf16[4,96,128]{2,0,1:T(4,128)(2,1)S(1)} %pad_maximum_fusion.13), channel_id=1, source_target_pairs={{0,16},{16,32},{32,48},{48,64},{64,80},{80,96},{96,112},{112,128},... | collective-permute-start | bytes 294920 | tf_op jit(solution)/shard_map/ppermute | solution.py:23
  163.6 1.9 %collective-permute-start.17 = (bf16[3,96,128]{2,1,0:T(8,128)(2,1)}, bf16[3,96,128]{2,1,0:T(8,128)(2,1)}, u32[]{:S(2)}, u32[]{:S(2)}) collective-permute-start(bf16[3,96,128]{2,1,0:T(8,128)(2,1)} %get-tuple-element.60), channel_id=1, source_target_pairs={{0,1},{1,2},{2,3},{3,4},{4,5},{5,6},{6,7},{7,8},{8,9},{9,10},{10,1... | collective-permute-start | bytes 221192 | tf_op jit(solution)/shard_map/ppermute | solution.py:18
  166.2 9.4 %collective-permute-start.18 = (bf16[3,96,128]{2,1,0:T(8,128)(2,1)}, bf16[3,96,128]{2,1,0:T(8,128)(2,1)}, u32[]{:S(2)}, u32[]{:S(2)}) collective-permute-start(bf16[3,96,128]{2,1,0:T(8,128)(2,1)} %get-tuple-element.61), channel_id=1, source_target_pairs={{1,0},{2,1},{3,2},{4,3},{5,4},{6,5},{7,6},{8,7},{9,8},{10,9},{11,1... | collective-permute-start | bytes 221192 | tf_op jit(solution)/shard_map/ppermute | solution.py:18
  178.4 3.3 %concatenate.125 = bf16[12,96,128]{2,0,1:T(8,128)(2,1)} concatenate(bf16[2,96,128]{2,0,1:T(2,128)(2,1)} %get-tuple-element.82, bf16[2,96,128]{2,0,1:T(2,128)(2,1)} %get-tuple-element.80, bf16[2,96,128]{2,0,1:T(2,128)(2,1)} %get-tuple-element.78, bf16[2,96,128]{2,0,1:T(2,128)(2,1)} %get-tuple-element.76, bf16[2,96,128]{2,0,1:T(2,128)(2,1)} %get-tuple-element.74, ...), dimensions={0} | concatenate | bytes 589824 | tf_op jit(solution)/shard_map/concatenate | solution.py:163
  181.7 2.0 %fusion.90 = f32[8,96,128]{2,0,1:T(8,128)} fusion(bf16[12,96,128]{2,0,1:T(8,128)(2,1)} %concatenate.125, f32[12]{0:T(128)S(1)} %eq.250, f32[8]{0:T(128)S(1)} %iota_convert_fusion), kind=kOutput, calls=%fused_computation.170 | convolution fusion | flops 2359392 | bytes 688208 | tf_op jit(solution)/shard_map/ks,spr->kpr/dot_general | solution.py:174
  183.7 2.5 %concatenate.124 = bf16[12,96,128]{2,0,1:T(8,128)(2,1)} concatenate(bf16[2,96,128]{2,0,1:T(2,128)(2,1)} %get-tuple-element.83, bf16[2,96,128]{2,0,1:T(2,128)(2,1)} %get-tuple-element.81, bf16[2,96,128]{2,0,1:T(2,128)(2,1)} %get-tuple-element.79, bf16[2,96,128]{2,0,1:T(2,128)(2,1)S(1)} %get-tuple-element.77, bf16[2,96,128]{2,0,1:T(2,128)(2,1)S(1)} %get-tuple-element.75, ...), dimensions={0} | concatenate | bytes 589824 | tf_op jit(solution)/shard_map/concatenate | solution.py:167
  186.3 2.3 %fusion.15 = f32[8,96,128]{2,1,0:T(8,128)S(1)} fusion(bf16[12,8]{0,1:T(8,128)(2,1)S(1)} %copy.60, bf16[12,96,96]{2,1,0:T(8,128)(2,1)} %copy-done.13, bf16[12,96,128]{2,0,1:T(8,128)(2,1)} %concatenate.124), kind=kOutput, calls=%fused_computation.20 | convolution fusion | flops 227377152 | bytes 909504 | tf_op jit(solution)/shard_map/kamb,mbr->kar/dot_general | solution.py:171
  188.6 2.8 %fusion.30 = f32[1,8,96,128]{3,2,1,0:T(8,128)} fusion(f32[8,96,128]{2,1,0:T(8,128)S(1)} %copy-done.10, f32[8,96,128]{2,1,0:T(8,128)S(1)} %fusion.15, bf16[8,96,14,96]{3,1,2,0:T(8,128)(2,1)S(1)} %bitcast_add_fusion, f32[8,96,128]{2,0,1:T(8,128)S(1)} %copy-done.11, f32[1,8,96,128]{3,2,1,0:T(8,128)S(1)} %copy-done, ...), kind=kOutput, calls=%fused_computation.36 | convolution fusion | flops 266158080 | bytes 4767744 | tf_op jit(solution)/shard_map/kamb,mbr->kar/dot_general | solution.py:169
  (141 shorter events, 22.1 us)
Async XLA Ops:
  0.0 4.7 %copy-start.14 = (s32[1,1,6]{2,1,0:T(1,128)S(1)}, s32[1,1,6]{2,1,0:T(1,128)}, u32[]{:S(2)}) copy-start(s32[1,1,6]{2,1,0:T(1,128)} %param.10) | copy-start | bytes 76
  2.8 19.4 %copy-start.3 = (bf16[8,96,128]{2,1,0:T(8,128)(2,1)}, bf16[8,96,128]{2,1,0:T(8,128)(2,1)S(1)}, u32[]{:S(2)}) copy-start(bf16[8,96,128]{2,1,0:T(8,128)(2,1)S(1)} %fusion.41) | copy-start | bytes 589828
  2.9 15.5 %copy-start.2 = (bf16[1,8,4,96,96]{4,3,2,1,0:T(8,128)(2,1)S(1)}, bf16[1,8,4,96,96]{4,3,2,1,0:T(8,128)(2,1)}, u32[]{:S(2)}) copy-start(bf16[1,8,4,96,96]{4,3,2,1,0:T(8,128)(2,1)} %param.8) | copy-start | bytes 1769476
  3.2 19.0 %copy-start.1 = (bf16[1,1,6,2,96,96]{5,4,3,2,1,0:T(8,128)(2,1)S(1)}, bf16[1,1,6,2,96,96]{5,4,3,2,1,0:T(8,128)(2,1)}, u32[]{:S(2)}) copy-start(bf16[1,1,6,2,96,96]{5,4,3,2,1,0:T(8,128)(2,1)} %param.11) | copy-start | bytes 663556
  5.9 52.5 %collective-permute-start.3 = (bf16[11,96,128]{2,1,0:T(8,128)(2,1)S(1)}, bf16[11,96,128]{2,1,0:T(8,128)(2,1)S(1)}, u32[]{:S(2)}, u32[]{:S(2)}) collective-permute-start(bf16[11,96,128]{2,1,0:T(8,128)(2,1)S(1)} %get-tuple-element.71), channel_id=1, source_target_pairs={{0,16},{16,32},{32,48},{48,64},{64,80},{80,96},{96,112},{112,128},... | collective-permute-start | bytes 811016 | tf_op jit(solution)/shard_map/ppermute | solution.py:23
  9.3 54.6 %collective-permute-start.4 = (bf16[11,96,128]{2,1,0:T(8,128)(2,1)}, bf16[11,96,128]{2,1,0:T(8,128)(2,1)}, u32[]{:S(2)}, u32[]{:S(2)}) collective-permute-start(bf16[11,96,128]{2,1,0:T(8,128)(2,1)} %get-tuple-element.67), channel_id=1, source_target_pairs={{0,32},{16,48},{32,64},{48,80},{64,96},{80,112},{96,128},{112,144}... | collective-permute-start | bytes 811016 | tf_op jit(solution)/shard_map/ppermute | solution.py:23
  12.8 53.1 %collective-permute-start.5 = (bf16[11,96,128]{2,1,0:T(8,128)(2,1)}, bf16[11,96,128]{2,1,0:T(8,128)(2,1)}, u32[]{:S(2)}, u32[]{:S(2)}) collective-permute-start(bf16[11,96,128]{2,1,0:T(8,128)(2,1)} %get-tuple-element.68), channel_id=1, source_target_pairs={{0,48},{16,64},{32,80},{48,96},{64,112},{80,128},{96,144},{112,160... | collective-permute-start | bytes 811016 | tf_op jit(solution)/shard_map/ppermute | solution.py:23
  15.3 60.1 %collective-permute-start.6 = (bf16[11,96,128]{2,1,0:T(8,128)(2,1)}, bf16[11,96,128]{2,1,0:T(8,128)(2,1)}, u32[]{:S(2)}, u32[]{:S(2)}) collective-permute-start(bf16[11,96,128]{2,1,0:T(8,128)(2,1)} %get-tuple-element.69), channel_id=1, source_target_pairs={{0,464},{16,480},{32,496},{48,0},{64,16},{80,32},{96,48},{112,64},... | collective-permute-start | bytes 811016 | tf_op jit(solution)/shard_map/ppermute | solution.py:23
  18.4 34.8 %collective-permute-start = (bf16[3,4,96,96]{3,2,1,0:T(8,128)(2,1)S(1)}, bf16[3,4,96,96]{3,2,1,0:T(8,128)(2,1)S(1)}, u32[]{:S(2)}, u32[]{:S(2)}) collective-permute-start(bf16[3,4,96,96]{3,2,1,0:T(8,128)(2,1)S(1)} %slice_bitcast_fusion), channel_id=1, source_target_pairs={{0,1},{1,2},{2,3},{3,4},{4,5},{5,6},{6,7},{7,8},{8,9},{9,10},{10,1... | collective-permute-start | bytes 663560 | tf_op jit(solution)/shard_map/ppermute | solution.py:18
  23.3 37.5 %copy-start.13 = (bf16[12,96,96]{2,1,0:T(8,128)(2,1)}, bf16[12,96,96]{2,1,0:T(8,128)(2,1)S(1)}, u32[]{:S(2)}) copy-start(bf16[12,96,96]{2,1,0:T(8,128)(2,1)S(1)} %bitcast_dynamic-update-slice_fusion) | copy-start | bytes 663556
  53.2 22.3 %collective-permute-start.7 = (bf16[11,96,128]{2,1,0:T(8,128)(2,1)}, bf16[11,96,128]{2,1,0:T(8,128)(2,1)}, u32[]{:S(2)}, u32[]{:S(2)}) collective-permute-start(bf16[11,96,128]{2,1,0:T(8,128)(2,1)} %get-tuple-element.70), channel_id=1, source_target_pairs={{0,480},{16,496},{32,0},{48,16},{64,32},{80,48},{96,64},{112,80},{... | collective-permute-start | bytes 811016 | tf_op jit(solution)/shard_map/ppermute | solution.py:23
  58.4 2.4 %copy-start.12 = (bf16[11,96,128]{2,1,0:T(8,128)(2,1)}, bf16[11,96,128]{2,1,0:T(8,128)(2,1)S(1)}, u32[]{:S(2)}) copy-start(bf16[11,96,128]{2,1,0:T(8,128)(2,1)S(1)} %collective-permute-done.3.refs_0_) | copy-start | bytes 811012
  58.4 17.0 %collective-permute-start.8 = (bf16[11,96,128]{2,1,0:T(8,128)(2,1)}, bf16[11,96,128]{2,1,0:T(8,128)(2,1)}, u32[]{:S(2)}, u32[]{:S(2)}) collective-permute-start(bf16[11,96,128]{2,1,0:T(8,128)(2,1)} %get-tuple-element.66), channel_id=1, source_target_pairs={{0,496},{16,0},{32,16},{48,32},{64,48},{80,64},{96,80},{112,96},{1... | collective-permute-start | bytes 811016 | tf_op jit(solution)/shard_map/ppermute | solution.py:23
  64.0 21.5 %collective-permute-start.1 = (bf16[3,96,128]{2,1,0:T(8,128)(2,1)}, bf16[3,96,128]{2,1,0:T(8,128)(2,1)}, u32[]{:S(2)}, u32[]{:S(2)}) collective-permute-start(bf16[3,96,128]{2,1,0:T(8,128)(2,1)} %get-tuple-element.64), channel_id=1, source_target_pairs={{0,1},{1,2},{2,3},{3,4},{4,5},{5,6},{6,7},{7,8},{8,9},{9,10},{10,1... | collective-permute-start | bytes 221192 | tf_op jit(solution)/shard_map/ppermute | solution.py:18
  65.9 19.6 %copy-start = (f32[1,8,96,128]{3,2,1,0:T(8,128)S(1)}, f32[1,8,96,128]{3,2,1,0:T(8,128)}, u32[]{:S(2)}) copy-start(f32[1,8,96,128]{3,2,1,0:T(8,128)} %param.7) | copy-start | bytes 1179652
  65.9 19.6 %collective-permute-start.2 = (bf16[3,96,128]{2,1,0:T(8,128)(2,1)S(1)}, bf16[3,96,128]{2,1,0:T(8,128)(2,1)}, u32[]{:S(2)}, u32[]{:S(2)}) collective-permute-start(bf16[3,96,128]{2,1,0:T(8,128)(2,1)S(1)} %get-tuple-element.65), channel_id=1, source_target_pairs={{1,0},{2,1},{3,2},{4,3},{5,4},{6,5},{7,6},{8,7},{9,8},{10,9},{11,1... | collective-permute-start | bytes 221192 | tf_op jit(solution)/shard_map/ppermute | solution.py:18
  88.5 7.0 %copy-start.4 = (bf16[8,96,128]{2,1,0:T(8,128)(2,1)}, bf16[8,96,128]{2,1,0:T(8,128)(2,1)S(1)}, u32[]{:S(2)}) copy-start(bf16[8,96,128]{2,1,0:T(8,128)(2,1)S(1)} %get-tuple-element.130) | copy-start | bytes 589828
  90.7 22.8 %collective-permute-start.16 = (bf16[4,96,128]{2,0,1:T(4,128)(2,1)S(1)}, bf16[4,96,128]{2,0,1:T(4,128)(2,1)S(1)}, u32[]{:S(2)}, u32[]{:S(2)}) collective-permute-start(bf16[4,96,128]{2,0,1:T(4,128)(2,1)S(1)} %pad_maximum_fusion.12), channel_id=1, source_target_pairs={{0,496},{16,0},{32,16},{48,32},{64,48},{80,64},{96,80},{112,96},{1... | collective-permute-start | bytes 294920 | tf_op jit(solution)/shard_map/ppermute | solution.py:23
  95.5 21.8 %collective-permute-start.15 = (bf16[4,96,128]{2,0,1:T(4,128)(2,1)S(1)}, bf16[4,96,128]{2,0,1:T(4,128)(2,1)S(1)}, u32[]{:S(2)}, u32[]{:S(2)}) collective-permute-start(bf16[4,96,128]{2,0,1:T(4,128)(2,1)S(1)} %pad_maximum_fusion.11), channel_id=1, source_target_pairs={{0,480},{16,496},{32,0},{48,16},{64,32},{80,48},{96,64},{112,80},{... | collective-permute-start | bytes 294920 | tf_op jit(solution)/shard_map/ppermute | solution.py:23
  101.5 18.5 %collective-permute-start.14 = (bf16[4,96,128]{2,0,1:T(4,128)(2,1)S(1)}, bf16[4,96,128]{2,0,1:T(4,128)(2,1)S(1)}, u32[]{:S(2)}, u32[]{:S(2)}) collective-permute-start(bf16[4,96,128]{2,0,1:T(4,128)(2,1)S(1)} %pad_maximum_fusion.10), channel_id=1, source_target_pairs={{0,464},{16,480},{32,496},{48,0},{64,16},{80,32},{96,48},{112,64},... | collective-permute-start | bytes 294920 | tf_op jit(solution)/shard_map/ppermute | solution.py:23
  103.7 20.5 %collective-permute-start.13 = (bf16[4,96,128]{2,0,1:T(4,128)(2,1)S(1)}, bf16[4,96,128]{2,0,1:T(4,128)(2,1)S(1)}, u32[]{:S(2)}, u32[]{:S(2)}) collective-permute-start(bf16[4,96,128]{2,0,1:T(4,128)(2,1)S(1)} %pad_maximum_fusion.9), channel_id=1, source_target_pairs={{0,48},{16,64},{32,80},{48,96},{64,112},{80,128},{96,144},{112,160... | collective-permute-start | bytes 294920 | tf_op jit(solution)/shard_map/ppermute | solution.py:23
  111.5 13.4 %collective-permute-start.12 = (bf16[4,96,128]{2,0,1:T(4,128)(2,1)S(1)}, bf16[4,96,128]{2,0,1:T(4,128)(2,1)S(1)}, u32[]{:S(2)}, u32[]{:S(2)}) collective-permute-start(bf16[4,96,128]{2,0,1:T(4,128)(2,1)S(1)} %pad_maximum_fusion.8), channel_id=1, source_target_pairs={{0,32},{16,48},{32,64},{48,80},{64,96},{80,112},{96,128},{112,144}... | collective-permute-start | bytes 294920 | tf_op jit(solution)/shard_map/ppermute | solution.py:23
  113.5 12.1 %collective-permute-start.11 = (bf16[4,96,128]{2,0,1:T(4,128)(2,1)S(1)}, bf16[4,96,128]{2,0,1:T(4,128)(2,1)S(1)}, u32[]{:S(2)}, u32[]{:S(2)}) collective-permute-start(bf16[4,96,128]{2,0,1:T(4,128)(2,1)S(1)} %pad_maximum_fusion.7), channel_id=1, source_target_pairs={{0,16},{16,32},{32,48},{48,64},{64,80},{80,96},{96,112},{112,128},... | collective-permute-start | bytes 294920 | tf_op jit(solution)/shard_map/ppermute | solution.py:23
  117.3 19.1 %collective-permute-start.10 = (bf16[3,96,128]{2,1,0:T(8,128)(2,1)}, bf16[3,96,128]{2,1,0:T(8,128)(2,1)}, u32[]{:S(2)}, u32[]{:S(2)}) collective-permute-start(bf16[3,96,128]{2,1,0:T(8,128)(2,1)} %get-tuple-element.63), channel_id=1, source_target_pairs={{1,0},{2,1},{3,2},{4,3},{5,4},{6,5},{7,6},{8,7},{9,8},{10,9},{11,1... | collective-permute-start | bytes 221192 | tf_op jit(solution)/shard_map/ppermute | solution.py:18
  120.0 17.0 %collective-permute-start.9 = (bf16[3,96,128]{2,1,0:T(8,128)(2,1)}, bf16[3,96,128]{2,1,0:T(8,128)(2,1)}, u32[]{:S(2)}, u32[]{:S(2)}) collective-permute-start(bf16[3,96,128]{2,1,0:T(8,128)(2,1)} %get-tuple-element.62), channel_id=1, source_target_pairs={{0,1},{1,2},{2,3},{3,4},{4,5},{5,6},{6,7},{7,8},{8,9},{9,10},{10,1... | collective-permute-start | bytes 221192 | tf_op jit(solution)/shard_map/ppermute | solution.py:18
  134.2 2.9 %copy-start.5 = (bf16[8,96,128]{2,1,0:T(8,128)(2,1)S(1)}, bf16[8,96,128]{2,1,0:T(8,128)(2,1)}, u32[]{:S(2)}) copy-start(bf16[8,96,128]{2,1,0:T(8,128)(2,1)} %copy-done.4) | copy-start | bytes 589828
  134.2 2.9 %copy-start.6 = (f32[8,96,128]{2,1,0:T(8,128)S(1)}, f32[8,96,128]{2,1,0:T(8,128)}, u32[]{:S(2)}) copy-start(f32[8,96,128]{2,1,0:T(8,128)} %get-tuple-element.131) | copy-start | bytes 1179652
  134.2 2.9 %copy-start.7 = (f32[8,96,128]{2,0,1:T(8,128)S(1)}, f32[8,96,128]{2,0,1:T(8,128)}, u32[]{:S(2)}) copy-start(f32[8,96,128]{2,0,1:T(8,128)} %fusion.92) | copy-start | bytes 1179652
  139.7 4.8 %copy-start.8 = (bf16[8,96,128]{2,1,0:T(8,128)(2,1)}, bf16[8,96,128]{2,1,0:T(8,128)(2,1)S(1)}, u32[]{:S(2)}) copy-start(bf16[8,96,128]{2,1,0:T(8,128)(2,1)S(1)} %get-tuple-element.132) | copy-start | bytes 589828
  142.0 18.1 %collective-permute-start.24 = (bf16[4,96,128]{2,0,1:T(4,128)(2,1)S(1)}, bf16[4,96,128]{2,0,1:T(4,128)(2,1)S(1)}, u32[]{:S(2)}, u32[]{:S(2)}) collective-permute-start(bf16[4,96,128]{2,0,1:T(4,128)(2,1)S(1)} %pad_maximum_fusion.18), channel_id=1, source_target_pairs={{0,496},{16,0},{32,16},{48,32},{64,48},{80,64},{96,80},{112,96},{1... | collective-permute-start | bytes 294920 | tf_op jit(solution)/shard_map/ppermute | solution.py:23
  144.5 19.1 %collective-permute-start.23 = (bf16[4,96,128]{2,0,1:T(4,128)(2,1)S(1)}, bf16[4,96,128]{2,0,1:T(4,128)(2,1)S(1)}, u32[]{:S(2)}, u32[]{:S(2)}) collective-permute-start(bf16[4,96,128]{2,0,1:T(4,128)(2,1)S(1)} %pad_maximum_fusion.17), channel_id=1, source_target_pairs={{0,480},{16,496},{32,0},{48,16},{64,32},{80,48},{96,64},{112,80},{... | collective-permute-start | bytes 294920 | tf_op jit(solution)/shard_map/ppermute | solution.py:23
  147.0 19.2 %collective-permute-start.22 = (bf16[4,96,128]{2,0,1:T(4,128)(2,1)S(1)}, bf16[4,96,128]{2,0,1:T(4,128)(2,1)S(1)}, u32[]{:S(2)}, u32[]{:S(2)}) collective-permute-start(bf16[4,96,128]{2,0,1:T(4,128)(2,1)S(1)} %pad_maximum_fusion.16), channel_id=1, source_target_pairs={{0,464},{16,480},{32,496},{48,0},{64,16},{80,32},{96,48},{112,64},... | collective-permute-start | bytes 294920 | tf_op jit(solution)/shard_map/ppermute | solution.py:23
  149.0 27.2 %collective-permute-start.21 = (bf16[4,96,128]{2,0,1:T(4,128)(2,1)S(1)}, bf16[4,96,128]{2,0,1:T(4,128)(2,1)S(1)}, u32[]{:S(2)}, u32[]{:S(2)}) collective-permute-start(bf16[4,96,128]{2,0,1:T(4,128)(2,1)S(1)} %pad_maximum_fusion.15), channel_id=1, source_target_pairs={{0,48},{16,64},{32,80},{48,96},{64,112},{80,128},{96,144},{112,160... | collective-permute-start | bytes 294920 | tf_op jit(solution)/shard_map/ppermute | solution.py:23
  157.0 20.0 %collective-permute-start.20 = (bf16[4,96,128]{2,0,1:T(4,128)(2,1)S(1)}, bf16[4,96,128]{2,0,1:T(4,128)(2,1)S(1)}, u32[]{:S(2)}, u32[]{:S(2)}) collective-permute-start(bf16[4,96,128]{2,0,1:T(4,128)(2,1)S(1)} %pad_maximum_fusion.14), channel_id=1, source_target_pairs={{0,32},{16,48},{32,64},{48,80},{64,96},{80,112},{96,128},{112,144}... | collective-permute-start | bytes 294920 | tf_op jit(solution)/shard_map/ppermute | solution.py:23
  160.0 17.7 %collective-permute-start.19 = (bf16[4,96,128]{2,0,1:T(4,128)(2,1)S(1)}, bf16[4,96,128]{2,0,1:T(4,128)(2,1)S(1)}, u32[]{:S(2)}, u32[]{:S(2)}) collective-permute-start(bf16[4,96,128]{2,0,1:T(4,128)(2,1)S(1)} %pad_maximum_fusion.13), channel_id=1, source_target_pairs={{0,16},{16,32},{32,48},{48,64},{64,80},{80,96},{96,112},{112,128},... | collective-permute-start | bytes 294920 | tf_op jit(solution)/shard_map/ppermute | solution.py:23
  163.6 25.0 %collective-permute-start.17 = (bf16[3,96,128]{2,1,0:T(8,128)(2,1)}, bf16[3,96,128]{2,1,0:T(8,128)(2,1)}, u32[]{:S(2)}, u32[]{:S(2)}) collective-permute-start(bf16[3,96,128]{2,1,0:T(8,128)(2,1)} %get-tuple-element.60), channel_id=1, source_target_pairs={{0,1},{1,2},{2,3},{3,4},{4,5},{5,6},{6,7},{7,8},{8,9},{9,10},{10,1... | collective-permute-start | bytes 221192 | tf_op jit(solution)/shard_map/ppermute | solution.py:18
  166.2 22.4 %collective-permute-start.18 = (bf16[3,96,128]{2,1,0:T(8,128)(2,1)}, bf16[3,96,128]{2,1,0:T(8,128)(2,1)}, u32[]{:S(2)}, u32[]{:S(2)}) collective-permute-start(bf16[3,96,128]{2,1,0:T(8,128)(2,1)} %get-tuple-element.61), channel_id=1, source_target_pairs={{1,0},{2,1},{3,2},{4,3},{5,4},{6,5},{7,6},{8,7},{9,8},{10,9},{11,1... | collective-permute-start | bytes 221192 | tf_op jit(solution)/shard_map/ppermute | solution.py:18
  178.4 10.2 %copy-start.9 = (bf16[8,96,128]{2,1,0:T(8,128)(2,1)S(1)}, bf16[8,96,128]{2,1,0:T(8,128)(2,1)}, u32[]{:S(2)}) copy-start(bf16[8,96,128]{2,1,0:T(8,128)(2,1)} %copy-done.8) | copy-start | bytes 589828
  186.3 2.3 %copy-start.10 = (f32[8,96,128]{2,1,0:T(8,128)S(1)}, f32[8,96,128]{2,1,0:T(8,128)}, u32[]{:S(2)}) copy-start(f32[8,96,128]{2,1,0:T(8,128)} %get-tuple-element.133) | copy-start | bytes 1179652
  186.3 2.3 %copy-start.11 = (f32[8,96,128]{2,0,1:T(8,128)S(1)}, f32[8,96,128]{2,0,1:T(8,128)}, u32[]{:S(2)}) copy-start(f32[8,96,128]{2,0,1:T(8,128)} %fusion.90) | copy-start | bytes 1179652

commit v11 on v9

--- a/solution.py
+++ b/solution.py
@@ -151,8 +151,11 @@
             received.append(got)
             fetched[bucket_of[-s]] = got[:slots]
             landed.append(got[slots:])
-        low = shifted_open(probe_bf[knots - 3 :], "seg", 1)
-        high = shifted_open(probe_bf[:3], "seg", -1)
+        tail_rows, head_rows = probe_bf[knots - 3 :], probe_bf[:3]
+        if turn > 0:
+            tail_rows, head_rows, _ = lax.optimization_barrier((tail_rows, head_rows, received[0]))
+        low = shifted_open(tail_rows, "seg", 1)
+        high = shifted_open(head_rows, "seg", -1)
         if answer_pick is None:
             first_fetched, landed, heard = unpack_call(first_pick, received)
             heard = heard[:, :slots].astype(jnp.float32)

time: 157 us -> 175 us (1.11)
  the two profiles are of different devices: /device:TPU:24 before, /device:TPU:159 now
where the time goes in v11:
time: 175 us; the launch traced here: 174 us
  starting transfers between devices  92.5 us (53%)
  waiting for transfers between devices  45.4 us (26%)
  matrix products  13.8 us (8%)
  other arithmetic  10.6 us (6%)
  local copies, waits for them, and re-layouts  8.69 us (5%)
  Pallas kernels  2.21 us (1%)
    ppermute x18, starting transfers between devices, shifted_ring(): lax.ppermute(value, axis, [(i, (i + steps) % count) for i in range(count)])  60.2 us
    ppermute x7, starting transfers between devices, shifted_open(): lax.ppermute(value, axis, [(source, source + steps) for source in range(i...  32.3 us
    ppermute x7, waiting for transfers between devices, shifted_open(): lax.ppermute(value, axis, [(source, source + steps) for source in range(i...  31.2 us
    ppermute x18, waiting for transfers between devices, shifted_ring(): lax.ppermute(value, axis, [(i, (i + steps) % count) for i in range(count)])  14.2 us
    dot_general x2, matrix products, body(): jnp.einsum('kamb,mbr->kar', weight, stacked, preferred_element_type=jnp.f...  5.39 us
  transfers between devices with their start and end apart: 25, of which 8 were waited for; matrix products, arithmetic and copies ran while one was open for 12% of the time, Pallas kernels for 1%

profile of v11, /device:TPU:159, one launch (start us, length us, event | category | flops | bytes accessed | tf_op | source)
XLA Modules:
  0.0 174.1 jit_solution(7271829219399595035)
XLA Ops:
  0.0 1.0 slice_bitcast_fusion
  1.0 8.5 %collective-permute-start = (bf16[3,4,96,96]{3,2,1,0:T(8,128)(2,1)S(1)}, bf16[3,4,96,96]{3,2,1,0:T(8,128)(2,1)S(1)}, u32[]{:S(2)}, u32[]{:S(2)}) collective-permute-start(bf16[3,4,96,96]{3,2,1,0:T(8,128)(2,1)S(1)} %slice_bitcast_fusion), channel_id=1, source_target_pairs={{0,1},{1,2},{2,3},{3,4},{4,5},{5,6},{6,7},{7,8},{8,9},{9,10},{10,1... | collective-permute-start | bytes 663560 | tf_op jit(solution)/shard_map/ppermute | solution.py:18
  12.2 1.0 fusion.27
  14.0 1.1 fusion.42
  15.1 2.9 %collective-permute-start.8 = (bf16[11,96,128]{2,1,0:T(8,128)(2,1)S(1)}, bf16[11,96,128]{2,1,0:T(8,128)(2,1)S(1)}, u32[]{:S(2)}, u32[]{:S(2)}) collective-permute-start(bf16[11,96,128]{2,1,0:T(8,128)(2,1)S(1)} %get-tuple-element.74), channel_id=1, source_target_pairs={{0,496},{16,0},{32,16},{48,32},{64,48},{80,64},{96,80},{112,96},{1... | collective-permute-start | bytes 811016 | tf_op jit(solution)/shard_map/ppermute | solution.py:23
  18.0 2.6 %collective-permute-start.4 = (bf16[11,96,128]{2,1,0:T(8,128)(2,1)}, bf16[11,96,128]{2,1,0:T(8,128)(2,1)}, u32[]{:S(2)}, u32[]{:S(2)}) collective-permute-start(bf16[11,96,128]{2,1,0:T(8,128)(2,1)} %get-tuple-element.75), channel_id=1, source_target_pairs={{0,32},{16,48},{32,64},{48,80},{64,96},{80,112},{96,128},{112,144}... | collective-permute-start | bytes 811016 | tf_op jit(solution)/shard_map/ppermute | solution.py:23
  20.6 4.2 %collective-permute-start.5 = (bf16[11,96,128]{2,1,0:T(8,128)(2,1)}, bf16[11,96,128]{2,1,0:T(8,128)(2,1)}, u32[]{:S(2)}, u32[]{:S(2)}) collective-permute-start(bf16[11,96,128]{2,1,0:T(8,128)(2,1)} %get-tuple-element.76), channel_id=1, source_target_pairs={{0,48},{16,64},{32,80},{48,96},{64,112},{80,128},{96,144},{112,160... | collective-permute-start | bytes 811016 | tf_op jit(solution)/shard_map/ppermute | solution.py:23
  24.8 1.9 %collective-permute-start.6 = (bf16[11,96,128]{2,1,0:T(8,128)(2,1)}, bf16[11,96,128]{2,1,0:T(8,128)(2,1)}, u32[]{:S(2)}, u32[]{:S(2)}) collective-permute-start(bf16[11,96,128]{2,1,0:T(8,128)(2,1)} %get-tuple-element.77), channel_id=1, source_target_pairs={{0,464},{16,480},{32,496},{48,0},{64,16},{80,32},{96,48},{112,64},... | collective-permute-start | bytes 811016 | tf_op jit(solution)/shard_map/ppermute | solution.py:23
  28.2 1.7 multiply_bitcast_fusion
  30.6 3.3 %collective-permute-done = bf16[3,4,96,96]{3,2,1,0:T(8,128)(2,1)S(1)} collective-permute-done((bf16[3,4,96,96]{3,2,1,0:T(8,128)(2,1)S(1)}, bf16[3,4,96,96]{3,2,1,0:T(8,128)(2,1)S(1)}, u32[]{:S(2)}, u32[]{:S(2)}) %collective-permute-start) | collective-permute-done | bytes 221216 | tf_op jit(solution)/shard_map/ppermute | solution.py:18
  33.9 2.4 %collective-permute-start.7 = (bf16[11,96,128]{2,1,0:T(8,128)(2,1)}, bf16[11,96,128]{2,1,0:T(8,128)(2,1)}, u32[]{:S(2)}, u32[]{:S(2)}) collective-permute-start(bf16[11,96,128]{2,1,0:T(8,128)(2,1)} %get-tuple-element.78), channel_id=1, source_target_pairs={{0,480},{16,496},{32,0},{48,16},{64,32},{80,48},{96,64},{112,80},{... | collective-permute-start | bytes 811016 | tf_op jit(solution)/shard_map/ppermute | solution.py:23
  36.4 0.9 maximum_bitcast_fusion.3
  37.3 0.8 copy.52
  38.1 0.8 copy.53
  38.9 0.8 copy.54
  39.7 7.8 %collective-permute-start.3 = (bf16[11,96,128]{2,1,0:T(8,128)(2,1)}, bf16[11,96,128]{2,1,0:T(8,128)(2,1)}, u32[]{:S(2)}, u32[]{:S(2)}) collective-permute-start(bf16[11,96,128]{2,1,0:T(8,128)(2,1)} %get-tuple-element.79), channel_id=1, source_target_pairs={{0,16},{16,32},{32,48},{48,64},{64,80},{80,96},{96,112},{112,128},... | collective-permute-start | bytes 811016 | tf_op jit(solution)/shard_map/ppermute | solution.py:23
  47.5 3.2 %bitcast_add_fusion = bf16[8,96,14,96]{3,1,2,0:T(8,128)(2,1)S(1)} fusion(bf16[8,14]{1,0:T(8,128)(2,1)S(1)} %fusion.63, bf16[8,96,96]{1,2,0:T(8,128)(2,1)} %copy.54, bf16[8,14]{1,0:T(8,128)(2,1)S(1)} %get-tuple-element.147, bf16[8,96,96]{1,2,0:T(8,128)(2,1)} %copy.53, bf16[8,14]{1,0:T(8,128)(2,1)S(1)} %get-tuple-element.146, bf16[8,96,96]{1,2,0:T(8,128)(2,1)} %copy.52, ...), kind=kLoop, calls=%fused_computation.3 | loop fusion | flops 13418496 | bytes 3098144 | tf_op jit(solution)/shard_map/add | solution.py:94
  50.7 10.1 %collective-permute-start.1 = (bf16[3,96,128]{2,1,0:T(8,128)(2,1)}, bf16[3,96,128]{2,1,0:T(8,128)(2,1)S(1)}, u32[]{:S(2)}, u32[]{:S(2)}) collective-permute-start(bf16[3,96,128]{2,1,0:T(8,128)(2,1)} %get-tuple-element.72), channel_id=1, source_target_pairs={{0,1},{1,2},{2,3},{3,4},{4,5},{5,6},{6,7},{7,8},{8,9},{9,10},{10,1... | collective-permute-start | bytes 221192 | tf_op jit(solution)/shard_map/ppermute | solution.py:18
  60.9 1.9 %collective-permute-start.2 = (bf16[3,96,128]{2,1,0:T(8,128)(2,1)S(1)}, bf16[3,96,128]{2,1,0:T(8,128)(2,1)}, u32[]{:S(2)}, u32[]{:S(2)}) collective-permute-start(bf16[3,96,128]{2,1,0:T(8,128)(2,1)S(1)} %get-tuple-element.73), channel_id=1, source_target_pairs={{1,0},{2,1},{3,2},{4,3},{5,4},{6,5},{7,6},{8,7},{9,8},{10,9},{11,1... | collective-permute-start | bytes 221192 | tf_op jit(solution)/shard_map/ppermute | solution.py:18
  62.8 2.2 %shard_map.55 = (bf16[12,96,128]{2,1,0:T(8,128)(2,1)}, bf16[12,96,128]{2,1,0:T(8,128)(2,1)}, bf16[6,128]{1,0:T(8,128)(2,1)}) custom-call(s32[6,2]{1,0:T(8,128)} %copy.63.pick_ref, bf16[11,96,128]{2,1,0:T(8,128)(2,1)} %collective-permute-done.3.refs_0_, bf16[11,96,128]{2,1,0:T(8,128)(2,1)} %collective-permute-done.4.refs_1_, ...), custom_call_target="tpu_custom_call" | custom-call | tf_op jit(solution)/shard_map/pallas_call | solution.py:45
  65.8 1.3 fusion.25
  67.1 2.2 %convolution_bitcast_fusion = f32[8,96,128]{2,1,0:T(8,128)S(1)} fusion(bf16[12,96,128]{2,1,0:T(8,128)(2,1)} %get-tuple-element.24, bf16[12,8]{0,1:T(8,128)(2,1)S(1)} %copy.56, bf16[12,96,96]{2,1,0:T(8,128)(2,1)} %copy-done.6), kind=kOutput, calls=%fused_computation.13 | convolution fusion | flops 227377152 | bytes 909504 | tf_op jit(solution)/shard_map/kamb,mbr->kar/dot_general | solution.py:175
  69.9 2.2 %collective-permute-done.2 = bf16[3,96,128]{2,1,0:T(8,128)(2,1)} collective-permute-done((bf16[3,96,128]{2,1,0:T(8,128)(2,1)S(1)}, bf16[3,96,128]{2,1,0:T(8,128)(2,1)}, u32[]{:S(2)}, u32[]{:S(2)}) %collective-permute-start.2) | collective-permute-done | bytes 73760 | tf_op jit(solution)/shard_map/ppermute | solution.py:18
  72.1 2.6 %fusion.49 = (bf16[8,96,128]{2,1,0:T(8,128)(2,1)S(1)}, f32[8,96,128]{2,1,0:T(8,128)}) fusion(f32[1,8,96,128]{3,2,1,0:T(8,128)S(1)} %copy-done.2, f32[8,96,128]{2,0,1:T(8,128)S(1)} %fusion.25, f32[8,96,128]{2,1,0:T(8,128)S(1)} %convolution_bitcast_fusion, bf16[8,96,14,96]{3,1,2,0:T(8,128)(2,1)S(1)} %bitcast_add_fusion, ...), kind=kOutput, calls=%fused_computation.134 | convolution fusion | flops 265273344 | bytes 4177920 | tf_op jit(solution)/shard_map/kamb,mbr->kar/dot_general | solution.py:173
  76.4 4.2 %collective-permute-start.9 = (bf16[4,96,128]{2,1,0:T(8,128)(2,1)S(1)}, bf16[4,96,128]{2,1,0:T(8,128)(2,1)S(1)}, u32[]{:S(2)}, u32[]{:S(2)}) collective-permute-start(bf16[4,96,128]{2,1,0:T(8,128)(2,1)S(1)} %pad_maximum_fusion.30), channel_id=1, source_target_pairs={{0,16},{16,32},{32,48},{48,64},{64,80},{80,96},{96,112},{112,128},... | collective-permute-start | bytes 294920 | tf_op jit(solution)/shard_map/ppermute | solution.py:23
  80.6 1.9 %collective-permute-start.12 = (bf16[4,96,128]{2,1,0:T(8,128)(2,1)S(1)}, bf16[4,96,128]{2,1,0:T(8,128)(2,1)S(1)}, u32[]{:S(2)}, u32[]{:S(2)}) collective-permute-start(bf16[4,96,128]{2,1,0:T(8,128)(2,1)S(1)} %pad_maximum_fusion.31), channel_id=1, source_target_pairs={{0,32},{16,48},{32,64},{48,80},{64,96},{80,112},{96,128},{112,144}... | collective-permute-start | bytes 294920 | tf_op jit(solution)/shard_map/ppermute | solution.py:23
  82.5 1.9 %collective-permute-start.13 = (bf16[4,96,128]{2,1,0:T(8,128)(2,1)S(1)}, bf16[4,96,128]{2,1,0:T(8,128)(2,1)S(1)}, u32[]{:S(2)}, u32[]{:S(2)}) collective-permute-start(bf16[4,96,128]{2,1,0:T(8,128)(2,1)S(1)} %pad_maximum_fusion.32), channel_id=1, source_target_pairs={{0,48},{16,64},{32,80},{48,96},{64,112},{80,128},{96,144},{112,160... | collective-permute-start | bytes 294920 | tf_op jit(solution)/shard_map/ppermute | solution.py:23
  84.5 3.6 %collective-permute-start.14 = (bf16[4,96,128]{2,1,0:T(8,128)(2,1)S(1)}, bf16[4,96,128]{2,1,0:T(8,128)(2,1)S(1)}, u32[]{:S(2)}, u32[]{:S(2)}) collective-permute-start(bf16[4,96,128]{2,1,0:T(8,128)(2,1)S(1)} %pad_maximum_fusion.33), channel_id=1, source_target_pairs={{0,464},{16,480},{32,496},{48,0},{64,16},{80,32},{96,48},{112,64},... | collective-permute-start | bytes 294920 | tf_op jit(solution)/shard_map/ppermute | solution.py:23
  88.2 3.4 %collective-permute-start.15 = (bf16[4,96,128]{2,1,0:T(8,128)(2,1)S(1)}, bf16[4,96,128]{2,1,0:T(8,128)(2,1)S(1)}, u32[]{:S(2)}, u32[]{:S(2)}) collective-permute-start(bf16[4,96,128]{2,1,0:T(8,128)(2,1)S(1)} %pad_maximum_fusion.34), channel_id=1, source_target_pairs={{0,480},{16,496},{32,0},{48,16},{64,32},{80,48},{96,64},{112,80},{... | collective-permute-start | bytes 294920 | tf_op jit(solution)/shard_map/ppermute | solution.py:23
  91.5 5.6 %collective-permute-start.10 = (bf16[3,96,128]{2,1,0:T(8,128)(2,1)S(1)}, bf16[3,96,128]{2,1,0:T(8,128)(2,1)S(1)}, u32[]{:S(2)}, u32[]{:S(2)}) collective-permute-start(bf16[3,96,128]{2,1,0:T(8,128)(2,1)S(1)} %copy-done.8), channel_id=1, source_target_pairs={{0,1},{1,2},{2,3},{3,4},{4,5},{5,6},{6,7},{7,8},{8,9},{9,10},{10,1... | collective-permute-start | bytes 221192 | tf_op jit(solution)/shard_map/ppermute | solution.py:18
  97.2 1.4 collective-permute-done.10
  98.6 1.9 %collective-permute-start.11 = (bf16[3,96,128]{2,1,0:T(8,128)(2,1)S(1)}, bf16[3,96,128]{2,1,0:T(8,128)(2,1)S(1)}, u32[]{:S(2)}, u32[]{:S(2)}) collective-permute-start(bf16[3,96,128]{2,1,0:T(8,128)(2,1)S(1)} %get-tuple-element.28), channel_id=1, source_target_pairs={{1,0},{2,1},{3,2},{4,3},{5,4},{6,5},{7,6},{8,7},{9,8},{10,9},{11,1... | collective-permute-start | bytes 221192 | tf_op jit(solution)/shard_map/ppermute | solution.py:18
  100.5 10.2 %collective-permute-done.11 = bf16[3,96,128]{2,1,0:T(8,128)(2,1)S(1)} collective-permute-done((bf16[3,96,128]{2,1,0:T(8,128)(2,1)S(1)}, bf16[3,96,128]{2,1,0:T(8,128)(2,1)S(1)}, u32[]{:S(2)}, u32[]{:S(2)}) %collective-permute-start.11) | collective-permute-done | bytes 73760 | tf_op jit(solution)/shard_map/ppermute | solution.py:18
  110.7 5.3 %collective-permute-start.16 = (bf16[4,96,128]{2,1,0:T(8,128)(2,1)S(1)}, bf16[4,96,128]{2,1,0:T(8,128)(2,1)S(1)}, u32[]{:S(2)}, u32[]{:S(2)}) collective-permute-start(bf16[4,96,128]{2,1,0:T(8,128)(2,1)S(1)} %pad_maximum_fusion.35), channel_id=1, source_target_pairs={{0,496},{16,0},{32,16},{48,32},{64,48},{80,64},{96,80},{112,96},{1... | collective-permute-start | bytes 294920 | tf_op jit(solution)/shard_map/ppermute | solution.py:23
  116.2 5.4 %collective-permute-done.16 = bf16[4,96,128]{2,1,0:T(8,128)(2,1)S(1)} collective-permute-done((bf16[4,96,128]{2,1,0:T(8,128)(2,1)S(1)}, bf16[4,96,128]{2,1,0:T(8,128)(2,1)S(1)}, u32[]{:S(2)}, u32[]{:S(2)}) %collective-permute-start.16) | collective-permute-done | bytes 98336 | tf_op jit(solution)/shard_map/ppermute | solution.py:23
  122.0 2.3 %fusion.32 = (bf16[8,96,128]{2,1,0:T(8,128)(2,1)S(1)}, f32[8,96,128]{2,1,0:T(8,128)S(1)}) fusion(f32[8,96,128]{2,1,0:T(8,128)S(1)} %copy-done.5, f32[1,8,96,128]{3,2,1,0:T(8,128)S(1)} %copy-done.3, f32[8,96,128]{2,0,1:T(8,128)S(1)} %fusion.23, bf16[26,96,128]{2,1,0:T(8,128)(2,1)S(1)} %get-tuple-element.93, bf16[8,96,12,96]{3,1,2,0:T(8,128)(2,1)S(1)} %copy-done.4, ...), kind=kOutput, calls=%fused_computation.55 | convolution fusion | flops 493535232 | bytes 6242304 | tf_op jit(solution)/shard_map/kamb,mbr->kar/dot_general | solution.py:179
  125.1 1.9 %collective-permute-start.17 = (bf16[4,96,128]{2,1,0:T(8,128)(2,1)S(1)}, bf16[4,96,128]{2,1,0:T(8,128)(2,1)S(1)}, u32[]{:S(2)}, u32[]{:S(2)}) collective-permute-start(bf16[4,96,128]{2,1,0:T(8,128)(2,1)S(1)} %pad_maximum_fusion.36), channel_id=1, source_target_pairs={{0,16},{16,32},{32,48},{48,64},{64,80},{80,96},{96,112},{112,128},... | collective-permute-start | bytes 294920 | tf_op jit(solution)/shard_map/ppermute | solution.py:23
  127.1 1.9 %collective-permute-start.20 = (bf16[4,96,128]{2,1,0:T(8,128)(2,1)S(1)}, bf16[4,96,128]{2,1,0:T(8,128)(2,1)S(1)}, u32[]{:S(2)}, u32[]{:S(2)}) collective-permute-start(bf16[4,96,128]{2,1,0:T(8,128)(2,1)S(1)} %pad_maximum_fusion.37), channel_id=1, source_target_pairs={{0,32},{16,48},{32,64},{48,80},{64,96},{80,112},{96,128},{112,144}... | collective-permute-start | bytes 294920 | tf_op jit(solution)/shard_map/ppermute | solution.py:23
  129.0 1.9 %collective-permute-start.21 = (bf16[4,96,128]{2,1,0:T(8,128)(2,1)S(1)}, bf16[4,96,128]{2,1,0:T(8,128)(2,1)S(1)}, u32[]{:S(2)}, u32[]{:S(2)}) collective-permute-start(bf16[4,96,128]{2,1,0:T(8,128)(2,1)S(1)} %pad_maximum_fusion.38), channel_id=1, source_target_pairs={{0,48},{16,64},{32,80},{48,96},{64,112},{80,128},{96,144},{112,160... | collective-permute-start | bytes 294920 | tf_op jit(solution)/shard_map/ppermute | solution.py:23
  131.0 4.0 %collective-permute-start.22 = (bf16[4,96,128]{2,1,0:T(8,128)(2,1)S(1)}, bf16[4,96,128]{2,1,0:T(8,128)(2,1)S(1)}, u32[]{:S(2)}, u32[]{:S(2)}) collective-permute-start(bf16[4,96,128]{2,1,0:T(8,128)(2,1)S(1)} %pad_maximum_fusion.39), channel_id=1, source_target_pairs={{0,464},{16,480},{32,496},{48,0},{64,16},{80,32},{96,48},{112,64},... | collective-permute-start | bytes 294920 | tf_op jit(solution)/shard_map/ppermute | solution.py:23
  135.0 3.0 %collective-permute-start.23 = (bf16[4,96,128]{2,1,0:T(8,128)(2,1)S(1)}, bf16[4,96,128]{2,1,0:T(8,128)(2,1)S(1)}, u32[]{:S(2)}, u32[]{:S(2)}) collective-permute-start(bf16[4,96,128]{2,1,0:T(8,128)(2,1)S(1)} %pad_maximum_fusion.40), channel_id=1, source_target_pairs={{0,480},{16,496},{32,0},{48,16},{64,32},{80,48},{96,64},{112,80},{... | collective-permute-start | bytes 294920 | tf_op jit(solution)/shard_map/ppermute | solution.py:23
  138.0 2.4 %collective-permute-start.18 = (bf16[3,96,128]{2,1,0:T(8,128)(2,1)S(1)}, bf16[3,96,128]{2,1,0:T(8,128)(2,1)S(1)}, u32[]{:S(2)}, u32[]{:S(2)}) collective-permute-start(bf16[3,96,128]{2,1,0:T(8,128)(2,1)S(1)} %get-tuple-element.29), channel_id=1, source_target_pairs={{0,1},{1,2},{2,3},{3,4},{4,5},{5,6},{6,7},{7,8},{8,9},{9,10},{10,1... | collective-permute-start | bytes 221192 | tf_op jit(solution)/shard_map/ppermute | solution.py:18
  140.4 4.2 %collective-permute-done.18 = bf16[3,96,128]{2,1,0:T(8,128)(2,1)S(1)} collective-permute-done((bf16[3,96,128]{2,1,0:T(8,128)(2,1)S(1)}, bf16[3,96,128]{2,1,0:T(8,128)(2,1)S(1)}, u32[]{:S(2)}, u32[]{:S(2)}) %collective-permute-start.18) | collective-permute-done | bytes 73760 | tf_op jit(solution)/shard_map/ppermute | solution.py:18
  144.6 1.9 %collective-permute-start.19 = (bf16[3,96,128]{2,1,0:T(8,128)(2,1)S(1)}, bf16[3,96,128]{2,1,0:T(8,128)(2,1)S(1)}, u32[]{:S(2)}, u32[]{:S(2)}) collective-permute-start(bf16[3,96,128]{2,1,0:T(8,128)(2,1)S(1)} %get-tuple-element.30), channel_id=1, source_target_pairs={{1,0},{2,1},{3,2},{4,3},{5,4},{6,5},{7,6},{8,7},{9,8},{10,9},{11,1... | collective-permute-start | bytes 221192 | tf_op jit(solution)/shard_map/ppermute | solution.py:18
  146.6 10.0 %collective-permute-done.19 = bf16[3,96,128]{2,1,0:T(8,128)(2,1)S(1)} collective-permute-done((bf16[3,96,128]{2,1,0:T(8,128)(2,1)S(1)}, bf16[3,96,128]{2,1,0:T(8,128)(2,1)S(1)}, u32[]{:S(2)}, u32[]{:S(2)}) %collective-permute-start.19) | collective-permute-done | bytes 73760 | tf_op jit(solution)/shard_map/ppermute | solution.py:18
  156.5 5.3 %collective-permute-start.24 = (bf16[4,96,128]{2,1,0:T(8,128)(2,1)S(1)}, bf16[4,96,128]{2,1,0:T(8,128)(2,1)S(1)}, u32[]{:S(2)}, u32[]{:S(2)}) collective-permute-start(bf16[4,96,128]{2,1,0:T(8,128)(2,1)S(1)} %pad_maximum_fusion.41), channel_id=1, source_target_pairs={{0,496},{16,0},{32,16},{48,32},{64,48},{80,64},{96,80},{112,96},{1... | collective-permute-start | bytes 294920 | tf_op jit(solution)/shard_map/ppermute | solution.py:23
  162.0 8.7 %collective-permute-done.24 = bf16[4,96,128]{2,1,0:T(8,128)(2,1)S(1)} collective-permute-done((bf16[4,96,128]{2,1,0:T(8,128)(2,1)S(1)}, bf16[4,96,128]{2,1,0:T(8,128)(2,1)S(1)}, u32[]{:S(2)}, u32[]{:S(2)}) %collective-permute-start.24) | collective-permute-done | bytes 98336 | tf_op jit(solution)/shard_map/ppermute | solution.py:23
  171.0 3.1 %fusion.11 = f32[1,8,96,128]{3,2,1,0:T(8,128)} fusion(f32[8,96,128]{2,1,0:T(8,128)S(1)} %get-tuple-element.141, bf16[8,96,12,96]{3,1,2,0:T(8,128)(2,1)S(1)} %copy-done.4, bf16[8,96,14,96]{3,1,2,0:T(8,128)(2,1)S(1)} %bitcast_add_fusion, bf16[26,96,128]{2,1,0:T(8,128)(2,1)S(1)} %get-tuple-element.81, f32[8,96,128]{2,0,1:T(8,128)S(1)} %fusion.21, ...), kind=kOutput, calls=%fused_computation.22 | convolution fusion | flops 494125056 | bytes 6438912 | tf_op jit(solution)/shard_map/kamb,mbr->kar/dot_general | solution.py:179
  (132 shorter events, 10.3 us)
Async XLA Ops:
  0.0 13.7 %copy-start = (bf16[1,1,6,2,96,96]{5,4,3,2,1,0:T(8,128)(2,1)S(1)}, bf16[1,1,6,2,96,96]{5,4,3,2,1,0:T(8,128)(2,1)}, u32[]{:S(2)}) copy-start(bf16[1,1,6,2,96,96]{5,4,3,2,1,0:T(8,128)(2,1)} %param.11) | copy-start | bytes 663556
  1.0 32.9 %collective-permute-start = (bf16[3,4,96,96]{3,2,1,0:T(8,128)(2,1)S(1)}, bf16[3,4,96,96]{3,2,1,0:T(8,128)(2,1)S(1)}, u32[]{:S(2)}, u32[]{:S(2)}) collective-permute-start(bf16[3,4,96,96]{3,2,1,0:T(8,128)(2,1)S(1)} %slice_bitcast_fusion), channel_id=1, source_target_pairs={{0,1},{1,2},{2,3},{3,4},{4,5},{5,6},{6,7},{7,8},{8,9},{9,10},{10,1... | collective-permute-start | bytes 663560 | tf_op jit(solution)/shard_map/ppermute | solution.py:18
  13.2 14.2 %copy-start.10 = (s32[1,1,6]{2,1,0:T(1,128)S(1)}, s32[1,1,6]{2,1,0:T(1,128)}, u32[]{:S(2)}) copy-start(s32[1,1,6]{2,1,0:T(1,128)} %param.10) | copy-start | bytes 76
  14.0 22.4 %copy-start.1 = (bf16[1,8,4,96,96]{4,3,2,1,0:T(8,128)(2,1)S(1)}, bf16[1,8,4,96,96]{4,3,2,1,0:T(8,128)(2,1)}, u32[]{:S(2)}) copy-start(bf16[1,8,4,96,96]{4,3,2,1,0:T(8,128)(2,1)} %param.8) | copy-start | bytes 1769476
  15.1 24.6 %collective-permute-start.8 = (bf16[11,96,128]{2,1,0:T(8,128)(2,1)S(1)}, bf16[11,96,128]{2,1,0:T(8,128)(2,1)S(1)}, u32[]{:S(2)}, u32[]{:S(2)}) collective-permute-start(bf16[11,96,128]{2,1,0:T(8,128)(2,1)S(1)} %get-tuple-element.74), channel_id=1, source_target_pairs={{0,496},{16,0},{32,16},{48,32},{64,48},{80,64},{96,80},{112,96},{1... | collective-permute-start | bytes 811016 | tf_op jit(solution)/shard_map/ppermute | solution.py:23
  18.0 32.7 %collective-permute-start.4 = (bf16[11,96,128]{2,1,0:T(8,128)(2,1)}, bf16[11,96,128]{2,1,0:T(8,128)(2,1)}, u32[]{:S(2)}, u32[]{:S(2)}) collective-permute-start(bf16[11,96,128]{2,1,0:T(8,128)(2,1)} %get-tuple-element.75), channel_id=1, source_target_pairs={{0,32},{16,48},{32,64},{48,80},{64,96},{80,112},{96,128},{112,144}... | collective-permute-start | bytes 811016 | tf_op jit(solution)/shard_map/ppermute | solution.py:23
  20.6 40.3 %collective-permute-start.5 = (bf16[11,96,128]{2,1,0:T(8,128)(2,1)}, bf16[11,96,128]{2,1,0:T(8,128)(2,1)}, u32[]{:S(2)}, u32[]{:S(2)}) collective-permute-start(bf16[11,96,128]{2,1,0:T(8,128)(2,1)} %get-tuple-element.76), channel_id=1, source_target_pairs={{0,48},{16,64},{32,80},{48,96},{64,112},{80,128},{96,144},{112,160... | collective-permute-start | bytes 811016 | tf_op jit(solution)/shard_map/ppermute | solution.py:23
  24.8 38.0 %collective-permute-start.6 = (bf16[11,96,128]{2,1,0:T(8,128)(2,1)}, bf16[11,96,128]{2,1,0:T(8,128)(2,1)}, u32[]{:S(2)}, u32[]{:S(2)}) collective-permute-start(bf16[11,96,128]{2,1,0:T(8,128)(2,1)} %get-tuple-element.77), channel_id=1, source_target_pairs={{0,464},{16,480},{32,496},{48,0},{64,16},{80,32},{96,48},{112,64},... | collective-permute-start | bytes 811016 | tf_op jit(solution)/shard_map/ppermute | solution.py:23
  28.0 8.4 %copy-start.6 = (bf16[12,96,96]{2,1,0:T(8,128)(2,1)}, bf16[12,96,96]{2,1,0:T(8,128)(2,1)S(1)}, u32[]{:S(2)}) copy-start(bf16[12,96,96]{2,1,0:T(8,128)(2,1)S(1)} %constant_dynamic-update-slice_fusion) | copy-start | bytes 663556
  33.9 28.9 %collective-permute-start.7 = (bf16[11,96,128]{2,1,0:T(8,128)(2,1)}, bf16[11,96,128]{2,1,0:T(8,128)(2,1)}, u32[]{:S(2)}, u32[]{:S(2)}) collective-permute-start(bf16[11,96,128]{2,1,0:T(8,128)(2,1)} %get-tuple-element.78), channel_id=1, source_target_pairs={{0,480},{16,496},{32,0},{48,16},{64,32},{80,48},{96,64},{112,80},{... | collective-permute-start | bytes 811016 | tf_op jit(solution)/shard_map/ppermute | solution.py:23
  39.7 7.8 %copy-start.7 = (bf16[11,96,128]{2,1,0:T(8,128)(2,1)}, bf16[11,96,128]{2,1,0:T(8,128)(2,1)S(1)}, u32[]{:S(2)}) copy-start(bf16[11,96,128]{2,1,0:T(8,128)(2,1)S(1)} %collective-permute-done.8.refs_5_) | copy-start | bytes 811012
  39.7 23.1 %collective-permute-start.3 = (bf16[11,96,128]{2,1,0:T(8,128)(2,1)}, bf16[11,96,128]{2,1,0:T(8,128)(2,1)}, u32[]{:S(2)}, u32[]{:S(2)}) collective-permute-start(bf16[11,96,128]{2,1,0:T(8,128)(2,1)} %get-tuple-element.79), channel_id=1, source_target_pairs={{0,16},{16,32},{32,48},{48,64},{64,80},{80,96},{96,112},{112,128},... | collective-permute-start | bytes 811016 | tf_op jit(solution)/shard_map/ppermute | solution.py:23
  50.7 18.5 %collective-permute-start.1 = (bf16[3,96,128]{2,1,0:T(8,128)(2,1)}, bf16[3,96,128]{2,1,0:T(8,128)(2,1)S(1)}, u32[]{:S(2)}, u32[]{:S(2)}) collective-permute-start(bf16[3,96,128]{2,1,0:T(8,128)(2,1)} %get-tuple-element.72), channel_id=1, source_target_pairs={{0,1},{1,2},{2,3},{3,4},{4,5},{5,6},{6,7},{7,8},{8,9},{9,10},{10,1... | collective-permute-start | bytes 221192 | tf_op jit(solution)/shard_map/ppermute | solution.py:18
  60.9 11.2 %collective-permute-start.2 = (bf16[3,96,128]{2,1,0:T(8,128)(2,1)S(1)}, bf16[3,96,128]{2,1,0:T(8,128)(2,1)}, u32[]{:S(2)}, u32[]{:S(2)}) collective-permute-start(bf16[3,96,128]{2,1,0:T(8,128)(2,1)S(1)} %get-tuple-element.73), channel_id=1, source_target_pairs={{1,0},{2,1},{3,2},{4,3},{5,4},{6,5},{7,6},{8,7},{9,8},{10,9},{11,1... | collective-permute-start | bytes 221192 | tf_op jit(solution)/shard_map/ppermute | solution.py:18
  65.8 6.3 %copy-start.2 = (f32[1,8,96,128]{3,2,1,0:T(8,128)S(1)}, f32[1,8,96,128]{3,2,1,0:T(8,128)}, u32[]{:S(2)}) copy-start(f32[1,8,96,128]{3,2,1,0:T(8,128)} %param.7) | copy-start | bytes 1179652
  69.3 0.6 copy-start.9
  75.5 16.1 %copy-start.8 = (bf16[3,96,128]{2,1,0:T(8,128)(2,1)S(1)}, bf16[3,96,128]{2,1,0:T(8,128)(2,1)}, u32[]{:S(2)}) copy-start(bf16[3,96,128]{2,1,0:T(8,128)(2,1)} %get-tuple-element.27) | copy-start | bytes 221188
  76.0 45.9 %copy-start.3 = (f32[1,8,96,128]{3,2,1,0:T(8,128)S(1)}, f32[1,8,96,128]{3,2,1,0:T(8,128)}, u32[]{:S(2)}) copy-start(f32[1,8,96,128]{3,2,1,0:T(8,128)} %param.7) | copy-start | bytes 1179652
  76.0 45.9 %copy-start.4 = (bf16[8,96,12,96]{3,1,2,0:T(8,128)(2,1)S(1)}, bf16[8,96,12,96]{3,1,2,0:T(8,128)(2,1)}, u32[]{:S(2)}) copy-start(bf16[8,96,12,96]{3,1,2,0:T(8,128)(2,1)} %multiply_bitcast_fusion) | copy-start | bytes 5308420
  76.0 45.9 %copy-start.5 = (f32[8,96,128]{2,1,0:T(8,128)S(1)}, f32[8,96,128]{2,1,0:T(8,128)}, u32[]{:S(2)}) copy-start(f32[8,96,128]{2,1,0:T(8,128)} %get-tuple-element.139) | copy-start | bytes 1179652
  76.4 15.1 %collective-permute-start.9 = (bf16[4,96,128]{2,1,0:T(8,128)(2,1)S(1)}, bf16[4,96,128]{2,1,0:T(8,128)(2,1)S(1)}, u32[]{:S(2)}, u32[]{:S(2)}) collective-permute-start(bf16[4,96,128]{2,1,0:T(8,128)(2,1)S(1)} %pad_maximum_fusion.30), channel_id=1, source_target_pairs={{0,16},{16,32},{32,48},{48,64},{64,80},{80,96},{96,112},{112,128},... | collective-permute-start | bytes 294920 | tf_op jit(solution)/shard_map/ppermute | solution.py:23
  80.6 35.5 %collective-permute-start.12 = (bf16[4,96,128]{2,1,0:T(8,128)(2,1)S(1)}, bf16[4,96,128]{2,1,0:T(8,128)(2,1)S(1)}, u32[]{:S(2)}, u32[]{:S(2)}) collective-permute-start(bf16[4,96,128]{2,1,0:T(8,128)(2,1)S(1)} %pad_maximum_fusion.31), channel_id=1, source_target_pairs={{0,32},{16,48},{32,64},{48,80},{64,96},{80,112},{96,128},{112,144}... | collective-permute-start | bytes 294920 | tf_op jit(solution)/shard_map/ppermute | solution.py:23
  82.5 33.6 %collective-permute-start.13 = (bf16[4,96,128]{2,1,0:T(8,128)(2,1)S(1)}, bf16[4,96,128]{2,1,0:T(8,128)(2,1)S(1)}, u32[]{:S(2)}, u32[]{:S(2)}) collective-permute-start(bf16[4,96,128]{2,1,0:T(8,128)(2,1)S(1)} %pad_maximum_fusion.32), channel_id=1, source_target_pairs={{0,48},{16,64},{32,80},{48,96},{64,112},{80,128},{96,144},{112,160... | collective-permute-start | bytes 294920 | tf_op jit(solution)/shard_map/ppermute | solution.py:23
  84.5 31.7 %collective-permute-start.14 = (bf16[4,96,128]{2,1,0:T(8,128)(2,1)S(1)}, bf16[4,96,128]{2,1,0:T(8,128)(2,1)S(1)}, u32[]{:S(2)}, u32[]{:S(2)}) collective-permute-start(bf16[4,96,128]{2,1,0:T(8,128)(2,1)S(1)} %pad_maximum_fusion.33), channel_id=1, source_target_pairs={{0,464},{16,480},{32,496},{48,0},{64,16},{80,32},{96,48},{112,64},... | collective-permute-start | bytes 294920 | tf_op jit(solution)/shard_map/ppermute | solution.py:23
  88.2 28.0 %collective-permute-start.15 = (bf16[4,96,128]{2,1,0:T(8,128)(2,1)S(1)}, bf16[4,96,128]{2,1,0:T(8,128)(2,1)S(1)}, u32[]{:S(2)}, u32[]{:S(2)}) collective-permute-start(bf16[4,96,128]{2,1,0:T(8,128)(2,1)S(1)} %pad_maximum_fusion.34), channel_id=1, source_target_pairs={{0,480},{16,496},{32,0},{48,16},{64,32},{80,48},{96,64},{112,80},{... | collective-permute-start | bytes 294920 | tf_op jit(solution)/shard_map/ppermute | solution.py:23
  91.5 7.0 %collective-permute-start.10 = (bf16[3,96,128]{2,1,0:T(8,128)(2,1)S(1)}, bf16[3,96,128]{2,1,0:T(8,128)(2,1)S(1)}, u32[]{:S(2)}, u32[]{:S(2)}) collective-permute-start(bf16[3,96,128]{2,1,0:T(8,128)(2,1)S(1)} %copy-done.8), channel_id=1, source_target_pairs={{0,1},{1,2},{2,3},{3,4},{4,5},{5,6},{6,7},{7,8},{8,9},{9,10},{10,1... | collective-permute-start | bytes 221192 | tf_op jit(solution)/shard_map/ppermute | solution.py:18
  98.6 12.1 %collective-permute-start.11 = (bf16[3,96,128]{2,1,0:T(8,128)(2,1)S(1)}, bf16[3,96,128]{2,1,0:T(8,128)(2,1)S(1)}, u32[]{:S(2)}, u32[]{:S(2)}) collective-permute-start(bf16[3,96,128]{2,1,0:T(8,128)(2,1)S(1)} %get-tuple-element.28), channel_id=1, source_target_pairs={{1,0},{2,1},{3,2},{4,3},{5,4},{6,5},{7,6},{8,7},{9,8},{10,9},{11,1... | collective-permute-start | bytes 221192 | tf_op jit(solution)/shard_map/ppermute | solution.py:18
  110.7 11.0 %collective-permute-start.16 = (bf16[4,96,128]{2,1,0:T(8,128)(2,1)S(1)}, bf16[4,96,128]{2,1,0:T(8,128)(2,1)S(1)}, u32[]{:S(2)}, u32[]{:S(2)}) collective-permute-start(bf16[4,96,128]{2,1,0:T(8,128)(2,1)S(1)} %pad_maximum_fusion.35), channel_id=1, source_target_pairs={{0,496},{16,0},{32,16},{48,32},{64,48},{80,64},{96,80},{112,96},{1... | collective-permute-start | bytes 294920 | tf_op jit(solution)/shard_map/ppermute | solution.py:23
  125.1 12.9 %collective-permute-start.17 = (bf16[4,96,128]{2,1,0:T(8,128)(2,1)S(1)}, bf16[4,96,128]{2,1,0:T(8,128)(2,1)S(1)}, u32[]{:S(2)}, u32[]{:S(2)}) collective-permute-start(bf16[4,96,128]{2,1,0:T(8,128)(2,1)S(1)} %pad_maximum_fusion.36), channel_id=1, source_target_pairs={{0,16},{16,32},{32,48},{48,64},{64,80},{80,96},{96,112},{112,128},... | collective-permute-start | bytes 294920 | tf_op jit(solution)/shard_map/ppermute | solution.py:23
  127.1 34.8 %collective-permute-start.20 = (bf16[4,96,128]{2,1,0:T(8,128)(2,1)S(1)}, bf16[4,96,128]{2,1,0:T(8,128)(2,1)S(1)}, u32[]{:S(2)}, u32[]{:S(2)}) collective-permute-start(bf16[4,96,128]{2,1,0:T(8,128)(2,1)S(1)} %pad_maximum_fusion.37), channel_id=1, source_target_pairs={{0,32},{16,48},{32,64},{48,80},{64,96},{80,112},{96,128},{112,144}... | collective-permute-start | bytes 294920 | tf_op jit(solution)/shard_map/ppermute | solution.py:23
  129.0 32.9 %collective-permute-start.21 = (bf16[4,96,128]{2,1,0:T(8,128)(2,1)S(1)}, bf16[4,96,128]{2,1,0:T(8,128)(2,1)S(1)}, u32[]{:S(2)}, u32[]{:S(2)}) collective-permute-start(bf16[4,96,128]{2,1,0:T(8,128)(2,1)S(1)} %pad_maximum_fusion.38), channel_id=1, source_target_pairs={{0,48},{16,64},{32,80},{48,96},{64,112},{80,128},{96,144},{112,160... | collective-permute-start | bytes 294920 | tf_op jit(solution)/shard_map/ppermute | solution.py:23
  131.0 31.0 %collective-permute-start.22 = (bf16[4,96,128]{2,1,0:T(8,128)(2,1)S(1)}, bf16[4,96,128]{2,1,0:T(8,128)(2,1)S(1)}, u32[]{:S(2)}, u32[]{:S(2)}) collective-permute-start(bf16[4,96,128]{2,1,0:T(8,128)(2,1)S(1)} %pad_maximum_fusion.39), channel_id=1, source_target_pairs={{0,464},{16,480},{32,496},{48,0},{64,16},{80,32},{96,48},{112,64},... | collective-permute-start | bytes 294920 | tf_op jit(solution)/shard_map/ppermute | solution.py:23
  135.0 26.9 %collective-permute-start.23 = (bf16[4,96,128]{2,1,0:T(8,128)(2,1)S(1)}, bf16[4,96,128]{2,1,0:T(8,128)(2,1)S(1)}, u32[]{:S(2)}, u32[]{:S(2)}) collective-permute-start(bf16[4,96,128]{2,1,0:T(8,128)(2,1)S(1)} %pad_maximum_fusion.40), channel_id=1, source_target_pairs={{0,480},{16,496},{32,0},{48,16},{64,32},{80,48},{96,64},{112,80},{... | collective-permute-start | bytes 294920 | tf_op jit(solution)/shard_map/ppermute | solution.py:23
  138.0 6.6 %collective-permute-start.18 = (bf16[3,96,128]{2,1,0:T(8,128)(2,1)S(1)}, bf16[3,96,128]{2,1,0:T(8,128)(2,1)S(1)}, u32[]{:S(2)}, u32[]{:S(2)}) collective-permute-start(bf16[3,96,128]{2,1,0:T(8,128)(2,1)S(1)} %get-tuple-element.29), channel_id=1, source_target_pairs={{0,1},{1,2},{2,3},{3,4},{4,5},{5,6},{6,7},{7,8},{8,9},{9,10},{10,1... | collective-permute-start | bytes 221192 | tf_op jit(solution)/shard_map/ppermute | solution.py:18
  144.6 11.9 %collective-permute-start.19 = (bf16[3,96,128]{2,1,0:T(8,128)(2,1)S(1)}, bf16[3,96,128]{2,1,0:T(8,128)(2,1)S(1)}, u32[]{:S(2)}, u32[]{:S(2)}) collective-permute-start(bf16[3,96,128]{2,1,0:T(8,128)(2,1)S(1)} %get-tuple-element.30), channel_id=1, source_target_pairs={{1,0},{2,1},{3,2},{4,3},{5,4},{6,5},{7,6},{8,7},{9,8},{10,9},{11,1... | collective-permute-start | bytes 221192 | tf_op jit(solution)/shard_map/ppermute | solution.py:18
  156.5 14.2 %collective-permute-start.24 = (bf16[4,96,128]{2,1,0:T(8,128)(2,1)S(1)}, bf16[4,96,128]{2,1,0:T(8,128)(2,1)S(1)}, u32[]{:S(2)}, u32[]{:S(2)}) collective-permute-start(bf16[4,96,128]{2,1,0:T(8,128)(2,1)S(1)} %pad_maximum_fusion.41), channel_id=1, source_target_pairs={{0,496},{16,0},{32,16},{48,32},{64,48},{80,64},{96,80},{112,96},{1... | collective-permute-start | bytes 294920 | tf_op jit(solution)/shard_map/ppermute | solution.py:23

commit v12 on v9

--- a/solution.py
+++ b/solution.py
@@ -107,6 +107,9 @@
     )
     weight = jnp.concatenate([band_weight, fetch_weight], axis=2)
     first_pick = jnp.stack([far_knot[bucket_of[-s]] for s in shifts])
+    weight, band_weight, fetch_weight, direction_seed = lax.optimization_barrier(
+        (weight, band_weight, fetch_weight, right_rows)
+    )
     answer_pick = None
     land_place = None
 
@@ -115,7 +118,7 @@
     coeff = radius / center
     solution = jnp.zeros(right_rows.shape, jnp.float32)
     residual = right_rows
-    direction = right_rows / center
+    direction = direction_seed / center
     own_rows = buckets * slots
     for turn in range(ITERS):
         probe_bf = direction.astype(jnp.bfloat16)

time: 157 us -> 210 us (1.34)
  waiting for transfers between devices: 7.8 us -> 64.8 us
  starting transfers between devices: 112 us -> 97.2 us
  other arithmetic: 10.6 us -> 17.5 us
  local copies, waits for them, and re-layouts: 8.69 us -> 13.1 us
    ppermute x18, waiting for transfers between devices: 4.14 us -> 32.7 us  [shifted_ring(): lax.ppermute(value, axis, [(i, (i + steps) % count) for i in range(count)])]
    ppermute x7, waiting for transfers between devices: 3.66 us -> 32.1 us  [shifted_open(): lax.ppermute(value, axis, [(source, source + steps) for source in range(i...]
    ppermute x7, starting transfers between devices: 43.7 us -> 33.8 us  [shifted_open(): lax.ppermute(value, axis, [(source, source + steps) for source in range(i...]
    concatenate x0 -> x1, other arithmetic: none -> 5.02 us  [body(): weight = jnp.concatenate([band_weight, fetch_weight], axis=2)]
    ppermute x18, starting transfers between devices: 67.9 us -> 63.5 us  [shifted_ring(): lax.ppermute(value, axis, [(i, (i + steps) % count) for i in range(count)])]
    unnamed x43 -> x51, local copies, waits for them, and re-layouts: 0.98 us -> 4.36 us
  transfers between devices with their start and end apart: 25 -> 25, of which waited for: 5 -> 9; matrix products, arithmetic and copies ran while one was open for 14% -> 11% of each run, Pallas kernels for 1% -> 1%
where the time goes in v12:
time: 210 us; the launch traced here: 208 us
  starting transfers between devices  97.2 us (46%)
  waiting for transfers between devices  64.8 us (31%)
  other arithmetic  17.5 us (8%)
  local copies, waits for them, and re-layouts  13.1 us (6%)
  matrix products  12.4 us (6%)
  Pallas kernels  2.21 us (1%)
    ppermute x18, starting transfers between devices, shifted_ring(): lax.ppermute(value, axis, [(i, (i + steps) % count) for i in range(count)])  63.5 us
    ppermute x7, starting transfers between devices, shifted_open(): lax.ppermute(value, axis, [(source, source + steps) for source in range(i...  33.8 us
    ppermute x18, waiting for transfers between devices, shifted_ring(): lax.ppermute(value, axis, [(i, (i + steps) % count) for i in range(count)])  32.7 us
    ppermute x7, waiting for transfers between devices, shifted_open(): lax.ppermute(value, axis, [(source, source + steps) for source in range(i...  32.1 us
    concatenate x1, other arithmetic, body(): weight = jnp.concatenate([band_weight, fetch_weight], axis=2)  5.02 us
    unnamed x51, local copies, waits for them, and re-layouts  4.36 us
  transfers between devices with their start and end apart: 25, of which 9 were waited for; matrix products, arithmetic and copies ran while one was open for 11% of the time, Pallas kernels for 1%

profile of v12, /device:TPU:24, one launch (start us, length us, event | category | flops | bytes accessed | tf_op | source)
XLA Modules:
  0.0 208.2 jit_solution(7766909880980102837)
XLA Ops:
  0.0 1.1 slice_bitcast_fusion
  1.1 8.8 %collective-permute-start = (bf16[3,4,96,96]{3,2,1,0:T(8,128)(2,1)S(1)}, bf16[3,4,96,96]{3,2,1,0:T(8,128)(2,1)S(1)}, u32[]{:S(2)}, u32[]{:S(2)}) collective-permute-start(bf16[3,4,96,96]{3,2,1,0:T(8,128)(2,1)S(1)} %slice_bitcast_fusion), channel_id=1, source_target_pairs={{0,1},{1,2},{2,3},{3,4},{4,5},{5,6},{6,7},{7,8},{8,9},{9,10},{10,1... | collective-permute-start | bytes 663560 | tf_op jit(solution)/shard_map/ppermute | solution.py:18
  14.8 0.8 constant_dynamic-update-slice_fusion.2
  19.0 1.7 multiply_bitcast_fusion
  22.6 0.9 maximum_bitcast_fusion.3
  24.0 3.2 %bitcast_add_fusion = bf16[8,96,14,96]{3,1,2,0:T(8,128)(2,1)S(1)} fusion(bf16[8,14]{1,0:T(8,128)(2,1)S(1)} %fusion.57, bf16[8,96,96]{1,2,0:T(8,128)(2,1)S(1)} %copy.54, bf16[8,14]{1,0:T(8,128)(2,1)} %get-tuple-element.147, bf16[8,96,96]{1,2,0:T(8,128)(2,1)S(1)} %copy.53, bf16[8,14]{1,0:T(8,128)(2,1)} %get-tuple-element.146, bf16[8,96,96]{1,2,0:T(8,128)(2,1)S(1)} %copy.52, ...), kind=kLoop, calls=%fused_computation.1 | loop fusion | flops 13418496 | bytes 3098144 | tf_op jit(solution)/shard_map/add | solution.py:94
  27.2 5.0 %pad_maximum_fusion = bf16[8,96,26,96]{3,1,2,0:T(8,128)(2,1)} fusion(bf16[8,96,12,96]{3,1,2,0:T(8,128)(2,1)} %multiply_bitcast_fusion, bf16[8,96,14,96]{3,1,2,0:T(8,128)(2,1)S(1)} %bitcast_add_fusion), kind=kLoop, calls=%fused_computation | loop fusion | flops 1916928 | bytes 7667712 | tf_op jit(solution)/shard_map/concatenate | solution.py:108
  33.1 1.1 fusion.36
  34.2 1.9 collective-permute-start.3
  36.8 3.4 %collective-permute-start.4 = (bf16[11,96,128]{2,1,0:T(8,128)(2,1)}, bf16[11,96,128]{2,1,0:T(8,128)(2,1)}, u32[]{:S(2)}, u32[]{:S(2)}) collective-permute-start(bf16[11,96,128]{2,1,0:T(8,128)(2,1)} %get-tuple-element.75), channel_id=1, source_target_pairs={{0,32},{16,48},{32,64},{48,80},{64,96},{80,112},{96,128},{112,144}... | collective-permute-start | bytes 811016 | tf_op jit(solution)/shard_map/ppermute | solution.py:23
  40.2 4.0 %collective-permute-start.5 = (bf16[11,96,128]{2,1,0:T(8,128)(2,1)}, bf16[11,96,128]{2,1,0:T(8,128)(2,1)}, u32[]{:S(2)}, u32[]{:S(2)}) collective-permute-start(bf16[11,96,128]{2,1,0:T(8,128)(2,1)} %get-tuple-element.76), channel_id=1, source_target_pairs={{0,48},{16,64},{32,80},{48,96},{64,112},{80,128},{96,144},{112,160... | collective-permute-start | bytes 811016 | tf_op jit(solution)/shard_map/ppermute | solution.py:23
  44.2 17.4 %collective-permute-start.6 = (bf16[11,96,128]{2,1,0:T(8,128)(2,1)}, bf16[11,96,128]{2,1,0:T(8,128)(2,1)}, u32[]{:S(2)}, u32[]{:S(2)}) collective-permute-start(bf16[11,96,128]{2,1,0:T(8,128)(2,1)} %get-tuple-element.77), channel_id=1, source_target_pairs={{0,464},{16,480},{32,496},{48,0},{64,16},{80,32},{96,48},{112,64},... | collective-permute-start | bytes 811016 | tf_op jit(solution)/shard_map/ppermute | solution.py:23
  61.7 4.2 %collective-permute-start.7 = (bf16[11,96,128]{2,1,0:T(8,128)(2,1)}, bf16[11,96,128]{2,1,0:T(8,128)(2,1)}, u32[]{:S(2)}, u32[]{:S(2)}) collective-permute-start(bf16[11,96,128]{2,1,0:T(8,128)(2,1)} %get-tuple-element.78), channel_id=1, source_target_pairs={{0,480},{16,496},{32,0},{48,16},{64,32},{80,48},{96,64},{112,80},{... | collective-permute-start | bytes 811016 | tf_op jit(solution)/shard_map/ppermute | solution.py:23
  65.9 1.9 collective-permute-start.8
  68.7 1.6 fusion.79
  70.2 10.5 %collective-permute-start.1 = (bf16[3,96,128]{2,1,0:T(8,128)(2,1)}, bf16[3,96,128]{2,1,0:T(8,128)(2,1)}, u32[]{:S(2)}, u32[]{:S(2)}) collective-permute-start(bf16[3,96,128]{2,1,0:T(8,128)(2,1)} %get-tuple-element.72), channel_id=1, source_target_pairs={{0,1},{1,2},{2,3},{3,4},{4,5},{5,6},{6,7},{7,8},{8,9},{9,10},{10,1... | collective-permute-start | bytes 221192 | tf_op jit(solution)/shard_map/ppermute | solution.py:18
  80.7 1.9 collective-permute-start.2
  82.7 2.2 %shard_map.55 = (bf16[12,96,128]{2,1,0:T(8,128)(2,1)}, bf16[12,96,128]{2,1,0:T(8,128)(2,1)}, bf16[6,128]{1,0:T(8,128)(2,1)}) custom-call(s32[6,2]{1,0:T(8,128)} %copy.63.pick_ref, bf16[11,96,128]{2,1,0:T(8,128)(2,1)} %collective-permute-done.3.refs_0_, bf16[11,96,128]{2,1,0:T(8,128)(2,1)} %collective-permute-done.4.refs_1_, ...), custom_call_target="tpu_custom_call" | custom-call | tf_op jit(solution)/shard_map/pallas_call | solution.py:45
  86.2 3.2 %convolution_bitcast_fusion.2 = f32[8,96,128]{2,1,0:T(8,128)} fusion(bf16[8,96,12,96]{3,1,2,0:T(8,128)(2,1)} %multiply_bitcast_fusion, bf16[12,96,128]{2,1,0:T(8,128)(2,1)} %get-tuple-element.27), kind=kOutput, calls=%fused_computation.11 | convolution fusion | flops 226492416 | bytes 2457600 | tf_op jit(solution)/shard_map/kamb,mbr->kar/dot_general | solution.py:175
  89.4 1.0 fusion.20
  91.3 3.4 %collective-permute-done.2 = bf16[3,96,128]{2,1,0:T(8,128)(2,1)} collective-permute-done((bf16[3,96,128]{2,1,0:T(8,128)(2,1)S(1)}, bf16[3,96,128]{2,1,0:T(8,128)(2,1)}, u32[]{:S(2)}, u32[]{:S(2)}) %collective-permute-start.2) | collective-permute-done | bytes 73760 | tf_op jit(solution)/shard_map/ppermute | solution.py:18
  94.7 2.3 %fusion.43 = (bf16[8,96,128]{2,1,0:T(8,128)(2,1)S(1)}, f32[8,96,128]{2,1,0:T(8,128)S(1)}) fusion(f32[8,96,128]{2,1,0:T(8,128)S(1)} %bitcast.218, f32[8,96,128]{2,0,1:T(8,128)} %fusion.20, f32[8,96,128]{2,1,0:T(8,128)} %convolution_bitcast_fusion.2, bf16[8,96,14,96]{3,1,2,0:T(8,128)(2,1)S(1)} %bitcast_add_fusion, ...), kind=kOutput, calls=%fused_computation.130 | convolution fusion | flops 265273344 | bytes 4571136 | tf_op jit(solution)/shard_map/kamb,mbr->kar/dot_general | solution.py:173
  98.0 1.9 collective-permute-start.16
  99.9 5.8 %collective-permute-start.15 = (bf16[4,96,128]{2,1,0:T(8,128)(2,1)S(1)}, bf16[4,96,128]{2,1,0:T(8,128)(2,1)S(1)}, u32[]{:S(2)}, u32[]{:S(2)}) collective-permute-start(bf16[4,96,128]{2,1,0:T(8,128)(2,1)S(1)} %pad_maximum_fusion.12), channel_id=1, source_target_pairs={{0,480},{16,496},{32,0},{48,16},{64,32},{80,48},{96,64},{112,80},{... | collective-permute-start | bytes 294920 | tf_op jit(solution)/shard_map/ppermute | solution.py:23
  105.8 3.0 %collective-permute-start.14 = (bf16[4,96,128]{2,1,0:T(8,128)(2,1)S(1)}, bf16[4,96,128]{2,1,0:T(8,128)(2,1)S(1)}, u32[]{:S(2)}, u32[]{:S(2)}) collective-permute-start(bf16[4,96,128]{2,1,0:T(8,128)(2,1)S(1)} %pad_maximum_fusion.11), channel_id=1, source_target_pairs={{0,464},{16,480},{32,496},{48,0},{64,16},{80,32},{96,48},{112,64},... | collective-permute-start | bytes 294920 | tf_op jit(solution)/shard_map/ppermute | solution.py:23
  108.8 2.6 %collective-permute-start.13 = (bf16[4,96,128]{2,1,0:T(8,128)(2,1)S(1)}, bf16[4,96,128]{2,1,0:T(8,128)(2,1)S(1)}, u32[]{:S(2)}, u32[]{:S(2)}) collective-permute-start(bf16[4,96,128]{2,1,0:T(8,128)(2,1)S(1)} %pad_maximum_fusion.10), channel_id=1, source_target_pairs={{0,48},{16,64},{32,80},{48,96},{64,112},{80,128},{96,144},{112,160... | collective-permute-start | bytes 294920 | tf_op jit(solution)/shard_map/ppermute | solution.py:23
  111.4 5.6 %collective-permute-start.9 = (bf16[3,96,128]{2,1,0:T(8,128)(2,1)S(1)}, bf16[3,96,128]{2,1,0:T(8,128)(2,1)S(1)}, u32[]{:S(2)}, u32[]{:S(2)}) collective-permute-start(bf16[3,96,128]{2,1,0:T(8,128)(2,1)S(1)} %get-tuple-element.71), channel_id=1, source_target_pairs={{0,1},{1,2},{2,3},{3,4},{4,5},{5,6},{6,7},{7,8},{8,9},{9,10},{10,1... | collective-permute-start | bytes 221192 | tf_op jit(solution)/shard_map/ppermute | solution.py:18
  117.1 2.1 %collective-permute-done.9 = bf16[3,96,128]{2,1,0:T(8,128)(2,1)S(1)} collective-permute-done((bf16[3,96,128]{2,1,0:T(8,128)(2,1)S(1)}, bf16[3,96,128]{2,1,0:T(8,128)(2,1)S(1)}, u32[]{:S(2)}, u32[]{:S(2)}) %collective-permute-start.9) | collective-permute-done | bytes 73760 | tf_op jit(solution)/shard_map/ppermute | solution.py:18
  119.1 1.9 collective-permute-start.10
  121.1 11.5 %collective-permute-done.10 = bf16[3,96,128]{2,1,0:T(8,128)(2,1)S(1)} collective-permute-done((bf16[3,96,128]{2,1,0:T(8,128)(2,1)S(1)}, bf16[3,96,128]{2,1,0:T(8,128)(2,1)S(1)}, u32[]{:S(2)}, u32[]{:S(2)}) %collective-permute-start.10) | collective-permute-done | bytes 73760 | tf_op jit(solution)/shard_map/ppermute | solution.py:18
  132.6 1.9 collective-permute-start.11
  134.6 7.9 %collective-permute-done.11 = bf16[4,96,128]{2,1,0:T(8,128)(2,1)S(1)} collective-permute-done((bf16[4,96,128]{2,1,0:T(8,128)(2,1)S(1)}, bf16[4,96,128]{2,1,0:T(8,128)(2,1)S(1)}, u32[]{:S(2)}, u32[]{:S(2)}) %collective-permute-start.11) | collective-permute-done | bytes 98336 | tf_op jit(solution)/shard_map/ppermute | solution.py:23
  142.4 1.9 collective-permute-start.12
  144.4 8.5 %collective-permute-done.12 = bf16[4,96,128]{2,1,0:T(8,128)(2,1)S(1)} collective-permute-done((bf16[4,96,128]{2,1,0:T(8,128)(2,1)S(1)}, bf16[4,96,128]{2,1,0:T(8,128)(2,1)S(1)}, u32[]{:S(2)}, u32[]{:S(2)}) %collective-permute-start.12) | collective-permute-done | bytes 98336 | tf_op jit(solution)/shard_map/ppermute | solution.py:23
  153.3 1.3 fusion.26
  155.5 1.9 collective-permute-start.24
  157.5 1.9 collective-permute-start.23
  159.4 1.9 collective-permute-start.22
  161.4 3.7 %collective-permute-start.21 = (bf16[4,96,128]{2,1,0:T(8,128)(2,1)S(1)}, bf16[4,96,128]{2,1,0:T(8,128)(2,1)S(1)}, u32[]{:S(2)}, u32[]{:S(2)}) collective-permute-start(bf16[4,96,128]{2,1,0:T(8,128)(2,1)S(1)} %pad_maximum_fusion.16), channel_id=1, source_target_pairs={{0,48},{16,64},{32,80},{48,96},{64,112},{80,128},{96,144},{112,160... | collective-permute-start | bytes 294920 | tf_op jit(solution)/shard_map/ppermute | solution.py:23
  165.1 3.2 %collective-permute-start.17 = (bf16[3,96,128]{2,1,0:T(8,128)(2,1)S(1)}, bf16[3,96,128]{2,1,0:T(8,128)(2,1)S(1)}, u32[]{:S(2)}, u32[]{:S(2)}) collective-permute-start(bf16[3,96,128]{2,1,0:T(8,128)(2,1)S(1)} %get-tuple-element.69), channel_id=1, source_target_pairs={{0,1},{1,2},{2,3},{3,4},{4,5},{5,6},{6,7},{7,8},{8,9},{9,10},{10,1... | collective-permute-start | bytes 221192 | tf_op jit(solution)/shard_map/ppermute | solution.py:18
  168.3 3.0 %collective-permute-done.17 = bf16[3,96,128]{2,1,0:T(8,128)(2,1)S(1)} collective-permute-done((bf16[3,96,128]{2,1,0:T(8,128)(2,1)S(1)}, bf16[3,96,128]{2,1,0:T(8,128)(2,1)S(1)}, u32[]{:S(2)}, u32[]{:S(2)}) %collective-permute-start.17) | collective-permute-done | bytes 73760 | tf_op jit(solution)/shard_map/ppermute | solution.py:18
  171.4 1.9 collective-permute-start.18
  173.3 12.1 %collective-permute-done.18 = bf16[3,96,128]{2,1,0:T(8,128)(2,1)S(1)} collective-permute-done((bf16[3,96,128]{2,1,0:T(8,128)(2,1)S(1)}, bf16[3,96,128]{2,1,0:T(8,128)(2,1)S(1)}, u32[]{:S(2)}, u32[]{:S(2)}) %collective-permute-start.18) | collective-permute-done | bytes 73760 | tf_op jit(solution)/shard_map/ppermute | solution.py:18
  185.4 2.0 collective-permute-start.19
  187.4 7.8 %collective-permute-done.19 = bf16[4,96,128]{2,1,0:T(8,128)(2,1)S(1)} collective-permute-done((bf16[4,96,128]{2,1,0:T(8,128)(2,1)S(1)}, bf16[4,96,128]{2,1,0:T(8,128)(2,1)S(1)}, u32[]{:S(2)}, u32[]{:S(2)}) %collective-permute-start.19) | collective-permute-done | bytes 98336 | tf_op jit(solution)/shard_map/ppermute | solution.py:23
  195.2 1.9 collective-permute-start.20
  197.2 8.5 %collective-permute-done.20 = bf16[4,96,128]{2,1,0:T(8,128)(2,1)S(1)} collective-permute-done((bf16[4,96,128]{2,1,0:T(8,128)(2,1)S(1)}, bf16[4,96,128]{2,1,0:T(8,128)(2,1)S(1)}, u32[]{:S(2)}, u32[]{:S(2)}) %collective-permute-start.20) | collective-permute-done | bytes 98336 | tf_op jit(solution)/shard_map/ppermute | solution.py:23
  206.0 2.1 %fusion.10 = f32[1,8,96,128]{3,2,1,0:T(8,128)} fusion(f32[8,96,128]{2,1,0:T(8,128)S(1)} %get-tuple-element.141, bf16[8,96,26,96]{3,1,2,0:T(8,128)(2,1)S(1)} %bitcast.216, bf16[26,96,128]{2,1,0:T(8,128)(2,1)S(1)} %get-tuple-element.81, f32[8,96,128]{2,0,1:T(8,128)S(1)} %fusion.16, f32[8,96,128]{2,1,0:T(8,128)S(1)} %bitcast.220, ...), kind=kOutput, calls=%fused_computation.23 | convolution fusion | flops 492208128 | bytes 6438912 | tf_op jit(solution)/shard_map/kamb,mbr->kar/dot_general | solution.py:179
  (142 shorter events, 17.7 us)
Async XLA Ops:
  0.0 22.6 %copy-start.3 = (bf16[1,8,4,96,96]{4,3,2,1,0:T(8,128)(2,1)S(1)}, bf16[1,8,4,96,96]{4,3,2,1,0:T(8,128)(2,1)}, u32[]{:S(2)}) copy-start(bf16[1,8,4,96,96]{4,3,2,1,0:T(8,128)(2,1)} %param.8) | copy-start | bytes 1769476
  1.1 21.5 %collective-permute-start = (bf16[3,4,96,96]{3,2,1,0:T(8,128)(2,1)S(1)}, bf16[3,4,96,96]{3,2,1,0:T(8,128)(2,1)S(1)}, u32[]{:S(2)}, u32[]{:S(2)}) collective-permute-start(bf16[3,4,96,96]{3,2,1,0:T(8,128)(2,1)S(1)} %slice_bitcast_fusion), channel_id=1, source_target_pairs={{0,1},{1,2},{2,3},{3,4},{4,5},{5,6},{6,7},{7,8},{8,9},{9,10},{10,1... | collective-permute-start | bytes 663560 | tf_op jit(solution)/shard_map/ppermute | solution.py:18
  27.2 5.1 %copy-start = (f32[1,8,96,128]{3,2,1,0:T(8,128)S(1)}, f32[1,8,96,128]{3,2,1,0:T(8,128)}, u32[]{:S(2)}) copy-start(f32[1,8,96,128]{3,2,1,0:T(8,128)} %param.7) | copy-start | bytes 1179652
  27.2 5.1 %copy-start.12 = (s32[12]{0:T(128)S(1)}, s32[12]{0:T(128)}, u32[]{:S(2)}) copy-start(s32[12]{0:T(128)} %broadcast_select_fusion.2) | copy-start | bytes 148
  27.2 5.5 %copy-start.1 = (bf16[1,1,6,2,96,96]{5,4,3,2,1,0:T(8,128)(2,1)S(1)}, bf16[1,1,6,2,96,96]{5,4,3,2,1,0:T(8,128)(2,1)}, u32[]{:S(2)}) copy-start(bf16[1,1,6,2,96,96]{5,4,3,2,1,0:T(8,128)(2,1)} %param.11) | copy-start | bytes 663556
  32.2 0.8 copy-start.5
  32.2 0.8 copy-start.6
  32.3 0.8 copy-start.2
  34.2 31.7 %collective-permute-start.3 = (bf16[11,96,128]{2,1,0:T(8,128)(2,1)S(1)}, bf16[11,96,128]{2,1,0:T(8,128)(2,1)}, u32[]{:S(2)}, u32[]{:S(2)}) collective-permute-start(bf16[11,96,128]{2,1,0:T(8,128)(2,1)S(1)} %get-tuple-element.79), channel_id=1, source_target_pairs={{0,16},{16,32},{32,48},{48,64},{64,80},{80,96},{96,112},{112,128},... | collective-permute-start | bytes 811016 | tf_op jit(solution)/shard_map/ppermute | solution.py:23
  36.8 33.4 %collective-permute-start.4 = (bf16[11,96,128]{2,1,0:T(8,128)(2,1)}, bf16[11,96,128]{2,1,0:T(8,128)(2,1)}, u32[]{:S(2)}, u32[]{:S(2)}) collective-permute-start(bf16[11,96,128]{2,1,0:T(8,128)(2,1)} %get-tuple-element.75), channel_id=1, source_target_pairs={{0,32},{16,48},{32,64},{48,80},{64,96},{80,112},{96,128},{112,144}... | collective-permute-start | bytes 811016 | tf_op jit(solution)/shard_map/ppermute | solution.py:23
  40.2 40.5 %collective-permute-start.5 = (bf16[11,96,128]{2,1,0:T(8,128)(2,1)}, bf16[11,96,128]{2,1,0:T(8,128)(2,1)}, u32[]{:S(2)}, u32[]{:S(2)}) collective-permute-start(bf16[11,96,128]{2,1,0:T(8,128)(2,1)} %get-tuple-element.76), channel_id=1, source_target_pairs={{0,48},{16,64},{32,80},{48,96},{64,112},{80,128},{96,144},{112,160... | collective-permute-start | bytes 811016 | tf_op jit(solution)/shard_map/ppermute | solution.py:23
  44.2 38.4 %collective-permute-start.6 = (bf16[11,96,128]{2,1,0:T(8,128)(2,1)}, bf16[11,96,128]{2,1,0:T(8,128)(2,1)}, u32[]{:S(2)}, u32[]{:S(2)}) collective-permute-start(bf16[11,96,128]{2,1,0:T(8,128)(2,1)} %get-tuple-element.77), channel_id=1, source_target_pairs={{0,464},{16,480},{32,496},{48,0},{64,16},{80,32},{96,48},{112,64},... | collective-permute-start | bytes 811016 | tf_op jit(solution)/shard_map/ppermute | solution.py:23
  61.7 21.0 %collective-permute-start.7 = (bf16[11,96,128]{2,1,0:T(8,128)(2,1)}, bf16[11,96,128]{2,1,0:T(8,128)(2,1)}, u32[]{:S(2)}, u32[]{:S(2)}) collective-permute-start(bf16[11,96,128]{2,1,0:T(8,128)(2,1)} %get-tuple-element.78), channel_id=1, source_target_pairs={{0,480},{16,496},{32,0},{48,16},{64,32},{80,48},{96,64},{112,80},{... | collective-permute-start | bytes 811016 | tf_op jit(solution)/shard_map/ppermute | solution.py:23
  65.9 16.7 %collective-permute-start.8 = (bf16[11,96,128]{2,1,0:T(8,128)(2,1)}, bf16[11,96,128]{2,1,0:T(8,128)(2,1)}, u32[]{:S(2)}, u32[]{:S(2)}) collective-permute-start(bf16[11,96,128]{2,1,0:T(8,128)(2,1)} %get-tuple-element.74), channel_id=1, source_target_pairs={{0,496},{16,0},{32,16},{48,32},{64,48},{80,64},{96,80},{112,96},{1... | collective-permute-start | bytes 811016 | tf_op jit(solution)/shard_map/ppermute | solution.py:23
  70.2 21.1 %collective-permute-start.1 = (bf16[3,96,128]{2,1,0:T(8,128)(2,1)}, bf16[3,96,128]{2,1,0:T(8,128)(2,1)}, u32[]{:S(2)}, u32[]{:S(2)}) collective-permute-start(bf16[3,96,128]{2,1,0:T(8,128)(2,1)} %get-tuple-element.72), channel_id=1, source_target_pairs={{0,1},{1,2},{2,3},{3,4},{4,5},{5,6},{6,7},{7,8},{8,9},{9,10},{10,1... | collective-permute-start | bytes 221192 | tf_op jit(solution)/shard_map/ppermute | solution.py:18
  80.7 14.0 %collective-permute-start.2 = (bf16[3,96,128]{2,1,0:T(8,128)(2,1)S(1)}, bf16[3,96,128]{2,1,0:T(8,128)(2,1)}, u32[]{:S(2)}, u32[]{:S(2)}) collective-permute-start(bf16[3,96,128]{2,1,0:T(8,128)(2,1)S(1)} %get-tuple-element.73), channel_id=1, source_target_pairs={{1,0},{2,1},{3,2},{4,3},{5,4},{6,5},{7,6},{8,7},{9,8},{10,9},{11,1... | collective-permute-start | bytes 221192 | tf_op jit(solution)/shard_map/ppermute | solution.py:18
  86.2 3.2 %copy-start.4 = (bf16[12,96,128]{2,1,0:T(8,128)(2,1)S(1)}, bf16[12,96,128]{2,1,0:T(8,128)(2,1)}, u32[]{:S(2)}) copy-start(bf16[12,96,128]{2,1,0:T(8,128)(2,1)} %get-tuple-element.29) | copy-start | bytes 884740
  86.2 4.2 %copy-start.7 = (f32[2]{0:T(128)S(1)}, f32[2]{0:T(128)}, u32[]{:S(2)}) copy-start(f32[2]{0:T(128)} %get-tuple-element.105) | copy-start | bytes 28
  86.2 4.2 %copy-start.8 = (f32[2]{0:T(128)S(1)}, f32[2]{0:T(128)}, u32[]{:S(2)}) copy-start(f32[2]{0:T(128)} %get-tuple-element.106) | copy-start | bytes 28
  86.2 4.2 %copy-start.9 = (f32[2]{0:T(128)S(1)}, f32[2]{0:T(128)}, u32[]{:S(2)}) copy-start(f32[2]{0:T(128)} %get-tuple-element.107) | copy-start | bytes 28
  86.2 4.2 %copy-start.10 = (f32[2]{0:T(128)S(1)}, f32[2]{0:T(128)}, u32[]{:S(2)}) copy-start(f32[2]{0:T(128)} %get-tuple-element.108) | copy-start | bytes 28
  86.2 4.2 %copy-start.11 = (f32[2]{0:T(128)S(1)}, f32[2]{0:T(128)}, u32[]{:S(2)}) copy-start(f32[2]{0:T(128)} %get-tuple-element.109) | copy-start | bytes 28
  94.7 58.6 %slice-start = ((s8[5111808]{0:T(1024)(128)(4,1)}), s8[4194304]{0:T(1024)(128)(4,1)S(1)}, s32[]{:S(2)}) async-start(s8[5111808]{0:T(1024)(128)(4,1)} %bitcast.215), calls=%async_computation | async-start | bytes 8388608
  97.4 55.9 %slice-start.1 = ((s8[5111808]{0:T(1024)(128)(4,1)}), s8[917504]{0:T(1024)(128)(4,1)S(1)}, s32[]{:S(2)}) async-start(s8[5111808]{0:T(1024)(128)(4,1)} %bitcast.215), calls=%async_computation.1 | async-start | bytes 1835008
  98.0 55.0 %collective-permute-start.16 = (bf16[4,96,128]{2,1,0:T(8,128)(2,1)S(1)}, bf16[4,96,128]{2,1,0:T(8,128)(2,1)S(1)}, u32[]{:S(2)}, u32[]{:S(2)}) collective-permute-start(bf16[4,96,128]{2,1,0:T(8,128)(2,1)S(1)} %pad_maximum_fusion.13), channel_id=1, source_target_pairs={{0,496},{16,0},{32,16},{48,32},{64,48},{80,64},{96,80},{112,96},{1... | collective-permute-start | bytes 294920 | tf_op jit(solution)/shard_map/ppermute | solution.py:23
  99.9 53.0 %collective-permute-start.15 = (bf16[4,96,128]{2,1,0:T(8,128)(2,1)S(1)}, bf16[4,96,128]{2,1,0:T(8,128)(2,1)S(1)}, u32[]{:S(2)}, u32[]{:S(2)}) collective-permute-start(bf16[4,96,128]{2,1,0:T(8,128)(2,1)S(1)} %pad_maximum_fusion.12), channel_id=1, source_target_pairs={{0,480},{16,496},{32,0},{48,16},{64,32},{80,48},{96,64},{112,80},{... | collective-permute-start | bytes 294920 | tf_op jit(solution)/shard_map/ppermute | solution.py:23
  105.8 47.1 %collective-permute-start.14 = (bf16[4,96,128]{2,1,0:T(8,128)(2,1)S(1)}, bf16[4,96,128]{2,1,0:T(8,128)(2,1)S(1)}, u32[]{:S(2)}, u32[]{:S(2)}) collective-permute-start(bf16[4,96,128]{2,1,0:T(8,128)(2,1)S(1)} %pad_maximum_fusion.11), channel_id=1, source_target_pairs={{0,464},{16,480},{32,496},{48,0},{64,16},{80,32},{96,48},{112,64},... | collective-permute-start | bytes 294920 | tf_op jit(solution)/shard_map/ppermute | solution.py:23
  108.8 44.1 %collective-permute-start.13 = (bf16[4,96,128]{2,1,0:T(8,128)(2,1)S(1)}, bf16[4,96,128]{2,1,0:T(8,128)(2,1)S(1)}, u32[]{:S(2)}, u32[]{:S(2)}) collective-permute-start(bf16[4,96,128]{2,1,0:T(8,128)(2,1)S(1)} %pad_maximum_fusion.10), channel_id=1, source_target_pairs={{0,48},{16,64},{32,80},{48,96},{64,112},{80,128},{96,144},{112,160... | collective-permute-start | bytes 294920 | tf_op jit(solution)/shard_map/ppermute | solution.py:23
  111.4 7.8 %collective-permute-start.9 = (bf16[3,96,128]{2,1,0:T(8,128)(2,1)S(1)}, bf16[3,96,128]{2,1,0:T(8,128)(2,1)S(1)}, u32[]{:S(2)}, u32[]{:S(2)}) collective-permute-start(bf16[3,96,128]{2,1,0:T(8,128)(2,1)S(1)} %get-tuple-element.71), channel_id=1, source_target_pairs={{0,1},{1,2},{2,3},{3,4},{4,5},{5,6},{6,7},{7,8},{8,9},{9,10},{10,1... | collective-permute-start | bytes 221192 | tf_op jit(solution)/shard_map/ppermute | solution.py:18
  119.1 13.5 %collective-permute-start.10 = (bf16[3,96,128]{2,1,0:T(8,128)(2,1)S(1)}, bf16[3,96,128]{2,1,0:T(8,128)(2,1)S(1)}, u32[]{:S(2)}, u32[]{:S(2)}) collective-permute-start(bf16[3,96,128]{2,1,0:T(8,128)(2,1)S(1)} %get-tuple-element.70), channel_id=1, source_target_pairs={{1,0},{2,1},{3,2},{4,3},{5,4},{6,5},{7,6},{8,7},{9,8},{10,9},{11,1... | collective-permute-start | bytes 221192 | tf_op jit(solution)/shard_map/ppermute | solution.py:18
  132.6 9.8 %collective-permute-start.11 = (bf16[4,96,128]{2,1,0:T(8,128)(2,1)S(1)}, bf16[4,96,128]{2,1,0:T(8,128)(2,1)S(1)}, u32[]{:S(2)}, u32[]{:S(2)}) collective-permute-start(bf16[4,96,128]{2,1,0:T(8,128)(2,1)S(1)} %pad_maximum_fusion.8), channel_id=1, source_target_pairs={{0,16},{16,32},{32,48},{48,64},{64,80},{80,96},{96,112},{112,128},... | collective-permute-start | bytes 294920 | tf_op jit(solution)/shard_map/ppermute | solution.py:23
  142.4 10.4 %collective-permute-start.12 = (bf16[4,96,128]{2,1,0:T(8,128)(2,1)S(1)}, bf16[4,96,128]{2,1,0:T(8,128)(2,1)S(1)}, u32[]{:S(2)}, u32[]{:S(2)}) collective-permute-start(bf16[4,96,128]{2,1,0:T(8,128)(2,1)S(1)} %pad_maximum_fusion.9), channel_id=1, source_target_pairs={{0,32},{16,48},{32,64},{48,80},{64,96},{80,112},{96,128},{112,144}... | collective-permute-start | bytes 294920 | tf_op jit(solution)/shard_map/ppermute | solution.py:23
  155.5 50.2 %collective-permute-start.24 = (bf16[4,96,128]{2,1,0:T(8,128)(2,1)S(1)}, bf16[4,96,128]{2,1,0:T(8,128)(2,1)S(1)}, u32[]{:S(2)}, u32[]{:S(2)}) collective-permute-start(bf16[4,96,128]{2,1,0:T(8,128)(2,1)S(1)} %pad_maximum_fusion.19), channel_id=1, source_target_pairs={{0,496},{16,0},{32,16},{48,32},{64,48},{80,64},{96,80},{112,96},{1... | collective-permute-start | bytes 294920 | tf_op jit(solution)/shard_map/ppermute | solution.py:23
  157.5 48.3 %collective-permute-start.23 = (bf16[4,96,128]{2,1,0:T(8,128)(2,1)S(1)}, bf16[4,96,128]{2,1,0:T(8,128)(2,1)S(1)}, u32[]{:S(2)}, u32[]{:S(2)}) collective-permute-start(bf16[4,96,128]{2,1,0:T(8,128)(2,1)S(1)} %pad_maximum_fusion.18), channel_id=1, source_target_pairs={{0,480},{16,496},{32,0},{48,16},{64,32},{80,48},{96,64},{112,80},{... | collective-permute-start | bytes 294920 | tf_op jit(solution)/shard_map/ppermute | solution.py:23
  159.4 46.3 %collective-permute-start.22 = (bf16[4,96,128]{2,1,0:T(8,128)(2,1)S(1)}, bf16[4,96,128]{2,1,0:T(8,128)(2,1)S(1)}, u32[]{:S(2)}, u32[]{:S(2)}) collective-permute-start(bf16[4,96,128]{2,1,0:T(8,128)(2,1)S(1)} %pad_maximum_fusion.17), channel_id=1, source_target_pairs={{0,464},{16,480},{32,496},{48,0},{64,16},{80,32},{96,48},{112,64},... | collective-permute-start | bytes 294920 | tf_op jit(solution)/shard_map/ppermute | solution.py:23
  161.4 44.3 %collective-permute-start.21 = (bf16[4,96,128]{2,1,0:T(8,128)(2,1)S(1)}, bf16[4,96,128]{2,1,0:T(8,128)(2,1)S(1)}, u32[]{:S(2)}, u32[]{:S(2)}) collective-permute-start(bf16[4,96,128]{2,1,0:T(8,128)(2,1)S(1)} %pad_maximum_fusion.16), channel_id=1, source_target_pairs={{0,48},{16,64},{32,80},{48,96},{64,112},{80,128},{96,144},{112,160... | collective-permute-start | bytes 294920 | tf_op jit(solution)/shard_map/ppermute | solution.py:23
  165.1 6.2 %collective-permute-start.17 = (bf16[3,96,128]{2,1,0:T(8,128)(2,1)S(1)}, bf16[3,96,128]{2,1,0:T(8,128)(2,1)S(1)}, u32[]{:S(2)}, u32[]{:S(2)}) collective-permute-start(bf16[3,96,128]{2,1,0:T(8,128)(2,1)S(1)} %get-tuple-element.69), channel_id=1, source_target_pairs={{0,1},{1,2},{2,3},{3,4},{4,5},{5,6},{6,7},{7,8},{8,9},{9,10},{10,1... | collective-permute-start | bytes 221192 | tf_op jit(solution)/shard_map/ppermute | solution.py:18
  171.4 14.0 %collective-permute-start.18 = (bf16[3,96,128]{2,1,0:T(8,128)(2,1)S(1)}, bf16[3,96,128]{2,1,0:T(8,128)(2,1)S(1)}, u32[]{:S(2)}, u32[]{:S(2)}) collective-permute-start(bf16[3,96,128]{2,1,0:T(8,128)(2,1)S(1)} %get-tuple-element.68), channel_id=1, source_target_pairs={{1,0},{2,1},{3,2},{4,3},{5,4},{6,5},{7,6},{8,7},{9,8},{10,9},{11,1... | collective-permute-start | bytes 221192 | tf_op jit(solution)/shard_map/ppermute | solution.py:18
  185.4 9.8 %collective-permute-start.19 = (bf16[4,96,128]{2,1,0:T(8,128)(2,1)S(1)}, bf16[4,96,128]{2,1,0:T(8,128)(2,1)S(1)}, u32[]{:S(2)}, u32[]{:S(2)}) collective-permute-start(bf16[4,96,128]{2,1,0:T(8,128)(2,1)S(1)} %pad_maximum_fusion.14), channel_id=1, source_target_pairs={{0,16},{16,32},{32,48},{48,64},{64,80},{80,96},{96,112},{112,128},... | collective-permute-start | bytes 294920 | tf_op jit(solution)/shard_map/ppermute | solution.py:23
  195.2 10.4 %collective-permute-start.20 = (bf16[4,96,128]{2,1,0:T(8,128)(2,1)S(1)}, bf16[4,96,128]{2,1,0:T(8,128)(2,1)S(1)}, u32[]{:S(2)}, u32[]{:S(2)}) collective-permute-start(bf16[4,96,128]{2,1,0:T(8,128)(2,1)S(1)} %pad_maximum_fusion.15), channel_id=1, source_target_pairs={{0,32},{16,48},{32,64},{48,80},{64,96},{80,112},{96,128},{112,144}... | collective-permute-start | bytes 294920 | tf_op jit(solution)/shard_map/ppermute | solution.py:23

commit v13 on v9

--- a/solution.py
+++ b/solution.py
@@ -67,7 +67,7 @@
         b - (group_span - 1) if b < group_span - 1 else b - group_span + 2 for b in range(buckets)
     ]
     bucket_of = {o: b for b, o in enumerate(offsets)}
-    shifts = [o for o in offsets if o > 0] + [o for o in offsets if o < 0]
+    shifts = [o for o in offsets if o > 0] + [o for o in offsets if o < 0][::-1]
 
     boundary_blocks = shifted_open(blocks[knots - 3 :], "seg", 1)
     lower_blocks = jnp.concatenate([boundary_blocks, blocks], axis=0)

time: 157 us -> 158 us (level)
    ppermute x18, starting transfers between devices: 67.9 us -> 65.9 us  [shifted_ring(): lax.ppermute(value, axis, [(i, (i + steps) % count) for i in range(count)])]
    ppermute x18, waiting for transfers between devices: 4.14 us -> 5.81 us  [shifted_ring(): lax.ppermute(value, axis, [(i, (i + steps) % count) for i in range(count)])]
  transfers between devices with their start and end apart: 25 -> 25, of which waited for: 5 -> 3; matrix products, arithmetic and copies ran while one was open for 14% -> 13% of each run, Pallas kernels for 1% -> 1%
where the time goes in v13:
time: 158 us; the launch traced here: 157 us
  starting transfers between devices  111 us (70%)
  matrix products  13.8 us (9%)
  other arithmetic  10.6 us (7%)
  waiting for transfers between devices  9.21 us (6%)
  local copies, waits for them, and re-layouts  8.64 us (5%)
  Pallas kernels  2.21 us (1%)
    ppermute x18, starting transfers between devices, shifted_ring(): lax.ppermute(value, axis, [(i, (i + steps) % count) for i in range(count)])  65.9 us
    ppermute x7, starting transfers between devices, shifted_open(): lax.ppermute(value, axis, [(source, source + steps) for source in range(i...  45.2 us
    ppermute x18, waiting for transfers between devices, shifted_ring(): lax.ppermute(value, axis, [(i, (i + steps) % count) for i in range(count)])  5.81 us
    dot_general x2, matrix products, body(): jnp.einsum('kamb,mbr->kar', weight, stacked, preferred_element_type=jnp.f...  5.39 us
    ppermute x7, waiting for transfers between devices, shifted_open(): lax.ppermute(value, axis, [(source, source + steps) for source in range(i...  3.39 us
    add x1, other arithmetic, body(): band_weight + jnp.einsum('km,kba->kamb', place, lower_blocks[3 - step:3 -...  3.18 us
  transfers between devices with their start and end apart: 25, of which 3 were waited for; matrix products, arithmetic and copies ran while one was open for 13% of the time, Pallas kernels for 1%

profile of v13, /device:TPU:24, one launch (start us, length us, event | category | flops | bytes accessed | tf_op | source)
XLA Modules:
  0.0 156.6 jit_solution(10120490183380845288)
XLA Ops:
  0.0 1.0 slice_bitcast_fusion
  1.0 8.8 %collective-permute-start = (bf16[3,4,96,96]{3,2,1,0:T(8,128)(2,1)S(1)}, bf16[3,4,96,96]{3,2,1,0:T(8,128)(2,1)S(1)}, u32[]{:S(2)}, u32[]{:S(2)}) collective-permute-start(bf16[3,4,96,96]{3,2,1,0:T(8,128)(2,1)S(1)} %slice_bitcast_fusion), channel_id=1, source_target_pairs={{0,1},{1,2},{2,3},{3,4},{4,5},{5,6},{6,7},{7,8},{8,9},{9,10},{10,1... | collective-permute-start | bytes 663560 | tf_op jit(solution)/shard_map/ppermute | solution.py:18
  9.8 0.7 iota_compare_fusion.8
  10.7 0.8 fusion.88
  11.5 0.7 fusion.73
  12.5 1.0 fusion.27
  14.3 1.2 fusion.42
  15.4 8.1 %collective-permute-start.8 = (bf16[11,96,128]{2,1,0:T(8,128)(2,1)S(1)}, bf16[11,96,128]{2,1,0:T(8,128)(2,1)S(1)}, u32[]{:S(2)}, u32[]{:S(2)}) collective-permute-start(bf16[11,96,128]{2,1,0:T(8,128)(2,1)S(1)} %get-tuple-element.66), channel_id=1, source_target_pairs={{0,464},{16,480},{32,496},{48,0},{64,16},{80,32},{96,48},{112,64},... | collective-permute-start | bytes 811016 | tf_op jit(solution)/shard_map/ppermute | solution.py:23
  23.6 2.5 %collective-permute-start.4 = (bf16[11,96,128]{2,1,0:T(8,128)(2,1)}, bf16[11,96,128]{2,1,0:T(8,128)(2,1)}, u32[]{:S(2)}, u32[]{:S(2)}) collective-permute-start(bf16[11,96,128]{2,1,0:T(8,128)(2,1)} %get-tuple-element.67), channel_id=1, source_target_pairs={{0,32},{16,48},{32,64},{48,80},{64,96},{80,112},{96,128},{112,144}... | collective-permute-start | bytes 811016 | tf_op jit(solution)/shard_map/ppermute | solution.py:23
  26.1 1.9 %collective-permute-start.5 = (bf16[11,96,128]{2,1,0:T(8,128)(2,1)}, bf16[11,96,128]{2,1,0:T(8,128)(2,1)}, u32[]{:S(2)}, u32[]{:S(2)}) collective-permute-start(bf16[11,96,128]{2,1,0:T(8,128)(2,1)} %get-tuple-element.68), channel_id=1, source_target_pairs={{0,48},{16,64},{32,80},{48,96},{64,112},{80,128},{96,144},{112,160... | collective-permute-start | bytes 811016 | tf_op jit(solution)/shard_map/ppermute | solution.py:23
  28.0 7.3 %collective-permute-start.6 = (bf16[11,96,128]{2,1,0:T(8,128)(2,1)}, bf16[11,96,128]{2,1,0:T(8,128)(2,1)}, u32[]{:S(2)}, u32[]{:S(2)}) collective-permute-start(bf16[11,96,128]{2,1,0:T(8,128)(2,1)} %get-tuple-element.69), channel_id=1, source_target_pairs={{0,496},{16,0},{32,16},{48,32},{64,48},{80,64},{96,80},{112,96},{1... | collective-permute-start | bytes 811016 | tf_op jit(solution)/shard_map/ppermute | solution.py:23
  36.8 1.7 %multiply_bitcast_fusion = bf16[8,96,12,96]{3,1,2,0:T(8,128)(2,1)} fusion(bf16[12,8]{0,1:T(8,128)(2,1)S(1)} %copy.56, bf16[12,96,96]{2,1,0:T(8,128)(2,1)S(1)} %constant_dynamic-update-slice_fusion), kind=kLoop, calls=%fused_computation.6 | loop fusion | flops 884736 | bytes 1990848 | tf_op jit(solution)/shard_map/kf,fab->kafb/transpose | solution.py:105
  38.6 0.7 copy.63.pick_ref
  39.2 3.2 %collective-permute-start.7 = (bf16[11,96,128]{2,1,0:T(8,128)(2,1)}, bf16[11,96,128]{2,1,0:T(8,128)(2,1)}, u32[]{:S(2)}, u32[]{:S(2)}) collective-permute-start(bf16[11,96,128]{2,1,0:T(8,128)(2,1)} %get-tuple-element.70), channel_id=1, source_target_pairs={{0,480},{16,496},{32,0},{48,16},{64,32},{80,48},{96,64},{112,80},{... | collective-permute-start | bytes 811016 | tf_op jit(solution)/shard_map/ppermute | solution.py:23
  42.5 0.9 maximum_bitcast_fusion.3
  43.4 0.8 copy.52
  44.2 0.8 copy.53
  45.0 0.8 copy.54
  45.8 1.9 %collective-permute-start.3 = (bf16[11,96,128]{2,1,0:T(8,128)(2,1)}, bf16[11,96,128]{2,1,0:T(8,128)(2,1)}, u32[]{:S(2)}, u32[]{:S(2)}) collective-permute-start(bf16[11,96,128]{2,1,0:T(8,128)(2,1)} %get-tuple-element.71), channel_id=1, source_target_pairs={{0,16},{16,32},{32,48},{48,64},{64,80},{80,96},{96,112},{112,128},... | collective-permute-start | bytes 811016 | tf_op jit(solution)/shard_map/ppermute | solution.py:23
  47.8 3.2 %bitcast_add_fusion = bf16[8,96,14,96]{3,1,2,0:T(8,128)(2,1)S(1)} fusion(bf16[8,14]{1,0:T(8,128)(2,1)S(1)} %fusion.63, bf16[8,96,96]{1,2,0:T(8,128)(2,1)} %copy.54, bf16[8,14]{1,0:T(8,128)(2,1)S(1)} %get-tuple-element.136, bf16[8,96,96]{1,2,0:T(8,128)(2,1)} %copy.53, bf16[8,14]{1,0:T(8,128)(2,1)S(1)} %get-tuple-element.135, bf16[8,96,96]{1,2,0:T(8,128)(2,1)} %copy.52, ...), kind=kLoop, calls=%fused_computation.3 | loop fusion | flops 13418496 | bytes 3098144 | tf_op jit(solution)/shard_map/add | solution.py:94
  50.9 10.6 %collective-permute-start.1 = (bf16[3,96,128]{2,1,0:T(8,128)(2,1)}, bf16[3,96,128]{2,1,0:T(8,128)(2,1)S(1)}, u32[]{:S(2)}, u32[]{:S(2)}) collective-permute-start(bf16[3,96,128]{2,1,0:T(8,128)(2,1)} %get-tuple-element.64), channel_id=1, source_target_pairs={{0,1},{1,2},{2,3},{3,4},{4,5},{5,6},{6,7},{7,8},{8,9},{9,10},{10,1... | collective-permute-start | bytes 221192 | tf_op jit(solution)/shard_map/ppermute | solution.py:18
  61.5 1.9 %collective-permute-start.2 = (bf16[3,96,128]{2,1,0:T(8,128)(2,1)S(1)}, bf16[3,96,128]{2,1,0:T(8,128)(2,1)}, u32[]{:S(2)}, u32[]{:S(2)}) collective-permute-start(bf16[3,96,128]{2,1,0:T(8,128)(2,1)S(1)} %get-tuple-element.65), channel_id=1, source_target_pairs={{1,0},{2,1},{3,2},{4,3},{5,4},{6,5},{7,6},{8,7},{9,8},{10,9},{11,1... | collective-permute-start | bytes 221192 | tf_op jit(solution)/shard_map/ppermute | solution.py:18
  63.5 2.2 %shard_map.55 = (bf16[12,96,128]{2,1,0:T(8,128)(2,1)}, bf16[12,96,128]{2,1,0:T(8,128)(2,1)}, bf16[6,128]{1,0:T(8,128)(2,1)}) custom-call(s32[6,2]{1,0:T(8,128)} %copy.63.pick_ref, bf16[11,96,128]{2,1,0:T(8,128)(2,1)} %collective-permute-done.3.refs_0_, bf16[11,96,128]{2,1,0:T(8,128)(2,1)} %collective-permute-done.4.refs_1_, ...), custom_call_target="tpu_custom_call" | custom-call | tf_op jit(solution)/shard_map/pallas_call | solution.py:45
  65.7 0.7 slice_convert_fusion
  66.5 1.3 fusion.25
  67.7 2.2 %convolution_bitcast_fusion = f32[8,96,128]{2,1,0:T(8,128)S(1)} fusion(bf16[12,96,128]{2,1,0:T(8,128)(2,1)} %get-tuple-element.20, bf16[12,8]{0,1:T(8,128)(2,1)S(1)} %copy.56, bf16[12,96,96]{2,1,0:T(8,128)(2,1)} %copy-done.6), kind=kOutput, calls=%fused_computation.13 | convolution fusion | flops 227377152 | bytes 909504 | tf_op jit(solution)/shard_map/kamb,mbr->kar/dot_general | solution.py:172
  70.5 3.4 %collective-permute-done.2 = bf16[3,96,128]{2,1,0:T(8,128)(2,1)} collective-permute-done((bf16[3,96,128]{2,1,0:T(8,128)(2,1)S(1)}, bf16[3,96,128]{2,1,0:T(8,128)(2,1)}, u32[]{:S(2)}, u32[]{:S(2)}) %collective-permute-start.2) | collective-permute-done | bytes 73760 | tf_op jit(solution)/shard_map/ppermute | solution.py:18
  73.9 2.6 %fusion.49 = (bf16[8,96,128]{2,1,0:T(8,128)(2,1)S(1)}, f32[8,96,128]{2,1,0:T(8,128)}) fusion(f32[1,8,96,128]{3,2,1,0:T(8,128)S(1)} %copy-done.2, f32[8,96,128]{2,0,1:T(8,128)S(1)} %fusion.25, f32[8,96,128]{2,1,0:T(8,128)S(1)} %convolution_bitcast_fusion, bf16[8,96,14,96]{3,1,2,0:T(8,128)(2,1)S(1)} %bitcast_add_fusion, ...), kind=kOutput, calls=%fused_computation.134 | convolution fusion | flops 265273344 | bytes 4177920 | tf_op jit(solution)/shard_map/kamb,mbr->kar/dot_general | solution.py:170
  77.8 2.2 %collective-permute-start.10 = (bf16[3,96,128]{2,1,0:T(8,128)(2,1)S(1)}, bf16[3,96,128]{2,1,0:T(8,128)(2,1)S(1)}, u32[]{:S(2)}, u32[]{:S(2)}) collective-permute-start(bf16[3,96,128]{2,1,0:T(8,128)(2,1)S(1)} %get-tuple-element.62), channel_id=1, source_target_pairs={{1,0},{2,1},{3,2},{4,3},{5,4},{6,5},{7,6},{8,7},{9,8},{10,9},{11,1... | collective-permute-start | bytes 221192 | tf_op jit(solution)/shard_map/ppermute | solution.py:18
  80.0 9.9 %collective-permute-start.9 = (bf16[3,96,128]{2,1,0:T(8,128)(2,1)}, bf16[3,96,128]{2,1,0:T(8,128)(2,1)S(1)}, u32[]{:S(2)}, u32[]{:S(2)}) collective-permute-start(bf16[3,96,128]{2,1,0:T(8,128)(2,1)} %get-tuple-element.63), channel_id=1, source_target_pairs={{0,1},{1,2},{2,3},{3,4},{4,5},{5,6},{6,7},{7,8},{8,9},{9,10},{10,1... | collective-permute-start | bytes 221192 | tf_op jit(solution)/shard_map/ppermute | solution.py:18
  90.3 1.9 %collective-permute-start.11 = (bf16[4,96,128]{2,1,0:T(8,128)(2,1)S(1)}, bf16[4,96,128]{2,1,0:T(8,128)(2,1)S(1)}, u32[]{:S(2)}, u32[]{:S(2)}) collective-permute-start(bf16[4,96,128]{2,1,0:T(8,128)(2,1)S(1)} %pad_maximum_fusion.30), channel_id=1, source_target_pairs={{0,16},{16,32},{32,48},{48,64},{64,80},{80,96},{96,112},{112,128},... | collective-permute-start | bytes 294920 | tf_op jit(solution)/shard_map/ppermute | solution.py:23
  92.3 1.9 %collective-permute-start.12 = (bf16[4,96,128]{2,1,0:T(8,128)(2,1)S(1)}, bf16[4,96,128]{2,1,0:T(8,128)(2,1)S(1)}, u32[]{:S(2)}, u32[]{:S(2)}) collective-permute-start(bf16[4,96,128]{2,1,0:T(8,128)(2,1)S(1)} %pad_maximum_fusion.31), channel_id=1, source_target_pairs={{0,32},{16,48},{32,64},{48,80},{64,96},{80,112},{96,128},{112,144}... | collective-permute-start | bytes 294920 | tf_op jit(solution)/shard_map/ppermute | solution.py:23
  94.2 1.9 %collective-permute-start.13 = (bf16[4,96,128]{2,1,0:T(8,128)(2,1)S(1)}, bf16[4,96,128]{2,1,0:T(8,128)(2,1)S(1)}, u32[]{:S(2)}, u32[]{:S(2)}) collective-permute-start(bf16[4,96,128]{2,1,0:T(8,128)(2,1)S(1)} %pad_maximum_fusion.32), channel_id=1, source_target_pairs={{0,48},{16,64},{32,80},{48,96},{64,112},{80,128},{96,144},{112,160... | collective-permute-start | bytes 294920 | tf_op jit(solution)/shard_map/ppermute | solution.py:23
  96.2 7.5 %collective-permute-start.14 = (bf16[4,96,128]{2,1,0:T(8,128)(2,1)S(1)}, bf16[4,96,128]{2,1,0:T(8,128)(2,1)S(1)}, u32[]{:S(2)}, u32[]{:S(2)}) collective-permute-start(bf16[4,96,128]{2,1,0:T(8,128)(2,1)S(1)} %pad_maximum_fusion.33), channel_id=1, source_target_pairs={{0,496},{16,0},{32,16},{48,32},{64,48},{80,64},{96,80},{112,96},{1... | collective-permute-start | bytes 294920 | tf_op jit(solution)/shard_map/ppermute | solution.py:23
  103.8 3.6 %collective-permute-start.15 = (bf16[4,96,128]{2,1,0:T(8,128)(2,1)S(1)}, bf16[4,96,128]{2,1,0:T(8,128)(2,1)S(1)}, u32[]{:S(2)}, u32[]{:S(2)}) collective-permute-start(bf16[4,96,128]{2,1,0:T(8,128)(2,1)S(1)} %pad_maximum_fusion.34), channel_id=1, source_target_pairs={{0,480},{16,496},{32,0},{48,16},{64,32},{80,48},{96,64},{112,80},{... | collective-permute-start | bytes 294920 | tf_op jit(solution)/shard_map/ppermute | solution.py:23
  107.5 3.2 %collective-permute-start.16 = (bf16[4,96,128]{2,1,0:T(8,128)(2,1)S(1)}, bf16[4,96,128]{2,1,0:T(8,128)(2,1)S(1)}, u32[]{:S(2)}, u32[]{:S(2)}) collective-permute-start(bf16[4,96,128]{2,1,0:T(8,128)(2,1)S(1)} %pad_maximum_fusion.35), channel_id=1, source_target_pairs={{0,464},{16,480},{32,496},{48,0},{64,16},{80,32},{96,48},{112,64},... | collective-permute-start | bytes 294920 | tf_op jit(solution)/shard_map/ppermute | solution.py:23
  110.9 2.9 %collective-permute-done.16 = bf16[4,96,128]{2,1,0:T(8,128)(2,1)S(1)} collective-permute-done((bf16[4,96,128]{2,1,0:T(8,128)(2,1)S(1)}, bf16[4,96,128]{2,1,0:T(8,128)(2,1)S(1)}, u32[]{:S(2)}, u32[]{:S(2)}) %collective-permute-start.16) | collective-permute-done | bytes 98336 | tf_op jit(solution)/shard_map/ppermute | solution.py:23
  114.1 2.3 %fusion.32 = (bf16[8,96,128]{2,1,0:T(8,128)(2,1)S(1)}, f32[8,96,128]{2,1,0:T(8,128)S(1)}) fusion(f32[8,96,128]{2,1,0:T(8,128)S(1)} %copy-done.5, f32[1,8,96,128]{3,2,1,0:T(8,128)S(1)} %copy-done.3, f32[8,96,128]{2,0,1:T(8,128)S(1)} %fusion.23, bf16[26,96,128]{2,1,0:T(8,128)(2,1)S(1)} %get-tuple-element.85, bf16[8,96,12,96]{3,1,2,0:T(8,128)(2,1)S(1)} %copy-done.4, ...), kind=kOutput, calls=%fused_computation.55 | convolution fusion | flops 493535232 | bytes 6242304 | tf_op jit(solution)/shard_map/kamb,mbr->kar/dot_general | solution.py:176
  116.9 1.9 %collective-permute-start.18 = (bf16[3,96,128]{2,1,0:T(8,128)(2,1)S(1)}, bf16[3,96,128]{2,1,0:T(8,128)(2,1)S(1)}, u32[]{:S(2)}, u32[]{:S(2)}) collective-permute-start(bf16[3,96,128]{2,1,0:T(8,128)(2,1)S(1)} %get-tuple-element.60), channel_id=1, source_target_pairs={{1,0},{2,1},{3,2},{4,3},{5,4},{6,5},{7,6},{8,7},{9,8},{10,9},{11,1... | collective-permute-start | bytes 221192 | tf_op jit(solution)/shard_map/ppermute | solution.py:18
  118.8 9.9 %collective-permute-start.17 = (bf16[3,96,128]{2,1,0:T(8,128)(2,1)S(1)}, bf16[3,96,128]{2,1,0:T(8,128)(2,1)S(1)}, u32[]{:S(2)}, u32[]{:S(2)}) collective-permute-start(bf16[3,96,128]{2,1,0:T(8,128)(2,1)S(1)} %get-tuple-element.61), channel_id=1, source_target_pairs={{0,1},{1,2},{2,3},{3,4},{4,5},{5,6},{6,7},{7,8},{8,9},{9,10},{10,1... | collective-permute-start | bytes 221192 | tf_op jit(solution)/shard_map/ppermute | solution.py:18
  129.1 1.9 %collective-permute-start.19 = (bf16[4,96,128]{2,1,0:T(8,128)(2,1)S(1)}, bf16[4,96,128]{2,1,0:T(8,128)(2,1)S(1)}, u32[]{:S(2)}, u32[]{:S(2)}) collective-permute-start(bf16[4,96,128]{2,1,0:T(8,128)(2,1)S(1)} %pad_maximum_fusion.36), channel_id=1, source_target_pairs={{0,16},{16,32},{32,48},{48,64},{64,80},{80,96},{96,112},{112,128},... | collective-permute-start | bytes 294920 | tf_op jit(solution)/shard_map/ppermute | solution.py:23
  131.1 1.9 %collective-permute-start.20 = (bf16[4,96,128]{2,1,0:T(8,128)(2,1)S(1)}, bf16[4,96,128]{2,1,0:T(8,128)(2,1)S(1)}, u32[]{:S(2)}, u32[]{:S(2)}) collective-permute-start(bf16[4,96,128]{2,1,0:T(8,128)(2,1)S(1)} %pad_maximum_fusion.37), channel_id=1, source_target_pairs={{0,32},{16,48},{32,64},{48,80},{64,96},{80,112},{96,128},{112,144}... | collective-permute-start | bytes 294920 | tf_op jit(solution)/shard_map/ppermute | solution.py:23
  133.0 1.9 %collective-permute-start.21 = (bf16[4,96,128]{2,1,0:T(8,128)(2,1)S(1)}, bf16[4,96,128]{2,1,0:T(8,128)(2,1)S(1)}, u32[]{:S(2)}, u32[]{:S(2)}) collective-permute-start(bf16[4,96,128]{2,1,0:T(8,128)(2,1)S(1)} %pad_maximum_fusion.38), channel_id=1, source_target_pairs={{0,48},{16,64},{32,80},{48,96},{64,112},{80,128},{96,144},{112,160... | collective-permute-start | bytes 294920 | tf_op jit(solution)/shard_map/ppermute | solution.py:23
  135.0 7.5 %collective-permute-start.22 = (bf16[4,96,128]{2,1,0:T(8,128)(2,1)S(1)}, bf16[4,96,128]{2,1,0:T(8,128)(2,1)S(1)}, u32[]{:S(2)}, u32[]{:S(2)}) collective-permute-start(bf16[4,96,128]{2,1,0:T(8,128)(2,1)S(1)} %pad_maximum_fusion.39), channel_id=1, source_target_pairs={{0,496},{16,0},{32,16},{48,32},{64,48},{80,64},{96,80},{112,96},{1... | collective-permute-start | bytes 294920 | tf_op jit(solution)/shard_map/ppermute | solution.py:23
  142.6 4.3 %collective-permute-start.23 = (bf16[4,96,128]{2,1,0:T(8,128)(2,1)S(1)}, bf16[4,96,128]{2,1,0:T(8,128)(2,1)S(1)}, u32[]{:S(2)}, u32[]{:S(2)}) collective-permute-start(bf16[4,96,128]{2,1,0:T(8,128)(2,1)S(1)} %pad_maximum_fusion.40), channel_id=1, source_target_pairs={{0,480},{16,496},{32,0},{48,16},{64,32},{80,48},{96,64},{112,80},{... | collective-permute-start | bytes 294920 | tf_op jit(solution)/shard_map/ppermute | solution.py:23
  146.9 3.2 %collective-permute-start.24 = (bf16[4,96,128]{2,1,0:T(8,128)(2,1)S(1)}, bf16[4,96,128]{2,1,0:T(8,128)(2,1)S(1)}, u32[]{:S(2)}, u32[]{:S(2)}) collective-permute-start(bf16[4,96,128]{2,1,0:T(8,128)(2,1)S(1)} %pad_maximum_fusion.41), channel_id=1, source_target_pairs={{0,464},{16,480},{32,496},{48,0},{64,16},{80,32},{96,48},{112,64},... | collective-permute-start | bytes 294920 | tf_op jit(solution)/shard_map/ppermute | solution.py:23
  150.3 2.9 %collective-permute-done.24 = bf16[4,96,128]{2,1,0:T(8,128)(2,1)S(1)} collective-permute-done((bf16[4,96,128]{2,1,0:T(8,128)(2,1)S(1)}, bf16[4,96,128]{2,1,0:T(8,128)(2,1)S(1)}, u32[]{:S(2)}, u32[]{:S(2)}) %collective-permute-start.24) | collective-permute-done | bytes 98336 | tf_op jit(solution)/shard_map/ppermute | solution.py:23
  153.5 3.1 %fusion.11 = f32[1,8,96,128]{3,2,1,0:T(8,128)} fusion(f32[8,96,128]{2,1,0:T(8,128)S(1)} %get-tuple-element.130, bf16[8,96,12,96]{3,1,2,0:T(8,128)(2,1)S(1)} %copy-done.4, bf16[8,96,14,96]{3,1,2,0:T(8,128)(2,1)S(1)} %bitcast_add_fusion, bf16[26,96,128]{2,1,0:T(8,128)(2,1)S(1)} %get-tuple-element.73, f32[8,96,128]{2,0,1:T(8,128)S(1)} %fusion.21, ...), kind=kOutput, calls=%fused_computation.22 | convolution fusion | flops 494125056 | bytes 6438912 | tf_op jit(solution)/shard_map/kamb,mbr->kar/dot_general | solution.py:176
  (131 shorter events, 6.9 us)
Async XLA Ops:
  0.0 13.9 %copy-start = (bf16[1,1,6,2,96,96]{5,4,3,2,1,0:T(8,128)(2,1)S(1)}, bf16[1,1,6,2,96,96]{5,4,3,2,1,0:T(8,128)(2,1)}, u32[]{:S(2)}) copy-start(bf16[1,1,6,2,96,96]{5,4,3,2,1,0:T(8,128)(2,1)} %param.11) | copy-start | bytes 663556
  1.0 38.2 %collective-permute-start = (bf16[3,4,96,96]{3,2,1,0:T(8,128)(2,1)S(1)}, bf16[3,4,96,96]{3,2,1,0:T(8,128)(2,1)S(1)}, u32[]{:S(2)}, u32[]{:S(2)}) collective-permute-start(bf16[3,4,96,96]{3,2,1,0:T(8,128)(2,1)S(1)} %slice_bitcast_fusion), channel_id=1, source_target_pairs={{0,1},{1,2},{2,3},{3,4},{4,5},{5,6},{6,7},{7,8},{8,9},{9,10},{10,1... | collective-permute-start | bytes 663560 | tf_op jit(solution)/shard_map/ppermute | solution.py:18
  12.5 22.9 %copy-start.9 = (s32[1,1,6]{2,1,0:T(1,128)S(1)}, s32[1,1,6]{2,1,0:T(1,128)}, u32[]{:S(2)}) copy-start(s32[1,1,6]{2,1,0:T(1,128)} %param.10) | copy-start | bytes 76
  14.3 28.2 %copy-start.1 = (bf16[1,8,4,96,96]{4,3,2,1,0:T(8,128)(2,1)S(1)}, bf16[1,8,4,96,96]{4,3,2,1,0:T(8,128)(2,1)}, u32[]{:S(2)}) copy-start(bf16[1,8,4,96,96]{4,3,2,1,0:T(8,128)(2,1)} %param.8) | copy-start | bytes 1769476
  15.4 30.4 %collective-permute-start.8 = (bf16[11,96,128]{2,1,0:T(8,128)(2,1)S(1)}, bf16[11,96,128]{2,1,0:T(8,128)(2,1)S(1)}, u32[]{:S(2)}, u32[]{:S(2)}) collective-permute-start(bf16[11,96,128]{2,1,0:T(8,128)(2,1)S(1)} %get-tuple-element.66), channel_id=1, source_target_pairs={{0,464},{16,480},{32,496},{48,0},{64,16},{80,32},{96,48},{112,64},... | collective-permute-start | bytes 811016 | tf_op jit(solution)/shard_map/ppermute | solution.py:23
  23.6 27.4 %collective-permute-start.4 = (bf16[11,96,128]{2,1,0:T(8,128)(2,1)}, bf16[11,96,128]{2,1,0:T(8,128)(2,1)}, u32[]{:S(2)}, u32[]{:S(2)}) collective-permute-start(bf16[11,96,128]{2,1,0:T(8,128)(2,1)} %get-tuple-element.67), channel_id=1, source_target_pairs={{0,32},{16,48},{32,64},{48,80},{64,96},{80,112},{96,128},{112,144}... | collective-permute-start | bytes 811016 | tf_op jit(solution)/shard_map/ppermute | solution.py:23
  26.1 35.4 %collective-permute-start.5 = (bf16[11,96,128]{2,1,0:T(8,128)(2,1)}, bf16[11,96,128]{2,1,0:T(8,128)(2,1)}, u32[]{:S(2)}, u32[]{:S(2)}) collective-permute-start(bf16[11,96,128]{2,1,0:T(8,128)(2,1)} %get-tuple-element.68), channel_id=1, source_target_pairs={{0,48},{16,64},{32,80},{48,96},{64,112},{80,128},{96,144},{112,160... | collective-permute-start | bytes 811016 | tf_op jit(solution)/shard_map/ppermute | solution.py:23
  28.0 35.4 %collective-permute-start.6 = (bf16[11,96,128]{2,1,0:T(8,128)(2,1)}, bf16[11,96,128]{2,1,0:T(8,128)(2,1)}, u32[]{:S(2)}, u32[]{:S(2)}) collective-permute-start(bf16[11,96,128]{2,1,0:T(8,128)(2,1)} %get-tuple-element.69), channel_id=1, source_target_pairs={{0,496},{16,0},{32,16},{48,32},{64,48},{80,64},{96,80},{112,96},{1... | collective-permute-start | bytes 811016 | tf_op jit(solution)/shard_map/ppermute | solution.py:23
  36.6 5.9 %copy-start.6 = (bf16[12,96,96]{2,1,0:T(8,128)(2,1)}, bf16[12,96,96]{2,1,0:T(8,128)(2,1)S(1)}, u32[]{:S(2)}) copy-start(bf16[12,96,96]{2,1,0:T(8,128)(2,1)S(1)} %constant_dynamic-update-slice_fusion) | copy-start | bytes 663556
  39.2 24.2 %collective-permute-start.7 = (bf16[11,96,128]{2,1,0:T(8,128)(2,1)}, bf16[11,96,128]{2,1,0:T(8,128)(2,1)}, u32[]{:S(2)}, u32[]{:S(2)}) collective-permute-start(bf16[11,96,128]{2,1,0:T(8,128)(2,1)} %get-tuple-element.70), channel_id=1, source_target_pairs={{0,480},{16,496},{32,0},{48,16},{64,32},{80,48},{96,64},{112,80},{... | collective-permute-start | bytes 811016 | tf_op jit(solution)/shard_map/ppermute | solution.py:23
  45.8 1.9 %copy-start.7 = (bf16[11,96,128]{2,1,0:T(8,128)(2,1)}, bf16[11,96,128]{2,1,0:T(8,128)(2,1)S(1)}, u32[]{:S(2)}) copy-start(bf16[11,96,128]{2,1,0:T(8,128)(2,1)S(1)} %collective-permute-done.8.refs_5_) | copy-start | bytes 811012
  45.8 17.7 %collective-permute-start.3 = (bf16[11,96,128]{2,1,0:T(8,128)(2,1)}, bf16[11,96,128]{2,1,0:T(8,128)(2,1)}, u32[]{:S(2)}, u32[]{:S(2)}) collective-permute-start(bf16[11,96,128]{2,1,0:T(8,128)(2,1)} %get-tuple-element.71), channel_id=1, source_target_pairs={{0,16},{16,32},{32,48},{48,64},{64,80},{80,96},{96,112},{112,128},... | collective-permute-start | bytes 811016 | tf_op jit(solution)/shard_map/ppermute | solution.py:23
  50.9 19.0 %collective-permute-start.1 = (bf16[3,96,128]{2,1,0:T(8,128)(2,1)}, bf16[3,96,128]{2,1,0:T(8,128)(2,1)S(1)}, u32[]{:S(2)}, u32[]{:S(2)}) collective-permute-start(bf16[3,96,128]{2,1,0:T(8,128)(2,1)} %get-tuple-element.64), channel_id=1, source_target_pairs={{0,1},{1,2},{2,3},{3,4},{4,5},{5,6},{6,7},{7,8},{8,9},{9,10},{10,1... | collective-permute-start | bytes 221192 | tf_op jit(solution)/shard_map/ppermute | solution.py:18
  61.5 12.4 %collective-permute-start.2 = (bf16[3,96,128]{2,1,0:T(8,128)(2,1)S(1)}, bf16[3,96,128]{2,1,0:T(8,128)(2,1)}, u32[]{:S(2)}, u32[]{:S(2)}) collective-permute-start(bf16[3,96,128]{2,1,0:T(8,128)(2,1)S(1)} %get-tuple-element.65), channel_id=1, source_target_pairs={{1,0},{2,1},{3,2},{4,3},{5,4},{6,5},{7,6},{8,7},{9,8},{10,9},{11,1... | collective-permute-start | bytes 221192 | tf_op jit(solution)/shard_map/ppermute | solution.py:18
  66.5 7.4 %copy-start.2 = (f32[1,8,96,128]{3,2,1,0:T(8,128)S(1)}, f32[1,8,96,128]{3,2,1,0:T(8,128)}, u32[]{:S(2)}) copy-start(f32[1,8,96,128]{3,2,1,0:T(8,128)} %param.7) | copy-start | bytes 1179652
  69.9 0.6 copy-start.8
  77.8 36.2 %copy-start.3 = (f32[1,8,96,128]{3,2,1,0:T(8,128)S(1)}, f32[1,8,96,128]{3,2,1,0:T(8,128)}, u32[]{:S(2)}) copy-start(f32[1,8,96,128]{3,2,1,0:T(8,128)} %param.7) | copy-start | bytes 1179652
  77.8 36.2 %copy-start.4 = (bf16[8,96,12,96]{3,1,2,0:T(8,128)(2,1)S(1)}, bf16[8,96,12,96]{3,1,2,0:T(8,128)(2,1)}, u32[]{:S(2)}) copy-start(bf16[8,96,12,96]{3,1,2,0:T(8,128)(2,1)} %multiply_bitcast_fusion) | copy-start | bytes 5308420
  77.8 36.2 %copy-start.5 = (f32[8,96,128]{2,1,0:T(8,128)S(1)}, f32[8,96,128]{2,1,0:T(8,128)}, u32[]{:S(2)}) copy-start(f32[8,96,128]{2,1,0:T(8,128)} %get-tuple-element.128) | copy-start | bytes 1179652
  77.8 26.0 %collective-permute-start.10 = (bf16[3,96,128]{2,1,0:T(8,128)(2,1)S(1)}, bf16[3,96,128]{2,1,0:T(8,128)(2,1)S(1)}, u32[]{:S(2)}, u32[]{:S(2)}) collective-permute-start(bf16[3,96,128]{2,1,0:T(8,128)(2,1)S(1)} %get-tuple-element.62), channel_id=1, source_target_pairs={{1,0},{2,1},{3,2},{4,3},{5,4},{6,5},{7,6},{8,7},{9,8},{10,9},{11,1... | collective-permute-start | bytes 221192 | tf_op jit(solution)/shard_map/ppermute | solution.py:18
  80.0 16.2 %collective-permute-start.9 = (bf16[3,96,128]{2,1,0:T(8,128)(2,1)}, bf16[3,96,128]{2,1,0:T(8,128)(2,1)S(1)}, u32[]{:S(2)}, u32[]{:S(2)}) collective-permute-start(bf16[3,96,128]{2,1,0:T(8,128)(2,1)} %get-tuple-element.63), channel_id=1, source_target_pairs={{0,1},{1,2},{2,3},{3,4},{4,5},{5,6},{6,7},{7,8},{8,9},{9,10},{10,1... | collective-permute-start | bytes 221192 | tf_op jit(solution)/shard_map/ppermute | solution.py:18
  90.3 17.2 %collective-permute-start.11 = (bf16[4,96,128]{2,1,0:T(8,128)(2,1)S(1)}, bf16[4,96,128]{2,1,0:T(8,128)(2,1)S(1)}, u32[]{:S(2)}, u32[]{:S(2)}) collective-permute-start(bf16[4,96,128]{2,1,0:T(8,128)(2,1)S(1)} %pad_maximum_fusion.30), channel_id=1, source_target_pairs={{0,16},{16,32},{32,48},{48,64},{64,80},{80,96},{96,112},{112,128},... | collective-permute-start | bytes 294920 | tf_op jit(solution)/shard_map/ppermute | solution.py:23
  92.3 18.5 %collective-permute-start.12 = (bf16[4,96,128]{2,1,0:T(8,128)(2,1)S(1)}, bf16[4,96,128]{2,1,0:T(8,128)(2,1)S(1)}, u32[]{:S(2)}, u32[]{:S(2)}) collective-permute-start(bf16[4,96,128]{2,1,0:T(8,128)(2,1)S(1)} %pad_maximum_fusion.31), channel_id=1, source_target_pairs={{0,32},{16,48},{32,64},{48,80},{64,96},{80,112},{96,128},{112,144}... | collective-permute-start | bytes 294920 | tf_op jit(solution)/shard_map/ppermute | solution.py:23
  94.2 16.6 %collective-permute-start.13 = (bf16[4,96,128]{2,1,0:T(8,128)(2,1)S(1)}, bf16[4,96,128]{2,1,0:T(8,128)(2,1)S(1)}, u32[]{:S(2)}, u32[]{:S(2)}) collective-permute-start(bf16[4,96,128]{2,1,0:T(8,128)(2,1)S(1)} %pad_maximum_fusion.32), channel_id=1, source_target_pairs={{0,48},{16,64},{32,80},{48,96},{64,112},{80,128},{96,144},{112,160... | collective-permute-start | bytes 294920 | tf_op jit(solution)/shard_map/ppermute | solution.py:23
  96.2 14.6 %collective-permute-start.14 = (bf16[4,96,128]{2,1,0:T(8,128)(2,1)S(1)}, bf16[4,96,128]{2,1,0:T(8,128)(2,1)S(1)}, u32[]{:S(2)}, u32[]{:S(2)}) collective-permute-start(bf16[4,96,128]{2,1,0:T(8,128)(2,1)S(1)} %pad_maximum_fusion.33), channel_id=1, source_target_pairs={{0,496},{16,0},{32,16},{48,32},{64,48},{80,64},{96,80},{112,96},{1... | collective-permute-start | bytes 294920 | tf_op jit(solution)/shard_map/ppermute | solution.py:23
  103.8 7.0 %collective-permute-start.15 = (bf16[4,96,128]{2,1,0:T(8,128)(2,1)S(1)}, bf16[4,96,128]{2,1,0:T(8,128)(2,1)S(1)}, u32[]{:S(2)}, u32[]{:S(2)}) collective-permute-start(bf16[4,96,128]{2,1,0:T(8,128)(2,1)S(1)} %pad_maximum_fusion.34), channel_id=1, source_target_pairs={{0,480},{16,496},{32,0},{48,16},{64,32},{80,48},{96,64},{112,80},{... | collective-permute-start | bytes 294920 | tf_op jit(solution)/shard_map/ppermute | solution.py:23
  107.5 6.2 %collective-permute-start.16 = (bf16[4,96,128]{2,1,0:T(8,128)(2,1)S(1)}, bf16[4,96,128]{2,1,0:T(8,128)(2,1)S(1)}, u32[]{:S(2)}, u32[]{:S(2)}) collective-permute-start(bf16[4,96,128]{2,1,0:T(8,128)(2,1)S(1)} %pad_maximum_fusion.35), channel_id=1, source_target_pairs={{0,464},{16,480},{32,496},{48,0},{64,16},{80,32},{96,48},{112,64},... | collective-permute-start | bytes 294920 | tf_op jit(solution)/shard_map/ppermute | solution.py:23
  116.9 25.7 %collective-permute-start.18 = (bf16[3,96,128]{2,1,0:T(8,128)(2,1)S(1)}, bf16[3,96,128]{2,1,0:T(8,128)(2,1)S(1)}, u32[]{:S(2)}, u32[]{:S(2)}) collective-permute-start(bf16[3,96,128]{2,1,0:T(8,128)(2,1)S(1)} %get-tuple-element.60), channel_id=1, source_target_pairs={{1,0},{2,1},{3,2},{4,3},{5,4},{6,5},{7,6},{8,7},{9,8},{10,9},{11,1... | collective-permute-start | bytes 221192 | tf_op jit(solution)/shard_map/ppermute | solution.py:18
  118.8 16.2 %collective-permute-start.17 = (bf16[3,96,128]{2,1,0:T(8,128)(2,1)S(1)}, bf16[3,96,128]{2,1,0:T(8,128)(2,1)S(1)}, u32[]{:S(2)}, u32[]{:S(2)}) collective-permute-start(bf16[3,96,128]{2,1,0:T(8,128)(2,1)S(1)} %get-tuple-element.61), channel_id=1, source_target_pairs={{0,1},{1,2},{2,3},{3,4},{4,5},{5,6},{6,7},{7,8},{8,9},{9,10},{10,1... | collective-permute-start | bytes 221192 | tf_op jit(solution)/shard_map/ppermute | solution.py:18
  129.1 17.8 %collective-permute-start.19 = (bf16[4,96,128]{2,1,0:T(8,128)(2,1)S(1)}, bf16[4,96,128]{2,1,0:T(8,128)(2,1)S(1)}, u32[]{:S(2)}, u32[]{:S(2)}) collective-permute-start(bf16[4,96,128]{2,1,0:T(8,128)(2,1)S(1)} %pad_maximum_fusion.36), channel_id=1, source_target_pairs={{0,16},{16,32},{32,48},{48,64},{64,80},{80,96},{96,112},{112,128},... | collective-permute-start | bytes 294920 | tf_op jit(solution)/shard_map/ppermute | solution.py:23
  131.1 19.1 %collective-permute-start.20 = (bf16[4,96,128]{2,1,0:T(8,128)(2,1)S(1)}, bf16[4,96,128]{2,1,0:T(8,128)(2,1)S(1)}, u32[]{:S(2)}, u32[]{:S(2)}) collective-permute-start(bf16[4,96,128]{2,1,0:T(8,128)(2,1)S(1)} %pad_maximum_fusion.37), channel_id=1, source_target_pairs={{0,32},{16,48},{32,64},{48,80},{64,96},{80,112},{96,128},{112,144}... | collective-permute-start | bytes 294920 | tf_op jit(solution)/shard_map/ppermute | solution.py:23
  133.0 17.2 %collective-permute-start.21 = (bf16[4,96,128]{2,1,0:T(8,128)(2,1)S(1)}, bf16[4,96,128]{2,1,0:T(8,128)(2,1)S(1)}, u32[]{:S(2)}, u32[]{:S(2)}) collective-permute-start(bf16[4,96,128]{2,1,0:T(8,128)(2,1)S(1)} %pad_maximum_fusion.38), channel_id=1, source_target_pairs={{0,48},{16,64},{32,80},{48,96},{64,112},{80,128},{96,144},{112,160... | collective-permute-start | bytes 294920 | tf_op jit(solution)/shard_map/ppermute | solution.py:23
  135.0 15.2 %collective-permute-start.22 = (bf16[4,96,128]{2,1,0:T(8,128)(2,1)S(1)}, bf16[4,96,128]{2,1,0:T(8,128)(2,1)S(1)}, u32[]{:S(2)}, u32[]{:S(2)}) collective-permute-start(bf16[4,96,128]{2,1,0:T(8,128)(2,1)S(1)} %pad_maximum_fusion.39), channel_id=1, source_target_pairs={{0,496},{16,0},{32,16},{48,32},{64,48},{80,64},{96,80},{112,96},{1... | collective-permute-start | bytes 294920 | tf_op jit(solution)/shard_map/ppermute | solution.py:23
  142.6 7.6 %collective-permute-start.23 = (bf16[4,96,128]{2,1,0:T(8,128)(2,1)S(1)}, bf16[4,96,128]{2,1,0:T(8,128)(2,1)S(1)}, u32[]{:S(2)}, u32[]{:S(2)}) collective-permute-start(bf16[4,96,128]{2,1,0:T(8,128)(2,1)S(1)} %pad_maximum_fusion.40), channel_id=1, source_target_pairs={{0,480},{16,496},{32,0},{48,16},{64,32},{80,48},{96,64},{112,80},{... | collective-permute-start | bytes 294920 | tf_op jit(solution)/shard_map/ppermute | solution.py:23
  146.9 6.2 %collective-permute-start.24 = (bf16[4,96,128]{2,1,0:T(8,128)(2,1)S(1)}, bf16[4,96,128]{2,1,0:T(8,128)(2,1)S(1)}, u32[]{:S(2)}, u32[]{:S(2)}) collective-permute-start(bf16[4,96,128]{2,1,0:T(8,128)(2,1)S(1)} %pad_maximum_fusion.41), channel_id=1, source_target_pairs={{0,464},{16,480},{32,496},{48,0},{64,16},{80,32},{96,48},{112,64},... | collective-permute-start | bytes 294920 | tf_op jit(solution)/shard_map/ppermute | solution.py:23
